TPU v7x, 32 devices: a whole 2x2x4 slice. The times are simulated.
32 devices in a mesh: tile: 8 (over y, x, core), member: 4 (over z).
Axes of the slice: x: 2, y: 2, z: 4, core: 2. Of those that a mesh axis runs over, the one named last changes fastest.
Arguments:
- alpha: float32 [12, 256, 2048], P('member', None, 'tile'), may hold values from -6 to 6
- ensemble: bfloat16 [12, 256, 3, 2048], P('member', None, None, 'tile'), may hold values from -4 to 4
- background: float32 [256, 3, 2048], P(None, None, 'tile'), may hold values from -6 to 6
- measured_values: float32 [256, 3, 2048], P(None, None, 'tile'), may hold values from -6 to 6
- precision_factor: float32 [256, 3, 2048], P(None, None, 'tile'), may hold values from 0.3 to 3
- depth: float32 [256, 2048], P(None, 'tile'), may hold values from 0.5 to 2
- loc_cols: float32 [256, 256], replicated
- loc_rows: float32 [256, 256], replicated
Outputs:
- cost_derivative: float32 [12, 256, 2048], P('member', None, 'tile')
- predicted_final: float32 [256, 3, 2048], P('member', None, 'tile')
All inputs are finite; a program needn't handle non-finite values.
Results may differ from a plain program's by a relative error of at most 0.0003.
Values sent between devices are 32-bit elements; how exact they have to be, the bound alone decides.
No kernel may reach another device: no remote copies, remote signals or barrier semaphores. Data moves between devices by JAX's collectives and lax.ppermute only.
A program may use at most 64 MiB of HBM per device.

v0:
```python
import jax
import jax.numpy as jnp
from jax import lax
from jax.sharding import PartitionSpec as P

STEPS = 2


COURANT = 0.3


def with_halo(x, sides, width):
    for axis, dim in sides:
        count, length = (lax.axis_size(axis), x.shape[dim])
        up = [(i, (i + 1) % count) for i in range(count)]
        down = [(j, i) for i, j in up]
        last = lax.slice_in_dim(x, length - width, length, axis=dim)
        leading = lax.slice_in_dim(x, 0, width, axis=dim)
        before = lax.ppermute(last, axis, up)
        after = lax.ppermute(leading, axis, down)
        x = jnp.concatenate([before, x, after], axis=dim)
    return x


def col_slope(padded):
    return 0.5 * (padded[2:, :, 1:-1] - padded[:-2, :, 1:-1])


def row_slope(padded):
    return 0.5 * (padded[1:-1, :, 2:] - padded[1:-1, :, :-2])


def height_update(free_elevation, depth3_triple, velocity_pad):
    return free_elevation - COURANT * depth3_triple * (
        col_slope(velocity_pad[:, 0:1]) + row_slope(velocity_pad[:, 1:2])
    )


def velocity_update(current_speed, height_pad):
    return current_speed - COURANT * jnp.concatenate(
        [col_slope(height_pad), row_slope(height_pad)], axis=1
    )


def adjoint_height(adj_height, velocity_pad):
    return adj_height + COURANT * (
        col_slope(velocity_pad[:, 0:1]) + row_slope(velocity_pad[:, 1:2])
    )


def adjoint_velocity(adj_velocity, weighted_pad):
    return adj_velocity + COURANT * jnp.concatenate(
        [col_slope(weighted_pad), row_slope(weighted_pad)], axis=1
    )


def widen_pair(field):
    return with_halo(field, (("tile", 2), ("member", 0)), 1)


def widen_single(field):
    return with_halo(field, (("tile", 2), ("member", 0)), 1)


def advance_dynamics(initial_state, depth3_triple, ensemble_coefficient, destination_array):
    free_elevation = initial_state[:, 0:1]
    current_speed = initial_state[:, 1:3]
    for repeat in range(STEPS):
        free_elevation = height_update(free_elevation, depth3_triple, widen_pair(current_speed))
        current_speed = velocity_update(current_speed, widen_single(free_elevation))
    predicted_final = jnp.concatenate([free_elevation, current_speed], axis=1)
    residual_difference = ensemble_coefficient * (predicted_final - destination_array)
    adj_height = residual_difference[:, 0:1]
    adj_velocity = residual_difference[:, 1:3]
    for repeat in range(STEPS):
        summed = adjoint_height(adj_height, widen_pair(adj_velocity))
        weighted = depth3_triple * summed
        adj_velocity = adjoint_velocity(adj_velocity, widen_single(weighted))
        adj_height = summed
    backward_pass = jnp.concatenate([adj_height, adj_velocity], axis=1)
    return (predicted_final, backward_pass)


def body(alpha, ensemble, background, measured_values, precision_factor, depth, loc_cols, loc_rows):
    highest = lax.Precision.HIGHEST
    region = loc_cols.shape[0]
    block_cols = region // lax.axis_size("member")
    col_start = lax.axis_index("member") * block_cols
    localized = jnp.einsum("cd,kdr->kcr", loc_cols, alpha, precision=highest)
    localized = jnp.einsum("kcr,qr->kcq", localized, loc_rows, precision=highest)
    pert_part = ensemble
    increment = lax.psum_scatter(
        jnp.sum(pert_part.astype(jnp.float32) * localized[:, :, None, :], axis=0),
        "member",
        scatter_dimension=0,
        tiled=True,
    )
    initial_state = lax.dynamic_slice_in_dim(background, col_start, block_cols, 0) + increment
    ensemble_coefficient = lax.dynamic_slice_in_dim(precision_factor, col_start, block_cols, 0)
    destination_array = lax.dynamic_slice_in_dim(measured_values, col_start, block_cols, 0)
    depth3_triple = lax.dynamic_slice_in_dim(depth, col_start, block_cols, 0)[:, None, :]
    predicted_final, backward_pass = advance_dynamics(
        initial_state, depth3_triple, ensemble_coefficient, destination_array
    )
    pert_part = ensemble
    projected = jnp.sum(
        pert_part.astype(jnp.float32)
        * lax.all_gather(backward_pass, "member", axis=0, tiled=True)[None],
        axis=2,
    )
    rows_done = jnp.einsum("knr,rq->knq", projected, loc_rows, precision=highest)
    cost_derivative = alpha + jnp.einsum("cd,kcq->kdq", loc_cols, rows_done, precision=highest)
    return (cost_derivative, predicted_final)


def solution(mesh):
    return jax.shard_map(
        body,
        mesh=mesh,
        in_specs=(
            P("member", None, "tile"),
            P("member", None, None, "tile"),
            P(None, None, "tile"),
            P(None, None, "tile"),
            P(None, None, "tile"),
            P(None, "tile"),
            P(),
            P(),
        ),
        out_specs=(P("member", None, "tile"), P("member", None, "tile")),
        check_vma=False,
    )
```

profile of v0, /device:TPU:0, one launch (start us, length us, event | category | flops | bytes accessed | tf_op | source)
XLA Modules:
  0.0 152.1 jit_solution(14191968128710701657)
XLA Ops:
  7.2 2.1 %convolution_bitcast_fusion.1 = f32[3,256,256]{2,1,0:T(8,128)S(1)} fusion(f32[3,256,256]{2,1,0:T(8,128)} %param.8, f32[256,256]{1,0:T(8,128)} %param.14), kind=kOutput, calls=%fused_computation.5 | convolution fusion | flops 603979776 | bytes 1835008 | tf_op jit(solution)/shard_map/cd,kdr->kcr/dot_general | solution.py:89
  11.8 26.1 %reduce-scatter.2.cloned.1.call-done = f32[64,3,256]{2,0,1:T(8,128)} async-done(((f32[256,3,256]{2,0,1:T(8,128)}), f32[64,3,256]{2,0,1:T(8,128)}) %reduce-scatter.2.cloned.1.call-update) | async-done | bytes 196624 | tf_op jit(solution)/shard_map/reduce_scatter | solution.py:92
  39.1 2.6 %collective-permute-start.1 = (f32[64,2,1]{2,0,1:T(8,128)S(1)}, f32[64,2,1]{2,0,1:T(8,128)S(1)}, u32[]{:S(2)}, u32[]{:S(2)}) collective-permute-start(f32[64,2,1]{2,0,1:T(8,128)S(1)} %get-tuple-element.20), channel_id=1, source_target_pairs={{4,0},{8,4},{12,8},{16,12},{20,16},{24,20},{28,24},{0,28},{5,1},{9... | collective-permute-start | bytes 1544 | tf_op jit(solution)/shard_map/ppermute | solution.py:20
  41.7 1.9 %collective-permute-done = f32[64,2,1]{2,0,1:T(8,128)S(1)} collective-permute-done((f32[64,2,1]{2,0,1:T(8,128)S(1)}, f32[64,2,1]{2,0,1:T(8,128)S(1)}, u32[]{:S(2)}, u32[]{:S(2)}) %collective-permute-start) | collective-permute-done | bytes 544 | tf_op jit(solution)/shard_map/ppermute | solution.py:19
  47.4 3.5 %collective-permute-done.3 = f32[1,2,258]{2,0,1:T(1,128)S(1)} collective-permute-done((f32[1,2,258]{2,0,1:T(1,128)S(1)}, f32[1,2,258]{2,0,1:T(1,128)S(1)}, u32[]{:S(2)}, u32[]{:S(2)}) %collective-permute-start.3) | collective-permute-done | bytes 2096 | tf_op jit(solution)/shard_map/ppermute | solution.py:19
  51.1 2.6 %collective-permute-start.5 = (f32[64,1,1]{2,0,1:T(8,128)S(1)}, f32[64,1,1]{2,0,1:T(8,128)S(1)}, u32[]{:S(2)}, u32[]{:S(2)}) collective-permute-start(f32[64,1,1]{2,0,1:T(8,128)S(1)} %get-tuple-element.48), channel_id=1, source_target_pairs={{4,0},{8,4},{12,8},{16,12},{20,16},{24,20},{28,24},{0,28},{5,1},{9... | collective-permute-start | bytes 776 | tf_op jit(solution)/shard_map/ppermute | solution.py:20
  55.4 2.0 %collective-permute-start.7 = (f32[1,1,258]{2,0,1:T(1,128)S(1)}, f32[1,1,258]{2,0,1:T(1,128)S(1)}, u32[]{:S(2)}, u32[]{:S(2)}) collective-permute-start(f32[1,1,258]{2,0,1:T(1,128)S(1)} %get-tuple-element.41), channel_id=1, source_target_pairs={{0,1},{1,2},{2,3},{3,0},{4,5},{5,6},{6,7},{7,4},{8,9},{9,10},{10,1... | collective-permute-start | bytes 3104 | tf_op jit(solution)/shard_map/ppermute | solution.py:19
  61.2 2.6 %collective-permute-start.9 = (f32[64,2,1]{2,0,1:T(8,128)S(1)}, f32[64,2,1]{2,0,1:T(8,128)S(1)}, u32[]{:S(2)}, u32[]{:S(2)}) collective-permute-start(f32[64,2,1]{2,0,1:T(8,128)S(1)} %get-tuple-element.36), channel_id=1, source_target_pairs={{4,0},{8,4},{12,8},{16,12},{20,16},{24,20},{28,24},{0,28},{5,1},{9... | collective-permute-start | bytes 1544 | tf_op jit(solution)/shard_map/ppermute | solution.py:20
  63.8 2.6 %collective-permute-done.8 = f32[64,2,1]{2,0,1:T(8,128)S(1)} collective-permute-done((f32[64,2,1]{2,0,1:T(8,128)S(1)}, f32[64,2,1]{2,0,1:T(8,128)S(1)}, u32[]{:S(2)}, u32[]{:S(2)}) %collective-permute-start.8) | collective-permute-done | bytes 544 | tf_op jit(solution)/shard_map/ppermute | solution.py:19
  66.6 2.0 %collective-permute-start.11 = (f32[1,2,258]{2,0,1:T(1,128)S(1)}, f32[1,2,258]{2,0,1:T(1,128)S(1)}, u32[]{:S(2)}, u32[]{:S(2)}) collective-permute-start(f32[1,2,258]{2,0,1:T(1,128)S(1)} %get-tuple-element.15), channel_id=1, source_target_pairs={{0,1},{1,2},{2,3},{3,0},{4,5},{5,6},{6,7},{7,4},{8,9},{9,10},{10,1... | collective-permute-start | bytes 6200 | tf_op jit(solution)/shard_map/ppermute | solution.py:19
  70.2 1.9 %collective-permute-done.11 = f32[1,2,258]{2,0,1:T(1,128)S(1)} collective-permute-done((f32[1,2,258]{2,0,1:T(1,128)S(1)}, f32[1,2,258]{2,0,1:T(1,128)S(1)}, u32[]{:S(2)}, u32[]{:S(2)}) %collective-permute-start.11) | collective-permute-done | bytes 2096 | tf_op jit(solution)/shard_map/ppermute | solution.py:19
  72.3 2.6 %collective-permute-start.13 = (f32[64,1,1]{2,0,1:T(8,128)S(1)}, f32[64,1,1]{2,0,1:T(8,128)S(1)}, u32[]{:S(2)}, u32[]{:S(2)}) collective-permute-start(f32[64,1,1]{2,0,1:T(8,128)S(1)} %get-tuple-element.46), channel_id=1, source_target_pairs={{4,0},{8,4},{12,8},{16,12},{20,16},{24,20},{28,24},{0,28},{5,1},{9... | collective-permute-start | bytes 776 | tf_op jit(solution)/shard_map/ppermute | solution.py:20
  76.6 2.0 %collective-permute-start.15 = (f32[1,1,258]{2,0,1:T(1,128)S(1)}, f32[1,1,258]{2,0,1:T(1,128)S(1)}, u32[]{:S(2)}, u32[]{:S(2)}) collective-permute-start(f32[1,1,258]{2,0,1:T(1,128)S(1)} %get-tuple-element.35), channel_id=1, source_target_pairs={{0,1},{1,2},{2,3},{3,0},{4,5},{5,6},{6,7},{7,4},{8,9},{9,10},{10,1... | collective-permute-start | bytes 3104 | tf_op jit(solution)/shard_map/ppermute | solution.py:19
  84.1 2.6 %collective-permute-start.17 = (f32[64,2,1]{2,0,1:T(8,128)S(1)}, f32[64,2,1]{2,0,1:T(8,128)S(1)}, u32[]{:S(2)}, u32[]{:S(2)}) collective-permute-start(f32[64,2,1]{2,0,1:T(8,128)S(1)} %get-tuple-element.18), channel_id=1, source_target_pairs={{4,0},{8,4},{12,8},{16,12},{20,16},{24,20},{28,24},{0,28},{5,1},{9... | collective-permute-start | bytes 1544 | tf_op jit(solution)/shard_map/ppermute | solution.py:20
  86.7 2.2 %collective-permute-done.16 = f32[64,2,1]{2,0,1:T(8,128)S(1)} collective-permute-done((f32[64,2,1]{2,0,1:T(8,128)S(1)}, f32[64,2,1]{2,0,1:T(8,128)S(1)}, u32[]{:S(2)}, u32[]{:S(2)}) %collective-permute-start.16) | collective-permute-done | bytes 544 | tf_op jit(solution)/shard_map/ppermute | solution.py:19
  92.6 2.0 %collective-permute-done.19 = f32[1,2,258]{2,0,1:T(1,128)S(1)} collective-permute-done((f32[1,2,258]{2,0,1:T(1,128)S(1)}, f32[1,2,258]{2,0,1:T(1,128)S(1)}, u32[]{:S(2)}, u32[]{:S(2)}) %collective-permute-start.19) | collective-permute-done | bytes 2096 | tf_op jit(solution)/shard_map/ppermute | solution.py:19
  94.9 2.6 %collective-permute-start.21 = (f32[64,1,1]{2,0,1:T(8,128)S(1)}, f32[64,1,1]{2,0,1:T(8,128)S(1)}, u32[]{:S(2)}, u32[]{:S(2)}) collective-permute-start(f32[64,1,1]{2,0,1:T(8,128)S(1)} %get-tuple-element.44), channel_id=1, source_target_pairs={{4,0},{8,4},{12,8},{16,12},{20,16},{24,20},{28,24},{0,28},{5,1},{9... | collective-permute-start | bytes 776 | tf_op jit(solution)/shard_map/ppermute | solution.py:20
  99.2 2.0 %collective-permute-start.23 = (f32[1,1,258]{2,0,1:T(1,128)S(1)}, f32[1,1,258]{2,0,1:T(1,128)S(1)}, u32[]{:S(2)}, u32[]{:S(2)}) collective-permute-start(f32[1,1,258]{2,0,1:T(1,128)S(1)} %get-tuple-element.31), channel_id=1, source_target_pairs={{0,1},{1,2},{2,3},{3,0},{4,5},{5,6},{6,7},{7,4},{8,9},{9,10},{10,1... | collective-permute-start | bytes 3104 | tf_op jit(solution)/shard_map/ppermute | solution.py:19
  104.9 2.6 %collective-permute-start.25 = (f32[64,2,1]{2,0,1:T(8,128)S(1)}, f32[64,2,1]{2,0,1:T(8,128)S(1)}, u32[]{:S(2)}, u32[]{:S(2)}) collective-permute-start(f32[64,2,1]{2,0,1:T(8,128)S(1)} %get-tuple-element.26), channel_id=1, source_target_pairs={{4,0},{8,4},{12,8},{16,12},{20,16},{24,20},{28,24},{0,28},{5,1},{9... | collective-permute-start | bytes 1544 | tf_op jit(solution)/shard_map/ppermute | solution.py:20
  107.6 2.2 %collective-permute-done.24 = f32[64,2,1]{2,0,1:T(8,128)S(1)} collective-permute-done((f32[64,2,1]{2,0,1:T(8,128)S(1)}, f32[64,2,1]{2,0,1:T(8,128)S(1)}, u32[]{:S(2)}, u32[]{:S(2)}) %collective-permute-start.24) | collective-permute-done | bytes 544 | tf_op jit(solution)/shard_map/ppermute | solution.py:19
  113.5 2.0 %collective-permute-done.27 = f32[1,2,258]{2,0,1:T(1,128)S(1)} collective-permute-done((f32[1,2,258]{2,0,1:T(1,128)S(1)}, f32[1,2,258]{2,0,1:T(1,128)S(1)}, u32[]{:S(2)}, u32[]{:S(2)}) %collective-permute-start.27) | collective-permute-done | bytes 2096 | tf_op jit(solution)/shard_map/ppermute | solution.py:19
  115.7 2.6 %collective-permute-start.29 = (f32[64,1,1]{2,0,1:T(8,128)S(1)}, f32[64,1,1]{2,0,1:T(8,128)S(1)}, u32[]{:S(2)}, u32[]{:S(2)}) collective-permute-start(f32[64,1,1]{2,0,1:T(8,128)S(1)} %get-tuple-element.42), channel_id=1, source_target_pairs={{4,0},{8,4},{12,8},{16,12},{20,16},{24,20},{28,24},{0,28},{5,1},{9... | collective-permute-start | bytes 776 | tf_op jit(solution)/shard_map/ppermute | solution.py:20
  120.1 2.0 %collective-permute-start.31 = (f32[1,1,258]{2,0,1:T(1,128)S(1)}, f32[1,1,258]{2,0,1:T(1,128)S(1)}, u32[]{:S(2)}, u32[]{:S(2)}) collective-permute-start(f32[1,1,258]{2,0,1:T(1,128)S(1)} %get-tuple-element.25), channel_id=1, source_target_pairs={{0,1},{1,2},{2,3},{3,0},{4,5},{5,6},{6,7},{7,4},{8,9},{9,10},{10,1... | collective-permute-start | bytes 3104 | tf_op jit(solution)/shard_map/ppermute | solution.py:19
  125.7 16.5 %all_gather.3 = f32[256,3,256]{2,0,1:T(8,128)S(1)} all-gather(f32[64,3,256]{2,0,1:T(8,128)S(1)} %pad_maximum_fusion.1), channel_id=1, replica_groups=mesh['tile'=8,'member'=4] {'member'}, dimensions={0}, use_global_device_ids=true | all-gather | bytes 983040 | tf_op jit(solution)/shard_map/all_gather | solution.py:108
  (95 shorter events, 43.6 us)
Async XLA Ops:
  7.2 30.7 %reduce-scatter.2.cloned.1.call-start = ((), (), s32[]{:S(2)}) async-start(), calls=%async_computation.1 | async-start | bytes 983040 | tf_op jit(solution)/shard_map/reduce_scatter | solution.py:92
  39.0 4.6 %collective-permute-start = (f32[64,2,1]{2,0,1:T(8,128)S(1)}, f32[64,2,1]{2,0,1:T(8,128)S(1)}, u32[]{:S(2)}, u32[]{:S(2)}) collective-permute-start(f32[64,2,1]{2,0,1:T(8,128)S(1)} %get-tuple-element.21), channel_id=1, source_target_pairs={{0,4},{4,8},{8,12},{12,16},{16,20},{20,24},{24,28},{28,0},{1,5},{5... | collective-permute-start | bytes 1544 | tf_op jit(solution)/shard_map/ppermute | solution.py:19
  39.1 4.6 %collective-permute-start.1 = (f32[64,2,1]{2,0,1:T(8,128)S(1)}, f32[64,2,1]{2,0,1:T(8,128)S(1)}, u32[]{:S(2)}, u32[]{:S(2)}) collective-permute-start(f32[64,2,1]{2,0,1:T(8,128)S(1)} %get-tuple-element.20), channel_id=1, source_target_pairs={{4,0},{8,4},{12,8},{16,12},{20,16},{24,20},{28,24},{0,28},{5,1},{9... | collective-permute-start | bytes 1544 | tf_op jit(solution)/shard_map/ppermute | solution.py:20
  45.5 5.4 %collective-permute-start.3 = (f32[1,2,258]{2,0,1:T(1,128)S(1)}, f32[1,2,258]{2,0,1:T(1,128)S(1)}, u32[]{:S(2)}, u32[]{:S(2)}) collective-permute-start(f32[1,2,258]{2,0,1:T(1,128)S(1)} %get-tuple-element.17), channel_id=1, source_target_pairs={{0,1},{1,2},{2,3},{3,0},{4,5},{5,6},{6,7},{7,4},{8,9},{9,10},{10,1... | collective-permute-start | bytes 6200 | tf_op jit(solution)/shard_map/ppermute | solution.py:19
  51.1 4.2 %collective-permute-start.4 = (f32[64,1,1]{2,0,1:T(8,128)S(1)}, f32[64,1,1]{2,0,1:T(8,128)S(1)}, u32[]{:S(2)}, u32[]{:S(2)}) collective-permute-start(f32[64,1,1]{2,0,1:T(8,128)S(1)} %get-tuple-element.49), channel_id=1, source_target_pairs={{0,4},{4,8},{8,12},{12,16},{16,20},{20,24},{24,28},{28,0},{1,5},{5... | collective-permute-start | bytes 776 | tf_op jit(solution)/shard_map/ppermute | solution.py:19
  51.1 4.2 %collective-permute-start.5 = (f32[64,1,1]{2,0,1:T(8,128)S(1)}, f32[64,1,1]{2,0,1:T(8,128)S(1)}, u32[]{:S(2)}, u32[]{:S(2)}) collective-permute-start(f32[64,1,1]{2,0,1:T(8,128)S(1)} %get-tuple-element.48), channel_id=1, source_target_pairs={{4,0},{8,4},{12,8},{16,12},{20,16},{24,20},{28,24},{0,28},{5,1},{9... | collective-permute-start | bytes 776 | tf_op jit(solution)/shard_map/ppermute | solution.py:20
  55.4 5.4 %collective-permute-start.7 = (f32[1,1,258]{2,0,1:T(1,128)S(1)}, f32[1,1,258]{2,0,1:T(1,128)S(1)}, u32[]{:S(2)}, u32[]{:S(2)}) collective-permute-start(f32[1,1,258]{2,0,1:T(1,128)S(1)} %get-tuple-element.41), channel_id=1, source_target_pairs={{0,1},{1,2},{2,3},{3,0},{4,5},{5,6},{6,7},{7,4},{8,9},{9,10},{10,1... | collective-permute-start | bytes 3104 | tf_op jit(solution)/shard_map/ppermute | solution.py:19
  61.1 5.3 %collective-permute-start.8 = (f32[64,2,1]{2,0,1:T(8,128)S(1)}, f32[64,2,1]{2,0,1:T(8,128)S(1)}, u32[]{:S(2)}, u32[]{:S(2)}) collective-permute-start(f32[64,2,1]{2,0,1:T(8,128)S(1)} %get-tuple-element.37), channel_id=1, source_target_pairs={{0,4},{4,8},{8,12},{12,16},{16,20},{20,24},{24,28},{28,0},{1,5},{5... | collective-permute-start | bytes 1544 | tf_op jit(solution)/shard_map/ppermute | solution.py:19
  61.2 5.3 %collective-permute-start.9 = (f32[64,2,1]{2,0,1:T(8,128)S(1)}, f32[64,2,1]{2,0,1:T(8,128)S(1)}, u32[]{:S(2)}, u32[]{:S(2)}) collective-permute-start(f32[64,2,1]{2,0,1:T(8,128)S(1)} %get-tuple-element.36), channel_id=1, source_target_pairs={{4,0},{8,4},{12,8},{16,12},{20,16},{24,20},{28,24},{0,28},{5,1},{9... | collective-permute-start | bytes 1544 | tf_op jit(solution)/shard_map/ppermute | solution.py:20
  66.6 5.4 %collective-permute-start.11 = (f32[1,2,258]{2,0,1:T(1,128)S(1)}, f32[1,2,258]{2,0,1:T(1,128)S(1)}, u32[]{:S(2)}, u32[]{:S(2)}) collective-permute-start(f32[1,2,258]{2,0,1:T(1,128)S(1)} %get-tuple-element.15), channel_id=1, source_target_pairs={{0,1},{1,2},{2,3},{3,0},{4,5},{5,6},{6,7},{7,4},{8,9},{9,10},{10,1... | collective-permute-start | bytes 6200 | tf_op jit(solution)/shard_map/ppermute | solution.py:19
  72.2 4.2 %collective-permute-start.12 = (f32[64,1,1]{2,0,1:T(8,128)S(1)}, f32[64,1,1]{2,0,1:T(8,128)S(1)}, u32[]{:S(2)}, u32[]{:S(2)}) collective-permute-start(f32[64,1,1]{2,0,1:T(8,128)S(1)} %get-tuple-element.47), channel_id=1, source_target_pairs={{0,4},{4,8},{8,12},{12,16},{16,20},{20,24},{24,28},{28,0},{1,5},{5... | collective-permute-start | bytes 776 | tf_op jit(solution)/shard_map/ppermute | solution.py:19
  72.3 4.2 %collective-permute-start.13 = (f32[64,1,1]{2,0,1:T(8,128)S(1)}, f32[64,1,1]{2,0,1:T(8,128)S(1)}, u32[]{:S(2)}, u32[]{:S(2)}) collective-permute-start(f32[64,1,1]{2,0,1:T(8,128)S(1)} %get-tuple-element.46), channel_id=1, source_target_pairs={{4,0},{8,4},{12,8},{16,12},{20,16},{24,20},{28,24},{0,28},{5,1},{9... | collective-permute-start | bytes 776 | tf_op jit(solution)/shard_map/ppermute | solution.py:20
  76.6 5.4 %collective-permute-start.15 = (f32[1,1,258]{2,0,1:T(1,128)S(1)}, f32[1,1,258]{2,0,1:T(1,128)S(1)}, u32[]{:S(2)}, u32[]{:S(2)}) collective-permute-start(f32[1,1,258]{2,0,1:T(1,128)S(1)} %get-tuple-element.35), channel_id=1, source_target_pairs={{0,1},{1,2},{2,3},{3,0},{4,5},{5,6},{6,7},{7,4},{8,9},{9,10},{10,1... | collective-permute-start | bytes 3104 | tf_op jit(solution)/shard_map/ppermute | solution.py:19
  84.0 4.9 %collective-permute-start.16 = (f32[64,2,1]{2,0,1:T(8,128)S(1)}, f32[64,2,1]{2,0,1:T(8,128)S(1)}, u32[]{:S(2)}, u32[]{:S(2)}) collective-permute-start(f32[64,2,1]{2,0,1:T(8,128)S(1)} %get-tuple-element.19), channel_id=1, source_target_pairs={{0,4},{4,8},{8,12},{12,16},{16,20},{20,24},{24,28},{28,0},{1,5},{5... | collective-permute-start | bytes 1544 | tf_op jit(solution)/shard_map/ppermute | solution.py:19
  84.1 4.8 %collective-permute-start.17 = (f32[64,2,1]{2,0,1:T(8,128)S(1)}, f32[64,2,1]{2,0,1:T(8,128)S(1)}, u32[]{:S(2)}, u32[]{:S(2)}) collective-permute-start(f32[64,2,1]{2,0,1:T(8,128)S(1)} %get-tuple-element.18), channel_id=1, source_target_pairs={{4,0},{8,4},{12,8},{16,12},{20,16},{24,20},{28,24},{0,28},{5,1},{9... | collective-permute-start | bytes 1544 | tf_op jit(solution)/shard_map/ppermute | solution.py:20
  89.2 5.4 %collective-permute-start.19 = (f32[1,2,258]{2,0,1:T(1,128)S(1)}, f32[1,2,258]{2,0,1:T(1,128)S(1)}, u32[]{:S(2)}, u32[]{:S(2)}) collective-permute-start(f32[1,2,258]{2,0,1:T(1,128)S(1)} %get-tuple-element.13), channel_id=1, source_target_pairs={{0,1},{1,2},{2,3},{3,0},{4,5},{5,6},{6,7},{7,4},{8,9},{9,10},{10,1... | collective-permute-start | bytes 6200 | tf_op jit(solution)/shard_map/ppermute | solution.py:19
  94.9 4.2 %collective-permute-start.20 = (f32[64,1,1]{2,0,1:T(8,128)S(1)}, f32[64,1,1]{2,0,1:T(8,128)S(1)}, u32[]{:S(2)}, u32[]{:S(2)}) collective-permute-start(f32[64,1,1]{2,0,1:T(8,128)S(1)} %get-tuple-element.45), channel_id=1, source_target_pairs={{0,4},{4,8},{8,12},{12,16},{16,20},{20,24},{24,28},{28,0},{1,5},{5... | collective-permute-start | bytes 776 | tf_op jit(solution)/shard_map/ppermute | solution.py:19
  94.9 4.2 %collective-permute-start.21 = (f32[64,1,1]{2,0,1:T(8,128)S(1)}, f32[64,1,1]{2,0,1:T(8,128)S(1)}, u32[]{:S(2)}, u32[]{:S(2)}) collective-permute-start(f32[64,1,1]{2,0,1:T(8,128)S(1)} %get-tuple-element.44), channel_id=1, source_target_pairs={{4,0},{8,4},{12,8},{16,12},{20,16},{24,20},{28,24},{0,28},{5,1},{9... | collective-permute-start | bytes 776 | tf_op jit(solution)/shard_map/ppermute | solution.py:20
  99.2 5.4 %collective-permute-start.23 = (f32[1,1,258]{2,0,1:T(1,128)S(1)}, f32[1,1,258]{2,0,1:T(1,128)S(1)}, u32[]{:S(2)}, u32[]{:S(2)}) collective-permute-start(f32[1,1,258]{2,0,1:T(1,128)S(1)} %get-tuple-element.31), channel_id=1, source_target_pairs={{0,1},{1,2},{2,3},{3,0},{4,5},{5,6},{6,7},{7,4},{8,9},{9,10},{10,1... | collective-permute-start | bytes 3104 | tf_op jit(solution)/shard_map/ppermute | solution.py:19
  104.9 4.9 %collective-permute-start.24 = (f32[64,2,1]{2,0,1:T(8,128)S(1)}, f32[64,2,1]{2,0,1:T(8,128)S(1)}, u32[]{:S(2)}, u32[]{:S(2)}) collective-permute-start(f32[64,2,1]{2,0,1:T(8,128)S(1)} %get-tuple-element.27), channel_id=1, source_target_pairs={{0,4},{4,8},{8,12},{12,16},{16,20},{20,24},{24,28},{28,0},{1,5},{5... | collective-permute-start | bytes 1544 | tf_op jit(solution)/shard_map/ppermute | solution.py:19
  104.9 4.8 %collective-permute-start.25 = (f32[64,2,1]{2,0,1:T(8,128)S(1)}, f32[64,2,1]{2,0,1:T(8,128)S(1)}, u32[]{:S(2)}, u32[]{:S(2)}) collective-permute-start(f32[64,2,1]{2,0,1:T(8,128)S(1)} %get-tuple-element.26), channel_id=1, source_target_pairs={{4,0},{8,4},{12,8},{16,12},{20,16},{24,20},{28,24},{0,28},{5,1},{9... | collective-permute-start | bytes 1544 | tf_op jit(solution)/shard_map/ppermute | solution.py:20
  110.1 5.4 %collective-permute-start.27 = (f32[1,2,258]{2,0,1:T(1,128)S(1)}, f32[1,2,258]{2,0,1:T(1,128)S(1)}, u32[]{:S(2)}, u32[]{:S(2)}) collective-permute-start(f32[1,2,258]{2,0,1:T(1,128)S(1)} %get-tuple-element.11), channel_id=1, source_target_pairs={{0,1},{1,2},{2,3},{3,0},{4,5},{5,6},{6,7},{7,4},{8,9},{9,10},{10,1... | collective-permute-start | bytes 6200 | tf_op jit(solution)/shard_map/ppermute | solution.py:19
  115.7 4.2 %collective-permute-start.28 = (f32[64,1,1]{2,0,1:T(8,128)S(1)}, f32[64,1,1]{2,0,1:T(8,128)S(1)}, u32[]{:S(2)}, u32[]{:S(2)}) collective-permute-start(f32[64,1,1]{2,0,1:T(8,128)S(1)} %get-tuple-element.43), channel_id=1, source_target_pairs={{0,4},{4,8},{8,12},{12,16},{16,20},{20,24},{24,28},{28,0},{1,5},{5... | collective-permute-start | bytes 776 | tf_op jit(solution)/shard_map/ppermute | solution.py:19
  120.1 5.4 %collective-permute-start.31 = (f32[1,1,258]{2,0,1:T(1,128)S(1)}, f32[1,1,258]{2,0,1:T(1,128)S(1)}, u32[]{:S(2)}, u32[]{:S(2)}) collective-permute-start(f32[1,1,258]{2,0,1:T(1,128)S(1)} %get-tuple-element.25), channel_id=1, source_target_pairs={{0,1},{1,2},{2,3},{3,0},{4,5},{5,6},{6,7},{7,4},{8,9},{9,10},{10,1... | collective-permute-start | bytes 3104 | tf_op jit(solution)/shard_map/ppermute | solution.py:19
  (14 other events, 104.0 us)
Sparse Core Ops, SparseCore 0:
  11.9 25.9 reduce-scatter.1
where the time goes:
time: 152 us
  waiting for transfers between devices  70.5 us (46%)
  starting transfers between devices  37.7 us (25%)
  blocking collectives  16.5 us (11%)
  between operations  14.4 us (9%)
  other arithmetic  5.99 us (4%)
  matrix products  4.55 us (3%)
  local copies, waits for them, and re-layouts  2.58 us (2%)
    ppermute x16, waiting for transfers between devices, with_halo(): before = lax.ppermute(last, axis, up)  32.1 us
    reduce_scatter x1, waiting for transfers between devices, body(): lax.psum_scatter(jnp.sum(pert_part.astype(jnp.float32) * localized[:, :,...  26.1 us
    ppermute x16, starting transfers between devices, with_halo(): after = lax.ppermute(leading, axis, down)  23.5 us
    all_gather x1, blocking collectives, body(): lax.all_gather(backward_pass, 'member', axis=0, tiled=True)[None]  16.5 us
    ppermute x16, starting transfers between devices, with_halo(): before = lax.ppermute(last, axis, up)  14.1 us
    ppermute x16, waiting for transfers between devices, with_halo(): after = lax.ppermute(leading, axis, down)  12.2 us
  transfers between devices with their start and end apart: 33, of which 25 were waited for; matrix products, arithmetic and copies ran while one was open for 0% of the time, Pallas kernels for 0%

commit v1 on v0

v1 whole, which is shorter than its diff:
```python
import jax
import jax.numpy as jnp
from jax import lax
from jax.sharding import PartitionSpec as P

STEPS = 2
COURANT = 0.3
HALO = 4 * STEPS


def shift_rows(x, sides):
    count = lax.axis_size("tile")
    up = [(i, (i + 1) % count) for i in range(count)]
    down = [(j, i) for i, j in up]
    lo, hi = sides
    before = lax.ppermute(hi, "tile", up)
    after = lax.ppermute(lo, "tile", down)
    return before, after


def col_slope(f):
    return 0.5 * (jnp.roll(f, -1, 0) - jnp.roll(f, 1, 0))


def row_slope(f):
    return 0.5 * (jnp.roll(f, -1, 1) - jnp.roll(f, 1, 1))


def dynamics(h, u, v, dep, prec, meas):
    for _ in range(STEPS):
        h = h - COURANT * dep * (col_slope(u) + row_slope(v))
        u = u - COURANT * col_slope(h)
        v = v - COURANT * row_slope(h)
    pred = (h, u, v)
    a, p, q = (prec[i] * (pred[i] - meas[i]) for i in range(3))
    for _ in range(STEPS):
        e = a + COURANT * (col_slope(p) + row_slope(q))
        w = dep * e
        p = p + COURANT * col_slope(w)
        q = q + COURANT * row_slope(w)
        a = e
    return pred, (a, p, q)


def body(alpha, ensemble, background, measured_values, precision_factor, depth, loc_cols, loc_rows):
    highest = lax.Precision.HIGHEST
    ncol, nfield, nrow = background.shape
    block_cols = ncol // lax.axis_size("member")
    col_start = lax.axis_index("member") * block_cols

    inputs = jnp.concatenate(
        [background, measured_values, precision_factor, depth[:, None, :]], axis=1
    )
    in_before, in_after = shift_rows(inputs, (inputs[:, :, :HALO], inputs[:, :, -HALO:]))

    localized = jnp.einsum("cd,kdr->kcr", loc_cols, alpha, precision=highest)
    localized = jnp.einsum("kcr,qr->kcq", localized, loc_rows, precision=highest)
    ens = ensemble.astype(jnp.float32)
    partial = jnp.sum(ens * localized[:, :, None, :], axis=0).transpose(1, 0, 2)
    p_before, p_after = shift_rows(partial, (partial[:, :, :HALO], partial[:, :, -HALO:]))
    halo = jnp.concatenate([p_before, p_after], axis=2).transpose(0, 2, 1)
    summed = lax.psum(jnp.concatenate([partial, halo], axis=1), "member")
    incr_main = summed[:, :ncol]
    incr_halo = summed[:, ncol:].transpose(0, 2, 1)
    incr = jnp.concatenate(
        [incr_halo[:, :, :HALO], incr_main, incr_halo[:, :, HALO:]], axis=2
    )
    ext = jnp.concatenate([in_before, inputs, in_after], axis=2)

    state = [ext[:, i] + incr[i] for i in range(nfield)]
    meas = [ext[:, nfield + i] for i in range(nfield)]
    prec = [ext[:, 2 * nfield + i] for i in range(nfield)]
    dep = ext[:, 3 * nfield]
    pred, adj = dynamics(*state, dep, prec, meas)

    inner = slice(HALO, HALO + nrow)
    pred = jnp.stack([f[:, inner] for f in pred], axis=1)
    predicted_final = lax.dynamic_slice_in_dim(pred, col_start, block_cols, 0)
    adj = jnp.stack([f[:, inner] for f in adj], axis=1)
    projected = jnp.sum(ens * adj[None], axis=2)
    rows_done = jnp.einsum("knr,rq->knq", projected, loc_rows, precision=highest)
    cost_derivative = alpha + jnp.einsum("cd,kcq->kdq", loc_cols, rows_done, precision=highest)
    return (cost_derivative, predicted_final)


def solution(mesh):
    return jax.shard_map(
        body,
        mesh=mesh,
        in_specs=(
            P("member", None, "tile"),
            P("member", None, None, "tile"),
            P(None, None, "tile"),
            P(None, None, "tile"),
            P(None, None, "tile"),
            P(None, "tile"),
            P(),
            P(),
        ),
        out_specs=(P("member", None, "tile"), P("member", None, "tile")),
        check_vma=False,
    )
```

time: 152 us -> 97.3 us (0.64)
  starting transfers between devices: 37.7 us -> 6.41 us
  waiting for transfers between devices: 70.5 us -> 44.7 us
  blocking collectives: 16.5 us -> 0 us
  local copies, waits for them, and re-layouts: 2.58 us -> 17.8 us
  other arithmetic: 5.99 us -> 8.66 us
    psum x0 -> x1, waiting for transfers between devices: none -> 36.3 us  [body(): summed = lax.psum(jnp.concatenate([partial, halo], axis=1), 'member')]
    ppermute x32 -> x4, waiting for transfers between devices: 44.4 us -> 8.35 us  [the longest x2 6.95 us: shift_rows(): before = lax.ppermute(hi, 'tile', up)]
    ppermute x32 -> x4, starting transfers between devices: 37.6 us -> 6.37 us  [the longest x2 4.05 us: shift_rows(): after = lax.ppermute(lo, 'tile', down)]
    reduce_scatter x1 -> x0, waiting for transfers between devices: 26.1 us -> none  [body(): lax.psum_scatter(jnp.sum(pert_part.astype(jnp.float32) * localized[:, :,...]
    all_gather x1 -> x0, blocking collectives: 16.5 us -> none  [body(): lax.all_gather(backward_pass, 'member', axis=0, tiled=True)[None]]
    unnamed x12 -> x33, local copies, waits for them, and re-layouts: 1.94 us -> 8.74 us
    slice x10 -> x36, local copies, waits for them, and re-layouts: 0.64 us -> 6.75 us  [the longest x2 4.36 us: body(): incr_main = summed[:, :ncol]]
    concatenate x1 -> x3, other arithmetic: 0.02 us -> 4.09 us  [the longest x1 1.92 us: body(): ext = jnp.concatenate([in_before, inputs, in_after], axis=2)]
  transfers between devices with their start and end apart: 33 -> 5, of which waited for: 25 -> 3; matrix products, arithmetic and copies ran while one was open for 0% -> 8% of each run, Pallas kernels for 0% -> 0%
where the time goes in v1:
time: 97.3 us; the launch traced here: 96.8 us
  waiting for transfers between devices  44.7 us (46%)
  local copies, waits for them, and re-layouts  17.8 us (18%)
  between operations  14.6 us (15%)
  other arithmetic  8.66 us (9%)
  starting transfers between devices  6.41 us (7%)
  matrix products  4.61 us (5%)
    psum x1, waiting for transfers between devices, body(): summed = lax.psum(jnp.concatenate([partial, halo], axis=1), 'member')  36.3 us
    unnamed x33, local copies, waits for them, and re-layouts  8.74 us
    ppermute x2, waiting for transfers between devices, shift_rows(): before = lax.ppermute(hi, 'tile', up)  6.95 us
    slice x2, local copies, waits for them, and re-layouts, body(): incr_main = summed[:, :ncol]  4.36 us
    ppermute x2, starting transfers between devices, shift_rows(): after = lax.ppermute(lo, 'tile', down)  4.05 us
    ppermute x2, starting transfers between devices, shift_rows(): before = lax.ppermute(hi, 'tile', up)  2.32 us
    dot_general x1, matrix products, body(): localized = jnp.einsum('cd,kdr->kcr', loc_cols, alpha, precision=highest)  2.14 us
  transfers between devices with their start and end apart: 5, of which 3 were waited for; matrix products, arithmetic and copies ran while one was open for 8% of the time, Pallas kernels for 0%

profile of v1, /device:TPU:0, one launch (start us, length us, event | category | flops | bytes accessed | tf_op | source)
XLA Modules:
  0.0 96.8 jit_solution(17737798604623052066)
XLA Ops:
  7.2 2.1 %convolution_bitcast_fusion.1 = f32[3,256,256]{2,1,0:T(8,128)S(1)} fusion(f32[3,256,256]{2,1,0:T(8,128)} %param.8, f32[256,256]{1,0:T(8,128)} %param.14), kind=kOutput, calls=%fused_computation.6 | convolution fusion | flops 603979776 | bytes 1835008 | tf_op jit(solution)/shard_map/cd,kdr->kcr/dot_general | solution.py:56
  9.4 0.8 fusion.48
  11.2 2.9 %collective-permute-start.3 = (f32[3,256,8]{2,1,0:T(8,128)S(1)}, f32[3,256,8]{2,1,0:T(8,128)S(1)}, u32[]{:S(2)}, u32[]{:S(2)}) collective-permute-start(f32[3,256,8]{2,1,0:T(8,128)S(1)} %get-tuple-element.21), channel_id=1, source_target_pairs={{4,0},{8,4},{12,8},{16,12},{20,16},{24,20},{28,24},{0,28},{5,1},{9... | collective-permute-start | bytes 73736 | tf_op jit(solution)/shard_map/ppermute | solution.py:17
  14.1 6.9 %collective-permute-done.2 = f32[3,256,8]{2,1,0:T(8,128)S(1)} collective-permute-done((f32[3,256,8]{2,1,0:T(8,128)S(1)}, f32[3,256,8]{2,1,0:T(8,128)S(1)}, u32[]{:S(2)}, u32[]{:S(2)}) %collective-permute-start.2) | collective-permute-done | bytes 24608 | tf_op jit(solution)/shard_map/ppermute | solution.py:16
  21.2 1.4 %collective-permute-done.3 = f32[3,256,8]{2,1,0:T(8,128)S(1)} collective-permute-done((f32[3,256,8]{2,1,0:T(8,128)S(1)}, f32[3,256,8]{2,1,0:T(8,128)S(1)}, u32[]{:S(2)}, u32[]{:S(2)}) %collective-permute-start.3) | collective-permute-done | bytes 24608 | tf_op jit(solution)/shard_map/ppermute | solution.py:17
  22.7 1.0 %pad_maximum_fusion.1 = f32[3,272,256]{2,1,0:T(8,128)} fusion(f32[3,16,256]{2,1,0:T(8,128)S(1)} %maximum_bitcast_fusion, f32[3,256,256]{2,1,0:T(8,128)S(1)} %bitcast.109), kind=kLoop, calls=%fused_computation.8 | loop fusion | flops 208896 | bytes 1671168 | tf_op jit(solution)/shard_map/concatenate | solution.py:62
  24.0 1.7 %copy.16 = f32[256,3,256]{0,2,1:T(8,128)S(1)} copy(f32[256,3,256]{2,0,1:T(8,128)} %param.11) | data formatting | bytes 1572864 | tf_op args[3]
  25.7 1.7 %copy.17 = f32[256,3,256]{0,2,1:T(8,128)S(1)} copy(f32[256,3,256]{2,0,1:T(8,128)} %param.12) | data formatting | bytes 1572864 | tf_op args[4]
  27.6 1.8 %collective-permute-start = (f32[256,10,8]{0,2,1:T(8,128)S(1)}, f32[256,10,8]{0,2,1:T(8,128)S(1)}, u32[]{:S(2)}, u32[]{:S(2)}) collective-permute-start(f32[256,10,8]{0,2,1:T(8,128)S(1)} %get-tuple-element.18), channel_id=1, source_target_pairs={{0,4},{4,8},{8,12},{12,16},{16,20},{20,24},{24,28},{28,0},{1,5},{5... | collective-permute-start | bytes 245768 | tf_op jit(solution)/shard_map/ppermute | solution.py:16
  29.4 1.1 %collective-permute-start.1 = (f32[256,10,8]{0,2,1:T(8,128)S(1)}, f32[256,10,8]{0,2,1:T(8,128)S(1)}, u32[]{:S(2)}, u32[]{:S(2)}) collective-permute-start(f32[256,10,8]{0,2,1:T(8,128)S(1)} %get-tuple-element.19), channel_id=1, source_target_pairs={{4,0},{8,4},{12,8},{16,12},{20,16},{24,20},{28,24},{0,28},{5,1},{9... | collective-permute-start | bytes 245768 | tf_op jit(solution)/shard_map/ppermute | solution.py:17
  30.5 2.3 %copy.22 = f32[3,256,256]{1,2,0:T(8,128)} copy(f32[3,256,256]{2,1,0:T(8,128)} %param.8) | data formatting | bytes 1572864 | tf_op args[0]
  32.8 1.9 %pad_maximum_fusion = f32[256,10,272]{0,2,1:T(8,128)S(1)} fusion(f32[256,10,8]{0,2,1:T(8,128)S(1)} %collective-permute-done.1, f32[256,1,256]{0,2,1:T(8,128)S(1)} %bitcast.111, f32[256,3,256]{0,2,1:T(8,128)} %copy-done.3, f32[256,3,256]{0,2,1:T(8,128)} %copy-done.2, f32[256,3,256]{0,2,1:T(8,128)} %copy-done.1, f32[256,10,8]{0,2,1:T(8,128)S(1)} %collective-permute-done), kind=kLoop, calls=%fused_computation.2 | loop fusion | flops 3481600 | bytes 5570560 | tf_op jit(solution)/shard_map/concatenate | solution.py:68
  34.8 36.3 %all-reduce.2.cloned.1.call-done = f32[3,272,256]{2,1,0:T(8,128)} async-done(((f32[3,272,256]{2,1,0:T(8,128)}), f32[3,272,256]{2,1,0:T(8,128)}) %all-reduce.2.cloned.1.call-update) | async-done | bytes 835600 | tf_op jit(solution)/shard_map/psum | solution.py:62
  71.1 0.8 slice_bitcast_fusion.17
  71.9 2.1 %slice.378 = f32[3,256,256]{2,1,0:T(8,128)} slice(f32[3,272,256]{2,1,0:T(8,128)} %all-reduce.2.cloned.1.call-done), slice={[0:3], [0:256], [0:256]} | slice | bytes 1572864 | tf_op jit(solution)/shard_map/slice | solution.py:63
  74.0 2.3 %copy.20 = f32[3,256,256]{1,2,0:T(8,128)} copy(f32[3,256,256]{2,1,0:T(8,128)} %slice.378) | data formatting | bytes 1572864 | tf_op jit(solution)/shard_map/slice | solution.py:63
  76.3 1.2 %pad_maximum_fusion.2 = f32[3,256,272]{1,2,0:T(8,128)S(1)} fusion(f32[3,256,8]{1,2,0:T(8,128)S(1)} %get-tuple-element.87, f32[3,256,256]{1,2,0:T(8,128)} %copy.20, f32[3,256,8]{1,2,0:T(8,128)S(1)} %get-tuple-element.86), kind=kLoop, calls=%fused_computation.9 | loop fusion | flops 417792 | bytes 1671168 | tf_op jit(solution)/shard_map/concatenate | solution.py:65
  81.8 0.9 fusion.52
  83.2 0.8 copy.24
  84.4 1.2 %copy.21 = f32[256,3,256]{2,0,1:T(8,128)} copy(f32[256,3,256]{0,2,1:T(8,128)S(1)} %pad_maximum_fusion.3) | data formatting | bytes 1572864 | tf_op jit(solution)/shard_map/stack | solution.py:79
  85.6 1.5 %fusion.1 = f32[3,256,256]{2,1,0:T(8,128)S(1)} fusion(bf16[3,256,3,256]{3,1,2,0:T(8,128)(2,1)S(1)} %copy-done.5, f32[256,3,256]{2,0,1:T(8,128)} %copy.21), kind=kLoop, calls=%fused_computation.4 | loop fusion | flops 1572864 | bytes 2752512 | tf_op jit(solution)/shard_map/reduce_sum | solution.py:80
  87.1 0.9 fusion.46
  88.0 0.8 fusion.2
  88.8 1.1 %copy.23 = f32[3,256,256]{2,1,0:T(8,128)} copy(f32[3,256,256]{1,2,0:T(8,128)S(1)} %fusion.2) | data formatting | bytes 1572864
  (88 shorter events, 6.5 us)
Async XLA Ops:
  7.2 2.2 %copy-start = (f32[256,256]{1,0:T(8,128)S(1)}, f32[256,256]{1,0:T(8,128)}, u32[]{:S(2)}) copy-start(f32[256,256]{1,0:T(8,128)} %param.15) | copy-start | bytes 786436
  7.2 3.0 %copy-start.4 = (bf16[3,256,3,256]{3,1,2,0:T(8,128)(2,1)S(1)}, bf16[3,256,3,256]{3,1,2,0:T(8,128)(2,1)}, u32[]{:S(2)}) copy-start(bf16[3,256,3,256]{3,1,2,0:T(8,128)(2,1)} %param.9) | copy-start | bytes 3538948
  7.2 63.9 %all-reduce.2.cloned.1.call-start = ((), (), s32[]{:S(2)}) async-start(), calls=%async_computation | async-start | bytes 1671168 | tf_op jit(solution)/shard_map/psum | solution.py:62
  10.5 13.2 %copy-start.11 = (f32[256,3,256]{2,0,1:T(8,128)S(1)}, f32[256,3,256]{2,0,1:T(8,128)}, u32[]{:S(2)}) copy-start(f32[256,3,256]{2,0,1:T(8,128)} %param.10) | copy-start | bytes 2359300
  10.7 10.4 %collective-permute-start.2 = (f32[3,256,8]{2,1,0:T(8,128)S(1)}, f32[3,256,8]{2,1,0:T(8,128)S(1)}, u32[]{:S(2)}, u32[]{:S(2)}) collective-permute-start(f32[3,256,8]{2,1,0:T(8,128)S(1)} %get-tuple-element.20), channel_id=1, source_target_pairs={{0,4},{4,8},{8,12},{12,16},{16,20},{20,24},{24,28},{28,0},{1,5},{5... | collective-permute-start | bytes 73736 | tf_op jit(solution)/shard_map/ppermute | solution.py:16
  11.2 11.4 %collective-permute-start.3 = (f32[3,256,8]{2,1,0:T(8,128)S(1)}, f32[3,256,8]{2,1,0:T(8,128)S(1)}, u32[]{:S(2)}, u32[]{:S(2)}) collective-permute-start(f32[3,256,8]{2,1,0:T(8,128)S(1)} %get-tuple-element.21), channel_id=1, source_target_pairs={{4,0},{8,4},{12,8},{16,12},{20,16},{24,20},{28,24},{0,28},{5,1},{9... | collective-permute-start | bytes 73736 | tf_op jit(solution)/shard_map/ppermute | solution.py:17
  23.7 3.7 %copy-start.12 = (f32[256,256]{1,0:T(8,128)S(1)}, f32[256,256]{1,0:T(8,128)}, u32[]{:S(2)}) copy-start(f32[256,256]{1,0:T(8,128)} %param.13) | copy-start | bytes 786436
  24.0 3.6 %copy-start.1 = (f32[256,3,256]{0,2,1:T(8,128)}, f32[256,3,256]{0,2,1:T(8,128)S(1)}, u32[]{:S(2)}) copy-start(f32[256,3,256]{0,2,1:T(8,128)S(1)} %copy.15) | copy-start | bytes 2359300
  25.7 7.1 %copy-start.2 = (f32[256,3,256]{0,2,1:T(8,128)}, f32[256,3,256]{0,2,1:T(8,128)S(1)}, u32[]{:S(2)}) copy-start(f32[256,3,256]{0,2,1:T(8,128)S(1)} %copy.16) | copy-start | bytes 2359300
  27.4 5.4 %copy-start.3 = (f32[256,3,256]{0,2,1:T(8,128)}, f32[256,3,256]{0,2,1:T(8,128)S(1)}, u32[]{:S(2)}) copy-start(f32[256,3,256]{0,2,1:T(8,128)S(1)} %copy.17) | copy-start | bytes 2359300
  27.6 5.2 %collective-permute-start = (f32[256,10,8]{0,2,1:T(8,128)S(1)}, f32[256,10,8]{0,2,1:T(8,128)S(1)}, u32[]{:S(2)}, u32[]{:S(2)}) collective-permute-start(f32[256,10,8]{0,2,1:T(8,128)S(1)} %get-tuple-element.18), channel_id=1, source_target_pairs={{0,4},{4,8},{8,12},{12,16},{16,20},{20,24},{24,28},{28,0},{1,5},{5... | collective-permute-start | bytes 245768 | tf_op jit(solution)/shard_map/ppermute | solution.py:16
  29.4 3.4 %collective-permute-start.1 = (f32[256,10,8]{0,2,1:T(8,128)S(1)}, f32[256,10,8]{0,2,1:T(8,128)S(1)}, u32[]{:S(2)}, u32[]{:S(2)}) collective-permute-start(f32[256,10,8]{0,2,1:T(8,128)S(1)} %get-tuple-element.19), channel_id=1, source_target_pairs={{4,0},{8,4},{12,8},{16,12},{20,16},{24,20},{28,24},{0,28},{5,1},{9... | collective-permute-start | bytes 245768 | tf_op jit(solution)/shard_map/ppermute | solution.py:17
  81.1 0.7 copy-start.6
  82.7 1.4 %copy-start.9 = (f32[256,272]{0,1:T(8,128)S(1)}, f32[256,272]{0,1:T(8,128)}, u32[]{:S(2)}) copy-start(f32[256,272]{0,1:T(8,128)} %get-tuple-element.7) | copy-start | bytes 835588
  82.9 1.3 %copy-start.7 = (f32[256,272]{0,1:T(8,128)S(1)}, f32[256,272]{0,1:T(8,128)}, u32[]{:S(2)}) copy-start(f32[256,272]{0,1:T(8,128)} %copy-done.6) | copy-start | bytes 835588
  84.1 1.5 %copy-start.5 = (bf16[3,256,3,256]{3,1,2,0:T(8,128)(2,1)S(1)}, bf16[3,256,3,256]{3,1,2,0:T(8,128)(2,1)}, u32[]{:S(2)}) copy-start(bf16[3,256,3,256]{3,1,2,0:T(8,128)(2,1)} %param.9) | copy-start | bytes 3538948
  84.4 3.6 %copy-start.10 = (f32[256,256]{1,0:T(8,128)S(1)}, f32[256,256]{1,0:T(8,128)}, u32[]{:S(2)}) copy-start(f32[256,256]{1,0:T(8,128)} %param.14) | copy-start | bytes 786436
  85.6 2.4 %copy-start.8 = (f32[3,256,256]{1,2,0:T(8,128)S(1)}, f32[3,256,256]{1,2,0:T(8,128)}, u32[]{:S(2)}) copy-start(f32[3,256,256]{1,2,0:T(8,128)} %copy.22) | copy-start | bytes 2359300
Sparse Core Ops, SparseCore 0:
  23.8 47.2 all-reduce.1

commit v2 on v1

--- a/solution.py
+++ b/solution.py
@@ -42,6 +42,26 @@
     return pred, (a, p, q)
 
 
+def member_sum(x):
+    count = lax.axis_size("member")
+    me = lax.axis_index("member")
+    rows, lanes = x.shape
+    piece = -(-rows // (8 * count)) * 8
+    x = jnp.pad(x, ((0, piece * count - rows), (0, 0))).reshape(count, piece, lanes)
+    acc = lax.dynamic_index_in_dim(x, me, 0, keepdims=False)
+    for s in range(1, count):
+        shift = [(i, (i + s) % count) for i in range(count)]
+        sent = lax.dynamic_index_in_dim(x, (me + s) % count, 0, keepdims=False)
+        acc = acc + lax.ppermute(sent, "member", shift)
+    out = jnp.zeros_like(x)
+    out = lax.dynamic_update_index_in_dim(out, acc, me, 0)
+    for s in range(1, count):
+        shift = [(i, (i + s) % count) for i in range(count)]
+        got = lax.ppermute(acc, "member", shift)
+        out = lax.dynamic_update_index_in_dim(out, got, (me + count - s) % count, 0)
+    return out.reshape(piece * count, lanes)[:rows]
+
+
 def body(alpha, ensemble, background, measured_values, precision_factor, depth, loc_cols, loc_rows):
     highest = lax.Precision.HIGHEST
     ncol, nfield, nrow = background.shape
@@ -51,21 +71,23 @@
     inputs = jnp.concatenate(
         [background, measured_values, precision_factor, depth[:, None, :]], axis=1
     )
-    in_before, in_after = shift_rows(inputs, (inputs[:, :, :HALO], inputs[:, :, -HALO:]))
-
     localized = jnp.einsum("cd,kdr->kcr", loc_cols, alpha, precision=highest)
     localized = jnp.einsum("kcr,qr->kcq", localized, loc_rows, precision=highest)
     ens = ensemble.astype(jnp.float32)
-    partial = jnp.sum(ens * localized[:, :, None, :], axis=0).transpose(1, 0, 2)
-    p_before, p_after = shift_rows(partial, (partial[:, :, :HALO], partial[:, :, -HALO:]))
-    halo = jnp.concatenate([p_before, p_after], axis=2).transpose(0, 2, 1)
-    summed = lax.psum(jnp.concatenate([partial, halo], axis=1), "member")
-    incr_main = summed[:, :ncol]
-    incr_halo = summed[:, ncol:].transpose(0, 2, 1)
+    partial = jnp.sum(ens * localized[:, :, None, :], axis=0)
+    both = jnp.concatenate([partial, inputs], axis=1)
+    before, after = shift_rows(both, (both[:, :, :HALO], both[:, :, -HALO:]))
+    halo = jnp.concatenate([before[:, :nfield], after[:, :nfield]], axis=2).transpose(1, 2, 0)
+    flat = jnp.concatenate(
+        [partial.transpose(1, 0, 2).reshape(nfield * ncol, nrow),
+         halo.reshape(nfield * 2 * HALO, ncol)], axis=0)
+    summed = member_sum(flat)
+    incr_main = summed[: nfield * ncol].reshape(nfield, ncol, nrow)
+    incr_halo = summed[nfield * ncol:].reshape(nfield, 2 * HALO, ncol).transpose(0, 2, 1)
     incr = jnp.concatenate(
         [incr_halo[:, :, :HALO], incr_main, incr_halo[:, :, HALO:]], axis=2
     )
-    ext = jnp.concatenate([in_before, inputs, in_after], axis=2)
+    ext = jnp.concatenate([before[:, nfield:], inputs, after[:, nfield:]], axis=2)
 
     state = [ext[:, i] + incr[i] for i in range(nfield)]
     meas = [ext[:, nfield + i] for i in range(nfield)]

time: 97.3 us -> 79.2 us (0.81)
  the two profiles are of different devices: /device:TPU:0 before, /device:TPU:11 now
where the time goes in v2:
time: 79.2 us; the launch traced here: 78.1 us
  waiting for transfers between devices  32.8 us (41%)
  local copies, waits for them, and re-layouts  17.7 us (22%)
  other arithmetic  12.3 us (16%)
  starting transfers between devices  8.26 us (10%)
  matrix products  5.79 us (7%)
  between operations  1.25 us (2%)
    ppermute x3, waiting for transfers between devices, member_sum(): got = lax.ppermute(acc, 'member', shift)  14.6 us
    ppermute x3, waiting for transfers between devices, member_sum(): acc = acc + lax.ppermute(sent, 'member', shift)  13.8 us
    slice x3, local copies, waits for them, and re-layouts, body(): before, after = shift_rows(both, (both[:, :, :HALO], both[:, :, -HALO:]))  5.6 us
    concatenate x1, other arithmetic, body(): jnp.concatenate([before[:, nfield:], inputs, after[:, nfield:]], axis=2)  5.32 us
    unnamed x32, local copies, waits for them, and re-layouts  5.09 us
    ppermute x3, starting transfers between devices, member_sum(): acc = acc + lax.ppermute(sent, 'member', shift)  3.77 us
    ppermute x1, waiting for transfers between devices, shift_rows(): after = lax.ppermute(lo, 'tile', down)  3.58 us
    ppermute x3, starting transfers between devices, member_sum(): got = lax.ppermute(acc, 'member', shift)  2.71 us
  transfers between devices with their start and end apart: 8, of which 7 were waited for; matrix products, arithmetic and copies ran while one was open for 13% of the time, Pallas kernels for 0%

profile of v2, /device:TPU:11, one launch (start us, length us, event | category | flops | bytes accessed | tf_op | source)
XLA Modules:
  0.0 78.1 jit_solution(10060153335402070290)
XLA Ops:
  0.7 2.7 %convolution_bitcast_fusion.1 = f32[3,256,256]{1,2,0:T(8,128)S(1)} fusion(f32[3,256,256]{2,1,0:T(8,128)} %param.8, f32[256,256]{1,0:T(8,128)} %param.14), kind=kOutput, calls=%fused_computation.6 | convolution fusion | flops 603979776 | bytes 1835008 | tf_op jit(solution)/shard_map/cd,kdr->kcr/dot_general | solution.py:74
  3.4 1.4 %fusion.48 = f32[3,256,256]{2,1,0:T(8,128)S(1)} fusion(f32[3,256,256]{1,2,0:T(8,128)S(1)} %convolution_bitcast_fusion.1, f32[256,256]{1,0:T(8,128)S(1)} %copy-done), kind=kOutput, calls=%fused_computation.97 | convolution fusion | flops 603979776 | bytes 1835008 | tf_op jit(solution)/shard_map/kcr,qr->kcq/dot_general | solution.py:75
  6.3 1.8 %fusion.61 = (f32[256,13,8]{2,0,1:T(8,128)}, f32[256,13,8]{2,0,1:T(8,128)S(1)}) fusion(f32[256,13,256]{2,0,1:T(8,128)S(1)} %constant_dynamic-update-slice_fusion), kind=kLoop, calls=%fused_computation.119 | loop fusion | bytes 425984 | tf_op jit(solution)/shard_map/slice | solution.py:79
  8.2 2.6 %copy.33 = f32[256,13,8]{0,2,1:T(8,128)} copy(f32[256,13,8]{2,0,1:T(8,128)} %get-tuple-element.24) | data formatting | bytes 212992 | tf_op jit(solution)/shard_map/slice | solution.py:79
  10.8 1.8 %collective-permute-start = (f32[256,13,8]{0,2,1:T(8,128)}, f32[256,13,8]{0,2,1:T(8,128)}, u32[]{:S(2)}, u32[]{:S(2)}) collective-permute-start(f32[256,13,8]{0,2,1:T(8,128)} %copy.33), channel_id=1, source_target_pairs={{0,4},{4,8},{8,12},{12,16},{16,20},{20,24},{24,28},{28,0},{1,5},{5... | collective-permute-start | bytes 319496 | tf_op jit(solution)/shard_map/ppermute | solution.py:16
  12.6 1.1 %copy.34 = f32[256,13,8]{0,2,1:T(8,128)} copy(f32[256,13,8]{2,0,1:T(8,128)S(1)} %get-tuple-element.25) | data formatting | bytes 212992 | tf_op jit(solution)/shard_map/slice | solution.py:79
  13.7 0.9 %collective-permute-done = f32[256,13,8]{0,2,1:T(8,128)} collective-permute-done((f32[256,13,8]{0,2,1:T(8,128)}, f32[256,13,8]{0,2,1:T(8,128)}, u32[]{:S(2)}, u32[]{:S(2)}) %collective-permute-start) | collective-permute-done | bytes 106528 | tf_op jit(solution)/shard_map/ppermute | solution.py:16
  15.4 3.6 %collective-permute-done.1 = f32[256,13,8]{0,2,1:T(8,128)S(1)} collective-permute-done((f32[256,13,8]{0,2,1:T(8,128)}, f32[256,13,8]{0,2,1:T(8,128)S(1)}, u32[]{:S(2)}, u32[]{:S(2)}) %collective-permute-start.1) | collective-permute-done | bytes 106528 | tf_op jit(solution)/shard_map/ppermute | solution.py:17
  19.0 0.9 %copy-done.4 = f32[832,256]{1,0:T(8,128)} copy-done((f32[832,256]{1,0:T(8,128)}, f32[832,256]{1,0:T(8,128)S(1)}, u32[]{:S(2)}) %copy-start.4) | copy-done | bytes 851992
  20.8 1.3 %collective-permute-start.2 = (f32[208,256]{1,0:T(8,128)}, f32[208,256]{1,0:T(8,128)S(1)}, u32[]{:S(2)}, u32[]{:S(2)}) collective-permute-start(f32[208,256]{1,0:T(8,128)} %get-tuple-element.26), channel_id=1, source_target_pairs={{0,1},{1,2},{2,3},{3,0},{4,5},{5,6},{6,7},{7,4},{8,9},{9,10},{10,1... | collective-permute-start | bytes 638984 | tf_op jit(solution)/shard_map/ppermute | solution.py:55
  22.1 1.0 %collective-permute-start.3 = (f32[208,256]{1,0:T(8,128)}, f32[208,256]{1,0:T(8,128)}, u32[]{:S(2)}, u32[]{:S(2)}) collective-permute-start(f32[208,256]{1,0:T(8,128)} %get-tuple-element.28), channel_id=1, source_target_pairs={{0,2},{1,3},{2,0},{3,1},{4,6},{5,7},{6,4},{7,5},{8,10},{9,11},{10,... | collective-permute-start | bytes 638984 | tf_op jit(solution)/shard_map/ppermute | solution.py:55
  23.1 1.5 %collective-permute-start.4 = (f32[208,256]{1,0:T(8,128)}, f32[208,256]{1,0:T(8,128)}, u32[]{:S(2)}, u32[]{:S(2)}) collective-permute-start(f32[208,256]{1,0:T(8,128)} %get-tuple-element.27), channel_id=1, source_target_pairs={{0,3},{1,0},{2,1},{3,2},{4,7},{5,4},{6,5},{7,6},{8,11},{9,8},{10,9... | collective-permute-start | bytes 638984 | tf_op jit(solution)/shard_map/ppermute | solution.py:55
  24.6 1.1 %copy.40 = f32[3,256,256]{1,2,0:T(8,128)} copy(f32[3,256,256]{2,1,0:T(8,128)S(1)} %copy-done.5) | data formatting | bytes 1572864 | tf_op args[0]
  27.5 9.2 %collective-permute-done.2 = f32[208,256]{1,0:T(8,128)S(1)} collective-permute-done((f32[208,256]{1,0:T(8,128)}, f32[208,256]{1,0:T(8,128)S(1)}, u32[]{:S(2)}, u32[]{:S(2)}) %collective-permute-start.2) | collective-permute-done | bytes 213024 | tf_op jit(solution)/shard_map/ppermute | solution.py:55
  36.7 3.0 %collective-permute-done.3 = f32[208,256]{1,0:T(8,128)} collective-permute-done((f32[208,256]{1,0:T(8,128)}, f32[208,256]{1,0:T(8,128)}, u32[]{:S(2)}, u32[]{:S(2)}) %collective-permute-start.3) | collective-permute-done | bytes 213024 | tf_op jit(solution)/shard_map/ppermute | solution.py:55
  39.7 1.6 %collective-permute-done.4 = f32[208,256]{1,0:T(8,128)} collective-permute-done((f32[208,256]{1,0:T(8,128)}, f32[208,256]{1,0:T(8,128)}, u32[]{:S(2)}, u32[]{:S(2)}) %collective-permute-start.4) | collective-permute-done | bytes 213024 | tf_op jit(solution)/shard_map/ppermute | solution.py:55
  41.3 1.2 %bitcast_dynamic-update-slice_fusion.3 = (f32[4,208,256]{2,1,0:T(8,128)S(1)}, f32[208,256]{1,0:T(8,128)S(1)}) fusion(f32[4,208,256]{2,1,0:T(8,128)S(1)} %broadcast_in_dim.22, s32[]{:T(128)S(6)} %select_n.42, f32[208,256]{1,0:T(8,128)} %collective-permute-done.4, f32[208,256]{1,0:T(8,128)} %collective-permute-done.3, ...), kind=kLoop, calls=%fused_computation.104 | loop fusion | flops 159744 | bytes 1277956 | tf_op jit(solution)/shard_map/jit(dynamic_update_index_in_dim)/dynamic_update_slice | solution.py:57
  42.6 5.3 %pad_maximum_fusion = f32[256,10,272]{2,0,1:T(8,128)} fusion(f32[256,10,8]{2,0,1:T(8,128)S(1)} %copy.36, f32[256,1,256]{2,0,1:T(8,128)S(1)} %bitcast.143, f32[256,3,256]{2,0,1:T(8,128)} %param.12, f32[256,3,256]{2,0,1:T(8,128)} %param.11, f32[256,3,256]{2,0,1:T(8,128)} %param.10, f32[256,10,8]{2,0,1:T(8,128)S(1)} %copy.35), kind=kLoop, calls=%fused_computation | loop fusion | flops 3481600 | bytes 5570560 | tf_op jit(solution)/shard_map/concatenate | solution.py:90
  47.9 1.2 %collective-permute-start.6 = (f32[208,256]{1,0:T(8,128)S(1)}, f32[208,256]{1,0:T(8,128)S(1)}, u32[]{:S(2)}, u32[]{:S(2)}) collective-permute-start(f32[208,256]{1,0:T(8,128)S(1)} %get-tuple-element.19), channel_id=1, source_target_pairs={{0,2},{1,3},{2,0},{3,1},{4,6},{5,7},{6,4},{7,5},{8,10},{9,11},{10,... | collective-permute-start | bytes 638984 | tf_op jit(solution)/shard_map/ppermute | solution.py:60
  49.2 1.4 %collective-permute-start.7 = (f32[208,256]{1,0:T(8,128)S(1)}, f32[208,256]{1,0:T(8,128)S(1)}, u32[]{:S(2)}, u32[]{:S(2)}) collective-permute-start(f32[208,256]{1,0:T(8,128)S(1)} %get-tuple-element.19), channel_id=1, source_target_pairs={{0,3},{1,0},{2,1},{3,2},{4,7},{5,4},{6,5},{7,6},{8,11},{9,8},{10,9... | collective-permute-start | bytes 638984 | tf_op jit(solution)/shard_map/ppermute | solution.py:60
  50.6 12.3 %collective-permute-done.6 = f32[208,256]{1,0:T(8,128)S(1)} collective-permute-done((f32[208,256]{1,0:T(8,128)S(1)}, f32[208,256]{1,0:T(8,128)S(1)}, u32[]{:S(2)}, u32[]{:S(2)}) %collective-permute-start.6) | collective-permute-done | bytes 213024 | tf_op jit(solution)/shard_map/ppermute | solution.py:60
  62.9 2.3 %collective-permute-done.7 = f32[208,256]{1,0:T(8,128)S(1)} collective-permute-done((f32[208,256]{1,0:T(8,128)S(1)}, f32[208,256]{1,0:T(8,128)S(1)}, u32[]{:S(2)}, u32[]{:S(2)}) %collective-permute-start.7) | collective-permute-done | bytes 213024 | tf_op jit(solution)/shard_map/ppermute | solution.py:60
  66.1 1.4 %fusion.11 = (f32[256,272]{1,0:T(8,128)S(1)}, f32[256,272]{1,0:T(8,128)S(1)}) fusion(f32[3,256,272]{2,1,0:T(8,128)S(1)} %pad_maximum_fusion.1, f32[256,10,272]{2,0,1:T(8,128)} %pad_maximum_fusion), kind=kLoop, calls=%fused_computation.31 | loop fusion | flops 139264 | bytes 1671168 | tf_op jit(solution)/shard_map/add | solution.py:92
  76.2 1.1 %copy.41 = f32[3,256,256]{2,1,0:T(8,128)} copy(f32[3,256,256]{1,2,0:T(8,128)S(1)} %fusion.2) | data formatting | bytes 1572864
  (104 shorter events, 14.9 us)
Async XLA Ops:
  0.6 2.7 %copy-start = (f32[256,256]{1,0:T(8,128)S(1)}, f32[256,256]{1,0:T(8,128)}, u32[]{:S(2)}) copy-start(f32[256,256]{1,0:T(8,128)} %param.15) | copy-start | bytes 786436
  0.6 4.2 %copy-start.2 = (bf16[3,256,3,256]{3,1,2,0:T(8,128)(2,1)S(1)}, bf16[3,256,3,256]{3,1,2,0:T(8,128)(2,1)}, u32[]{:S(2)}) copy-start(bf16[3,256,3,256]{3,1,2,0:T(8,128)(2,1)} %param.9) | copy-start | bytes 3538948
  3.4 1.8 %copy-start.6 = (f32[256,3,256]{2,0,1:T(8,128)S(1)}, f32[256,3,256]{2,0,1:T(8,128)}, u32[]{:S(2)}) copy-start(f32[256,3,256]{2,0,1:T(8,128)} %param.10) | copy-start | bytes 2359300
  4.8 1.1 %copy-start.7 = (f32[256,3,256]{2,0,1:T(8,128)S(1)}, f32[256,3,256]{2,0,1:T(8,128)}, u32[]{:S(2)}) copy-start(f32[256,3,256]{2,0,1:T(8,128)} %param.11) | copy-start | bytes 2359300
  4.8 1.4 %copy-start.8 = (f32[256,3,256]{2,0,1:T(8,128)S(1)}, f32[256,3,256]{2,0,1:T(8,128)}, u32[]{:S(2)}) copy-start(f32[256,3,256]{2,0,1:T(8,128)} %param.12) | copy-start | bytes 2359300
  5.1 1.2 %copy-start.11 = (f32[256,256]{1,0:T(8,128)S(1)}, f32[256,256]{1,0:T(8,128)}, u32[]{:S(2)}) copy-start(f32[256,256]{1,0:T(8,128)} %param.13) | copy-start | bytes 786436
  8.2 16.4 %copy-start.5 = (f32[3,256,256]{2,1,0:T(8,128)S(1)}, f32[3,256,256]{2,1,0:T(8,128)}, u32[]{:S(2)}) copy-start(f32[3,256,256]{2,1,0:T(8,128)} %param.8) | copy-start | bytes 2359300
  10.8 3.8 %collective-permute-start = (f32[256,13,8]{0,2,1:T(8,128)}, f32[256,13,8]{0,2,1:T(8,128)}, u32[]{:S(2)}, u32[]{:S(2)}) collective-permute-start(f32[256,13,8]{0,2,1:T(8,128)} %copy.33), channel_id=1, source_target_pairs={{0,4},{4,8},{8,12},{12,16},{16,20},{20,24},{24,28},{28,0},{1,5},{5... | collective-permute-start | bytes 319496 | tf_op jit(solution)/shard_map/ppermute | solution.py:16
  13.7 5.2 %collective-permute-start.1 = (f32[256,13,8]{0,2,1:T(8,128)}, f32[256,13,8]{0,2,1:T(8,128)S(1)}, u32[]{:S(2)}, u32[]{:S(2)}) collective-permute-start(f32[256,13,8]{0,2,1:T(8,128)} %copy.34), channel_id=1, source_target_pairs={{4,0},{8,4},{12,8},{16,12},{20,16},{24,20},{28,24},{0,28},{5,1},{9... | collective-permute-start | bytes 319496 | tf_op jit(solution)/shard_map/ppermute | solution.py:17
  19.0 0.9 %copy-start.4 = (f32[832,256]{1,0:T(8,128)}, f32[832,256]{1,0:T(8,128)S(1)}, u32[]{:S(2)}) copy-start(f32[832,256]{1,0:T(8,128)S(1)} %select_maximum_fusion) | copy-start | bytes 2555908
  20.8 15.9 %collective-permute-start.2 = (f32[208,256]{1,0:T(8,128)}, f32[208,256]{1,0:T(8,128)S(1)}, u32[]{:S(2)}, u32[]{:S(2)}) collective-permute-start(f32[208,256]{1,0:T(8,128)} %get-tuple-element.26), channel_id=1, source_target_pairs={{0,1},{1,2},{2,3},{3,0},{4,5},{5,6},{6,7},{7,4},{8,9},{9,10},{10,1... | collective-permute-start | bytes 638984 | tf_op jit(solution)/shard_map/ppermute | solution.py:55
  22.1 17.6 %collective-permute-start.3 = (f32[208,256]{1,0:T(8,128)}, f32[208,256]{1,0:T(8,128)}, u32[]{:S(2)}, u32[]{:S(2)}) collective-permute-start(f32[208,256]{1,0:T(8,128)} %get-tuple-element.28), channel_id=1, source_target_pairs={{0,2},{1,3},{2,0},{3,1},{4,6},{5,7},{6,4},{7,5},{8,10},{9,11},{10,... | collective-permute-start | bytes 638984 | tf_op jit(solution)/shard_map/ppermute | solution.py:55
  23.1 18.1 %collective-permute-start.4 = (f32[208,256]{1,0:T(8,128)}, f32[208,256]{1,0:T(8,128)}, u32[]{:S(2)}, u32[]{:S(2)}) collective-permute-start(f32[208,256]{1,0:T(8,128)} %get-tuple-element.27), channel_id=1, source_target_pairs={{0,3},{1,0},{2,1},{3,2},{4,7},{5,4},{6,5},{7,6},{8,11},{9,8},{10,9... | collective-permute-start | bytes 638984 | tf_op jit(solution)/shard_map/ppermute | solution.py:55
  24.6 18.0 %copy-start.12 = (f32[256,256]{1,0:T(8,128)S(1)}, f32[256,256]{1,0:T(8,128)}, u32[]{:S(2)}) copy-start(f32[256,256]{1,0:T(8,128)} %param.13) | copy-start | bytes 786436
  42.5 8.1 %collective-permute-start.5 = (f32[208,256]{1,0:T(8,128)S(1)}, f32[208,256]{1,0:T(8,128)S(1)}, u32[]{:S(2)}, u32[]{:S(2)}) collective-permute-start(f32[208,256]{1,0:T(8,128)S(1)} %get-tuple-element.19), channel_id=1, source_target_pairs={{0,1},{1,2},{2,3},{3,0},{4,5},{5,6},{6,7},{7,4},{8,9},{9,10},{10,1... | collective-permute-start | bytes 638984 | tf_op jit(solution)/shard_map/ppermute | solution.py:60
  47.9 15.0 %collective-permute-start.6 = (f32[208,256]{1,0:T(8,128)S(1)}, f32[208,256]{1,0:T(8,128)S(1)}, u32[]{:S(2)}, u32[]{:S(2)}) collective-permute-start(f32[208,256]{1,0:T(8,128)S(1)} %get-tuple-element.19), channel_id=1, source_target_pairs={{0,2},{1,3},{2,0},{3,1},{4,6},{5,7},{6,4},{7,5},{8,10},{9,11},{10,... | collective-permute-start | bytes 638984 | tf_op jit(solution)/shard_map/ppermute | solution.py:60
  49.2 16.0 %collective-permute-start.7 = (f32[208,256]{1,0:T(8,128)S(1)}, f32[208,256]{1,0:T(8,128)S(1)}, u32[]{:S(2)}, u32[]{:S(2)}) collective-permute-start(f32[208,256]{1,0:T(8,128)S(1)} %get-tuple-element.19), channel_id=1, source_target_pairs={{0,3},{1,0},{2,1},{3,2},{4,7},{5,4},{6,5},{7,6},{8,11},{9,8},{10,9... | collective-permute-start | bytes 638984 | tf_op jit(solution)/shard_map/ppermute | solution.py:60
  66.1 2.4 %copy-start.1 = (f32[256,10,272]{2,0,1:T(8,128)S(1)}, f32[256,10,272]{2,0,1:T(8,128)}, u32[]{:S(2)}) copy-start(f32[256,10,272]{2,0,1:T(8,128)} %pad_maximum_fusion) | copy-start | bytes 8355844
  73.0 1.3 %copy-start.3 = (bf16[3,256,3,256]{3,1,2,0:T(8,128)(2,1)S(1)}, bf16[3,256,3,256]{3,1,2,0:T(8,128)(2,1)}, u32[]{:S(2)}) copy-start(bf16[3,256,3,256]{3,1,2,0:T(8,128)(2,1)} %param.9) | copy-start | bytes 3538948
  74.1 1.3 %copy-start.9 = (f32[3,256,256]{1,2,0:T(8,128)S(1)}, f32[3,256,256]{1,2,0:T(8,128)}, u32[]{:S(2)}) copy-start(f32[3,256,256]{1,2,0:T(8,128)} %copy.40) | copy-start | bytes 2359300
  74.1 1.3 %copy-start.10 = (f32[256,256]{1,0:T(8,128)S(1)}, f32[256,256]{1,0:T(8,128)}, u32[]{:S(2)}) copy-start(f32[256,256]{1,0:T(8,128)} %param.14) | copy-start | bytes 786436

commit v3 on v2

--- a/solution.py
+++ b/solution.py
@@ -62,37 +62,53 @@
     return out.reshape(piece * count, lanes)[:rows]
 
 
+def member_gather_sum(x):
+    count = lax.axis_size("member")
+    me = lax.axis_index("member")
+    pieces = jnp.zeros((count,) + x.shape, x.dtype)
+    pieces = lax.dynamic_update_index_in_dim(pieces, x, me, 0)
+    for s in range(1, count):
+        shift = [(i, (i + s) % count) for i in range(count)]
+        got = lax.ppermute(x, "member", shift)
+        pieces = lax.dynamic_update_index_in_dim(pieces, got, (me + count - s) % count, 0)
+    total = pieces[0]
+    for i in range(1, count):
+        total = total + pieces[i]
+    return total
+
+
 def body(alpha, ensemble, background, measured_values, precision_factor, depth, loc_cols, loc_rows):
     highest = lax.Precision.HIGHEST
     ncol, nfield, nrow = background.shape
     block_cols = ncol // lax.axis_size("member")
     col_start = lax.axis_index("member") * block_cols
 
-    inputs = jnp.concatenate(
-        [background, measured_values, precision_factor, depth[:, None, :]], axis=1
-    )
     localized = jnp.einsum("cd,kdr->kcr", loc_cols, alpha, precision=highest)
     localized = jnp.einsum("kcr,qr->kcq", localized, loc_rows, precision=highest)
     ens = ensemble.astype(jnp.float32)
     partial = jnp.sum(ens * localized[:, :, None, :], axis=0)
-    both = jnp.concatenate([partial, inputs], axis=1)
-    before, after = shift_rows(both, (both[:, :, :HALO], both[:, :, -HALO:]))
-    halo = jnp.concatenate([before[:, :nfield], after[:, :nfield]], axis=2).transpose(1, 2, 0)
-    flat = jnp.concatenate(
-        [partial.transpose(1, 0, 2).reshape(nfield * ncol, nrow),
-         halo.reshape(nfield * 2 * HALO, ncol)], axis=0)
-    summed = member_sum(flat)
-    incr_main = summed[: nfield * ncol].reshape(nfield, ncol, nrow)
-    incr_halo = summed[nfield * ncol:].reshape(nfield, 2 * HALO, ncol).transpose(0, 2, 1)
-    incr = jnp.concatenate(
-        [incr_halo[:, :, :HALO], incr_main, incr_halo[:, :, HALO:]], axis=2
-    )
-    ext = jnp.concatenate([before[:, nfield:], inputs, after[:, nfield:]], axis=2)
 
-    state = [ext[:, i] + incr[i] for i in range(nfield)]
-    meas = [ext[:, nfield + i] for i in range(nfield)]
-    prec = [ext[:, 2 * nfield + i] for i in range(nfield)]
-    dep = ext[:, 3 * nfield]
+    def edge(part):
+        return jnp.concatenate(
+            [partial[:, :, part], background[:, :, part], measured_values[:, :, part],
+             precision_factor[:, :, part], depth[:, None, part]], axis=1)
+
+    before, after = shift_rows(None, (edge(slice(0, HALO)), edge(slice(nrow - HALO, nrow))))
+    summed = member_sum(partial.transpose(1, 0, 2).reshape(nfield * ncol, nrow))
+    incr_main = summed.reshape(nfield, ncol, nrow)
+    halo = member_gather_sum(jnp.concatenate([before[:, :nfield], after[:, :nfield]], axis=2))
+
+    def extend(main, lo, hi):
+        return jnp.concatenate([lo, main, hi], axis=1)
+
+    state = [extend(background[:, i] + incr_main[i],
+                    before[:, nfield + i] + halo[:, i, :HALO],
+                    after[:, nfield + i] + halo[:, i, HALO:]) for i in range(nfield)]
+    meas = [extend(measured_values[:, i], before[:, 2 * nfield + i], after[:, 2 * nfield + i])
+            for i in range(nfield)]
+    prec = [extend(precision_factor[:, i], before[:, 3 * nfield + i], after[:, 3 * nfield + i])
+            for i in range(nfield)]
+    dep = extend(depth, before[:, 4 * nfield], after[:, 4 * nfield])
     pred, adj = dynamics(*state, dep, prec, meas)
 
     inner = slice(HALO, HALO + nrow)

time: 79.2 us -> 108 us (1.36)
  local copies, waits for them, and re-layouts: 17.7 us -> 58.8 us
  waiting for transfers between devices: 32.8 us -> 15.3 us
  starting transfers between devices: 8.26 us -> 16.7 us
  other arithmetic: 12.3 us -> 8.86 us
    unnamed x32 -> x94, local copies, waits for them, and re-layouts: 5.09 us -> 22 us
    squeeze x0 -> x15, local copies, waits for them, and re-layouts: none -> 16.5 us  [the longest x3 3.74 us: body(): after[:, 2 * nfield + i]]
    ppermute x3, waiting for transfers between devices: 13.8 us -> 0.01 us  [member_sum(): acc = acc + lax.ppermute(sent, 'member', shift)]
    ppermute x0 -> x3, starting transfers between devices: none -> 6.16 us  [member_gather_sum(): got = lax.ppermute(x, 'member', shift)]
    concatenate x3 -> x1, other arithmetic: 5.86 us -> 0.34 us  [extend(): return jnp.concatenate([lo, main, hi], axis=1)]
    add x0 -> x6, local copies, waits for them, and re-layouts: none -> 4.78 us  [the longest x3 2.39 us: body(): before[:, nfield + i] + halo[:, i, :HALO]]
    ppermute x3, waiting for transfers between devices: 14.6 us -> 12.1 us  [member_sum(): got = lax.ppermute(acc, 'member', shift)]
    ppermute x1, waiting for transfers between devices: 3.58 us -> 1.47 us  [shift_rows(): after = lax.ppermute(lo, 'tile', down)]
  transfers between devices with their start and end apart: 8 -> 11, of which waited for: 7 -> 4; matrix products, arithmetic and copies ran while one was open for 13% -> 47% of each run, Pallas kernels for 0% -> 0%
where the time goes in v3:
time: 108 us; the launch traced here: 107 us
  local copies, waits for them, and re-layouts  58.8 us (54%)
  starting transfers between devices  16.7 us (15%)
  waiting for transfers between devices  15.3 us (14%)
  other arithmetic  8.86 us (8%)
  matrix products  5.7 us (5%)
  between operations  1.44 us (1%)
    unnamed x94, local copies, waits for them, and re-layouts  22 us
    ppermute x3, waiting for transfers between devices, member_sum(): got = lax.ppermute(acc, 'member', shift)  12.1 us
    ppermute x3, starting transfers between devices, member_gather_sum(): got = lax.ppermute(x, 'member', shift)  6.16 us
    ppermute x3, starting transfers between devices, member_sum(): got = lax.ppermute(acc, 'member', shift)  4.12 us
    ppermute x3, starting transfers between devices, member_sum(): acc = acc + lax.ppermute(sent, 'member', shift)  3.77 us
    squeeze x3, local copies, waits for them, and re-layouts, body(): after[:, 2 * nfield + i]  3.74 us
    squeeze x3, local copies, waits for them, and re-layouts, body(): after[:, 3 * nfield + i]  3.74 us
    slice x19, local copies, waits for them, and re-layouts, row_slope(): return 0.5 * (jnp.roll(f, -1, 1) - jnp.roll(f, 1, 1))  3.72 us
  transfers between devices with their start and end apart: 11, of which 4 were waited for; matrix products, arithmetic and copies ran while one was open for 47% of the time, Pallas kernels for 0%

profile of v3, /device:TPU:11, one launch (start us, length us, event | category | flops | bytes accessed | tf_op | source)
XLA Modules:
  0.0 106.7 jit_solution(2248306464059217172)
XLA Ops:
  0.7 2.6 %convolution_bitcast_fusion.1 = f32[3,256,256]{1,2,0:T(8,128)S(1)} fusion(f32[3,256,256]{2,1,0:T(8,128)} %param.8, f32[256,256]{1,0:T(8,128)} %param.14), kind=kOutput, calls=%fused_computation.5 | convolution fusion | flops 603979776 | bytes 1835008 | tf_op jit(solution)/shard_map/cd,kdr->kcr/dot_general | solution.py:86
  3.3 1.4 %fusion.39 = f32[3,256,256]{2,1,0:T(8,128)S(1)} fusion(f32[3,256,256]{1,2,0:T(8,128)S(1)} %convolution_bitcast_fusion.1, f32[256,256]{1,0:T(8,128)S(1)} %copy-done), kind=kOutput, calls=%fused_computation.84 | convolution fusion | flops 603979776 | bytes 1835008 | tf_op jit(solution)/shard_map/kcr,qr->kcq/dot_general | solution.py:87
  8.2 1.5 %collective-permute-start.7 = (f32[192,256]{1,0:T(8,128)}, f32[192,256]{1,0:T(8,128)}, u32[]{:S(2)}, u32[]{:S(2)}) collective-permute-start(f32[192,256]{1,0:T(8,128)} %get-tuple-element.28), channel_id=1, source_target_pairs={{0,3},{1,0},{2,1},{3,2},{4,7},{5,4},{6,5},{7,6},{8,11},{9,8},{10,9... | collective-permute-start | bytes 589832 | tf_op jit(solution)/shard_map/ppermute | solution.py:55
  12.5 2.1 %fusion.63 = (f32[256,3,8]{2,0,1:T(8,128)}, f32[256,3,8]{2,0,1:T(8,128)}) fusion(f32[256,3,256]{2,0,1:T(8,128)} %param.10), kind=kLoop, calls=%fused_computation.155 | loop fusion | bytes 98304 | tf_op jit(solution)/shard_map/slice | solution.py:93
  14.6 1.7 %copy.84 = f32[256,3,8]{0,2,1:T(8,128)} copy(f32[256,3,8]{2,0,1:T(8,128)} %get-tuple-element.34) | data formatting | bytes 49152
  17.3 1.8 %copy.85 = f32[256,3,8]{0,2,1:T(8,128)} copy(f32[256,3,8]{2,0,1:T(8,128)} %get-tuple-element.32) | data formatting | bytes 49152
  19.1 2.2 %fusion.61 = (f32[256,3,8]{2,0,1:T(8,128)}, f32[256,3,8]{2,0,1:T(8,128)}) fusion(f32[256,3,256]{2,0,1:T(8,128)} %param.12), kind=kLoop, calls=%fused_computation.153 | loop fusion | bytes 98304 | tf_op jit(solution)/shard_map/slice | solution.py:94
  21.2 1.8 %copy.86 = f32[256,3,8]{0,2,1:T(8,128)} copy(f32[256,3,8]{2,0,1:T(8,128)} %get-tuple-element.30) | data formatting | bytes 49152
  23.2 1.4 %constant_dynamic-update-slice_fusion.3 = f32[256,13,8]{0,2,1:T(8,128)} fusion(f32[256,13,8]{0,2,1:T(8,128)} %constant_dynamic-update-slice_fusion.4, f32[256,3,8]{0,2,1:T(8,128)} %copy.84), kind=kLoop, calls=%fused_computation.118 | loop fusion | bytes 49152
  27.8 2.6 %collective-permute-start = (f32[256,13,8]{0,2,1:T(8,128)}, f32[256,13,8]{0,2,1:T(8,128)S(1)}, u32[]{:S(2)}, u32[]{:S(2)}) collective-permute-start(f32[256,13,8]{0,2,1:T(8,128)} %constant_dynamic-update-slice_fusion), channel_id=1, source_target_pairs={{0,4},{4,8},{8,12},{12,16},{16,20},{20,24},{24,28},{28,0},{1,5},{5... | collective-permute-start | bytes 319496 | tf_op jit(solution)/shard_map/ppermute | solution.py:16
  36.1 2.6 %slice_bitcast_fusion.11 = (f32[256,256]{1,0:T(8,128)}, f32[256,256]{1,0:T(8,128)}, f32[256,256]{1,0:T(8,128)}, f32[256,256]{1,0:T(8,128)}, f32[256,256]{1,0:T(8,128)}, /*index=5*/f32[256,256]{1,0:T(8,128)}) fusion(f32[256,3,256]{2,0,1:T(8,128)} %param.11, f32[256,3,256]{2,0,1:T(8,128)} %param.12), kind=kLoop, calls=%fused_computation.92 | loop fusion | bytes 3145728 | tf_op jit(solution)/shard_map/squeeze | solution.py:107
  39.8 1.5 %collective-permute-done.1 = f32[256,13,8]{0,2,1:T(8,128)S(1)} collective-permute-done((f32[256,13,8]{0,2,1:T(8,128)}, f32[256,13,8]{0,2,1:T(8,128)S(1)}, u32[]{:S(2)}, u32[]{:S(2)}) %collective-permute-start.1) | collective-permute-done | bytes 106528 | tf_op jit(solution)/shard_map/ppermute | solution.py:17
  41.4 3.1 %collective-permute-start.3 = (f32[256,3,16]{0,2,1:T(8,128)S(1)}, f32[256,3,16]{0,2,1:T(8,128)S(1)}, u32[]{:S(2)}, u32[]{:S(2)}) collective-permute-start(f32[256,3,16]{0,2,1:T(8,128)S(1)} %pad_maximum_fusion.8), channel_id=1, source_target_pairs={{0,2},{1,3},{2,0},{3,1},{4,6},{5,7},{6,4},{7,5},{8,10},{9,11},{10,... | collective-permute-start | bytes 147464 | tf_op jit(solution)/shard_map/ppermute | solution.py:72
  44.7 3.0 %collective-permute-start.4 = (f32[256,3,16]{0,2,1:T(8,128)S(1)}, f32[256,3,16]{0,2,1:T(8,128)S(1)}, u32[]{:S(2)}, u32[]{:S(2)}) collective-permute-start(f32[256,3,16]{0,2,1:T(8,128)S(1)} %pad_maximum_fusion.8), channel_id=1, source_target_pairs={{0,3},{1,0},{2,1},{3,2},{4,7},{5,4},{6,5},{7,6},{8,11},{9,8},{10,9... | collective-permute-start | bytes 147464 | tf_op jit(solution)/shard_map/ppermute | solution.py:72
  47.7 1.5 %collective-permute-done.4 = f32[256,3,16]{0,2,1:T(8,128)S(1)} collective-permute-done((f32[256,3,16]{0,2,1:T(8,128)S(1)}, f32[256,3,16]{0,2,1:T(8,128)S(1)}, u32[]{:S(2)}, u32[]{:S(2)}) %collective-permute-start.4) | collective-permute-done | bytes 49184 | tf_op jit(solution)/shard_map/ppermute | solution.py:72
  50.7 1.9 %bitcast_dynamic-update-slice_fusion.3 = (f32[4,192,256]{2,1,0:T(8,128)S(1)}, f32[192,256]{1,0:T(8,128)}) fusion(f32[4,192,256]{2,1,0:T(8,128)S(1)} %broadcast_in_dim.47, s32[]{:T(128)S(6)} %select_n.53, f32[192,256]{1,0:T(8,128)} %collective-permute-done.7, f32[192,256]{1,0:T(8,128)} %collective-permute-done.6, f32[192,256]{1,0:T(8,128)} %collective-permute-done.5, ...), kind=kLoop, calls=%fused_computation.99 | loop fusion | flops 147456 | bytes 1179652 | tf_op jit(solution)/shard_map/jit(dynamic_update_index_in_dim)/dynamic_update_slice | solution.py:57
  62.2 1.5 %copy.74 = f32[256,8]{1,0:T(8,128)} copy(f32[256,8]{0,1:T(8,128)} %get-tuple-element.110) | data formatting | bytes 16384 | tf_op jit(solution)/shard_map/squeeze | solution.py:109
  63.8 1.5 %copy.76 = f32[256,8]{1,0:T(8,128)} copy(f32[256,8]{0,1:T(8,128)} %get-tuple-element.109) | data formatting | bytes 16384 | tf_op jit(solution)/shard_map/squeeze | solution.py:107
  65.3 1.5 %copy.75 = f32[256,8]{1,0:T(8,128)} copy(f32[256,8]{0,1:T(8,128)} %get-tuple-element.120) | data formatting | bytes 16384 | tf_op jit(solution)/shard_map/squeeze | solution.py:109
  66.8 1.5 %copy.77 = f32[256,8]{1,0:T(8,128)} copy(f32[256,8]{0,1:T(8,128)} %get-tuple-element.119) | data formatting | bytes 16384 | tf_op jit(solution)/shard_map/squeeze | solution.py:107
  69.8 1.5 %copy.57 = f32[256,8]{1,0:T(8,128)} copy(f32[256,8]{0,1:T(8,128)} %get-tuple-element.118) | data formatting | bytes 16384 | tf_op jit(solution)/shard_map/squeeze | solution.py:109
  71.3 1.5 %copy.69 = f32[256,8]{1,0:T(8,128)} copy(f32[256,8]{0,1:T(8,128)} %get-tuple-element.123) | data formatting | bytes 16384 | tf_op jit(solution)/shard_map/squeeze | solution.py:107
  72.8 3.9 %collective-permute-start.9 = (f32[192,256]{1,0:T(8,128)}, f32[192,256]{1,0:T(8,128)S(1)}, u32[]{:S(2)}, u32[]{:S(2)}) collective-permute-start(f32[192,256]{1,0:T(8,128)} %get-tuple-element.17), channel_id=1, source_target_pairs={{0,2},{1,3},{2,0},{3,1},{4,6},{5,7},{6,4},{7,5},{8,10},{9,11},{10,... | collective-permute-start | bytes 589832 | tf_op jit(solution)/shard_map/ppermute | solution.py:60
  77.8 12.1 %collective-permute-done.9 = f32[192,256]{1,0:T(8,128)S(1)} collective-permute-done((f32[192,256]{1,0:T(8,128)}, f32[192,256]{1,0:T(8,128)S(1)}, u32[]{:S(2)}, u32[]{:S(2)}) %collective-permute-start.9) | collective-permute-done | bytes 196640 | tf_op jit(solution)/shard_map/ppermute | solution.py:60
  (200 shorter events, 47.7 us)
Async XLA Ops:
  0.6 2.7 %copy-start = (f32[256,256]{1,0:T(8,128)S(1)}, f32[256,256]{1,0:T(8,128)}, u32[]{:S(2)}) copy-start(f32[256,256]{1,0:T(8,128)} %param.15) | copy-start | bytes 786436
  3.3 1.5 %copy-start.2 = (bf16[3,256,3,256]{3,1,2,0:T(8,128)(2,1)S(1)}, bf16[3,256,3,256]{3,1,2,0:T(8,128)(2,1)}, u32[]{:S(2)}) copy-start(bf16[3,256,3,256]{3,1,2,0:T(8,128)(2,1)} %param.9) | copy-start | bytes 3538948
  5.9 44.7 %collective-permute-start.5 = (f32[192,256]{1,0:T(8,128)}, f32[192,256]{1,0:T(8,128)}, u32[]{:S(2)}, u32[]{:S(2)}) collective-permute-start(f32[192,256]{1,0:T(8,128)} %get-tuple-element.27), channel_id=1, source_target_pairs={{0,1},{1,2},{2,3},{3,0},{4,5},{5,6},{6,7},{7,4},{8,9},{9,10},{10,1... | collective-permute-start | bytes 589832 | tf_op jit(solution)/shard_map/ppermute | solution.py:55
  7.2 43.4 %collective-permute-start.6 = (f32[192,256]{1,0:T(8,128)}, f32[192,256]{1,0:T(8,128)}, u32[]{:S(2)}, u32[]{:S(2)}) collective-permute-start(f32[192,256]{1,0:T(8,128)} %get-tuple-element.29), channel_id=1, source_target_pairs={{0,2},{1,3},{2,0},{3,1},{4,6},{5,7},{6,4},{7,5},{8,10},{9,11},{10,... | collective-permute-start | bytes 589832 | tf_op jit(solution)/shard_map/ppermute | solution.py:55
  8.2 42.4 %collective-permute-start.7 = (f32[192,256]{1,0:T(8,128)}, f32[192,256]{1,0:T(8,128)}, u32[]{:S(2)}, u32[]{:S(2)}) collective-permute-start(f32[192,256]{1,0:T(8,128)} %get-tuple-element.28), channel_id=1, source_target_pairs={{0,3},{1,0},{2,1},{3,2},{4,7},{5,4},{6,5},{7,6},{8,11},{9,8},{10,9... | collective-permute-start | bytes 589832 | tf_op jit(solution)/shard_map/ppermute | solution.py:55
  10.7 5.6 %copy-start.4 = (f32[256,3,256]{2,0,1:T(8,128)S(1)}, f32[256,3,256]{2,0,1:T(8,128)}, u32[]{:S(2)}) copy-start(f32[256,3,256]{2,0,1:T(8,128)} %param.11) | copy-start | bytes 2359300
  17.3 5.7 %copy-start.1 = (f32[256,256]{1,0:T(8,128)S(1)}, f32[256,256]{1,0:T(8,128)}, u32[]{:S(2)}) copy-start(f32[256,256]{1,0:T(8,128)} %param.13) | copy-start | bytes 786436
  19.1 11.3 %copy-start.7 = (f32[256,3,8]{2,0,1:T(8,128)S(1)}, f32[256,3,8]{2,0,1:T(8,128)}, u32[]{:S(2)}) copy-start(f32[256,3,8]{2,0,1:T(8,128)} %get-tuple-element.37) | copy-start | bytes 73732
  21.2 9.9 %copy-start.8 = (f32[256,3,8]{2,0,1:T(8,128)S(1)}, f32[256,3,8]{2,0,1:T(8,128)}, u32[]{:S(2)}) copy-start(f32[256,3,8]{2,0,1:T(8,128)} %get-tuple-element.35) | copy-start | bytes 73732
  27.8 12.0 %collective-permute-start = (f32[256,13,8]{0,2,1:T(8,128)}, f32[256,13,8]{0,2,1:T(8,128)S(1)}, u32[]{:S(2)}, u32[]{:S(2)}) collective-permute-start(f32[256,13,8]{0,2,1:T(8,128)} %constant_dynamic-update-slice_fusion), channel_id=1, source_target_pairs={{0,4},{4,8},{8,12},{12,16},{16,20},{20,24},{24,28},{28,0},{1,5},{5... | collective-permute-start | bytes 319496 | tf_op jit(solution)/shard_map/ppermute | solution.py:16
  36.0 2.6 %copy-start.3 = (f32[3,256,256]{2,1,0:T(8,128)S(1)}, f32[3,256,256]{2,1,0:T(8,128)}, u32[]{:S(2)}) copy-start(f32[3,256,256]{2,1,0:T(8,128)} %param.8) | copy-start | bytes 2359300
  36.0 5.2 %collective-permute-start.1 = (f32[256,13,8]{0,2,1:T(8,128)}, f32[256,13,8]{0,2,1:T(8,128)S(1)}, u32[]{:S(2)}, u32[]{:S(2)}) collective-permute-start(f32[256,13,8]{0,2,1:T(8,128)} %constant_dynamic-update-slice_fusion.5), channel_id=1, source_target_pairs={{4,0},{8,4},{12,8},{16,12},{20,16},{24,20},{28,24},{0,28},{5,1},{9... | collective-permute-start | bytes 319496 | tf_op jit(solution)/shard_map/ppermute | solution.py:17
  41.3 9.4 %copy-start.36 = (f32[256,13,8]{0,2,1:T(8,128)}, f32[256,13,8]{0,2,1:T(8,128)S(1)}, u32[]{:S(2)}) copy-start(f32[256,13,8]{0,2,1:T(8,128)S(1)} %collective-permute-done.1) | copy-start | bytes 319492
  41.3 3.4 %collective-permute-start.2 = (f32[256,3,16]{0,2,1:T(8,128)S(1)}, f32[256,3,16]{0,2,1:T(8,128)S(1)}, u32[]{:S(2)}, u32[]{:S(2)}) collective-permute-start(f32[256,3,16]{0,2,1:T(8,128)S(1)} %pad_maximum_fusion.8), channel_id=1, source_target_pairs={{0,1},{1,2},{2,3},{3,0},{4,5},{5,6},{6,7},{7,4},{8,9},{9,10},{10,1... | collective-permute-start | bytes 147464 | tf_op jit(solution)/shard_map/ppermute | solution.py:72
  41.4 6.3 %collective-permute-start.3 = (f32[256,3,16]{0,2,1:T(8,128)S(1)}, f32[256,3,16]{0,2,1:T(8,128)S(1)}, u32[]{:S(2)}, u32[]{:S(2)}) collective-permute-start(f32[256,3,16]{0,2,1:T(8,128)S(1)} %pad_maximum_fusion.8), channel_id=1, source_target_pairs={{0,2},{1,3},{2,0},{3,1},{4,6},{5,7},{6,4},{7,5},{8,10},{9,11},{10,... | collective-permute-start | bytes 147464 | tf_op jit(solution)/shard_map/ppermute | solution.py:72
  44.7 4.5 %collective-permute-start.4 = (f32[256,3,16]{0,2,1:T(8,128)S(1)}, f32[256,3,16]{0,2,1:T(8,128)S(1)}, u32[]{:S(2)}, u32[]{:S(2)}) collective-permute-start(f32[256,3,16]{0,2,1:T(8,128)S(1)} %pad_maximum_fusion.8), channel_id=1, source_target_pairs={{0,3},{1,0},{2,1},{3,2},{4,7},{5,4},{6,5},{7,6},{8,11},{9,8},{10,9... | collective-permute-start | bytes 147464 | tf_op jit(solution)/shard_map/ppermute | solution.py:72
  50.7 1.9 %copy-start.37 = (f32[256,13,8]{0,2,1:T(8,128)S(1)}, f32[256,13,8]{0,2,1:T(8,128)}, u32[]{:S(2)}) copy-start(f32[256,13,8]{0,2,1:T(8,128)} %copy-done.36) | copy-start | bytes 319492
  52.6 24.3 %collective-permute-start.8 = (f32[192,256]{1,0:T(8,128)}, f32[192,256]{1,0:T(8,128)}, u32[]{:S(2)}, u32[]{:S(2)}) collective-permute-start(f32[192,256]{1,0:T(8,128)} %get-tuple-element.17), channel_id=1, source_target_pairs={{0,1},{1,2},{2,3},{3,0},{4,5},{5,6},{6,7},{7,4},{8,9},{9,10},{10,1... | collective-permute-start | bytes 589832 | tf_op jit(solution)/shard_map/ppermute | solution.py:60
  62.2 27.8 %copy-start.5 = (f32[256,3,256]{2,0,1:T(8,128)S(1)}, f32[256,3,256]{2,0,1:T(8,128)}, u32[]{:S(2)}) copy-start(f32[256,3,256]{2,0,1:T(8,128)} %param.10) | copy-start | bytes 2359300
  72.8 17.2 %collective-permute-start.9 = (f32[192,256]{1,0:T(8,128)}, f32[192,256]{1,0:T(8,128)S(1)}, u32[]{:S(2)}, u32[]{:S(2)}) collective-permute-start(f32[192,256]{1,0:T(8,128)} %get-tuple-element.17), channel_id=1, source_target_pairs={{0,2},{1,3},{2,0},{3,1},{4,6},{5,7},{6,4},{7,5},{8,10},{9,11},{10,... | collective-permute-start | bytes 589832 | tf_op jit(solution)/shard_map/ppermute | solution.py:60
  76.7 13.3 %collective-permute-start.10 = (f32[192,256]{1,0:T(8,128)}, f32[192,256]{1,0:T(8,128)S(1)}, u32[]{:S(2)}, u32[]{:S(2)}) collective-permute-start(f32[192,256]{1,0:T(8,128)} %get-tuple-element.17), channel_id=1, source_target_pairs={{0,3},{1,0},{2,1},{3,2},{4,7},{5,4},{6,5},{7,6},{8,11},{9,8},{10,9... | collective-permute-start | bytes 589832 | tf_op jit(solution)/shard_map/ppermute | solution.py:60
  94.7 1.1 %copy-start.31 = (f32[256,8]{1,0:T(8,128)S(1)}, f32[256,8]{1,0:T(8,128)}, u32[]{:S(2)}) copy-start(f32[256,8]{1,0:T(8,128)} %copy.73) | copy-start | bytes 24580
  96.3 1.1 %copy-start.27 = (f32[256,8]{1,0:T(8,128)S(1)}, f32[256,8]{1,0:T(8,128)}, u32[]{:S(2)}) copy-start(f32[256,8]{1,0:T(8,128)} %copy.77) | copy-start | bytes 24580
  102.9 1.2 %copy-start.9 = (f32[256,256]{1,0:T(8,128)S(1)}, f32[256,256]{1,0:T(8,128)}, u32[]{:S(2)}) copy-start(f32[256,256]{1,0:T(8,128)} %param.14) | copy-start | bytes 786436
  (25 other events, 25.8 us)

commit v4 on v2

--- a/solution.py
+++ b/solution.py
@@ -62,6 +62,23 @@
     return out.reshape(piece * count, lanes)[:rows]
 
 
+def member_gather_sum(x):
+    count = lax.axis_size("member")
+    me = lax.axis_index("member")
+    pieces = [None] * count
+    pieces[0] = x
+    for s in range(1, count):
+        shift = [(i, (i + s) % count) for i in range(count)]
+        pieces[s] = lax.ppermute(x, "member", shift)
+    total = None
+    for src in range(count):
+        term = pieces[0]
+        for s in range(1, count):
+            term = jnp.where((me + count - s) % count == src, pieces[s], term)
+        total = term if total is None else total + term
+    return total
+
+
 def body(alpha, ensemble, background, measured_values, precision_factor, depth, loc_cols, loc_rows):
     highest = lax.Precision.HIGHEST
     ncol, nfield, nrow = background.shape
@@ -71,19 +88,25 @@
     inputs = jnp.concatenate(
         [background, measured_values, precision_factor, depth[:, None, :]], axis=1
     )
-    localized = jnp.einsum("cd,kdr->kcr", loc_cols, alpha, precision=highest)
-    localized = jnp.einsum("kcr,qr->kcq", localized, loc_rows, precision=highest)
+    mem = alpha.shape[0]
+    cols_b = jnp.broadcast_to(loc_cols, (mem,) + loc_cols.shape)
+    rows_b = jnp.broadcast_to(loc_rows, (mem,) + loc_rows.shape)
+    def batched(lhs_dim, rhs_dim):
+        return (((lhs_dim,), (rhs_dim,)), ((0,), (0,)))
+
+    localized = lax.dot_general(cols_b, alpha, batched(2, 1), precision=highest)
+    localized = lax.dot_general(localized, rows_b, batched(2, 2), precision=highest)
     ens = ensemble.astype(jnp.float32)
     partial = jnp.sum(ens * localized[:, :, None, :], axis=0)
     both = jnp.concatenate([partial, inputs], axis=1)
-    before, after = shift_rows(both, (both[:, :, :HALO], both[:, :, -HALO:]))
-    halo = jnp.concatenate([before[:, :nfield], after[:, :nfield]], axis=2).transpose(1, 2, 0)
-    flat = jnp.concatenate(
-        [partial.transpose(1, 0, 2).reshape(nfield * ncol, nrow),
-         halo.reshape(nfield * 2 * HALO, ncol)], axis=0)
-    summed = member_sum(flat)
-    incr_main = summed[: nfield * ncol].reshape(nfield, ncol, nrow)
-    incr_halo = summed[nfield * ncol:].reshape(nfield, 2 * HALO, ncol).transpose(0, 2, 1)
+    before, after = shift_rows(
+        None, (both[:, :, :HALO].transpose(1, 2, 0), both[:, :, -HALO:].transpose(1, 2, 0)))
+    halo = jnp.concatenate([before[:nfield], after[:nfield]], axis=1)
+    before = before.transpose(2, 0, 1)
+    after = after.transpose(2, 0, 1)
+    summed = member_sum(partial.transpose(1, 0, 2).reshape(nfield * ncol, nrow))
+    incr_main = summed.reshape(nfield, ncol, nrow)
+    incr_halo = member_gather_sum(halo).transpose(0, 2, 1)
     incr = jnp.concatenate(
         [incr_halo[:, :, :HALO], incr_main, incr_halo[:, :, HALO:]], axis=2
     )
@@ -100,8 +123,8 @@
     predicted_final = lax.dynamic_slice_in_dim(pred, col_start, block_cols, 0)
     adj = jnp.stack([f[:, inner] for f in adj], axis=1)
     projected = jnp.sum(ens * adj[None], axis=2)
-    rows_done = jnp.einsum("knr,rq->knq", projected, loc_rows, precision=highest)
-    cost_derivative = alpha + jnp.einsum("cd,kcq->kdq", loc_cols, rows_done, precision=highest)
+    rows_done = lax.dot_general(projected, rows_b, batched(2, 1), precision=highest)
+    cost_derivative = alpha + lax.dot_general(cols_b, rows_done, batched(1, 1), precision=highest)
     return (cost_derivative, predicted_final)
 
 

time: 79.2 us -> 72 us (0.909)
  waiting for transfers between devices: 32.8 us -> 22.8 us
  starting transfers between devices: 8.26 us -> 11.9 us
    ppermute x3, waiting for transfers between devices: 13.8 us -> 4.95 us  [member_sum(): acc = acc + lax.ppermute(sent, 'member', shift)]
    slice x7 -> x2, local copies, waits for them, and re-layouts: 6.4 us -> 0.82 us  [body(): halo = jnp.concatenate([before[:nfield], after[:nfield]], axis=1)]
    transpose x0 -> x3, local copies, waits for them, and re-layouts: none -> 5.58 us  [the longest x2 4.47 us: body(): both[:, :, -HALO:].transpose(1, 2, 0)]
    ppermute x0 -> x3, starting transfers between devices: none -> 4.68 us  [member_gather_sum(): pieces[s] = lax.ppermute(x, 'member', shift)]
    ppermute x1, waiting for transfers between devices: 3.58 us -> 0.13 us  [shift_rows(): after = lax.ppermute(lo, 'tile', down)]
    ppermute x3, waiting for transfers between devices: 14.6 us -> 16.9 us  [member_sum(): got = lax.ppermute(acc, 'member', shift)]
    slice x2, local copies, waits for them, and re-layouts: 0.4 us -> 2.39 us  [body(): after[:, nfield:]]
    unnamed x32 -> x36, local copies, waits for them, and re-layouts: 5.09 us -> 3.58 us
  transfers between devices with their start and end apart: 8 -> 11, of which waited for: 7 -> 6; matrix products, arithmetic and copies ran while one was open for 13% -> 21% of each run, Pallas kernels for 0% -> 0%
where the time goes in v4:
time: 72 us; the launch traced here: 71.6 us
  waiting for transfers between devices  22.8 us (32%)
  local copies, waits for them, and re-layouts  18.1 us (25%)
  other arithmetic  12.4 us (17%)
  starting transfers between devices  11.9 us (17%)
  matrix products  5.25 us (7%)
  between operations  1.25 us (2%)
    ppermute x3, waiting for transfers between devices, member_sum(): got = lax.ppermute(acc, 'member', shift)  16.9 us
    concatenate x1, other arithmetic, body(): jnp.concatenate([before[:, nfield:], inputs, after[:, nfield:]], axis=2)  5.38 us
    ppermute x3, waiting for transfers between devices, member_sum(): acc = acc + lax.ppermute(sent, 'member', shift)  4.95 us
    ppermute x3, starting transfers between devices, member_gather_sum(): pieces[s] = lax.ppermute(x, 'member', shift)  4.68 us
    transpose x2, local copies, waits for them, and re-layouts, body(): both[:, :, -HALO:].transpose(1, 2, 0)  4.47 us
    unnamed x36, local copies, waits for them, and re-layouts  3.58 us
    ppermute x3, starting transfers between devices, member_sum(): got = lax.ppermute(acc, 'member', shift)  3.11 us
    slice x2, local copies, waits for them, and re-layouts, body(): after[:, nfield:]  2.39 us
  transfers between devices with their start and end apart: 11, of which 6 were waited for; matrix products, arithmetic and copies ran while one was open for 21% of the time, Pallas kernels for 0%

profile of v4, /device:TPU:11, one launch (start us, length us, event | category | flops | bytes accessed | tf_op | source)
XLA Modules:
  0.0 71.6 jit_solution(9645508530719659952)
XLA Ops:
  0.7 2.1 %fusion.43 = f32[3,256,256]{2,1,0:T(8,128)S(1)} fusion(f32[3,256,256]{2,1,0:T(8,128)} %param.8, f32[256,256]{1,0:T(8,128)} %param.14), kind=kOutput, calls=%fused_computation.81 | convolution fusion | flops 603979776 | bytes 1835008 | tf_op jit(solution)/shard_map/dot_general | solution.py:97
  5.2 1.8 %slice_bitcast_fusion.1 = (f32[13,8,256]{1,2,0:T(8,128)}, f32[13,8,256]{1,2,0:T(8,128)S(1)}) fusion(f32[256,13,256]{2,0,1:T(8,128)S(1)} %constant_dynamic-update-slice_fusion), kind=kLoop, calls=%fused_computation.6 | loop fusion | bytes 425984 | tf_op jit(solution)/shard_map/transpose | solution.py:103
  7.0 2.6 %copy.23 = f32[13,8,256]{2,1,0:T(8,128)} copy(f32[13,8,256]{1,2,0:T(8,128)} %get-tuple-element.22) | data formatting | bytes 212992 | tf_op jit(solution)/shard_map/transpose | solution.py:103
  9.7 1.8 %collective-permute-start = (f32[13,8,256]{2,1,0:T(8,128)}, f32[13,8,256]{2,1,0:T(8,128)}, u32[]{:S(2)}, u32[]{:S(2)}) collective-permute-start(f32[13,8,256]{2,1,0:T(8,128)} %copy.23), channel_id=1, source_target_pairs={{0,4},{4,8},{8,12},{12,16},{16,20},{20,24},{24,28},{28,0},{1,5},{5... | collective-permute-start | bytes 319496 | tf_op jit(solution)/shard_map/ppermute | solution.py:16
  11.5 1.1 %copy.24 = f32[13,8,256]{2,1,0:T(8,128)} copy(f32[13,8,256]{1,2,0:T(8,128)S(1)} %get-tuple-element.23) | data formatting | bytes 212992 | tf_op jit(solution)/shard_map/transpose | solution.py:103
  13.4 1.3 %collective-permute-start.5 = (f32[192,256]{1,0:T(8,128)}, f32[192,256]{1,0:T(8,128)}, u32[]{:S(2)}, u32[]{:S(2)}) collective-permute-start(f32[192,256]{1,0:T(8,128)} %get-tuple-element.24), channel_id=1, source_target_pairs={{0,1},{1,2},{2,3},{3,0},{4,5},{5,6},{6,7},{7,4},{8,9},{9,10},{10,1... | collective-permute-start | bytes 589832 | tf_op jit(solution)/shard_map/ppermute | solution.py:55
  14.7 1.0 %collective-permute-start.6 = (f32[192,256]{1,0:T(8,128)}, f32[192,256]{1,0:T(8,128)}, u32[]{:S(2)}, u32[]{:S(2)}) collective-permute-start(f32[192,256]{1,0:T(8,128)} %get-tuple-element.26), channel_id=1, source_target_pairs={{0,2},{1,3},{2,0},{3,1},{4,6},{5,7},{6,4},{7,5},{8,10},{9,11},{10,... | collective-permute-start | bytes 589832 | tf_op jit(solution)/shard_map/ppermute | solution.py:55
  15.7 1.1 %copy.30 = f32[3,256,256]{1,2,0:T(8,128)} copy(f32[3,256,256]{2,1,0:T(8,128)S(1)} %copy-done.4) | data formatting | bytes 1572864 | tf_op args[0]
  18.5 1.3 %collective-permute-start.2 = (f32[3,16,256]{2,1,0:T(8,128)}, f32[3,16,256]{2,1,0:T(8,128)}, u32[]{:S(2)}, u32[]{:S(2)}) collective-permute-start(f32[3,16,256]{2,1,0:T(8,128)} %pad_maximum_fusion.7), channel_id=1, source_target_pairs={{0,3},{1,0},{2,1},{3,2},{4,7},{5,4},{6,5},{7,6},{8,11},{9,8},{10,9... | collective-permute-start | bytes 147464 | tf_op jit(solution)/shard_map/ppermute | solution.py:72
  19.8 1.1 %collective-permute-start.3 = (f32[3,16,256]{2,1,0:T(8,128)}, f32[3,16,256]{2,1,0:T(8,128)}, u32[]{:S(2)}, u32[]{:S(2)}) collective-permute-start(f32[3,16,256]{2,1,0:T(8,128)} %pad_maximum_fusion.7), channel_id=1, source_target_pairs={{0,2},{1,3},{2,0},{3,1},{4,6},{5,7},{6,4},{7,5},{8,10},{9,11},{10,... | collective-permute-start | bytes 147464 | tf_op jit(solution)/shard_map/ppermute | solution.py:72
  21.0 2.2 %collective-permute-start.4 = (f32[3,16,256]{2,1,0:T(8,128)}, f32[3,16,256]{2,1,0:T(8,128)}, u32[]{:S(2)}, u32[]{:S(2)}) collective-permute-start(f32[3,16,256]{2,1,0:T(8,128)} %pad_maximum_fusion.7), channel_id=1, source_target_pairs={{0,1},{1,2},{2,3},{3,0},{4,5},{5,6},{6,7},{7,4},{8,9},{9,10},{10,1... | collective-permute-start | bytes 147464 | tf_op jit(solution)/shard_map/ppermute | solution.py:72
  23.2 0.9 %slice.373 = f32[256,10,8]{0,2,1:T(8,128)S(1)} slice(f32[256,13,8]{0,2,1:T(8,128)} %bitcast.2), slice={[0:256], [3:13], [0:8]} | slice | bytes 163840 | tf_op jit(solution)/shard_map/slice | solution.py:113
  24.4 0.9 %slice.375 = f32[256,10,8]{0,2,1:T(8,128)S(1)} slice(f32[256,13,8]{0,2,1:T(8,128)} %bitcast.129), slice={[0:256], [3:13], [0:8]} | slice | bytes 163840 | tf_op jit(solution)/shard_map/slice | solution.py:113
  25.3 1.5 %copy.26 = f32[256,10,8]{2,0,1:T(8,128)} copy(f32[256,10,8]{0,2,1:T(8,128)S(1)} %slice.375) | data formatting | bytes 163840 | tf_op jit(solution)/shard_map/slice | solution.py:113
  26.9 5.4 %pad_maximum_fusion = f32[256,10,272]{2,0,1:T(8,128)} fusion(f32[256,10,8]{2,0,1:T(8,128)} %copy.26, f32[256,1,256]{2,0,1:T(8,128)S(1)} %bitcast.128, f32[256,3,256]{2,0,1:T(8,128)} %param.12, f32[256,3,256]{2,0,1:T(8,128)} %param.11, f32[256,3,256]{2,0,1:T(8,128)S(1)} %copy-done.6, f32[256,10,8]{2,0,1:T(8,128)S(1)} %copy.25), kind=kLoop, calls=%fused_computation | loop fusion | flops 3481600 | bytes 5570560 | tf_op jit(solution)/shard_map/concatenate | solution.py:113
  33.0 0.9 %add_bitcast_fusion = f32[3,256,16]{1,2,0:T(8,128)S(1)} fusion(f32[3,16,256]{2,1,0:T(8,128)} %collective-permute-done.2, f32[3,16,256]{2,1,0:T(8,128)} %collective-permute-done.3, f32[3,16,256]{2,1,0:T(8,128)} %collective-permute-done.4, pred[]{:T(512)S(6)} %eq.66, pred[]{:T(512)S(6)} %eq.65, pred[]{:T(512)S(6)} %eq.64, pred[]{:T(512)S(6)} %eq.63, ...), kind=kLoop, calls=%fused_computation.114 | loop fusion | flops 196608 | bytes 245772 | tf_op jit(solution)/shard_map/transpose | solution.py:109
  33.9 4.9 %collective-permute-done.7 = f32[192,256]{1,0:T(8,128)S(1)} collective-permute-done((f32[192,256]{1,0:T(8,128)S(1)}, f32[192,256]{1,0:T(8,128)S(1)}, u32[]{:S(2)}, u32[]{:S(2)}) %collective-permute-start.7) | collective-permute-done | bytes 196640 | tf_op jit(solution)/shard_map/ppermute | solution.py:55
  38.9 1.1 %bitcast_dynamic-update-slice_fusion.3 = (f32[4,192,256]{2,1,0:T(8,128)S(1)}, f32[192,256]{1,0:T(8,128)S(1)}) fusion(f32[4,192,256]{2,1,0:T(8,128)S(1)} %broadcast_in_dim.30, s32[]{:T(128)S(6)} %select_n.167, f32[192,256]{1,0:T(8,128)S(1)} %collective-permute-done.7, f32[192,256]{1,0:T(8,128)} %collective-permute-done.6, ...), kind=kLoop, calls=%fused_computation.106 | loop fusion | flops 147456 | bytes 1179652 | tf_op jit(solution)/shard_map/jit(dynamic_update_index_in_dim)/dynamic_update_slice | solution.py:57
  40.4 2.4 %collective-permute-start.9 = (f32[192,256]{1,0:T(8,128)S(1)}, f32[192,256]{1,0:T(8,128)S(1)}, u32[]{:S(2)}, u32[]{:S(2)}) collective-permute-start(f32[192,256]{1,0:T(8,128)S(1)} %get-tuple-element.17), channel_id=1, source_target_pairs={{0,2},{1,3},{2,0},{3,1},{4,6},{5,7},{6,4},{7,5},{8,10},{9,11},{10,... | collective-permute-start | bytes 589832 | tf_op jit(solution)/shard_map/ppermute | solution.py:60
  43.5 1.5 %collective-permute-done.8 = f32[192,256]{1,0:T(8,128)S(1)} collective-permute-done((f32[192,256]{1,0:T(8,128)S(1)}, f32[192,256]{1,0:T(8,128)S(1)}, u32[]{:S(2)}, u32[]{:S(2)}) %collective-permute-start.8) | collective-permute-done | bytes 196640 | tf_op jit(solution)/shard_map/ppermute | solution.py:60
  45.0 11.0 %collective-permute-done.9 = f32[192,256]{1,0:T(8,128)S(1)} collective-permute-done((f32[192,256]{1,0:T(8,128)S(1)}, f32[192,256]{1,0:T(8,128)S(1)}, u32[]{:S(2)}, u32[]{:S(2)}) %collective-permute-start.9) | collective-permute-done | bytes 196640 | tf_op jit(solution)/shard_map/ppermute | solution.py:60
  56.0 4.4 %collective-permute-done.10 = f32[192,256]{1,0:T(8,128)S(1)} collective-permute-done((f32[192,256]{1,0:T(8,128)S(1)}, f32[192,256]{1,0:T(8,128)S(1)}, u32[]{:S(2)}, u32[]{:S(2)}) %collective-permute-start.10) | collective-permute-done | bytes 196640 | tf_op jit(solution)/shard_map/ppermute | solution.py:60
  67.5 1.4 %fusion.38 = f32[3,256,256]{1,2,0:T(8,128)S(1)} fusion(f32[3,256,256]{2,1,0:T(8,128)S(1)} %fusion.1, f32[256,256]{1,0:T(8,128)S(1)} %copy-done), kind=kOutput, calls=%fused_computation.76 | convolution fusion | flops 603979776 | bytes 1835008 | tf_op jit(solution)/shard_map/dot_general | solution.py:126
  69.8 1.1 %copy.31 = f32[3,256,256]{2,1,0:T(8,128)} copy(f32[3,256,256]{1,2,0:T(8,128)S(1)} %fusion.2) | data formatting | bytes 1572864
  (112 shorter events, 15.2 us)
Async XLA Ops:
  0.6 2.2 %copy-start = (f32[256,256]{1,0:T(8,128)S(1)}, f32[256,256]{1,0:T(8,128)}, u32[]{:S(2)}) copy-start(f32[256,256]{1,0:T(8,128)} %param.15) | copy-start | bytes 786436
  0.6 3.0 %copy-start.2 = (bf16[3,256,3,256]{3,1,2,0:T(8,128)(2,1)S(1)}, bf16[3,256,3,256]{3,1,2,0:T(8,128)(2,1)}, u32[]{:S(2)}) copy-start(bf16[3,256,3,256]{3,1,2,0:T(8,128)(2,1)} %param.9) | copy-start | bytes 3538948
  2.8 1.2 %copy-start.5 = (f32[256,3,256]{2,0,1:T(8,128)S(1)}, f32[256,3,256]{2,0,1:T(8,128)}, u32[]{:S(2)}) copy-start(f32[256,3,256]{2,0,1:T(8,128)} %param.10) | copy-start | bytes 2359300
  3.7 1.4 %copy-start.8 = (f32[256,3,256]{2,0,1:T(8,128)S(1)}, f32[256,3,256]{2,0,1:T(8,128)}, u32[]{:S(2)}) copy-start(f32[256,3,256]{2,0,1:T(8,128)} %param.12) | copy-start | bytes 2359300
  7.0 8.7 %copy-start.4 = (f32[3,256,256]{2,1,0:T(8,128)S(1)}, f32[3,256,256]{2,1,0:T(8,128)}, u32[]{:S(2)}) copy-start(f32[3,256,256]{2,1,0:T(8,128)} %param.8) | copy-start | bytes 2359300
  9.7 7.2 %collective-permute-start = (f32[13,8,256]{2,1,0:T(8,128)}, f32[13,8,256]{2,1,0:T(8,128)}, u32[]{:S(2)}, u32[]{:S(2)}) collective-permute-start(f32[13,8,256]{2,1,0:T(8,128)} %copy.23), channel_id=1, source_target_pairs={{0,4},{4,8},{8,12},{12,16},{16,20},{20,24},{24,28},{28,0},{1,5},{5... | collective-permute-start | bytes 319496 | tf_op jit(solution)/shard_map/ppermute | solution.py:16
  12.6 14.3 %copy-start.12 = (f32[256,256]{1,0:T(8,128)S(1)}, f32[256,256]{1,0:T(8,128)}, u32[]{:S(2)}) copy-start(f32[256,256]{1,0:T(8,128)} %param.13) | copy-start | bytes 786436
  12.6 5.2 %collective-permute-start.1 = (f32[13,8,256]{2,1,0:T(8,128)}, f32[13,8,256]{2,1,0:T(8,128)S(1)}, u32[]{:S(2)}, u32[]{:S(2)}) collective-permute-start(f32[13,8,256]{2,1,0:T(8,128)} %copy.24), channel_id=1, source_target_pairs={{4,0},{8,4},{12,8},{16,12},{20,16},{24,20},{28,24},{0,28},{5,1},{9... | collective-permute-start | bytes 319496 | tf_op jit(solution)/shard_map/ppermute | solution.py:17
  13.4 20.5 %collective-permute-start.5 = (f32[192,256]{1,0:T(8,128)}, f32[192,256]{1,0:T(8,128)}, u32[]{:S(2)}, u32[]{:S(2)}) collective-permute-start(f32[192,256]{1,0:T(8,128)} %get-tuple-element.24), channel_id=1, source_target_pairs={{0,1},{1,2},{2,3},{3,0},{4,5},{5,6},{6,7},{7,4},{8,9},{9,10},{10,1... | collective-permute-start | bytes 589832 | tf_op jit(solution)/shard_map/ppermute | solution.py:55
  14.7 19.2 %collective-permute-start.6 = (f32[192,256]{1,0:T(8,128)}, f32[192,256]{1,0:T(8,128)}, u32[]{:S(2)}, u32[]{:S(2)}) collective-permute-start(f32[192,256]{1,0:T(8,128)} %get-tuple-element.26), channel_id=1, source_target_pairs={{0,2},{1,3},{2,0},{3,1},{4,6},{5,7},{6,4},{7,5},{8,10},{9,11},{10,... | collective-permute-start | bytes 589832 | tf_op jit(solution)/shard_map/ppermute | solution.py:55
  16.9 10.0 %copy-start.6 = (f32[256,3,256]{2,0,1:T(8,128)S(1)}, f32[256,3,256]{2,0,1:T(8,128)}, u32[]{:S(2)}) copy-start(f32[256,3,256]{2,0,1:T(8,128)} %param.10) | copy-start | bytes 2359300
  17.8 5.3 %copy-start.14 = (f32[13,8,256]{2,1,0:T(8,128)}, f32[13,8,256]{2,1,0:T(8,128)S(1)}, u32[]{:S(2)}) copy-start(f32[13,8,256]{2,1,0:T(8,128)S(1)} %collective-permute-done.1) | copy-start | bytes 319492
  18.5 14.5 %collective-permute-start.2 = (f32[3,16,256]{2,1,0:T(8,128)}, f32[3,16,256]{2,1,0:T(8,128)}, u32[]{:S(2)}, u32[]{:S(2)}) collective-permute-start(f32[3,16,256]{2,1,0:T(8,128)} %pad_maximum_fusion.7), channel_id=1, source_target_pairs={{0,3},{1,0},{2,1},{3,2},{4,7},{5,4},{6,5},{7,6},{8,11},{9,8},{10,9... | collective-permute-start | bytes 147464 | tf_op jit(solution)/shard_map/ppermute | solution.py:72
  19.8 13.2 %collective-permute-start.3 = (f32[3,16,256]{2,1,0:T(8,128)}, f32[3,16,256]{2,1,0:T(8,128)}, u32[]{:S(2)}, u32[]{:S(2)}) collective-permute-start(f32[3,16,256]{2,1,0:T(8,128)} %pad_maximum_fusion.7), channel_id=1, source_target_pairs={{0,2},{1,3},{2,0},{3,1},{4,6},{5,7},{6,4},{7,5},{8,10},{9,11},{10,... | collective-permute-start | bytes 147464 | tf_op jit(solution)/shard_map/ppermute | solution.py:72
  21.0 12.0 %collective-permute-start.4 = (f32[3,16,256]{2,1,0:T(8,128)}, f32[3,16,256]{2,1,0:T(8,128)}, u32[]{:S(2)}, u32[]{:S(2)}) collective-permute-start(f32[3,16,256]{2,1,0:T(8,128)} %pad_maximum_fusion.7), channel_id=1, source_target_pairs={{0,1},{1,2},{2,3},{3,0},{4,5},{5,6},{6,7},{7,4},{8,9},{9,10},{10,1... | collective-permute-start | bytes 147464 | tf_op jit(solution)/shard_map/ppermute | solution.py:72
  26.8 6.1 %copy-start.13 = (f32[192,256]{1,0:T(8,128)S(1)}, f32[192,256]{1,0:T(8,128)}, u32[]{:S(2)}) copy-start(f32[192,256]{1,0:T(8,128)} %get-tuple-element.25) | copy-start | bytes 589828
  33.0 5.9 %collective-permute-start.7 = (f32[192,256]{1,0:T(8,128)S(1)}, f32[192,256]{1,0:T(8,128)S(1)}, u32[]{:S(2)}, u32[]{:S(2)}) collective-permute-start(f32[192,256]{1,0:T(8,128)S(1)} %copy-done.13), channel_id=1, source_target_pairs={{0,3},{1,0},{2,1},{3,2},{4,7},{5,4},{6,5},{7,6},{8,11},{9,8},{10,9... | collective-permute-start | bytes 589832 | tf_op jit(solution)/shard_map/ppermute | solution.py:55
  40.0 5.0 %collective-permute-start.8 = (f32[192,256]{1,0:T(8,128)S(1)}, f32[192,256]{1,0:T(8,128)S(1)}, u32[]{:S(2)}, u32[]{:S(2)}) collective-permute-start(f32[192,256]{1,0:T(8,128)S(1)} %get-tuple-element.17), channel_id=1, source_target_pairs={{0,1},{1,2},{2,3},{3,0},{4,5},{5,6},{6,7},{7,4},{8,9},{9,10},{10,1... | collective-permute-start | bytes 589832 | tf_op jit(solution)/shard_map/ppermute | solution.py:60
  40.4 20.5 %copy-start.1 = (f32[256,10,272]{2,0,1:T(8,128)S(1)}, f32[256,10,272]{2,0,1:T(8,128)}, u32[]{:S(2)}) copy-start(f32[256,10,272]{2,0,1:T(8,128)} %pad_maximum_fusion) | copy-start | bytes 8355844
  40.4 15.6 %collective-permute-start.9 = (f32[192,256]{1,0:T(8,128)S(1)}, f32[192,256]{1,0:T(8,128)S(1)}, u32[]{:S(2)}, u32[]{:S(2)}) collective-permute-start(f32[192,256]{1,0:T(8,128)S(1)} %get-tuple-element.17), channel_id=1, source_target_pairs={{0,2},{1,3},{2,0},{3,1},{4,6},{5,7},{6,4},{7,5},{8,10},{9,11},{10,... | collective-permute-start | bytes 589832 | tf_op jit(solution)/shard_map/ppermute | solution.py:60
  42.9 17.6 %collective-permute-start.10 = (f32[192,256]{1,0:T(8,128)S(1)}, f32[192,256]{1,0:T(8,128)S(1)}, u32[]{:S(2)}, u32[]{:S(2)}) collective-permute-start(f32[192,256]{1,0:T(8,128)S(1)} %get-tuple-element.17), channel_id=1, source_target_pairs={{0,3},{1,0},{2,1},{3,2},{4,7},{5,4},{6,5},{7,6},{8,11},{9,8},{10,9... | collective-permute-start | bytes 589832 | tf_op jit(solution)/shard_map/ppermute | solution.py:60
  65.9 1.3 %copy-start.3 = (bf16[3,256,3,256]{3,1,2,0:T(8,128)(2,1)S(1)}, bf16[3,256,3,256]{3,1,2,0:T(8,128)(2,1)}, u32[]{:S(2)}) copy-start(bf16[3,256,3,256]{3,1,2,0:T(8,128)(2,1)} %param.9) | copy-start | bytes 3538948
  67.1 1.8 %copy-start.9 = (f32[3,256,256]{1,2,0:T(8,128)S(1)}, f32[3,256,256]{1,2,0:T(8,128)}, u32[]{:S(2)}) copy-start(f32[3,256,256]{1,2,0:T(8,128)} %copy.30) | copy-start | bytes 2359300
  67.1 1.8 %copy-start.10 = (f32[256,256]{1,0:T(8,128)S(1)}, f32[256,256]{1,0:T(8,128)}, u32[]{:S(2)}) copy-start(f32[256,256]{1,0:T(8,128)} %param.14) | copy-start | bytes 786436
  (2 other events, 2.4 us)

commit v5 on v4

--- a/solution.py
+++ b/solution.py
@@ -42,7 +42,7 @@
     return pred, (a, p, q)
 
 
-def member_sum(x):
+def member_scatter(x):
     count = lax.axis_size("member")
     me = lax.axis_index("member")
     rows, lanes = x.shape
@@ -53,13 +53,19 @@
         shift = [(i, (i + s) % count) for i in range(count)]
         sent = lax.dynamic_index_in_dim(x, (me + s) % count, 0, keepdims=False)
         acc = acc + lax.ppermute(sent, "member", shift)
-    out = jnp.zeros_like(x)
+    return acc, jnp.zeros((rows,), x.dtype)
+
+
+def member_gather(acc, like):
+    count = lax.axis_size("member")
+    me = lax.axis_index("member")
+    out = jnp.zeros((count,) + acc.shape, acc.dtype)
     out = lax.dynamic_update_index_in_dim(out, acc, me, 0)
     for s in range(1, count):
         shift = [(i, (i + s) % count) for i in range(count)]
         got = lax.ppermute(acc, "member", shift)
         out = lax.dynamic_update_index_in_dim(out, got, (me + count - s) % count, 0)
-    return out.reshape(piece * count, lanes)[:rows]
+    return out.reshape(count * acc.shape[0], acc.shape[1])[: like.shape[0]]
 
 
 def member_gather_sum(x):
@@ -99,12 +105,14 @@
     ens = ensemble.astype(jnp.float32)
     partial = jnp.sum(ens * localized[:, :, None, :], axis=0)
     both = jnp.concatenate([partial, inputs], axis=1)
+    scattered = member_scatter(partial.transpose(1, 0, 2).reshape(nfield * ncol, nrow))
+    scattered, both = lax.optimization_barrier((scattered, both))
     before, after = shift_rows(
         None, (both[:, :, :HALO].transpose(1, 2, 0), both[:, :, -HALO:].transpose(1, 2, 0)))
     halo = jnp.concatenate([before[:nfield], after[:nfield]], axis=1)
     before = before.transpose(2, 0, 1)
     after = after.transpose(2, 0, 1)
-    summed = member_sum(partial.transpose(1, 0, 2).reshape(nfield * ncol, nrow))
+    summed = member_gather(*scattered)
     incr_main = summed.reshape(nfield, ncol, nrow)
     incr_halo = member_gather_sum(halo).transpose(0, 2, 1)
     incr = jnp.concatenate(

time: 72 us -> 72.5 us (level)
  the two profiles are of different devices: /device:TPU:11 before, /device:TPU:0 now
where the time goes in v5:
time: 72.5 us; the launch traced here: 72.1 us
  local copies, waits for them, and re-layouts  25.3 us (35%)
  starting transfers between devices  21.3 us (29%)
  other arithmetic  12.9 us (18%)
  waiting for transfers between devices  6.07 us (8%)
  matrix products  5.25 us (7%)
  between operations  1.23 us (2%)
    unnamed x28, local copies, waits for them, and re-layouts  9.11 us
    ppermute x3, starting transfers between devices, member_gather(): got = lax.ppermute(acc, 'member', shift)  8.91 us
    ppermute x3, starting transfers between devices, member_scatter(): acc = acc + lax.ppermute(sent, 'member', shift)  6.96 us
    transpose x2, local copies, waits for them, and re-layouts, body(): both[:, :, -HALO:].transpose(1, 2, 0)  5.7 us
    concatenate x1, other arithmetic, body(): jnp.concatenate([before[:, nfield:], inputs, after[:, nfield:]], axis=2)  5.32 us
    dynamic_update_slice x3, local copies, waits for them, and re-layouts, member_gather(): out = lax.dynamic_update_index_in_dim(out, got, (me + count - s) % count, 0)  4.11 us
    ppermute x3, waiting for transfers between devices, member_scatter(): acc = acc + lax.ppermute(sent, 'member', shift)  3.86 us
    ppermute x3, starting transfers between devices, member_gather_sum(): pieces[s] = lax.ppermute(x, 'member', shift)  2.79 us
  transfers between devices with their start and end apart: 11, of which 3 were waited for; matrix products, arithmetic and copies ran while one was open for 34% of the time, Pallas kernels for 0%

profile of v5, /device:TPU:0, one launch (start us, length us, event | category | flops | bytes accessed | tf_op | source)
XLA Modules:
  0.0 72.1 jit_solution(9584899364067687245)
XLA Ops:
  0.7 2.1 %fusion.43 = f32[3,256,256]{2,1,0:T(8,128)S(1)} fusion(f32[3,256,256]{2,1,0:T(8,128)} %param.8, f32[256,256]{1,0:T(8,128)} %param.14), kind=kOutput, calls=%fused_computation.81 | convolution fusion | flops 603979776 | bytes 1835008 | tf_op jit(solution)/shard_map/dot_general | solution.py:103
  4.8 3.0 %collective-permute-start = (f32[192,256]{1,0:T(8,128)}, f32[192,256]{1,0:T(8,128)S(1)}, u32[]{:S(2)}, u32[]{:S(2)}) collective-permute-start(f32[192,256]{1,0:T(8,128)} %get-tuple-element.26), channel_id=1, source_target_pairs={{0,1},{1,2},{2,3},{3,0},{4,5},{5,6},{6,7},{7,4},{8,9},{9,10},{10,1... | collective-permute-start | bytes 589832 | tf_op jit(solution)/shard_map/ppermute | solution.py:55
  7.8 2.6 %collective-permute-start.1 = (f32[192,256]{1,0:T(8,128)}, f32[192,256]{1,0:T(8,128)S(1)}, u32[]{:S(2)}, u32[]{:S(2)}) collective-permute-start(f32[192,256]{1,0:T(8,128)} %get-tuple-element.28), channel_id=1, source_target_pairs={{0,2},{1,3},{2,0},{3,1},{4,6},{5,7},{6,4},{7,5},{8,10},{9,11},{10,... | collective-permute-start | bytes 589832 | tf_op jit(solution)/shard_map/ppermute | solution.py:55
  10.4 1.4 %collective-permute-start.2 = (f32[192,256]{1,0:T(8,128)S(1)}, f32[192,256]{1,0:T(8,128)}, u32[]{:S(2)}, u32[]{:S(2)}) collective-permute-start(f32[192,256]{1,0:T(8,128)S(1)} %get-tuple-element.27), channel_id=1, source_target_pairs={{0,3},{1,0},{2,1},{3,2},{4,7},{5,4},{6,5},{7,6},{8,11},{9,8},{10,9... | collective-permute-start | bytes 589832 | tf_op jit(solution)/shard_map/ppermute | solution.py:55
  12.7 1.1 %copy.30 = f32[3,256,256]{1,2,0:T(8,128)} copy(f32[3,256,256]{2,1,0:T(8,128)S(1)} %copy-done.4) | data formatting | bytes 1572864 | tf_op args[0]
  14.8 2.1 %constant_dynamic-update-slice_fusion.2 = f32[256,13,256]{2,0,1:T(8,128)} fusion(f32[256,13,256]{2,0,1:T(8,128)} %constant_dynamic-update-slice_fusion.3, f32[256,3,256]{2,0,1:T(8,128)} %param.11), kind=kLoop, calls=%fused_computation.117 | loop fusion | bytes 1572864
  16.9 2.1 %constant_dynamic-update-slice_fusion.1 = f32[256,13,256]{2,0,1:T(8,128)} fusion(f32[256,13,256]{2,0,1:T(8,128)} %constant_dynamic-update-slice_fusion.2, f32[256,3,256]{2,0,1:T(8,128)} %param.12), kind=kLoop, calls=%fused_computation.116 | loop fusion | bytes 1572864
  19.7 3.9 %collective-permute-done.1 = f32[192,256]{1,0:T(8,128)S(1)} collective-permute-done((f32[192,256]{1,0:T(8,128)}, f32[192,256]{1,0:T(8,128)S(1)}, u32[]{:S(2)}, u32[]{:S(2)}) %collective-permute-start.1) | collective-permute-done | bytes 196640 | tf_op jit(solution)/shard_map/ppermute | solution.py:55
  24.2 1.1 %fusion.56 = f32[192,256]{1,0:T(8,128)S(1)} fusion(f32[192,256]{1,0:T(8,128)} %collective-permute-done.2, f32[192,256]{1,0:T(8,128)} %copy-done.10, f32[192,256]{1,0:T(8,128)S(1)} %collective-permute-done, f32[4,192,256]{2,1,0:T(8,128)S(1)} %bitcast.125, s32[]{:T(128)S(6)} %select_n.140), kind=kLoop, calls=%fused_computation.109 | loop fusion | flops 147456 | bytes 983044 | tf_op jit(solution)/shard_map/add | solution.py:55
  25.3 4.2 %collective-permute-start.8 = (f32[192,256]{1,0:T(8,128)S(1)}, f32[192,256]{1,0:T(8,128)}, u32[]{:S(2)}, u32[]{:S(2)}) collective-permute-start(f32[192,256]{1,0:T(8,128)S(1)} %fusion.56), channel_id=1, source_target_pairs={{0,1},{1,2},{2,3},{3,0},{4,5},{5,6},{6,7},{7,4},{8,9},{9,10},{10,1... | collective-permute-start | bytes 589832 | tf_op jit(solution)/shard_map/ppermute | solution.py:66
  29.5 2.2 %collective-permute-start.9 = (f32[192,256]{1,0:T(8,128)S(1)}, f32[192,256]{1,0:T(8,128)}, u32[]{:S(2)}, u32[]{:S(2)}) collective-permute-start(f32[192,256]{1,0:T(8,128)S(1)} %fusion.56), channel_id=1, source_target_pairs={{0,2},{1,3},{2,0},{3,1},{4,6},{5,7},{6,4},{7,5},{8,10},{9,11},{10,... | collective-permute-start | bytes 589832 | tf_op jit(solution)/shard_map/ppermute | solution.py:66
  31.6 3.8 %slice_bitcast_fusion.1 = (f32[13,8,256]{1,2,0:T(8,128)}, f32[13,8,256]{1,2,0:T(8,128)S(1)}) fusion(f32[256,13,256]{2,0,1:T(8,128)} %constant_dynamic-update-slice_fusion), kind=kLoop, calls=%fused_computation.6 | loop fusion | bytes 425984 | tf_op jit(solution)/shard_map/transpose | solution.py:111
  35.4 1.9 %copy.23 = f32[13,8,256]{2,1,0:T(8,128)S(1)} copy(f32[13,8,256]{1,2,0:T(8,128)} %get-tuple-element.24) | data formatting | bytes 212992 | tf_op jit(solution)/shard_map/transpose | solution.py:111
  37.8 2.7 %collective-permute-start.4 = (f32[13,8,256]{2,1,0:T(8,128)S(1)}, f32[13,8,256]{2,1,0:T(8,128)S(1)}, u32[]{:S(2)}, u32[]{:S(2)}) collective-permute-start(f32[13,8,256]{2,1,0:T(8,128)S(1)} %copy.24), channel_id=1, source_target_pairs={{4,0},{8,4},{12,8},{16,12},{20,16},{24,20},{28,24},{0,28},{5,1},{9... | collective-permute-start | bytes 319496 | tf_op jit(solution)/shard_map/ppermute | solution.py:17
  40.6 1.8 %collective-permute-done.3 = f32[13,8,256]{2,1,0:T(8,128)S(1)} collective-permute-done((f32[13,8,256]{2,1,0:T(8,128)S(1)}, f32[13,8,256]{2,1,0:T(8,128)S(1)}, u32[]{:S(2)}, u32[]{:S(2)}) %collective-permute-start.3) | collective-permute-done | bytes 106528 | tf_op jit(solution)/shard_map/ppermute | solution.py:16
  43.1 1.3 %collective-permute-start.6 = (f32[3,16,256]{2,1,0:T(8,128)S(1)}, f32[3,16,256]{2,1,0:T(8,128)}, u32[]{:S(2)}, u32[]{:S(2)}) collective-permute-start(f32[3,16,256]{2,1,0:T(8,128)S(1)} %pad_maximum_fusion.7), channel_id=1, source_target_pairs={{0,2},{1,3},{2,0},{3,1},{4,6},{5,7},{6,4},{7,5},{8,10},{9,11},{10,... | collective-permute-start | bytes 147464 | tf_op jit(solution)/shard_map/ppermute | solution.py:78
  44.3 1.2 %collective-permute-start.7 = (f32[3,16,256]{2,1,0:T(8,128)S(1)}, f32[3,16,256]{2,1,0:T(8,128)}, u32[]{:S(2)}, u32[]{:S(2)}) collective-permute-start(f32[3,16,256]{2,1,0:T(8,128)S(1)} %pad_maximum_fusion.7), channel_id=1, source_target_pairs={{0,1},{1,2},{2,3},{3,0},{4,5},{5,6},{6,7},{7,4},{8,9},{9,10},{10,1... | collective-permute-start | bytes 147464 | tf_op jit(solution)/shard_map/ppermute | solution.py:78
  46.4 5.3 %pad_maximum_fusion = f32[256,10,272]{2,0,1:T(8,128)} fusion(f32[256,10,8]{2,0,1:T(8,128)S(1)} %copy.26, f32[256,1,256]{2,0,1:T(8,128)S(1)} %bitcast.127, f32[256,3,256]{2,0,1:T(8,128)} %param.12, f32[256,3,256]{2,0,1:T(8,128)} %param.11, f32[256,3,256]{2,0,1:T(8,128)} %param.10, f32[256,10,8]{2,0,1:T(8,128)S(1)} %copy.25), kind=kLoop, calls=%fused_computation | loop fusion | flops 3481600 | bytes 5570560 | tf_op jit(solution)/shard_map/concatenate | solution.py:121
  51.7 2.6 %collective-permute-start.10 = (f32[192,256]{1,0:T(8,128)S(1)}, f32[192,256]{1,0:T(8,128)S(1)}, u32[]{:S(2)}, u32[]{:S(2)}) collective-permute-start(f32[192,256]{1,0:T(8,128)S(1)} %fusion.56), channel_id=1, source_target_pairs={{0,3},{1,0},{2,1},{3,2},{4,7},{5,4},{6,5},{7,6},{8,11},{9,8},{10,9... | collective-permute-start | bytes 589832 | tf_op jit(solution)/shard_map/ppermute | solution.py:66
  55.6 1.8 %bitcast_dynamic-update-slice_fusion.2 = f32[4,192,256]{2,1,0:T(8,128)} fusion(f32[4,192,256]{2,1,0:T(8,128)} %copy-done.7, s32[]{:T(128)S(6)} %select_n.146, f32[192,256]{1,0:T(8,128)} %collective-permute-done.8), kind=kLoop, calls=%fused_computation.105 | loop fusion | bytes 393220 | tf_op jit(solution)/shard_map/jit(dynamic_update_index_in_dim)/dynamic_update_slice | solution.py:67
  57.4 1.6 %bitcast_dynamic-update-slice_fusion.1 = f32[4,192,256]{2,1,0:T(8,128)} fusion(f32[4,192,256]{2,1,0:T(8,128)} %bitcast_dynamic-update-slice_fusion.2, s32[]{:T(128)S(6)} %select_n.144, f32[192,256]{1,0:T(8,128)} %collective-permute-done.9), kind=kLoop, calls=%fused_computation.104 | loop fusion | bytes 393220 | tf_op jit(solution)/shard_map/jit(dynamic_update_index_in_dim)/dynamic_update_slice | solution.py:67
  59.7 1.6 %pad_maximum_fusion.1 = f32[3,256,272]{2,1,0:T(8,128)S(1)} fusion(f32[3,256,8]{2,1,0:T(8,128)S(1)} %copy.28, f32[3,256,256]{2,1,0:T(8,128)} %bitcast.126, f32[3,256,8]{2,1,0:T(8,128)S(1)} %copy.27), kind=kLoop, calls=%fused_computation.9 | loop fusion | flops 417792 | bytes 1671168 | tf_op jit(solution)/shard_map/concatenate | solution.py:118
  67.9 1.4 %fusion.38 = f32[3,256,256]{1,2,0:T(8,128)S(1)} fusion(f32[3,256,256]{2,1,0:T(8,128)S(1)} %fusion.1, f32[256,256]{1,0:T(8,128)S(1)} %copy-done), kind=kOutput, calls=%fused_computation.76 | convolution fusion | flops 603979776 | bytes 1835008 | tf_op jit(solution)/shard_map/dot_general | solution.py:134
  70.2 1.1 %copy.31 = f32[3,256,256]{2,1,0:T(8,128)} copy(f32[3,256,256]{1,2,0:T(8,128)S(1)} %fusion.2) | data formatting | bytes 1572864
  (105 shorter events, 17.1 us)
Async XLA Ops:
  0.6 2.2 %copy-start = (f32[256,256]{1,0:T(8,128)S(1)}, f32[256,256]{1,0:T(8,128)}, u32[]{:S(2)}) copy-start(f32[256,256]{1,0:T(8,128)} %param.15) | copy-start | bytes 786436
  0.6 3.1 %copy-start.2 = (bf16[3,256,3,256]{3,1,2,0:T(8,128)(2,1)S(1)}, bf16[3,256,3,256]{3,1,2,0:T(8,128)(2,1)}, u32[]{:S(2)}) copy-start(bf16[3,256,3,256]{3,1,2,0:T(8,128)(2,1)} %param.9) | copy-start | bytes 3538948
  2.8 9.9 %copy-start.4 = (f32[3,256,256]{2,1,0:T(8,128)S(1)}, f32[3,256,256]{2,1,0:T(8,128)}, u32[]{:S(2)}) copy-start(f32[3,256,256]{2,1,0:T(8,128)} %param.8) | copy-start | bytes 2359300
  4.0 9.9 %copy-start.5 = (f32[256,3,256]{2,0,1:T(8,128)S(1)}, f32[256,3,256]{2,0,1:T(8,128)}, u32[]{:S(2)}) copy-start(f32[256,3,256]{2,0,1:T(8,128)} %param.10) | copy-start | bytes 2359300
  4.8 14.9 %collective-permute-start = (f32[192,256]{1,0:T(8,128)}, f32[192,256]{1,0:T(8,128)S(1)}, u32[]{:S(2)}, u32[]{:S(2)}) collective-permute-start(f32[192,256]{1,0:T(8,128)} %get-tuple-element.26), channel_id=1, source_target_pairs={{0,1},{1,2},{2,3},{3,0},{4,5},{5,6},{6,7},{7,4},{8,9},{9,10},{10,1... | collective-permute-start | bytes 589832 | tf_op jit(solution)/shard_map/ppermute | solution.py:55
  7.8 15.7 %collective-permute-start.1 = (f32[192,256]{1,0:T(8,128)}, f32[192,256]{1,0:T(8,128)S(1)}, u32[]{:S(2)}, u32[]{:S(2)}) collective-permute-start(f32[192,256]{1,0:T(8,128)} %get-tuple-element.28), channel_id=1, source_target_pairs={{0,2},{1,3},{2,0},{3,1},{4,6},{5,7},{6,4},{7,5},{8,10},{9,11},{10,... | collective-permute-start | bytes 589832 | tf_op jit(solution)/shard_map/ppermute | solution.py:55
  10.4 13.8 %collective-permute-start.2 = (f32[192,256]{1,0:T(8,128)S(1)}, f32[192,256]{1,0:T(8,128)}, u32[]{:S(2)}, u32[]{:S(2)}) collective-permute-start(f32[192,256]{1,0:T(8,128)S(1)} %get-tuple-element.27), channel_id=1, source_target_pairs={{0,3},{1,0},{2,1},{3,2},{4,7},{5,4},{6,5},{7,6},{8,11},{9,8},{10,9... | collective-permute-start | bytes 589832 | tf_op jit(solution)/shard_map/ppermute | solution.py:55
  12.7 6.2 %copy-start.9 = (f32[256,256]{1,0:T(8,128)S(1)}, f32[256,256]{1,0:T(8,128)}, u32[]{:S(2)}) copy-start(f32[256,256]{1,0:T(8,128)} %param.13) | copy-start | bytes 786436
  23.5 0.7 copy-start.10
  25.3 30.3 %collective-permute-start.8 = (f32[192,256]{1,0:T(8,128)S(1)}, f32[192,256]{1,0:T(8,128)}, u32[]{:S(2)}, u32[]{:S(2)}) collective-permute-start(f32[192,256]{1,0:T(8,128)S(1)} %fusion.56), channel_id=1, source_target_pairs={{0,1},{1,2},{2,3},{3,0},{4,5},{5,6},{6,7},{7,4},{8,9},{9,10},{10,1... | collective-permute-start | bytes 589832 | tf_op jit(solution)/shard_map/ppermute | solution.py:66
  29.5 27.9 %collective-permute-start.9 = (f32[192,256]{1,0:T(8,128)S(1)}, f32[192,256]{1,0:T(8,128)}, u32[]{:S(2)}, u32[]{:S(2)}) collective-permute-start(f32[192,256]{1,0:T(8,128)S(1)} %fusion.56), channel_id=1, source_target_pairs={{0,2},{1,3},{2,0},{3,1},{4,6},{5,7},{6,4},{7,5},{8,10},{9,11},{10,... | collective-permute-start | bytes 589832 | tf_op jit(solution)/shard_map/ppermute | solution.py:66
  37.3 5.1 %collective-permute-start.3 = (f32[13,8,256]{2,1,0:T(8,128)S(1)}, f32[13,8,256]{2,1,0:T(8,128)S(1)}, u32[]{:S(2)}, u32[]{:S(2)}) collective-permute-start(f32[13,8,256]{2,1,0:T(8,128)S(1)} %copy.23), channel_id=1, source_target_pairs={{0,4},{4,8},{8,12},{12,16},{16,20},{20,24},{24,28},{28,0},{1,5},{5... | collective-permute-start | bytes 319496 | tf_op jit(solution)/shard_map/ppermute | solution.py:16
  37.8 4.9 %collective-permute-start.4 = (f32[13,8,256]{2,1,0:T(8,128)S(1)}, f32[13,8,256]{2,1,0:T(8,128)S(1)}, u32[]{:S(2)}, u32[]{:S(2)}) collective-permute-start(f32[13,8,256]{2,1,0:T(8,128)S(1)} %copy.24), channel_id=1, source_target_pairs={{4,0},{8,4},{12,8},{16,12},{20,16},{24,20},{28,24},{0,28},{5,1},{9... | collective-permute-start | bytes 319496 | tf_op jit(solution)/shard_map/ppermute | solution.py:17
  40.6 5.0 %copy-start.7 = (f32[4,192,256]{2,1,0:T(8,128)}, f32[4,192,256]{2,1,0:T(8,128)S(1)}, u32[]{:S(2)}) copy-start(f32[4,192,256]{2,1,0:T(8,128)S(1)} %bitcast_dynamic-update-slice_fusion.3) | copy-start | bytes 2359300
  42.8 8.9 %collective-permute-start.5 = (f32[3,16,256]{2,1,0:T(8,128)S(1)}, f32[3,16,256]{2,1,0:T(8,128)}, u32[]{:S(2)}, u32[]{:S(2)}) collective-permute-start(f32[3,16,256]{2,1,0:T(8,128)S(1)} %pad_maximum_fusion.7), channel_id=1, source_target_pairs={{0,3},{1,0},{2,1},{3,2},{4,7},{5,4},{6,5},{7,6},{8,11},{9,8},{10,9... | collective-permute-start | bytes 147464 | tf_op jit(solution)/shard_map/ppermute | solution.py:78
  43.1 11.3 %collective-permute-start.6 = (f32[3,16,256]{2,1,0:T(8,128)S(1)}, f32[3,16,256]{2,1,0:T(8,128)}, u32[]{:S(2)}, u32[]{:S(2)}) collective-permute-start(f32[3,16,256]{2,1,0:T(8,128)S(1)} %pad_maximum_fusion.7), channel_id=1, source_target_pairs={{0,2},{1,3},{2,0},{3,1},{4,6},{5,7},{6,4},{7,5},{8,10},{9,11},{10,... | collective-permute-start | bytes 147464 | tf_op jit(solution)/shard_map/ppermute | solution.py:78
  44.3 10.0 %collective-permute-start.7 = (f32[3,16,256]{2,1,0:T(8,128)S(1)}, f32[3,16,256]{2,1,0:T(8,128)}, u32[]{:S(2)}, u32[]{:S(2)}) collective-permute-start(f32[3,16,256]{2,1,0:T(8,128)S(1)} %pad_maximum_fusion.7), channel_id=1, source_target_pairs={{0,1},{1,2},{2,3},{3,0},{4,5},{5,6},{6,7},{7,4},{8,9},{9,10},{10,1... | collective-permute-start | bytes 147464 | tf_op jit(solution)/shard_map/ppermute | solution.py:78
  51.7 7.3 %collective-permute-start.10 = (f32[192,256]{1,0:T(8,128)S(1)}, f32[192,256]{1,0:T(8,128)S(1)}, u32[]{:S(2)}, u32[]{:S(2)}) collective-permute-start(f32[192,256]{1,0:T(8,128)S(1)} %fusion.56), channel_id=1, source_target_pairs={{0,3},{1,0},{2,1},{3,2},{4,7},{5,4},{6,5},{7,6},{8,11},{9,8},{10,9... | collective-permute-start | bytes 589832 | tf_op jit(solution)/shard_map/ppermute | solution.py:66
  55.6 5.7 %copy-start.1 = (f32[256,10,272]{2,0,1:T(8,128)S(1)}, f32[256,10,272]{2,0,1:T(8,128)}, u32[]{:S(2)}) copy-start(f32[256,10,272]{2,0,1:T(8,128)} %pad_maximum_fusion) | copy-start | bytes 8355844
  66.4 1.3 %copy-start.3 = (bf16[3,256,3,256]{3,1,2,0:T(8,128)(2,1)S(1)}, bf16[3,256,3,256]{3,1,2,0:T(8,128)(2,1)}, u32[]{:S(2)}) copy-start(bf16[3,256,3,256]{3,1,2,0:T(8,128)(2,1)} %param.9) | copy-start | bytes 3538948
  67.5 1.8 %copy-start.6 = (f32[3,256,256]{1,2,0:T(8,128)S(1)}, f32[3,256,256]{1,2,0:T(8,128)}, u32[]{:S(2)}) copy-start(f32[3,256,256]{1,2,0:T(8,128)} %copy.30) | copy-start | bytes 2359300
  67.5 1.8 %copy-start.8 = (f32[256,256]{1,0:T(8,128)S(1)}, f32[256,256]{1,0:T(8,128)}, u32[]{:S(2)}) copy-start(f32[256,256]{1,0:T(8,128)} %param.14) | copy-start | bytes 786436

commit v6 on v5

--- a/solution.py
+++ b/solution.py
@@ -102,23 +102,23 @@
 
     localized = lax.dot_general(cols_b, alpha, batched(2, 1), precision=highest)
     localized = lax.dot_general(localized, rows_b, batched(2, 2), precision=highest)
+    in_before, in_after = shift_rows(
+        None, (inputs[:, :, :HALO].transpose(1, 2, 0), inputs[:, :, -HALO:].transpose(1, 2, 0)))
+    ext = jnp.concatenate(
+        [in_before.transpose(2, 0, 1), inputs, in_after.transpose(2, 0, 1)], axis=2)
     ens = ensemble.astype(jnp.float32)
     partial = jnp.sum(ens * localized[:, :, None, :], axis=0)
-    both = jnp.concatenate([partial, inputs], axis=1)
     scattered = member_scatter(partial.transpose(1, 0, 2).reshape(nfield * ncol, nrow))
-    scattered, both = lax.optimization_barrier((scattered, both))
-    before, after = shift_rows(
-        None, (both[:, :, :HALO].transpose(1, 2, 0), both[:, :, -HALO:].transpose(1, 2, 0)))
-    halo = jnp.concatenate([before[:nfield], after[:nfield]], axis=1)
-    before = before.transpose(2, 0, 1)
-    after = after.transpose(2, 0, 1)
+    scattered, partial, ext = lax.optimization_barrier((scattered, partial, ext))
+    p_before, p_after = shift_rows(
+        None, (partial[:, :, :HALO].transpose(1, 2, 0), partial[:, :, -HALO:].transpose(1, 2, 0)))
+    halo = jnp.concatenate([p_before, p_after], axis=1)
     summed = member_gather(*scattered)
     incr_main = summed.reshape(nfield, ncol, nrow)
     incr_halo = member_gather_sum(halo).transpose(0, 2, 1)
     incr = jnp.concatenate(
         [incr_halo[:, :, :HALO], incr_main, incr_halo[:, :, HALO:]], axis=2
     )
-    ext = jnp.concatenate([before[:, nfield:], inputs, after[:, nfield:]], axis=2)
 
     state = [ext[:, i] + incr[i] for i in range(nfield)]
     meas = [ext[:, nfield + i] for i in range(nfield)]

time: 72.5 us -> 104 us (1.43)
  the two profiles are of different devices: /device:TPU:0 before, /device:TPU:11 now
where the time goes in v6:
time: 104 us; the launch traced here: 102 us
  waiting for transfers between devices  52.5 us (50%)
  local copies, waits for them, and re-layouts  15.9 us (15%)
  other arithmetic  15.3 us (15%)
  starting transfers between devices  12.5 us (12%)
  matrix products  5.12 us (5%)
  between operations  1.16 us (1%)
    ppermute x3, waiting for transfers between devices, member_gather_sum(): pieces[s] = lax.ppermute(x, 'member', shift)  35.2 us
    ppermute x2, waiting for transfers between devices, shift_rows(): before = lax.ppermute(hi, 'tile', up)  7.22 us
    ppermute x3, waiting for transfers between devices, member_scatter(): acc = acc + lax.ppermute(sent, 'member', shift)  6.51 us
    concatenate x1, other arithmetic, body(): jnp.concatenate([in_before.transpose(2, 0, 1), inputs, in_after.transpose...  5.6 us
    ppermute x3, starting transfers between devices, member_scatter(): acc = acc + lax.ppermute(sent, 'member', shift)  3.78 us
    ppermute x2, starting transfers between devices, shift_rows(): before = lax.ppermute(hi, 'tile', up)  3.77 us
    ppermute x3, starting transfers between devices, member_gather_sum(): pieces[s] = lax.ppermute(x, 'member', shift)  2.89 us
    another operation x3, local copies, waits for them, and re-layouts, body(): pred = jnp.stack([f[:, inner] for f in pred], axis=1)  2.53 us
  transfers between devices with their start and end apart: 13, of which 8 were waited for; matrix products, arithmetic and copies ran while one was open for 17% of the time, Pallas kernels for 0%

profile of v6, /device:TPU:11, one launch (start us, length us, event | category | flops | bytes accessed | tf_op | source)
XLA Modules:
  0.0 102.4 jit_solution(3267882421947243318)
XLA Ops:
  0.6 1.9 %pad_maximum_fusion.1 = f32[256,10,256]{2,0,1:T(8,128)S(1)} fusion(f32[256,1,256]{2,0,1:T(8,128)} %bitcast.112, f32[256,3,256]{2,0,1:T(8,128)} %param.12, f32[256,3,256]{2,0,1:T(8,128)} %param.11, f32[256,3,256]{2,0,1:T(8,128)} %param.10), kind=kLoop, calls=%fused_computation.3 | loop fusion | flops 1966080 | bytes 5242880 | tf_op jit(solution)/shard_map/concatenate | solution.py:94
  5.7 2.0 %collective-permute-start.3 = (f32[10,8,256]{2,1,0:T(8,128)}, f32[10,8,256]{2,1,0:T(8,128)}, u32[]{:S(2)}, u32[]{:S(2)}) collective-permute-start(f32[10,8,256]{2,1,0:T(8,128)} %copy.36), channel_id=1, source_target_pairs={{0,4},{4,8},{8,12},{12,16},{16,20},{20,24},{24,28},{28,0},{1,5},{5... | collective-permute-start | bytes 245768 | tf_op jit(solution)/shard_map/ppermute | solution.py:16
  7.7 2.0 %fusion.40 = f32[3,256,256]{2,1,0:T(8,128)S(1)} fusion(f32[3,256,256]{2,1,0:T(8,128)} %param.8, f32[256,256]{1,0:T(8,128)} %param.14), kind=kOutput, calls=%fused_computation.79 | convolution fusion | flops 603979776 | bytes 1835008 | tf_op jit(solution)/shard_map/dot_general | solution.py:103
  11.6 1.3 %collective-permute-start = (f32[192,256]{1,0:T(8,128)}, f32[192,256]{1,0:T(8,128)}, u32[]{:S(2)}, u32[]{:S(2)}) collective-permute-start(f32[192,256]{1,0:T(8,128)} %get-tuple-element.32), channel_id=1, source_target_pairs={{0,1},{1,2},{2,3},{3,0},{4,5},{5,6},{6,7},{7,4},{8,9},{9,10},{10,1... | collective-permute-start | bytes 589832 | tf_op jit(solution)/shard_map/ppermute | solution.py:55
  12.9 1.0 collective-permute-start.1
  14.0 1.5 %collective-permute-start.2 = (f32[192,256]{1,0:T(8,128)}, f32[192,256]{1,0:T(8,128)}, u32[]{:S(2)}, u32[]{:S(2)}) collective-permute-start(f32[192,256]{1,0:T(8,128)} %get-tuple-element.33), channel_id=1, source_target_pairs={{0,3},{1,0},{2,1},{3,2},{4,7},{5,4},{6,5},{7,6},{8,11},{9,8},{10,9... | collective-permute-start | bytes 589832 | tf_op jit(solution)/shard_map/ppermute | solution.py:55
  15.4 1.3 %copy.39 = f32[10,8,256]{1,2,0:T(8,128)S(1)} copy(f32[10,8,256]{2,1,0:T(8,128)} %collective-permute-done.4) | data formatting | bytes 163840 | tf_op jit(solution)/shard_map/ppermute | solution.py:17
  16.7 2.4 %copy.37 = f32[10,8,256]{1,2,0:T(8,128)} copy(f32[10,8,256]{2,1,0:T(8,128)} %collective-permute-done.3) | data formatting | bytes 163840 | tf_op jit(solution)/shard_map/ppermute | solution.py:16
  19.1 5.6 %pad_maximum_fusion = f32[256,10,272]{2,0,1:T(8,128)} fusion(f32[256,10,8]{2,0,1:T(8,128)S(1)} %bitcast.109, f32[256,1,256]{2,0,1:T(8,128)} %bitcast.113, f32[256,3,256]{2,0,1:T(8,128)} %param.12, f32[256,3,256]{2,0,1:T(8,128)} %param.11, f32[256,3,256]{2,0,1:T(8,128)} %param.10, f32[256,10,8]{2,0,1:T(8,128)} %bitcast.110), kind=kLoop, calls=%fused_computation | loop fusion | flops 3481600 | bytes 5570560 | tf_op jit(solution)/shard_map/concatenate | solution.py:107
  24.7 1.7 %collective-permute-done = f32[192,256]{1,0:T(8,128)} collective-permute-done((f32[192,256]{1,0:T(8,128)}, f32[192,256]{1,0:T(8,128)}, u32[]{:S(2)}, u32[]{:S(2)}) %collective-permute-start) | collective-permute-done | bytes 196640 | tf_op jit(solution)/shard_map/ppermute | solution.py:55
  26.4 3.2 %collective-permute-done.1 = f32[192,256]{1,0:T(8,128)} collective-permute-done((f32[192,256]{1,0:T(8,128)}, f32[192,256]{1,0:T(8,128)}, u32[]{:S(2)}, u32[]{:S(2)}) %collective-permute-start.1) | collective-permute-done | bytes 196640 | tf_op jit(solution)/shard_map/ppermute | solution.py:55
  29.6 1.6 %collective-permute-done.2 = f32[192,256]{1,0:T(8,128)} collective-permute-done((f32[192,256]{1,0:T(8,128)}, f32[192,256]{1,0:T(8,128)}, u32[]{:S(2)}, u32[]{:S(2)}) %collective-permute-start.2) | collective-permute-done | bytes 196640 | tf_op jit(solution)/shard_map/ppermute | solution.py:55
  31.2 1.8 %fusion.51 = f32[192,256]{1,0:T(8,128)} fusion(f32[192,256]{1,0:T(8,128)} %collective-permute-done.2, f32[192,256]{1,0:T(8,128)} %collective-permute-done.1, f32[192,256]{1,0:T(8,128)} %collective-permute-done, f32[4,192,256]{2,1,0:T(8,128)S(1)} %bitcast.108, s32[]{:T(128)S(6)} %select_n.140), kind=kLoop, calls=%fused_computation.105 | loop fusion | flops 147456 | bytes 983044 | tf_op jit(solution)/shard_map/add | solution.py:55
  34.0 1.8 %collective-permute-start.5 = (f32[3,8,256]{1,2,0:T(8,128)}, f32[3,8,256]{1,2,0:T(8,128)}, u32[]{:S(2)}, u32[]{:S(2)}) collective-permute-start(f32[3,8,256]{1,2,0:T(8,128)} %get-tuple-element.30), channel_id=1, source_target_pairs={{0,4},{4,8},{8,12},{12,16},{16,20},{20,24},{24,28},{28,0},{1,5},{5... | collective-permute-start | bytes 73736 | tf_op jit(solution)/shard_map/ppermute | solution.py:16
  36.1 1.4 %collective-permute-start.11 = (f32[192,256]{1,0:T(8,128)}, f32[192,256]{1,0:T(8,128)S(1)}, u32[]{:S(2)}, u32[]{:S(2)}) collective-permute-start(f32[192,256]{1,0:T(8,128)} %fusion.51), channel_id=1, source_target_pairs={{0,2},{1,3},{2,0},{3,1},{4,6},{5,7},{6,4},{7,5},{8,10},{9,11},{10,... | collective-permute-start | bytes 589832 | tf_op jit(solution)/shard_map/ppermute | solution.py:66
  37.5 7.2 %collective-permute-done.5 = f32[3,8,256]{1,2,0:T(8,128)} collective-permute-done((f32[3,8,256]{1,2,0:T(8,128)}, f32[3,8,256]{1,2,0:T(8,128)}, u32[]{:S(2)}, u32[]{:S(2)}) %collective-permute-start.5) | collective-permute-done | bytes 24608 | tf_op jit(solution)/shard_map/ppermute | solution.py:16
  44.7 1.8 %collective-permute-done.6 = f32[3,8,256]{1,2,0:T(8,128)} collective-permute-done((f32[3,8,256]{1,2,0:T(8,128)S(1)}, f32[3,8,256]{1,2,0:T(8,128)}, u32[]{:S(2)}, u32[]{:S(2)}) %collective-permute-start.6) | collective-permute-done | bytes 24608 | tf_op jit(solution)/shard_map/ppermute | solution.py:17
  46.6 1.3 %pad_maximum_fusion.4 = f32[3,16,256]{1,2,0:T(8,128)S(1)} fusion(f32[3,8,256]{1,2,0:T(8,128)} %collective-permute-done.6, f32[3,8,256]{1,2,0:T(8,128)} %collective-permute-done.5), kind=kLoop, calls=%fused_computation.22 | loop fusion | flops 12288 | bytes 98304 | tf_op jit(solution)/shard_map/concatenate | solution.py:115
  48.5 2.3 %collective-permute-start.9 = (f32[3,16,256]{1,2,0:T(8,128)S(1)}, f32[3,16,256]{1,2,0:T(8,128)S(1)}, u32[]{:S(2)}, u32[]{:S(2)}) collective-permute-start(f32[3,16,256]{1,2,0:T(8,128)S(1)} %pad_maximum_fusion.4), channel_id=1, source_target_pairs={{0,1},{1,2},{2,3},{3,0},{4,5},{5,6},{6,7},{7,4},{8,9},{9,10},{10,1... | collective-permute-start | bytes 147464 | tf_op jit(solution)/shard_map/ppermute | solution.py:78
  51.8 24.7 %collective-permute-done.7 = f32[3,16,256]{1,2,0:T(8,128)S(1)} collective-permute-done((f32[3,16,256]{1,2,0:T(8,128)S(1)}, f32[3,16,256]{1,2,0:T(8,128)S(1)}, u32[]{:S(2)}, u32[]{:S(2)}) %collective-permute-start.7) | collective-permute-done | bytes 49184 | tf_op jit(solution)/shard_map/ppermute | solution.py:78
  76.5 10.5 %collective-permute-done.9 = f32[3,16,256]{1,2,0:T(8,128)S(1)} collective-permute-done((f32[3,16,256]{1,2,0:T(8,128)S(1)}, f32[3,16,256]{1,2,0:T(8,128)S(1)}, u32[]{:S(2)}, u32[]{:S(2)}) %collective-permute-start.9) | collective-permute-done | bytes 49184 | tf_op jit(solution)/shard_map/ppermute | solution.py:78
  87.5 1.7 %collective-permute-done.12 = f32[192,256]{1,0:T(8,128)S(1)} collective-permute-done((f32[192,256]{1,0:T(8,128)}, f32[192,256]{1,0:T(8,128)S(1)}, u32[]{:S(2)}, u32[]{:S(2)}) %collective-permute-start.12) | collective-permute-done | bytes 196640 | tf_op jit(solution)/shard_map/ppermute | solution.py:66
  98.3 1.4 %fusion.35 = f32[3,256,256]{1,2,0:T(8,128)S(1)} fusion(f32[3,256,256]{2,1,0:T(8,128)S(1)} %fusion.1, f32[256,256]{1,0:T(8,128)S(1)} %copy-done), kind=kOutput, calls=%fused_computation.74 | convolution fusion | flops 603979776 | bytes 1835008 | tf_op jit(solution)/shard_map/dot_general | solution.py:134
  100.6 1.1 %copy.42 = f32[3,256,256]{2,1,0:T(8,128)} copy(f32[3,256,256]{1,2,0:T(8,128)S(1)} %fusion.2) | data formatting | bytes 1572864
  (94 shorter events, 18.7 us)
Async XLA Ops:
  0.6 9.1 %copy-start = (f32[256,256]{1,0:T(8,128)S(1)}, f32[256,256]{1,0:T(8,128)}, u32[]{:S(2)}) copy-start(f32[256,256]{1,0:T(8,128)} %param.15) | copy-start | bytes 786436
  4.0 6.5 %copy-start.2 = (bf16[3,256,3,256]{3,1,2,0:T(8,128)(2,1)S(1)}, bf16[3,256,3,256]{3,1,2,0:T(8,128)(2,1)}, u32[]{:S(2)}) copy-start(bf16[3,256,3,256]{3,1,2,0:T(8,128)(2,1)} %param.9) | copy-start | bytes 3538948
  4.0 11.4 %collective-permute-start.4 = (f32[10,8,256]{2,1,0:T(8,128)}, f32[10,8,256]{2,1,0:T(8,128)}, u32[]{:S(2)}, u32[]{:S(2)}) collective-permute-start(f32[10,8,256]{2,1,0:T(8,128)} %copy.38), channel_id=1, source_target_pairs={{4,0},{8,4},{12,8},{16,12},{20,16},{24,20},{28,24},{0,28},{5,1},{9... | collective-permute-start | bytes 245768 | tf_op jit(solution)/shard_map/ppermute | solution.py:17
  5.7 11.0 %collective-permute-start.3 = (f32[10,8,256]{2,1,0:T(8,128)}, f32[10,8,256]{2,1,0:T(8,128)}, u32[]{:S(2)}, u32[]{:S(2)}) collective-permute-start(f32[10,8,256]{2,1,0:T(8,128)} %copy.36), channel_id=1, source_target_pairs={{0,4},{4,8},{8,12},{12,16},{16,20},{20,24},{24,28},{28,0},{1,5},{5... | collective-permute-start | bytes 245768 | tf_op jit(solution)/shard_map/ppermute | solution.py:16
  11.6 14.8 %collective-permute-start = (f32[192,256]{1,0:T(8,128)}, f32[192,256]{1,0:T(8,128)}, u32[]{:S(2)}, u32[]{:S(2)}) collective-permute-start(f32[192,256]{1,0:T(8,128)} %get-tuple-element.32), channel_id=1, source_target_pairs={{0,1},{1,2},{2,3},{3,0},{4,5},{5,6},{6,7},{7,4},{8,9},{9,10},{10,1... | collective-permute-start | bytes 589832 | tf_op jit(solution)/shard_map/ppermute | solution.py:55
  12.9 16.7 %collective-permute-start.1 = (f32[192,256]{1,0:T(8,128)}, f32[192,256]{1,0:T(8,128)}, u32[]{:S(2)}, u32[]{:S(2)}) collective-permute-start(f32[192,256]{1,0:T(8,128)} %get-tuple-element.34), channel_id=1, source_target_pairs={{0,2},{1,3},{2,0},{3,1},{4,6},{5,7},{6,4},{7,5},{8,10},{9,11},{10,... | collective-permute-start | bytes 589832 | tf_op jit(solution)/shard_map/ppermute | solution.py:55
  14.0 17.3 %collective-permute-start.2 = (f32[192,256]{1,0:T(8,128)}, f32[192,256]{1,0:T(8,128)}, u32[]{:S(2)}, u32[]{:S(2)}) collective-permute-start(f32[192,256]{1,0:T(8,128)} %get-tuple-element.33), channel_id=1, source_target_pairs={{0,3},{1,0},{2,1},{3,2},{4,7},{5,4},{6,5},{7,6},{8,11},{9,8},{10,9... | collective-permute-start | bytes 589832 | tf_op jit(solution)/shard_map/ppermute | solution.py:55
  24.7 11.1 %copy-start.3 = (f32[3,256,256]{2,1,0:T(8,128)S(1)}, f32[3,256,256]{2,1,0:T(8,128)}, u32[]{:S(2)}) copy-start(f32[3,256,256]{2,1,0:T(8,128)} %param.8) | copy-start | bytes 2359300
  34.0 10.7 %collective-permute-start.5 = (f32[3,8,256]{1,2,0:T(8,128)}, f32[3,8,256]{1,2,0:T(8,128)}, u32[]{:S(2)}, u32[]{:S(2)}) collective-permute-start(f32[3,8,256]{1,2,0:T(8,128)} %get-tuple-element.30), channel_id=1, source_target_pairs={{0,4},{4,8},{8,12},{12,16},{16,20},{20,24},{24,28},{28,0},{1,5},{5... | collective-permute-start | bytes 73736 | tf_op jit(solution)/shard_map/ppermute | solution.py:16
  35.8 10.8 %collective-permute-start.6 = (f32[3,8,256]{1,2,0:T(8,128)S(1)}, f32[3,8,256]{1,2,0:T(8,128)}, u32[]{:S(2)}, u32[]{:S(2)}) collective-permute-start(f32[3,8,256]{1,2,0:T(8,128)S(1)} %get-tuple-element.31), channel_id=1, source_target_pairs={{4,0},{8,4},{12,8},{16,12},{20,16},{24,20},{28,24},{0,28},{5,1},{9... | collective-permute-start | bytes 73736 | tf_op jit(solution)/shard_map/ppermute | solution.py:17
  36.1 51.3 %collective-permute-start.10 = (f32[192,256]{1,0:T(8,128)}, f32[192,256]{1,0:T(8,128)S(1)}, u32[]{:S(2)}, u32[]{:S(2)}) collective-permute-start(f32[192,256]{1,0:T(8,128)} %fusion.51), channel_id=1, source_target_pairs={{0,1},{1,2},{2,3},{3,0},{4,5},{5,6},{6,7},{7,4},{8,9},{9,10},{10,1... | collective-permute-start | bytes 589832 | tf_op jit(solution)/shard_map/ppermute | solution.py:66
  36.1 51.3 %collective-permute-start.11 = (f32[192,256]{1,0:T(8,128)}, f32[192,256]{1,0:T(8,128)S(1)}, u32[]{:S(2)}, u32[]{:S(2)}) collective-permute-start(f32[192,256]{1,0:T(8,128)} %fusion.51), channel_id=1, source_target_pairs={{0,2},{1,3},{2,0},{3,1},{4,6},{5,7},{6,4},{7,5},{8,10},{9,11},{10,... | collective-permute-start | bytes 589832 | tf_op jit(solution)/shard_map/ppermute | solution.py:66
  47.9 28.6 %collective-permute-start.7 = (f32[3,16,256]{1,2,0:T(8,128)S(1)}, f32[3,16,256]{1,2,0:T(8,128)S(1)}, u32[]{:S(2)}, u32[]{:S(2)}) collective-permute-start(f32[3,16,256]{1,2,0:T(8,128)S(1)} %pad_maximum_fusion.4), channel_id=1, source_target_pairs={{0,3},{1,0},{2,1},{3,2},{4,7},{5,4},{6,5},{7,6},{8,11},{9,8},{10,9... | collective-permute-start | bytes 147464 | tf_op jit(solution)/shard_map/ppermute | solution.py:78
  47.9 28.5 %collective-permute-start.8 = (f32[3,16,256]{1,2,0:T(8,128)S(1)}, f32[3,16,256]{1,2,0:T(8,128)S(1)}, u32[]{:S(2)}, u32[]{:S(2)}) collective-permute-start(f32[3,16,256]{1,2,0:T(8,128)S(1)} %pad_maximum_fusion.4), channel_id=1, source_target_pairs={{0,2},{1,3},{2,0},{3,1},{4,6},{5,7},{6,4},{7,5},{8,10},{9,11},{10,... | collective-permute-start | bytes 147464 | tf_op jit(solution)/shard_map/ppermute | solution.py:78
  48.5 38.5 %collective-permute-start.9 = (f32[3,16,256]{1,2,0:T(8,128)S(1)}, f32[3,16,256]{1,2,0:T(8,128)S(1)}, u32[]{:S(2)}, u32[]{:S(2)}) collective-permute-start(f32[3,16,256]{1,2,0:T(8,128)S(1)} %pad_maximum_fusion.4), channel_id=1, source_target_pairs={{0,1},{1,2},{2,3},{3,0},{4,5},{5,6},{6,7},{7,4},{8,9},{9,10},{10,1... | collective-permute-start | bytes 147464 | tf_op jit(solution)/shard_map/ppermute | solution.py:78
  76.4 12.7 %collective-permute-start.12 = (f32[192,256]{1,0:T(8,128)}, f32[192,256]{1,0:T(8,128)S(1)}, u32[]{:S(2)}, u32[]{:S(2)}) collective-permute-start(f32[192,256]{1,0:T(8,128)} %fusion.51), channel_id=1, source_target_pairs={{0,3},{1,0},{2,1},{3,2},{4,7},{5,4},{6,5},{7,6},{8,11},{9,8},{10,9... | collective-permute-start | bytes 589832 | tf_op jit(solution)/shard_map/ppermute | solution.py:66
  87.2 2.4 %copy-start.1 = (f32[256,10,272]{2,0,1:T(8,128)S(1)}, f32[256,10,272]{2,0,1:T(8,128)}, u32[]{:S(2)}) copy-start(f32[256,10,272]{2,0,1:T(8,128)} %pad_maximum_fusion) | copy-start | bytes 8355844
  98.0 1.7 %copy-start.4 = (f32[256,256]{1,0:T(8,128)S(1)}, f32[256,256]{1,0:T(8,128)}, u32[]{:S(2)}) copy-start(f32[256,256]{1,0:T(8,128)} %param.14) | copy-start | bytes 786436
  98.3 3.5 %copy-start.5 = (f32[256,1,256]{2,0,1:T(8,128)S(1)}, f32[256,1,256]{2,0,1:T(8,128)}, u32[]{:S(2)}) copy-start(f32[256,1,256]{2,0,1:T(8,128)} %slice_bitcast_fusion.9) | copy-start | bytes 786436
  98.3 3.5 %copy-start.6 = (f32[256,1,256]{2,0,1:T(8,128)S(1)}, f32[256,1,256]{2,0,1:T(8,128)}, u32[]{:S(2)}) copy-start(f32[256,1,256]{2,0,1:T(8,128)} %slice_bitcast_fusion.7) | copy-start | bytes 786436
  98.3 3.4 %copy-start.7 = (f32[256,1,256]{2,0,1:T(8,128)S(1)}, f32[256,1,256]{2,0,1:T(8,128)}, u32[]{:S(2)}) copy-start(f32[256,1,256]{2,0,1:T(8,128)} %slice_bitcast_fusion.8) | copy-start | bytes 786436

commit v7 on v6

--- a/solution.py
+++ b/solution.py
@@ -91,46 +91,55 @@
     block_cols = ncol // lax.axis_size("member")
     col_start = lax.axis_index("member") * block_cols
 
-    inputs = jnp.concatenate(
-        [background, measured_values, precision_factor, depth[:, None, :]], axis=1
-    )
     mem = alpha.shape[0]
     cols_b = jnp.broadcast_to(loc_cols, (mem,) + loc_cols.shape)
     rows_b = jnp.broadcast_to(loc_rows, (mem,) + loc_rows.shape)
+
     def batched(lhs_dim, rhs_dim):
         return (((lhs_dim,), (rhs_dim,)), ((0,), (0,)))
 
     localized = lax.dot_general(cols_b, alpha, batched(2, 1), precision=highest)
     localized = lax.dot_general(localized, rows_b, batched(2, 2), precision=highest)
-    in_before, in_after = shift_rows(
-        None, (inputs[:, :, :HALO].transpose(1, 2, 0), inputs[:, :, -HALO:].transpose(1, 2, 0)))
-    ext = jnp.concatenate(
-        [in_before.transpose(2, 0, 1), inputs, in_after.transpose(2, 0, 1)], axis=2)
     ens = ensemble.astype(jnp.float32)
     partial = jnp.sum(ens * localized[:, :, None, :], axis=0)
     scattered = member_scatter(partial.transpose(1, 0, 2).reshape(nfield * ncol, nrow))
-    scattered, partial, ext = lax.optimization_barrier((scattered, partial, ext))
-    p_before, p_after = shift_rows(
-        None, (partial[:, :, :HALO].transpose(1, 2, 0), partial[:, :, -HALO:].transpose(1, 2, 0)))
-    halo = jnp.concatenate([p_before, p_after], axis=1)
-    summed = member_gather(*scattered)
-    incr_main = summed.reshape(nfield, ncol, nrow)
-    incr_halo = member_gather_sum(halo).transpose(0, 2, 1)
-    incr = jnp.concatenate(
-        [incr_halo[:, :, :HALO], incr_main, incr_halo[:, :, HALO:]], axis=2
-    )
 
-    state = [ext[:, i] + incr[i] for i in range(nfield)]
-    meas = [ext[:, nfield + i] for i in range(nfield)]
-    prec = [ext[:, 2 * nfield + i] for i in range(nfield)]
-    dep = ext[:, 3 * nfield]
-    pred, adj = dynamics(*state, dep, prec, meas)
+    meas = [measured_values[:, i] for i in range(nfield)]
+    prec = [precision_factor[:, i] for i in range(nfield)]
+    fixed = meas + prec + [depth]
 
-    inner = slice(HALO, HALO + nrow)
-    pred = jnp.stack([f[:, inner] for f in pred], axis=1)
-    predicted_final = lax.dynamic_slice_in_dim(pred, col_start, block_cols, 0)
-    adj = jnp.stack([f[:, inner] for f in adj], axis=1)
-    projected = jnp.sum(ens * adj[None], axis=2)
+    def edges(planes, part):
+        return jnp.stack([p[:, part] for p in planes], axis=1)
+
+    lo, hi = slice(0, HALO), slice(nrow - HALO, nrow)
+    scattered, fixed_lo, fixed_hi = lax.optimization_barrier(
+        (scattered, edges(fixed, lo), edges(fixed, hi)))
+    incr = member_gather(*scattered).reshape(nfield, ncol, nrow)
+    state = [background[:, i] + incr[i] for i in range(nfield)]
+
+    before, after = shift_rows(None, (
+        jnp.concatenate([edges(state, lo), fixed_lo], axis=1),
+        jnp.concatenate([edges(state, hi), fixed_hi], axis=1)))
+    planes = state + fixed
+
+    pred, adj = dynamics(*state, depth, prec, meas)
+
+    def strip(pieces):
+        s = [jnp.concatenate(p, axis=1) for p in pieces]
+        return dynamics(*s[:nfield], s[-1], s[2 * nfield:3 * nfield], s[nfield:2 * nfield])
+
+    first = strip([(before[:, i], p[:, : 2 * HALO]) for i, p in enumerate(planes)])
+    last = strip([(p[:, nrow - 2 * HALO:], after[:, i]) for i, p in enumerate(planes)])
+    mid = slice(HALO, 2 * HALO)
+    inner = slice(HALO, nrow - HALO)
+
+    def assemble(k):
+        return jnp.stack([
+            jnp.concatenate([first[k][i][:, mid], f[:, inner], last[k][i][:, mid]], axis=1)
+            for i, f in enumerate((pred, adj)[k])], axis=1)
+
+    predicted_final = lax.dynamic_slice_in_dim(assemble(0), col_start, block_cols, 0)
+    projected = jnp.sum(ens * assemble(1)[None], axis=2)
     rows_done = lax.dot_general(projected, rows_b, batched(2, 1), precision=highest)
     cost_derivative = alpha + lax.dot_general(cols_b, rows_done, batched(1, 1), precision=highest)
     return (cost_derivative, predicted_final)

time: 104 us -> 128 us (1.23)
  local copies, waits for them, and re-layouts: 15.9 us -> 61.5 us
  waiting for transfers between devices: 52.5 us -> 20.7 us
  other arithmetic: 15.3 us -> 29.1 us
  starting transfers between devices: 12.5 us -> 7.18 us
    ppermute x3 -> x0, waiting for transfers between devices: 35.2 us -> none  [member_gather_sum(): pieces[s] = lax.ppermute(x, 'member', shift)]
    another operation x4 -> x27, local copies, waits for them, and re-layouts: 2.66 us -> 19 us  [edges(): return jnp.stack([p[:, part] for p in planes], axis=1)]
    ppermute x3, waiting for transfers between devices: 1.67 us -> 16.4 us  [member_gather(): got = lax.ppermute(acc, 'member', shift)]
    slice x1 -> x22, local copies, waits for them, and re-layouts: 0.18 us -> 11.4 us  [the longest x4 3.32 us: assemble(): f[:, inner]]
    slice x16 -> x45, local copies, waits for them, and re-layouts: 2.17 us -> 12.5 us  [row_slope(): return 0.5 * (jnp.roll(f, -1, 1) - jnp.roll(f, 1, 1))]
    unnamed x18 -> x140, local copies, waits for them, and re-layouts: 1.45 us -> 11.2 us
    mul x1 -> x5, other arithmetic: 0.33 us -> 8.49 us  [dynamics(): a, p, q = (prec[i] * (pred[i] - meas[i]) for i in range(3))]
    ppermute x2 -> x1, waiting for transfers between devices: 7.22 us -> 0.01 us  [shift_rows(): before = lax.ppermute(hi, 'tile', up)]
  transfers between devices with their start and end apart: 13 -> 8, of which waited for: 8 -> 5; matrix products, arithmetic and copies ran while one was open for 17% -> 24% of each run, Pallas kernels for 0% -> 0%
where the time goes in v7:
time: 128 us; the launch traced here: 126 us
  local copies, waits for them, and re-layouts  61.5 us (48%)
  other arithmetic  29.1 us (23%)
  waiting for transfers between devices  20.7 us (16%)
  starting transfers between devices  7.18 us (6%)
  matrix products  5.16 us (4%)
  between operations  2.34 us (2%)
    another operation x27, local copies, waits for them, and re-layouts, edges(): return jnp.stack([p[:, part] for p in planes], axis=1)  19 us
    ppermute x3, waiting for transfers between devices, member_gather(): got = lax.ppermute(acc, 'member', shift)  16.4 us
    slice x45, local copies, waits for them, and re-layouts, row_slope(): return 0.5 * (jnp.roll(f, -1, 1) - jnp.roll(f, 1, 1))  12.5 us
    unnamed x140, local copies, waits for them, and re-layouts  11.2 us
    mul x5, other arithmetic, dynamics(): a, p, q = (prec[i] * (pred[i] - meas[i]) for i in range(3))  8.49 us
    slice x44, local copies, waits for them, and re-layouts, col_slope(): return 0.5 * (jnp.roll(f, -1, 0) - jnp.roll(f, 1, 0))  6.11 us
    ppermute x3, waiting for transfers between devices, member_scatter(): acc = acc + lax.ppermute(sent, 'member', shift)  4.34 us
    mul x6, other arithmetic, dynamics(): w = dep * e  4.27 us
  transfers between devices with their start and end apart: 8, of which 5 were waited for; matrix products, arithmetic and copies ran while one was open for 24% of the time, Pallas kernels for 0%

profile of v7, /device:TPU:11, one launch (start us, length us, event | category | flops | bytes accessed | tf_op | source)
XLA Modules:
  0.0 126.0 jit_solution(3709531302536014033)
XLA Ops:
  0.7 2.1 %fusion.8 = f32[3,256,256]{2,1,0:T(8,128)S(1)} fusion(f32[3,256,256]{2,1,0:T(8,128)} %param.8, f32[256,256]{1,0:T(8,128)} %param.14), kind=kOutput, calls=%fused_computation.15 | convolution fusion | flops 603979776 | bytes 1835008 | tf_op jit(solution)/shard_map/dot_general | solution.py:101
  8.3 1.5 %collective-permute-start.2 = (f32[192,256]{1,0:T(8,128)}, f32[192,256]{1,0:T(8,128)}, u32[]{:S(2)}, u32[]{:S(2)}) collective-permute-start(f32[192,256]{1,0:T(8,128)} %get-tuple-element.55), channel_id=1, source_target_pairs={{0,3},{1,0},{2,1},{3,2},{4,7},{5,4},{6,5},{7,6},{8,11},{9,8},{10,9... | collective-permute-start | bytes 589832 | tf_op jit(solution)/shard_map/ppermute | solution.py:55
  22.3 1.5 %collective-permute-done.1 = f32[192,256]{1,0:T(8,128)} collective-permute-done((f32[192,256]{1,0:T(8,128)}, f32[192,256]{1,0:T(8,128)}, u32[]{:S(2)}, u32[]{:S(2)}) %collective-permute-start.1) | collective-permute-done | bytes 196640 | tf_op jit(solution)/shard_map/ppermute | solution.py:55
  23.8 2.8 %collective-permute-done.2 = f32[192,256]{1,0:T(8,128)} collective-permute-done((f32[192,256]{1,0:T(8,128)}, f32[192,256]{1,0:T(8,128)}, u32[]{:S(2)}, u32[]{:S(2)}) %collective-permute-start.2) | collective-permute-done | bytes 196640 | tf_op jit(solution)/shard_map/ppermute | solution.py:55
  29.8 4.1 %collective-permute-done.3 = f32[192,256]{1,0:T(8,128)S(1)} collective-permute-done((f32[192,256]{1,0:T(8,128)S(1)}, f32[192,256]{1,0:T(8,128)S(1)}, u32[]{:S(2)}, u32[]{:S(2)}) %collective-permute-start.3) | collective-permute-done | bytes 196640 | tf_op jit(solution)/shard_map/ppermute | solution.py:66
  34.0 10.7 %collective-permute-done.4 = f32[192,256]{1,0:T(8,128)S(1)} collective-permute-done((f32[192,256]{1,0:T(8,128)S(1)}, f32[192,256]{1,0:T(8,128)S(1)}, u32[]{:S(2)}, u32[]{:S(2)}) %collective-permute-start.4) | collective-permute-done | bytes 196640 | tf_op jit(solution)/shard_map/ppermute | solution.py:66
  44.8 1.5 %collective-permute-done.5 = f32[192,256]{1,0:T(8,128)S(1)} collective-permute-done((f32[192,256]{1,0:T(8,128)S(1)}, f32[192,256]{1,0:T(8,128)S(1)}, u32[]{:S(2)}, u32[]{:S(2)}) %collective-permute-start.5) | collective-permute-done | bytes 196640 | tf_op jit(solution)/shard_map/ppermute | solution.py:66
  58.1 1.6 %copy.358 = f32[256,1,8]{0,2,1:T(8,128)} copy(f32[256,1,8]{2,0,1:T(8,128)} %get-tuple-element.89) | data formatting | bytes 16384 | tf_op jit(solution)/shard_map/stack | solution.py:112
  59.6 1.6 %copy.359 = f32[256,1,8]{0,2,1:T(8,128)} copy(f32[256,1,8]{2,0,1:T(8,128)} %get-tuple-element.91) | data formatting | bytes 16384 | tf_op jit(solution)/shard_map/stack | solution.py:112
  61.2 1.6 %copy.360 = f32[256,1,8]{0,2,1:T(8,128)} copy(f32[256,1,8]{2,0,1:T(8,128)} %get-tuple-element.93) | data formatting | bytes 16384 | tf_op jit(solution)/shard_map/stack | solution.py:112
  62.8 1.5 %pad_maximum_fusion.13 = f32[256,10,8]{0,2,1:T(8,128)} fusion(f32[256,7,8]{0,2,1:T(8,128)} %copy-done.37, f32[256,1,8]{0,2,1:T(8,128)} %copy.360, f32[256,1,8]{0,2,1:T(8,128)} %copy.359, f32[256,1,8]{0,2,1:T(8,128)} %copy.358), kind=kLoop, calls=%fused_computation.245 | loop fusion | flops 61440 | bytes 163840 | tf_op jit(solution)/shard_map/concatenate | solution.py:122
  64.3 1.6 %collective-permute-start.6 = (f32[256,10,8]{0,2,1:T(8,128)}, f32[256,10,8]{0,2,1:T(8,128)}, u32[]{:S(2)}, u32[]{:S(2)}) collective-permute-start(f32[256,10,8]{0,2,1:T(8,128)} %pad_maximum_fusion.13), channel_id=1, source_target_pairs={{0,4},{4,8},{8,12},{12,16},{16,20},{20,24},{24,28},{28,0},{1,5},{5... | collective-permute-start | bytes 245768 | tf_op jit(solution)/shard_map/ppermute | solution.py:16
  65.8 1.6 %copy.373 = f32[256,1,8]{0,2,1:T(8,128)} copy(f32[256,1,8]{2,0,1:T(8,128)} %get-tuple-element.90) | data formatting | bytes 16384 | tf_op jit(solution)/shard_map/stack | solution.py:112
  67.4 1.6 %copy.374 = f32[256,1,8]{0,2,1:T(8,128)} copy(f32[256,1,8]{2,0,1:T(8,128)} %get-tuple-element.92) | data formatting | bytes 16384 | tf_op jit(solution)/shard_map/stack | solution.py:112
  69.0 1.6 %copy.375 = f32[256,1,8]{0,2,1:T(8,128)} copy(f32[256,1,8]{2,0,1:T(8,128)} %get-tuple-element.94) | data formatting | bytes 16384 | tf_op jit(solution)/shard_map/stack | solution.py:112
  70.5 1.5 %pad_maximum_fusion.14 = f32[256,10,8]{0,2,1:T(8,128)} fusion(f32[256,7,8]{0,2,1:T(8,128)} %copy-done.36, f32[256,1,8]{0,2,1:T(8,128)} %copy.375, f32[256,1,8]{0,2,1:T(8,128)} %copy.374, f32[256,1,8]{0,2,1:T(8,128)} %copy.373), kind=kLoop, calls=%fused_computation.246 | loop fusion | flops 61440 | bytes 163840 | tf_op jit(solution)/shard_map/concatenate | solution.py:121
  72.0 1.9 %slice_add_fusion.1 = f32[256,240]{1,0:T(8,128)} fusion(f32[256,256]{1,0:T(8,128)S(1)} %fusion.37, f32[1,256]{1,0:T(1,128)} %get-tuple-element.58, f32[255,256]{1,0:T(8,128)} %get-tuple-element.60, f32[255,256]{1,0:T(8,128)S(1)} %get-tuple-element.59, f32[1,256]{1,0:T(1,128)} %get-tuple-element.57), kind=kLoop, calls=%fused_computation.22 | loop fusion | flops 307200 | bytes 1015808 | tf_op jit(solution)/shard_map/add | solution.py:39
  78.8 1.5 %fusion.223 = (f32[256,1,8]{0,2,1:T(8,128)}, f32[256,1,8]{0,2,1:T(8,128)}, f32[256,1,8]{0,2,1:T(8,128)}, f32[256,1,8]{0,2,1:T(8,128)}, f32[256,1,8]{0,2,1:T(8,12...) fusion(f32[256,10,8]{0,2,1:T(8,128)} %collective-permute-done.6), kind=kLoop, calls=%fused_computation.374 | loop fusion | bytes 163840 | tf_op jit(solution)/shard_map/slice | solution.py:131
  83.9 1.5 %fusion.224 = (f32[256,1,8]{0,2,1:T(8,128)}, f32[256,1,8]{0,2,1:T(8,128)}, f32[256,1,8]{0,2,1:T(8,128)}, f32[256,1,8]{0,2,1:T(8,128)}, f32[256,1,8]{0,2,1:T(8,12...) fusion(f32[256,10,8]{0,2,1:T(8,128)} %collective-permute-done.7), kind=kLoop, calls=%fused_computation.375 | loop fusion | bytes 163840 | tf_op jit(solution)/shard_map/slice | solution.py:132
  95.6 1.7 %maximum_multiply_fusion.1 = (f32[256,24]{1,0:T(8,128)S(1)}, f32[256,24]{1,0:T(8,128)}) fusion(f32[256,16]{1,0:T(8,128)} %get-tuple-element.314, f32[256,8]{1,0:T(8,128)S(1)} %bitcast.176, f32[256,16]{1,0:T(8,128)} %get-tuple-element.310, f32[256,8]{1,0:T(8,128)S(1)} %bitcast.180, f32[256,24]{1,0:T(8,128)S(1)} %maximum_subtract_fusion.15, ...), kind=kLoop, calls=%fused_computation.166 | loop fusion | flops 55296 | bytes 172032 | tf_op jit(solution)/shard_map/mul | solution.py:35
  98.2 2.0 %maximum_multiply_fusion.2 = (f32[256,24]{1,0:T(8,128)S(1)}, f32[256,24]{1,0:T(8,128)}) fusion(f32[256,16]{1,0:T(8,128)} %get-tuple-element.316, f32[256,8]{1,0:T(8,128)S(1)} %bitcast.177, f32[256,16]{1,0:T(8,128)} %get-tuple-element.87, f32[256,8]{1,0:T(8,128)S(1)} %bitcast.181, f32[256,24]{1,0:T(8,128)S(1)} %maximum_subtract_fusion.17, ...), kind=kLoop, calls=%fused_computation.174 | loop fusion | flops 55296 | bytes 172032 | tf_op jit(solution)/shard_map/mul | solution.py:35
  106.8 1.8 %maximum_multiply_fusion.4 = (f32[256,24]{1,0:T(8,128)S(1)}, f32[256,24]{1,0:T(8,128)}) fusion(f32[256,8]{1,0:T(8,128)S(1)} %bitcast.178, f32[256,16]{1,0:T(8,128)} %get-tuple-element.313, f32[256,8]{1,0:T(8,128)S(1)} %bitcast.182, f32[256,16]{1,0:T(8,128)} %get-tuple-element.309, f32[256,24]{1,0:T(8,128)S(1)} %maximum_subtract_fusion.35, ...), kind=kLoop, calls=%fused_computation.212 | loop fusion | flops 55296 | bytes 172032 | tf_op jit(solution)/shard_map/mul | solution.py:35
  110.1 2.1 %maximum_multiply_fusion.5 = (f32[256,24]{1,0:T(8,128)S(1)}, f32[256,24]{1,0:T(8,128)}) fusion(f32[256,8]{1,0:T(8,128)S(1)} %bitcast.175, f32[256,16]{1,0:T(8,128)} %get-tuple-element.315, f32[256,8]{1,0:T(8,128)S(1)} %bitcast.179, f32[256,16]{1,0:T(8,128)} %get-tuple-element.88, f32[256,24]{1,0:T(8,128)S(1)} %maximum_subtract_fusion.37, ...), kind=kLoop, calls=%fused_computation.220 | loop fusion | flops 55296 | bytes 172032 | tf_op jit(solution)/shard_map/mul | solution.py:35
  114.0 1.5 %fusion.120 = (f32[256,24]{1,0:T(8,128)S(1)}, f32[256,24]{1,0:T(8,128)S(1)}) fusion(f32[256,24]{1,0:T(8,128)S(1)} %copy.379, f32[256,23]{1,0:T(8,128)} %get-tuple-element.264, f32[256,1]{1,0:T(8,128)} %get-tuple-element.266, f32[256,1]{1,0:T(8,128)} %get-tuple-element.265, f32[256,23]{1,0:T(8,128)} %get-tuple-element.263, f32[255,24]{1,0:T(8,128)} %get-tuple-element.256, ...), kind=kLoop, calls=%fused_computation.274 | loop fusion | flops 86016 | bytes 245760 | tf_op jit(solution)/shard_map/mul | solution.py:38
  (341 shorter events, 71.6 us)
Async XLA Ops:
  4.3 5.5 %copy-start.1 = (f32[256,256]{1,0:T(8,128)S(1)}, f32[256,256]{1,0:T(8,128)}, u32[]{:S(2)}) copy-start(f32[256,256]{1,0:T(8,128)} %param.13) | copy-start | bytes 786436
  4.3 5.7 %copy-start.4 = (f32[256,3,256]{2,0,1:T(8,128)S(1)}, f32[256,3,256]{2,0,1:T(8,128)}, u32[]{:S(2)}) copy-start(f32[256,3,256]{2,0,1:T(8,128)} %param.11) | copy-start | bytes 2359300
  6.0 16.3 %collective-permute-start = (f32[192,256]{1,0:T(8,128)}, f32[192,256]{1,0:T(8,128)}, u32[]{:S(2)}, u32[]{:S(2)}) collective-permute-start(f32[192,256]{1,0:T(8,128)} %get-tuple-element.54), channel_id=1, source_target_pairs={{0,1},{1,2},{2,3},{3,0},{4,5},{5,6},{6,7},{7,4},{8,9},{9,10},{10,1... | collective-permute-start | bytes 589832 | tf_op jit(solution)/shard_map/ppermute | solution.py:55
  7.3 16.5 %collective-permute-start.1 = (f32[192,256]{1,0:T(8,128)}, f32[192,256]{1,0:T(8,128)}, u32[]{:S(2)}, u32[]{:S(2)}) collective-permute-start(f32[192,256]{1,0:T(8,128)} %get-tuple-element.56), channel_id=1, source_target_pairs={{0,2},{1,3},{2,0},{3,1},{4,6},{5,7},{6,4},{7,5},{8,10},{9,11},{10,... | collective-permute-start | bytes 589832 | tf_op jit(solution)/shard_map/ppermute | solution.py:55
  8.3 18.3 %collective-permute-start.2 = (f32[192,256]{1,0:T(8,128)}, f32[192,256]{1,0:T(8,128)}, u32[]{:S(2)}, u32[]{:S(2)}) collective-permute-start(f32[192,256]{1,0:T(8,128)} %get-tuple-element.55), channel_id=1, source_target_pairs={{0,3},{1,0},{2,1},{3,2},{4,7},{5,4},{6,5},{7,6},{8,11},{9,8},{10,9... | collective-permute-start | bytes 589832 | tf_op jit(solution)/shard_map/ppermute | solution.py:55
  15.9 5.2 %copy-start.31 = (f32[256,1,8]{2,0,1:T(8,128)S(1)}, f32[256,1,8]{2,0,1:T(8,128)}, u32[]{:S(2)}) copy-start(f32[256,1,8]{2,0,1:T(8,128)} %get-tuple-element.170) | copy-start | bytes 24580
  15.9 5.3 %copy-start.33 = (f32[256,1,8]{2,0,1:T(8,128)S(1)}, f32[256,1,8]{2,0,1:T(8,128)}, u32[]{:S(2)}) copy-start(f32[256,1,8]{2,0,1:T(8,128)} %get-tuple-element.311) | copy-start | bytes 24580
  15.9 5.4 %copy-start.32 = (f32[256,1,8]{2,0,1:T(8,128)S(1)}, f32[256,1,8]{2,0,1:T(8,128)}, u32[]{:S(2)}) copy-start(f32[256,1,8]{2,0,1:T(8,128)} %get-tuple-element.164) | copy-start | bytes 24580
  22.2 11.8 %copy-start.37 = (f32[256,7,8]{0,2,1:T(8,128)}, f32[256,7,8]{0,2,1:T(8,128)S(1)}, u32[]{:S(2)}) copy-start(f32[256,7,8]{0,2,1:T(8,128)S(1)} %constant_dynamic-update-slice_fusion.7) | copy-start | bytes 172036
  22.3 11.7 %copy-start.36 = (f32[256,7,8]{0,2,1:T(8,128)}, f32[256,7,8]{0,2,1:T(8,128)S(1)}, u32[]{:S(2)}) copy-start(f32[256,7,8]{0,2,1:T(8,128)S(1)} %constant_dynamic-update-slice_fusion) | copy-start | bytes 172036
  27.9 18.4 %copy-start.19 = (f32[256,3,256]{2,0,1:T(8,128)S(1)}, f32[256,3,256]{2,0,1:T(8,128)}, u32[]{:S(2)}) copy-start(f32[256,3,256]{2,0,1:T(8,128)} %param.10) | copy-start | bytes 2359300
  27.9 6.0 %collective-permute-start.3 = (f32[192,256]{1,0:T(8,128)S(1)}, f32[192,256]{1,0:T(8,128)S(1)}, u32[]{:S(2)}, u32[]{:S(2)}) collective-permute-start(f32[192,256]{1,0:T(8,128)S(1)} %fusion.46), channel_id=1, source_target_pairs={{0,1},{1,2},{2,3},{3,0},{4,5},{5,6},{6,7},{7,4},{8,9},{9,10},{10,1... | collective-permute-start | bytes 589832 | tf_op jit(solution)/shard_map/ppermute | solution.py:66
  28.0 16.7 %collective-permute-start.4 = (f32[192,256]{1,0:T(8,128)S(1)}, f32[192,256]{1,0:T(8,128)S(1)}, u32[]{:S(2)}, u32[]{:S(2)}) collective-permute-start(f32[192,256]{1,0:T(8,128)S(1)} %fusion.46), channel_id=1, source_target_pairs={{0,2},{1,3},{2,0},{3,1},{4,6},{5,7},{6,4},{7,5},{8,10},{9,11},{10,... | collective-permute-start | bytes 589832 | tf_op jit(solution)/shard_map/ppermute | solution.py:66
  28.4 17.9 %collective-permute-start.5 = (f32[192,256]{1,0:T(8,128)S(1)}, f32[192,256]{1,0:T(8,128)S(1)}, u32[]{:S(2)}, u32[]{:S(2)}) collective-permute-start(f32[192,256]{1,0:T(8,128)S(1)} %fusion.46), channel_id=1, source_target_pairs={{0,3},{1,0},{2,1},{3,2},{4,7},{5,4},{6,5},{7,6},{8,11},{9,8},{10,9... | collective-permute-start | bytes 589832 | tf_op jit(solution)/shard_map/ppermute | solution.py:66
  64.3 14.6 %collective-permute-start.6 = (f32[256,10,8]{0,2,1:T(8,128)}, f32[256,10,8]{0,2,1:T(8,128)}, u32[]{:S(2)}, u32[]{:S(2)}) collective-permute-start(f32[256,10,8]{0,2,1:T(8,128)} %pad_maximum_fusion.13), channel_id=1, source_target_pairs={{0,4},{4,8},{8,12},{12,16},{16,20},{20,24},{24,28},{28,0},{1,5},{5... | collective-permute-start | bytes 245768 | tf_op jit(solution)/shard_map/ppermute | solution.py:16
  72.0 11.9 %collective-permute-start.7 = (f32[256,10,8]{0,2,1:T(8,128)}, f32[256,10,8]{0,2,1:T(8,128)}, u32[]{:S(2)}, u32[]{:S(2)}) collective-permute-start(f32[256,10,8]{0,2,1:T(8,128)} %pad_maximum_fusion.14), channel_id=1, source_target_pairs={{4,0},{8,4},{12,8},{16,12},{20,16},{24,20},{28,24},{0,28},{5,1},{9... | collective-permute-start | bytes 245768 | tf_op jit(solution)/shard_map/ppermute | solution.py:17
  77.2 3.7 %copy-start.38 = (f32[256,16]{0,1:T(8,128)S(1)}, f32[256,16]{0,1:T(8,128)}, u32[]{:S(2)}) copy-start(f32[256,16]{0,1:T(8,128)} %copy.398) | copy-start | bytes 49156
  91.3 4.1 %copy-start.49 = (f32[256,1,8]{0,2,1:T(8,128)S(1)}, f32[256,1,8]{0,2,1:T(8,128)}, u32[]{:S(2)}) copy-start(f32[256,1,8]{0,2,1:T(8,128)} %get-tuple-element.290) | copy-start | bytes 24580
  91.3 4.2 %copy-start.48 = (f32[256,1,8]{0,2,1:T(8,128)S(1)}, f32[256,1,8]{0,2,1:T(8,128)}, u32[]{:S(2)}) copy-start(f32[256,1,8]{0,2,1:T(8,128)} %get-tuple-element.289) | copy-start | bytes 24580
  98.2 3.6 %copy-start.41 = (f32[256,1,8]{0,2,1:T(8,128)S(1)}, f32[256,1,8]{0,2,1:T(8,128)}, u32[]{:S(2)}) copy-start(f32[256,1,8]{0,2,1:T(8,128)} %get-tuple-element.291) | copy-start | bytes 24580
  105.1 4.7 %copy-start.44 = (f32[256,1,8]{0,2,1:T(8,128)S(1)}, f32[256,1,8]{0,2,1:T(8,128)}, u32[]{:S(2)}) copy-start(f32[256,1,8]{0,2,1:T(8,128)} %get-tuple-element.298) | copy-start | bytes 24580
  105.9 4.1 %copy-start.43 = (f32[256,1,8]{0,2,1:T(8,128)S(1)}, f32[256,1,8]{0,2,1:T(8,128)}, u32[]{:S(2)}) copy-start(f32[256,1,8]{0,2,1:T(8,128)} %get-tuple-element.306) | copy-start | bytes 24580
  110.1 3.6 %copy-start.40 = (f32[256,1,8]{0,2,1:T(8,128)S(1)}, f32[256,1,8]{0,2,1:T(8,128)}, u32[]{:S(2)}) copy-start(f32[256,1,8]{0,2,1:T(8,128)} %get-tuple-element.297) | copy-start | bytes 24580
  110.1 3.7 %copy-start.39 = (f32[256,1,8]{0,2,1:T(8,128)S(1)}, f32[256,1,8]{0,2,1:T(8,128)}, u32[]{:S(2)}) copy-start(f32[256,1,8]{0,2,1:T(8,128)} %get-tuple-element.301) | copy-start | bytes 24580
  (36 other events, 58.9 us)

commit v8 on v7

--- a/solution.py
+++ b/solution.py
@@ -18,26 +18,22 @@
     return before, after
 
 
-def col_slope(f):
-    return 0.5 * (jnp.roll(f, -1, 0) - jnp.roll(f, 1, 0))
+def slope(f, axis):
+    return 0.5 * (jnp.roll(f, -1, axis) - jnp.roll(f, 1, axis))
 
 
-def row_slope(f):
-    return 0.5 * (jnp.roll(f, -1, 1) - jnp.roll(f, 1, 1))
-
-
-def dynamics(h, u, v, dep, prec, meas):
+def dynamics(h, u, v, dep, prec, meas, col=0, row=1):
     for _ in range(STEPS):
-        h = h - COURANT * dep * (col_slope(u) + row_slope(v))
-        u = u - COURANT * col_slope(h)
-        v = v - COURANT * row_slope(h)
+        h = h - COURANT * dep * (slope(u, col) + slope(v, row))
+        u = u - COURANT * slope(h, col)
+        v = v - COURANT * slope(h, row)
     pred = (h, u, v)
     a, p, q = (prec[i] * (pred[i] - meas[i]) for i in range(3))
     for _ in range(STEPS):
-        e = a + COURANT * (col_slope(p) + row_slope(q))
+        e = a + COURANT * (slope(p, col) + slope(q, row))
         w = dep * e
-        p = p + COURANT * col_slope(w)
-        q = q + COURANT * row_slope(w)
+        p = p + COURANT * slope(w, col)
+        q = q + COURANT * slope(w, row)
         a = e
     return pred, (a, p, q)
 
@@ -108,35 +104,34 @@
     prec = [precision_factor[:, i] for i in range(nfield)]
     fixed = meas + prec + [depth]
 
-    def edges(planes, part):
-        return jnp.stack([p[:, part] for p in planes], axis=1)
+    def ends(planes):
+        return (jnp.stack([p[:, : 2 * HALO] for p in planes]).transpose(0, 2, 1),
+                jnp.stack([p[:, nrow - 2 * HALO:] for p in planes]).transpose(0, 2, 1))
 
-    lo, hi = slice(0, HALO), slice(nrow - HALO, nrow)
-    scattered, fixed_lo, fixed_hi = lax.optimization_barrier(
-        (scattered, edges(fixed, lo), edges(fixed, hi)))
+    scattered, fixed_lo, fixed_hi = lax.optimization_barrier((scattered,) + ends(fixed))
     incr = member_gather(*scattered).reshape(nfield, ncol, nrow)
     state = [background[:, i] + incr[i] for i in range(nfield)]
-
-    before, after = shift_rows(None, (
-        jnp.concatenate([edges(state, lo), fixed_lo], axis=1),
-        jnp.concatenate([edges(state, hi), fixed_hi], axis=1)))
-    planes = state + fixed
+    state_lo, state_hi = ends(state)
+    own_lo = jnp.concatenate([state_lo, fixed_lo], axis=0)
+    own_hi = jnp.concatenate([state_hi, fixed_hi], axis=0)
+    before, after = shift_rows(None, (own_lo[:, :HALO], own_hi[:, HALO:]))
 
     pred, adj = dynamics(*state, depth, prec, meas)
 
-    def strip(pieces):
-        s = [jnp.concatenate(p, axis=1) for p in pieces]
-        return dynamics(*s[:nfield], s[-1], s[2 * nfield:3 * nfield], s[nfield:2 * nfield])
+    def strip(s):
+        return dynamics(*s[:nfield], s[-1], s[2 * nfield:3 * nfield], s[nfield:2 * nfield],
+                        col=1, row=0)
 
-    first = strip([(before[:, i], p[:, : 2 * HALO]) for i, p in enumerate(planes)])
-    last = strip([(p[:, nrow - 2 * HALO:], after[:, i]) for i, p in enumerate(planes)])
+    first = strip(jnp.concatenate([before, own_lo], axis=1))
+    last = strip(jnp.concatenate([own_hi, after], axis=1))
     mid = slice(HALO, 2 * HALO)
     inner = slice(HALO, nrow - HALO)
 
     def assemble(k):
-        return jnp.stack([
-            jnp.concatenate([first[k][i][:, mid], f[:, inner], last[k][i][:, mid]], axis=1)
-            for i, f in enumerate((pred, adj)[k])], axis=1)
+        lo = jnp.stack([f[mid] for f in first[k]]).transpose(2, 0, 1)
+        hi = jnp.stack([f[mid] for f in last[k]]).transpose(2, 0, 1)
+        block = jnp.stack([f[:, inner] for f in (pred, adj)[k]], axis=1)
+        return jnp.concatenate([lo, block, hi], axis=2)
 
     predicted_final = lax.dynamic_slice_in_dim(assemble(0), col_start, block_cols, 0)
     projected = jnp.sum(ens * assemble(1)[None], axis=2)

time: 128 us -> 103 us (0.80)
  other arithmetic: 29.1 us -> 13.6 us
  local copies, waits for them, and re-layouts: 61.5 us -> 54.6 us
  waiting for transfers between devices: 20.7 us -> 16.8 us
  starting transfers between devices: 7.18 us -> 9.62 us
    slice x111 -> x99, local copies, waits for them, and re-layouts: 30 us -> 7.38 us  [the longest x98 6.63 us: slope(): return 0.5 * (jnp.roll(f, -1, axis) - jnp.roll(f, 1, axis))]
    another operation x27 -> x45, local copies, waits for them, and re-layouts: 19 us -> 32.2 us  [the longest x17 15.8 us: ends(): jnp.stack([p[:, nrow - 2 * HALO:] for p in planes]).transpose(0, 2, 1)]
    mul x5 -> x3, other arithmetic: 8.49 us -> 1.09 us  [dynamics(): a, p, q = (prec[i] * (pred[i] - meas[i]) for i in range(3))]
    add x12 -> x6, other arithmetic: 4.8 us -> 0.43 us  [the longest x3 0.22 us: dynamics(): p = p + COURANT * slope(w, col)]
    ppermute x3, waiting for transfers between devices: 4.34 us -> 0.01 us  [member_scatter(): acc = acc + lax.ppermute(sent, 'member', shift)]
    mul x6, other arithmetic: 4.27 us -> 1.48 us  [dynamics(): w = dep * e]
    unnamed x140 -> x74, local copies, waits for them, and re-layouts: 11.2 us -> 13.3 us
    sub x12 -> x10, other arithmetic: 2.91 us -> 1.18 us  [the longest x6 0.77 us: dynamics(): h = h - COURANT * dep * (slope(u, col) + slope(v, row))]
  transfers between devices with their start and end apart: 8 -> 8, of which waited for: 5 -> 3; matrix products, arithmetic and copies ran while one was open for 24% -> 36% of each run, Pallas kernels for 0% -> 0%
where the time goes in v8:
time: 103 us; the launch traced here: 101 us
  local copies, waits for them, and re-layouts  54.6 us (53%)
  waiting for transfers between devices  16.8 us (16%)
  other arithmetic  13.6 us (13%)
  starting transfers between devices  9.62 us (9%)
  matrix products  5.16 us (5%)
  between operations  1.65 us (2%)
    ppermute x3, waiting for transfers between devices, member_gather(): got = lax.ppermute(acc, 'member', shift)  16.8 us
    another operation x17, local copies, waits for them, and re-layouts, ends(): jnp.stack([p[:, nrow - 2 * HALO:] for p in planes]).transpose(0, 2, 1)  15.8 us
    unnamed x74, local copies, waits for them, and re-layouts  13.3 us
    another operation x10, local copies, waits for them, and re-layouts, ends(): jnp.stack([p[:, :2 * HALO] for p in planes]).transpose(0, 2, 1)  12.4 us
    slice x98, local copies, waits for them, and re-layouts, slope(): return 0.5 * (jnp.roll(f, -1, axis) - jnp.roll(f, 1, axis))  6.63 us
    ppermute x3, starting transfers between devices, member_scatter(): acc = acc + lax.ppermute(sent, 'member', shift)  3.77 us
    ppermute x3, starting transfers between devices, member_gather(): got = lax.ppermute(acc, 'member', shift)  3.2 us
    another operation x4, local copies, waits for them, and re-layouts, assemble(): block = jnp.stack([f[:, inner] for f in (pred, adj)[k]], axis=1)  2.62 us
  transfers between devices with their start and end apart: 8, of which 3 were waited for; matrix products, arithmetic and copies ran while one was open for 36% of the time, Pallas kernels for 0%

profile of v8, /device:TPU:11, one launch (start us, length us, event | category | flops | bytes accessed | tf_op | source)
XLA Modules:
  0.0 101.4 jit_solution(7894674182071900118)
XLA Ops:
  0.7 2.1 %fusion.8 = f32[3,256,256]{2,1,0:T(8,128)S(1)} fusion(f32[3,256,256]{2,1,0:T(8,128)} %param.8, f32[256,256]{1,0:T(8,128)} %param.14), kind=kOutput, calls=%fused_computation.17 | convolution fusion | flops 603979776 | bytes 1835008 | tf_op jit(solution)/shard_map/dot_general | solution.py:97
  6.0 1.3 %collective-permute-start = (f32[192,256]{1,0:T(8,128)}, f32[192,256]{1,0:T(8,128)}, u32[]{:S(2)}, u32[]{:S(2)}) collective-permute-start(f32[192,256]{1,0:T(8,128)} %get-tuple-element.50), channel_id=1, source_target_pairs={{0,1},{1,2},{2,3},{3,0},{4,5},{5,6},{6,7},{7,4},{8,9},{9,10},{10,1... | collective-permute-start | bytes 589832 | tf_op jit(solution)/shard_map/ppermute | solution.py:51
  8.3 1.5 %collective-permute-start.2 = (f32[192,256]{1,0:T(8,128)}, f32[192,256]{1,0:T(8,128)}, u32[]{:S(2)}, u32[]{:S(2)}) collective-permute-start(f32[192,256]{1,0:T(8,128)} %get-tuple-element.51), channel_id=1, source_target_pairs={{0,3},{1,0},{2,1},{3,2},{4,7},{5,4},{6,5},{7,6},{8,11},{9,8},{10,9... | collective-permute-start | bytes 589832 | tf_op jit(solution)/shard_map/ppermute | solution.py:51
  15.4 1.6 %copy.41 = f32[1,256,16]{1,2,0:T(8,128)} copy(f32[1,256,16]{2,1,0:T(8,128)} %get-tuple-element.129) | data formatting | bytes 32768 | tf_op jit(solution)/shard_map/stack | solution.py:109
  17.0 1.8 %slice_bitcast_fusion.19 = (f32[1,256,16]{2,1,0:T(8,128)}, f32[1,256,16]{2,1,0:T(8,128)}, f32[1,256,16]{2,1,0:T(8,128)}, f32[1,256,16]{2,1,0:T(8,128)}) fusion(f32[256,256]{1,0:T(8,128)S(1)} %get-tuple-element.44, f32[256,256]{1,0:T(8,128)} %get-tuple-element.46), kind=kLoop, calls=%fused_computation.111 | loop fusion | bytes 131072 | tf_op jit(solution)/shard_map/stack | solution.py:109
  18.8 1.6 %copy.42 = f32[1,256,16]{1,2,0:T(8,128)} copy(f32[1,256,16]{2,1,0:T(8,128)} %get-tuple-element.272) | data formatting | bytes 32768 | tf_op jit(solution)/shard_map/stack | solution.py:109
  20.4 1.6 %copy.43 = f32[1,256,16]{1,2,0:T(8,128)} copy(f32[1,256,16]{2,1,0:T(8,128)} %get-tuple-element.125) | data formatting | bytes 32768 | tf_op jit(solution)/shard_map/stack | solution.py:109
  22.7 1.6 %copy.59 = f32[256,16]{0,1:T(8,128)} copy(f32[256,16]{1,0:T(8,128)} %get-tuple-element.123) | data formatting | bytes 32768
  24.3 1.6 %copy.32 = f32[1,256,16]{1,2,0:T(8,128)} copy(f32[1,256,16]{2,1,0:T(8,128)} %get-tuple-element.269) | data formatting | bytes 32768 | tf_op jit(solution)/shard_map/stack | solution.py:108
  27.3 1.6 %copy.33 = f32[1,256,16]{1,2,0:T(8,128)} copy(f32[1,256,16]{2,1,0:T(8,128)} %get-tuple-element.132) | data formatting | bytes 32768 | tf_op jit(solution)/shard_map/stack | solution.py:108
  28.8 1.6 %copy.34 = f32[1,256,16]{1,2,0:T(8,128)} copy(f32[1,256,16]{2,1,0:T(8,128)} %get-tuple-element.130) | data formatting | bytes 32768 | tf_op jit(solution)/shard_map/stack | solution.py:108
  30.4 1.6 %copy.35 = f32[1,256,16]{1,2,0:T(8,128)} copy(f32[1,256,16]{2,1,0:T(8,128)} %get-tuple-element.271) | data formatting | bytes 32768 | tf_op jit(solution)/shard_map/stack | solution.py:108
  32.0 1.6 %copy.36 = f32[1,256,16]{1,2,0:T(8,128)} copy(f32[1,256,16]{2,1,0:T(8,128)} %get-tuple-element.126) | data formatting | bytes 32768 | tf_op jit(solution)/shard_map/stack | solution.py:108
  41.1 1.3 %fusion.50 = f32[192,256]{1,0:T(8,128)S(1)} fusion(f32[192,256]{1,0:T(8,128)} %collective-permute-done.2, f32[192,256]{1,0:T(8,128)} %collective-permute-done.1, f32[192,256]{1,0:T(8,128)} %collective-permute-done, f32[4,192,256]{2,1,0:T(8,128)} %bitcast.293, s32[]{:T(128)S(6)} %select_n.42), kind=kLoop, calls=%fused_computation.101 | loop fusion | flops 147456 | bytes 983044 | tf_op jit(solution)/shard_map/add | solution.py:51
  42.4 3.1 %collective-permute-start.4 = (f32[192,256]{1,0:T(8,128)S(1)}, f32[192,256]{1,0:T(8,128)S(1)}, u32[]{:S(2)}, u32[]{:S(2)}) collective-permute-start(f32[192,256]{1,0:T(8,128)S(1)} %fusion.50), channel_id=1, source_target_pairs={{0,2},{1,3},{2,0},{3,1},{4,6},{5,7},{6,4},{7,5},{8,10},{9,11},{10,... | collective-permute-start | bytes 589832 | tf_op jit(solution)/shard_map/ppermute | solution.py:62
  45.7 1.6 %collective-permute-done.3 = f32[192,256]{1,0:T(8,128)S(1)} collective-permute-done((f32[192,256]{1,0:T(8,128)S(1)}, f32[192,256]{1,0:T(8,128)S(1)}, u32[]{:S(2)}, u32[]{:S(2)}) %collective-permute-start.3) | collective-permute-done | bytes 196640 | tf_op jit(solution)/shard_map/ppermute | solution.py:62
  47.3 11.4 %collective-permute-done.4 = f32[192,256]{1,0:T(8,128)S(1)} collective-permute-done((f32[192,256]{1,0:T(8,128)S(1)}, f32[192,256]{1,0:T(8,128)S(1)}, u32[]{:S(2)}, u32[]{:S(2)}) %collective-permute-start.4) | collective-permute-done | bytes 196640 | tf_op jit(solution)/shard_map/ppermute | solution.py:62
  58.8 3.8 %collective-permute-done.5 = f32[192,256]{1,0:T(8,128)S(1)} collective-permute-done((f32[192,256]{1,0:T(8,128)S(1)}, f32[192,256]{1,0:T(8,128)S(1)}, u32[]{:S(2)}, u32[]{:S(2)}) %collective-permute-start.5) | collective-permute-done | bytes 196640 | tf_op jit(solution)/shard_map/ppermute | solution.py:62
  74.6 1.6 %copy.46 = f32[1,256,16]{1,2,0:T(8,128)} copy(f32[1,256,16]{2,1,0:T(8,128)} %get-tuple-element.113) | data formatting | bytes 32768 | tf_op jit(solution)/shard_map/stack | solution.py:109
  76.2 1.6 %copy.47 = f32[1,256,16]{1,2,0:T(8,128)} copy(f32[1,256,16]{2,1,0:T(8,128)} %get-tuple-element.110) | data formatting | bytes 32768 | tf_op jit(solution)/shard_map/stack | solution.py:108
  78.5 1.6 %copy.49 = f32[1,256,16]{1,2,0:T(8,128)} copy(f32[1,256,16]{2,1,0:T(8,128)} %get-tuple-element.114) | data formatting | bytes 32768 | tf_op jit(solution)/shard_map/stack | solution.py:108
  84.4 1.6 %collective-permute-start.6 = (f32[10,8,256]{2,1,0:T(8,128)S(1)}, f32[10,8,256]{2,1,0:T(8,128)S(1)}, u32[]{:S(2)}, u32[]{:S(2)}) collective-permute-start(f32[10,8,256]{2,1,0:T(8,128)S(1)} %pad_maximum_fusion.7), channel_id=1, source_target_pairs={{0,4},{4,8},{8,12},{12,16},{16,20},{20,24},{24,28},{28,0},{1,5},{5... | collective-permute-start | bytes 245768 | tf_op jit(solution)/shard_map/ppermute | solution.py:16
  95.5 1.3 %pad_maximum_fusion = f32[256,3,256]{2,0,1:T(8,128)S(1)} fusion(f32[256,3,8]{2,0,1:T(8,128)S(1)} %bitcast.297, f32[256,1,240]{2,0,1:T(8,128)S(1)} %fusion.10, f32[256,1,240]{2,0,1:T(8,128)} %fusion.13, f32[256,1,240]{2,0,1:T(8,128)S(1)} %slice_bitcast_fusion.3, f32[256,3,8]{2,0,1:T(8,128)S(1)} %bitcast.296), kind=kLoop, calls=%fused_computation.6 | loop fusion | flops 786432 | bytes 1572864 | tf_op jit(solution)/shard_map/concatenate | solution.py:134
  97.1 1.4 %fusion.3 = f32[3,256,256]{1,2,0:T(8,128)S(1)} fusion(f32[3,256,256]{2,1,0:T(8,128)S(1)} %fusion.1, f32[256,256]{1,0:T(8,128)S(1)} %copy-done), kind=kOutput, calls=%fused_computation.12 | convolution fusion | flops 603979776 | bytes 1835008 | tf_op jit(solution)/shard_map/dot_general | solution.py:138
  (269 shorter events, 48.6 us)
Async XLA Ops:
  4.3 5.5 %copy-start.3 = (f32[3,256,256]{2,1,0:T(8,128)S(1)}, f32[3,256,256]{2,1,0:T(8,128)}, u32[]{:S(2)}) copy-start(f32[3,256,256]{2,1,0:T(8,128)} %param.8) | copy-start | bytes 2359300
  5.2 5.7 %copy-start.4 = (f32[256,3,256]{2,0,1:T(8,128)S(1)}, f32[256,3,256]{2,0,1:T(8,128)}, u32[]{:S(2)}) copy-start(f32[256,3,256]{2,0,1:T(8,128)} %param.11) | copy-start | bytes 2359300
  6.0 35.0 %collective-permute-start = (f32[192,256]{1,0:T(8,128)}, f32[192,256]{1,0:T(8,128)}, u32[]{:S(2)}, u32[]{:S(2)}) collective-permute-start(f32[192,256]{1,0:T(8,128)} %get-tuple-element.50), channel_id=1, source_target_pairs={{0,1},{1,2},{2,3},{3,0},{4,5},{5,6},{6,7},{7,4},{8,9},{9,10},{10,1... | collective-permute-start | bytes 589832 | tf_op jit(solution)/shard_map/ppermute | solution.py:51
  7.3 33.7 %collective-permute-start.1 = (f32[192,256]{1,0:T(8,128)}, f32[192,256]{1,0:T(8,128)}, u32[]{:S(2)}, u32[]{:S(2)}) collective-permute-start(f32[192,256]{1,0:T(8,128)} %get-tuple-element.52), channel_id=1, source_target_pairs={{0,2},{1,3},{2,0},{3,1},{4,6},{5,7},{6,4},{7,5},{8,10},{9,11},{10,... | collective-permute-start | bytes 589832 | tf_op jit(solution)/shard_map/ppermute | solution.py:51
  8.3 32.7 %collective-permute-start.2 = (f32[192,256]{1,0:T(8,128)}, f32[192,256]{1,0:T(8,128)}, u32[]{:S(2)}, u32[]{:S(2)}) collective-permute-start(f32[192,256]{1,0:T(8,128)} %get-tuple-element.51), channel_id=1, source_target_pairs={{0,3},{1,0},{2,1},{3,2},{4,7},{5,4},{6,5},{7,6},{8,11},{9,8},{10,9... | collective-permute-start | bytes 589832 | tf_op jit(solution)/shard_map/ppermute | solution.py:51
  14.6 7.4 %copy-start.1 = (f32[256,256]{1,0:T(8,128)S(1)}, f32[256,256]{1,0:T(8,128)}, u32[]{:S(2)}) copy-start(f32[256,256]{1,0:T(8,128)} %param.13) | copy-start | bytes 786436
  18.8 7.1 %copy-start.25 = (f32[1,256,16]{2,1,0:T(8,128)S(1)}, f32[1,256,16]{2,1,0:T(8,128)}, u32[]{:S(2)}) copy-start(f32[1,256,16]{2,1,0:T(8,128)} %get-tuple-element.136) | copy-start | bytes 49156
  18.8 15.7 %copy-start.16 = (f32[7,256,16]{1,2,0:T(8,128)S(1)}, f32[7,256,16]{1,2,0:T(8,128)}, u32[]{:S(2)}) copy-start(f32[7,256,16]{1,2,0:T(8,128)} %constant_dynamic-update-slice_fusion.13) | copy-start | bytes 344068
  18.8 15.7 %copy-start.26 = (f32[1,256,16]{1,2,0:T(8,128)S(1)}, f32[1,256,16]{1,2,0:T(8,128)}, u32[]{:S(2)}) copy-start(f32[1,256,16]{1,2,0:T(8,128)} %copy.40) | copy-start | bytes 49156
  37.4 8.2 %copy-start.17 = (f32[7,256,16]{1,2,0:T(8,128)}, f32[7,256,16]{1,2,0:T(8,128)S(1)}, u32[]{:S(2)}) copy-start(f32[7,256,16]{1,2,0:T(8,128)S(1)} %constant_dynamic-update-slice_fusion.7) | copy-start | bytes 344068
  41.0 6.3 %copy-start.19 = (f32[7,256,16]{1,2,0:T(8,128)}, f32[7,256,16]{1,2,0:T(8,128)S(1)}, u32[]{:S(2)}) copy-start(f32[7,256,16]{1,2,0:T(8,128)S(1)} %constant_dynamic-update-slice_fusion) | copy-start | bytes 344068
  42.4 20.2 %copy-start.15 = (f32[256,3,256]{2,0,1:T(8,128)S(1)}, f32[256,3,256]{2,0,1:T(8,128)}, u32[]{:S(2)}) copy-start(f32[256,3,256]{2,0,1:T(8,128)} %param.10) | copy-start | bytes 2359300
  42.4 4.9 %collective-permute-start.3 = (f32[192,256]{1,0:T(8,128)S(1)}, f32[192,256]{1,0:T(8,128)S(1)}, u32[]{:S(2)}, u32[]{:S(2)}) collective-permute-start(f32[192,256]{1,0:T(8,128)S(1)} %fusion.50), channel_id=1, source_target_pairs={{0,1},{1,2},{2,3},{3,0},{4,5},{5,6},{6,7},{7,4},{8,9},{9,10},{10,1... | collective-permute-start | bytes 589832 | tf_op jit(solution)/shard_map/ppermute | solution.py:62
  42.4 16.3 %collective-permute-start.4 = (f32[192,256]{1,0:T(8,128)S(1)}, f32[192,256]{1,0:T(8,128)S(1)}, u32[]{:S(2)}, u32[]{:S(2)}) collective-permute-start(f32[192,256]{1,0:T(8,128)S(1)} %fusion.50), channel_id=1, source_target_pairs={{0,2},{1,3},{2,0},{3,1},{4,6},{5,7},{6,4},{7,5},{8,10},{9,11},{10,... | collective-permute-start | bytes 589832 | tf_op jit(solution)/shard_map/ppermute | solution.py:62
  45.6 17.0 %collective-permute-start.5 = (f32[192,256]{1,0:T(8,128)S(1)}, f32[192,256]{1,0:T(8,128)S(1)}, u32[]{:S(2)}, u32[]{:S(2)}) collective-permute-start(f32[192,256]{1,0:T(8,128)S(1)} %fusion.50), channel_id=1, source_target_pairs={{0,3},{1,0},{2,1},{3,2},{4,7},{5,4},{6,5},{7,6},{8,11},{9,8},{10,9... | collective-permute-start | bytes 589832 | tf_op jit(solution)/shard_map/ppermute | solution.py:62
  70.8 3.2 %copy-start.24 = (f32[1,256,16]{2,1,0:T(8,128)S(1)}, f32[1,256,16]{2,1,0:T(8,128)}, u32[]{:S(2)}) copy-start(f32[1,256,16]{2,1,0:T(8,128)} %get-tuple-element.111) | copy-start | bytes 49156
  71.4 6.4 %copy-start.23 = (f32[1,256,16]{2,1,0:T(8,128)S(1)}, f32[1,256,16]{2,1,0:T(8,128)}, u32[]{:S(2)}) copy-start(f32[1,256,16]{2,1,0:T(8,128)} %get-tuple-element.112) | copy-start | bytes 49156
  72.3 13.7 %copy-start.9 = (f32[256,256]{1,0:T(8,128)S(1)}, f32[256,256]{1,0:T(8,128)}, u32[]{:S(2)}) copy-start(f32[256,256]{1,0:T(8,128)} %get-tuple-element.41) | copy-start | bytes 786436
  78.5 9.3 %copy-start.13 = (f32[255,256]{1,0:T(8,128)S(1)}, f32[255,256]{1,0:T(8,128)}, u32[]{:S(2)}) copy-start(f32[255,256]{1,0:T(8,128)} %get-tuple-element.56) | copy-start | bytes 783364
  80.1 7.5 %copy-start.14 = (f32[256,256]{1,0:T(8,128)S(1)}, f32[256,256]{1,0:T(8,128)}, u32[]{:S(2)}) copy-start(f32[256,256]{1,0:T(8,128)} %get-tuple-element.23) | copy-start | bytes 786436
  80.1 7.7 %copy-start.27 = (f32[1,256]{1,0:T(1,128)S(1)}, f32[1,256]{1,0:T(1,128)}, u32[]{:S(2)}) copy-start(f32[1,256]{1,0:T(1,128)} %get-tuple-element.53) | copy-start | bytes 3076
  80.1 7.7 %copy-start.28 = (f32[1,256]{1,0:T(1,128)S(1)}, f32[1,256]{1,0:T(1,128)}, u32[]{:S(2)}) copy-start(f32[1,256]{1,0:T(1,128)} %get-tuple-element.54) | copy-start | bytes 3076
  81.7 7.4 %collective-permute-start.7 = (f32[10,8,256]{2,1,0:T(8,128)S(1)}, f32[10,8,256]{2,1,0:T(8,128)S(1)}, u32[]{:S(2)}, u32[]{:S(2)}) collective-permute-start(f32[10,8,256]{2,1,0:T(8,128)S(1)} %pad_maximum_fusion.6), channel_id=1, source_target_pairs={{4,0},{8,4},{12,8},{16,12},{20,16},{24,20},{28,24},{0,28},{5,1},{9... | collective-permute-start | bytes 245768 | tf_op jit(solution)/shard_map/ppermute | solution.py:17
  84.4 5.8 %collective-permute-start.6 = (f32[10,8,256]{2,1,0:T(8,128)S(1)}, f32[10,8,256]{2,1,0:T(8,128)S(1)}, u32[]{:S(2)}, u32[]{:S(2)}) collective-permute-start(f32[10,8,256]{2,1,0:T(8,128)S(1)} %pad_maximum_fusion.7), channel_id=1, source_target_pairs={{0,4},{4,8},{8,12},{12,16},{16,20},{20,24},{24,28},{28,0},{1,5},{5... | collective-permute-start | bytes 245768 | tf_op jit(solution)/shard_map/ppermute | solution.py:16
  (13 other events, 20.0 us)

commit v9 on v8

--- a/solution.py
+++ b/solution.py
@@ -104,9 +104,13 @@
     prec = [precision_factor[:, i] for i in range(nfield)]
     fixed = meas + prec + [depth]
 
+    picked = jnp.concatenate([jnp.arange(2 * HALO), jnp.arange(nrow - 2 * HALO, nrow)])
+    select = (picked[:, None] == jnp.arange(nrow)[None, :]).astype(jnp.float32)
+
     def ends(planes):
-        return (jnp.stack([p[:, : 2 * HALO] for p in planes]).transpose(0, 2, 1),
-                jnp.stack([p[:, nrow - 2 * HALO:] for p in planes]).transpose(0, 2, 1))
+        cut = lax.dot_general(select, jnp.stack(planes), (((1,), (2,)), ((), ())),
+                              precision=highest).transpose(1, 0, 2)
+        return cut[:, : 2 * HALO], cut[:, 2 * HALO:]
 
     scattered, fixed_lo, fixed_hi = lax.optimization_barrier((scattered,) + ends(fixed))
     incr = member_gather(*scattered).reshape(nfield, ncol, nrow)
@@ -125,13 +129,17 @@
     first = strip(jnp.concatenate([before, own_lo], axis=1))
     last = strip(jnp.concatenate([own_hi, after], axis=1))
     mid = slice(HALO, 2 * HALO)
-    inner = slice(HALO, nrow - HALO)
+
+    placed = jnp.concatenate([jnp.arange(HALO), jnp.arange(nrow - HALO, nrow)])
+    place = (placed[:, None] == jnp.arange(nrow)[None, :]).astype(jnp.float32)
+    at_edge = (jnp.arange(nrow) < HALO) | (jnp.arange(nrow) >= nrow - HALO)
 
     def assemble(k):
-        lo = jnp.stack([f[mid] for f in first[k]]).transpose(2, 0, 1)
-        hi = jnp.stack([f[mid] for f in last[k]]).transpose(2, 0, 1)
-        block = jnp.stack([f[:, inner] for f in (pred, adj)[k]], axis=1)
-        return jnp.concatenate([lo, block, hi], axis=2)
+        rows = jnp.stack([jnp.concatenate([f[mid], g[mid]], axis=0)
+                          for f, g in zip(first[k], last[k])])
+        edge = lax.dot_general(rows, place, (((1,), (0,)), ((), ())), precision=highest)
+        return jnp.stack([jnp.where(at_edge, edge[i], f) for i, f in enumerate((pred, adj)[k])],
+                         axis=1)
 
     predicted_final = lax.dynamic_slice_in_dim(assemble(0), col_start, block_cols, 0)
     projected = jnp.sum(ens * assemble(1)[None], axis=2)

time: 103 us -> 68 us (0.66); the launches traced: 101 us -> 67.8 us
  local copies, waits for them, and re-layouts: 54.6 us -> 15.3 us
  waiting for transfers between devices: 16.8 us -> 26.9 us
  other arithmetic: 13.6 us -> 7.49 us
  matrix products: 5.16 us -> 9.35 us
  starting transfers between devices: 9.62 us -> 7.22 us
    another operation x43 -> x1, local copies, waits for them, and re-layouts: 32.2 us -> 0.72 us  [ends(): jnp.stack(planes)]
    ppermute x3, waiting for transfers between devices: 0.01 us -> 6.71 us  [member_scatter(): acc = acc + lax.ppermute(sent, 'member', shift)]
    unnamed x74 -> x28, local copies, waits for them, and re-layouts: 13.3 us -> 8.73 us
    dot_general x0 -> x4, matrix products: none -> 4.11 us  [the longest x2 3.06 us: ends(): lax.dot_general(select, jnp.stack(planes), (((1,), (2,)), ((), ())), prec...]
    slice x98 -> x83, local copies, waits for them, and re-layouts: 6.63 us -> 3.84 us  [slope(): return 0.5 * (jnp.roll(f, -1, axis) - jnp.roll(f, 1, axis))]
    ppermute x1, waiting for transfers between devices: 0.01 us -> 2.33 us  [shift_rows(): after = lax.ppermute(lo, 'tile', down)]
    concatenate x2, other arithmetic: 2.15 us -> 0.16 us  [the longest x1 0.08 us: body(): jnp.concatenate([jnp.arange(2 * HALO), jnp.arange(nrow - 2 * HALO, nrow)])]
    select_n x0 -> x4, other arithmetic: none -> 1.57 us  [assemble(): jnp.where(at_edge, edge[i], f)]
  transfers between devices with their start and end apart: 8 -> 8, of which waited for: 3 -> 7; matrix products, arithmetic and copies ran while one was open for 36% -> 16% of each run, Pallas kernels for 0% -> 0%
where the time goes in v9:
time: 68 us; the launch traced here: 67.8 us
  waiting for transfers between devices  26.9 us (40%)
  local copies, waits for them, and re-layouts  15.3 us (22%)
  matrix products  9.35 us (14%)
  other arithmetic  7.49 us (11%)
  starting transfers between devices  7.22 us (11%)
  between operations  1.51 us (2%)
    ppermute x3, waiting for transfers between devices, member_gather(): got = lax.ppermute(acc, 'member', shift)  16.4 us
    unnamed x28, local copies, waits for them, and re-layouts  8.73 us
    ppermute x3, waiting for transfers between devices, member_scatter(): acc = acc + lax.ppermute(sent, 'member', shift)  6.71 us
    slice x83, local copies, waits for them, and re-layouts, slope(): return 0.5 * (jnp.roll(f, -1, axis) - jnp.roll(f, 1, axis))  3.84 us
    ppermute x3, starting transfers between devices, member_scatter(): acc = acc + lax.ppermute(sent, 'member', shift)  3.77 us
    dot_general x2, matrix products, ends(): lax.dot_general(select, jnp.stack(planes), (((1,), (2,)), ((), ())), prec...  3.06 us
    ppermute x1, waiting for transfers between devices, shift_rows(): after = lax.ppermute(lo, 'tile', down)  2.33 us
    dot_general x1, matrix products, body(): localized = lax.dot_general(cols_b, alpha, batched(2, 1), precision=highest)  2.13 us
  transfers between devices with their start and end apart: 8, of which 7 were waited for; matrix products, arithmetic and copies ran while one was open for 16% of the time, Pallas kernels for 0%

profile of v9, /device:TPU:11, one launch (start us, length us, event | category | flops | bytes accessed | tf_op | source)
XLA Modules:
  0.0 67.8 jit_solution(2400541814904294342)
XLA Ops:
  0.7 2.1 %fusion.13 = f32[3,256,256]{2,1,0:T(8,128)S(1)} fusion(f32[3,256,256]{2,1,0:T(8,128)} %param.8, f32[256,256]{1,0:T(8,128)} %param.14), kind=kOutput, calls=%fused_computation.22 | convolution fusion | flops 603979776 | bytes 1835008 | tf_op jit(solution)/shard_map/dot_general | solution.py:97
  2.8 0.8 %fusion.10 = f32[3,256,256]{2,1,0:T(8,128)S(1)} fusion(f32[3,256,256]{2,1,0:T(8,128)S(1)} %fusion.13, f32[256,256]{1,0:T(8,128)S(1)} %copy-done), kind=kOutput, calls=%fused_computation.19 | convolution fusion | flops 603979776 | bytes 1835008 | tf_op jit(solution)/shard_map/dot_general | solution.py:98
  4.0 0.9 %copy-done.6 = f32[256,3,256]{2,0,1:T(8,128)} copy-done((f32[256,3,256]{2,0,1:T(8,128)}, f32[256,3,256]{2,0,1:T(8,128)S(1)}, u32[]{:S(2)}) %copy-start.6) | copy-done | bytes 786456
  4.9 0.8 %dynamic-slice_bitcast_fusion.2 = (f32[192,256]{1,0:T(8,128)}, f32[192,256]{1,0:T(8,128)}, f32[192,256]{1,0:T(8,128)}) fusion(f32[4,192,256]{2,1,0:T(8,128)S(1)} %bitcast.348, s32[]{:T(128)S(6)} %select_n.67, s32[]{:T(128)S(6)} %select_n.71, s32[]{:T(128)S(6)} %select_n.69), kind=kLoop, calls=%fused_computation.140 | loop fusion | bytes 1179660 | tf_op jit(solution)/shard_map/jit(dynamic_index_in_dim)/squeeze | solution.py:50
  5.7 1.3 %collective-permute-start = (f32[192,256]{1,0:T(8,128)}, f32[192,256]{1,0:T(8,128)}, u32[]{:S(2)}, u32[]{:S(2)}) collective-permute-start(f32[192,256]{1,0:T(8,128)} %get-tuple-element.43), channel_id=1, source_target_pairs={{0,1},{1,2},{2,3},{3,0},{4,5},{5,6},{6,7},{7,4},{8,9},{9,10},{10,1... | collective-permute-start | bytes 589832 | tf_op jit(solution)/shard_map/ppermute | solution.py:51
  7.0 1.0 %collective-permute-start.1 = (f32[192,256]{1,0:T(8,128)}, f32[192,256]{1,0:T(8,128)}, u32[]{:S(2)}, u32[]{:S(2)}) collective-permute-start(f32[192,256]{1,0:T(8,128)} %get-tuple-element.45), channel_id=1, source_target_pairs={{0,2},{1,3},{2,0},{3,1},{4,6},{5,7},{6,4},{7,5},{8,10},{9,11},{10,... | collective-permute-start | bytes 589832 | tf_op jit(solution)/shard_map/ppermute | solution.py:51
  8.0 1.5 %collective-permute-start.2 = (f32[192,256]{1,0:T(8,128)}, f32[192,256]{1,0:T(8,128)}, u32[]{:S(2)}, u32[]{:S(2)}) collective-permute-start(f32[192,256]{1,0:T(8,128)} %get-tuple-element.44), channel_id=1, source_target_pairs={{0,3},{1,0},{2,1},{3,2},{4,7},{5,4},{6,5},{7,6},{8,11},{9,8},{10,9... | collective-permute-start | bytes 589832 | tf_op jit(solution)/shard_map/ppermute | solution.py:51
  9.5 2.3 %copy.10 = f32[3,256,256]{1,2,0:T(8,128)} copy(f32[3,256,256]{2,1,0:T(8,128)} %param.8) | data formatting | bytes 1572864 | tf_op args[0]
  14.0 0.7 %bitcast_dynamic-update-slice_fusion.3 = f32[7,256,256]{2,1,0:T(8,128)} fusion(f32[7,256,256]{2,1,0:T(8,128)} %bitcast_dynamic-update-slice_fusion.4, f32[256,3,256]{2,0,1:T(8,128)S(1)} %copy-done.4), kind=kLoop, calls=%fused_computation.122 | loop fusion | bytes 524288
  17.0 2.5 %convolution_bitcast_fusion.1 = f32[7,32,256]{2,1,0:T(8,128)S(1)} fusion(f32[7,256,256]{2,1,0:T(8,128)} %bitcast_dynamic-update-slice_fusion, s32[32]{0:T(128)S(1)} %pad_add_fusion), kind=kOutput, calls=%fused_computation.6 | convolution fusion | flops 176168960 | bytes 2064512 | tf_op jit(solution)/shard_map/dot_general | solution.py:111
  19.6 3.9 %collective-permute-done.1 = f32[192,256]{1,0:T(8,128)} collective-permute-done((f32[192,256]{1,0:T(8,128)}, f32[192,256]{1,0:T(8,128)}, u32[]{:S(2)}, u32[]{:S(2)}) %collective-permute-start.1) | collective-permute-done | bytes 196640 | tf_op jit(solution)/shard_map/ppermute | solution.py:51
  23.5 2.8 %collective-permute-done.2 = f32[192,256]{1,0:T(8,128)} collective-permute-done((f32[192,256]{1,0:T(8,128)}, f32[192,256]{1,0:T(8,128)}, u32[]{:S(2)}, u32[]{:S(2)}) %collective-permute-start.2) | collective-permute-done | bytes 196640 | tf_op jit(solution)/shard_map/ppermute | solution.py:51
  26.4 1.3 %fusion.73 = f32[192,256]{1,0:T(8,128)S(1)} fusion(f32[192,256]{1,0:T(8,128)} %collective-permute-done.2, f32[192,256]{1,0:T(8,128)} %collective-permute-done.1, f32[192,256]{1,0:T(8,128)} %collective-permute-done, f32[4,192,256]{2,1,0:T(8,128)} %bitcast.349, s32[]{:T(128)S(6)} %select_n.65), kind=kLoop, calls=%fused_computation.137 | loop fusion | flops 147456 | bytes 983044 | tf_op jit(solution)/shard_map/add | solution.py:51
  28.1 1.4 %collective-permute-start.5 = (f32[192,256]{1,0:T(8,128)S(1)}, f32[192,256]{1,0:T(8,128)S(1)}, u32[]{:S(2)}, u32[]{:S(2)}) collective-permute-start(f32[192,256]{1,0:T(8,128)S(1)} %fusion.73), channel_id=1, source_target_pairs={{0,3},{1,0},{2,1},{3,2},{4,7},{5,4},{6,5},{7,6},{8,11},{9,8},{10,9... | collective-permute-start | bytes 589832 | tf_op jit(solution)/shard_map/ppermute | solution.py:62
  29.5 4.1 %collective-permute-done.3 = f32[192,256]{1,0:T(8,128)S(1)} collective-permute-done((f32[192,256]{1,0:T(8,128)S(1)}, f32[192,256]{1,0:T(8,128)S(1)}, u32[]{:S(2)}, u32[]{:S(2)}) %collective-permute-start.3) | collective-permute-done | bytes 196640 | tf_op jit(solution)/shard_map/ppermute | solution.py:62
  33.7 10.7 %collective-permute-done.4 = f32[192,256]{1,0:T(8,128)S(1)} collective-permute-done((f32[192,256]{1,0:T(8,128)S(1)}, f32[192,256]{1,0:T(8,128)S(1)}, u32[]{:S(2)}, u32[]{:S(2)}) %collective-permute-start.4) | collective-permute-done | bytes 196640 | tf_op jit(solution)/shard_map/ppermute | solution.py:62
  44.4 1.5 %collective-permute-done.5 = f32[192,256]{1,0:T(8,128)S(1)} collective-permute-done((f32[192,256]{1,0:T(8,128)S(1)}, f32[192,256]{1,0:T(8,128)S(1)}, u32[]{:S(2)}, u32[]{:S(2)}) %collective-permute-start.5) | collective-permute-done | bytes 196640 | tf_op jit(solution)/shard_map/ppermute | solution.py:62
  48.1 1.6 %collective-permute-start.6 = (f32[10,8,256]{2,1,0:T(8,128)S(1)}, f32[10,8,256]{2,1,0:T(8,128)S(1)}, u32[]{:S(2)}, u32[]{:S(2)}) collective-permute-start(f32[10,8,256]{2,1,0:T(8,128)S(1)} %pad_maximum_fusion.3), channel_id=1, source_target_pairs={{0,4},{4,8},{8,12},{12,16},{16,20},{20,24},{24,28},{28,0},{1,5},{5... | collective-permute-start | bytes 245768 | tf_op jit(solution)/shard_map/ppermute | solution.py:16
  49.8 1.5 %collective-permute-done.6 = f32[10,8,256]{2,1,0:T(8,128)S(1)} collective-permute-done((f32[10,8,256]{2,1,0:T(8,128)S(1)}, f32[10,8,256]{2,1,0:T(8,128)S(1)}, u32[]{:S(2)}, u32[]{:S(2)}) %collective-permute-start.6) | collective-permute-done | bytes 81952 | tf_op jit(solution)/shard_map/ppermute | solution.py:16
  52.2 2.3 %collective-permute-done.7 = f32[10,8,256]{2,1,0:T(8,128)S(1)} collective-permute-done((f32[10,8,256]{2,1,0:T(8,128)S(1)}, f32[10,8,256]{2,1,0:T(8,128)S(1)}, u32[]{:S(2)}, u32[]{:S(2)}) %collective-permute-start.7) | collective-permute-done | bytes 81952 | tf_op jit(solution)/shard_map/ppermute | solution.py:17
  61.7 0.9 %fusion.16 = (f32[256,1,256]{2,0,1:T(8,128)}, f32[256,1,256]{2,0,1:T(8,128)S(1)}) fusion(f32[3,256,256]{2,1,0:T(8,128)S(1)} %fusion.80, pred[256]{0:T(512)(128)(4,1)S(1)} %compare_or_fusion, f32[255,1,256]{2,0,1:T(8,128)S(1)} %get-tuple-element.55, f32[1,1,256]{2,0,1:T(1,128)S(1)} %get-tuple-element.59, f32[1,1,256]{2,0,1:T(1,128)S(1)} %get-tuple-element.58, ...), kind=kLoop, calls=%fused_computation.27 | loop fusion | flops 786432 | bytes 2359552 | tf_op jit(solution)/shard_map/jit(_where)/select_n | solution.py:141
  63.6 1.4 %fusion.8 = f32[3,256,256]{1,2,0:T(8,128)S(1)} fusion(f32[3,256,256]{2,1,0:T(8,128)S(1)} %fusion.1, f32[256,256]{1,0:T(8,128)S(1)} %copy-done), kind=kOutput, calls=%fused_computation.17 | convolution fusion | flops 603979776 | bytes 1835008 | tf_op jit(solution)/shard_map/dot_general | solution.py:146
  65.1 0.9 %fusion.2 = f32[3,256,256]{1,2,0:T(8,128)S(1)} fusion(f32[3,256,256]{1,2,0:T(8,128)S(1)} %copy-done.7, f32[3,256,256]{1,2,0:T(8,128)S(1)} %fusion.8, f32[256,256]{1,0:T(8,128)S(1)} %copy-done.8), kind=kOutput, calls=%fused_computation.5 | convolution fusion | flops 604176384 | bytes 2621440 | tf_op jit(solution)/shard_map/dot_general | solution.py:147
  65.9 1.1 %copy.11 = f32[3,256,256]{2,1,0:T(8,128)} copy(f32[3,256,256]{1,2,0:T(8,128)S(1)} %fusion.2) | data formatting | bytes 1572864
  (198 shorter events, 16.8 us)
Async XLA Ops:
  0.6 2.2 %copy-start = (f32[256,256]{1,0:T(8,128)S(1)}, f32[256,256]{1,0:T(8,128)}, u32[]{:S(2)}) copy-start(f32[256,256]{1,0:T(8,128)} %param.15) | copy-start | bytes 786436
  0.7 3.0 %copy-start.5 = (bf16[3,256,3,256]{3,1,2,0:T(8,128)(2,1)S(1)}, bf16[3,256,3,256]{3,1,2,0:T(8,128)(2,1)}, u32[]{:S(2)}) copy-start(bf16[3,256,3,256]{3,1,2,0:T(8,128)(2,1)} %param.9) | copy-start | bytes 3538948
  4.0 0.9 %copy-start.6 = (f32[256,3,256]{2,0,1:T(8,128)}, f32[256,3,256]{2,0,1:T(8,128)S(1)}, u32[]{:S(2)}) copy-start(f32[256,3,256]{2,0,1:T(8,128)S(1)} %fusion) | copy-start | bytes 2359300
  4.0 7.8 %copy-start.3 = (f32[256,3,256]{2,0,1:T(8,128)S(1)}, f32[256,3,256]{2,0,1:T(8,128)}, u32[]{:S(2)}) copy-start(f32[256,3,256]{2,0,1:T(8,128)} %param.11) | copy-start | bytes 2359300
  5.7 8.3 %copy-start.4 = (f32[256,3,256]{2,0,1:T(8,128)S(1)}, f32[256,3,256]{2,0,1:T(8,128)}, u32[]{:S(2)}) copy-start(f32[256,3,256]{2,0,1:T(8,128)} %param.12) | copy-start | bytes 2359300
  5.7 13.9 %collective-permute-start = (f32[192,256]{1,0:T(8,128)}, f32[192,256]{1,0:T(8,128)}, u32[]{:S(2)}, u32[]{:S(2)}) collective-permute-start(f32[192,256]{1,0:T(8,128)} %get-tuple-element.43), channel_id=1, source_target_pairs={{0,1},{1,2},{2,3},{3,0},{4,5},{5,6},{6,7},{7,4},{8,9},{9,10},{10,1... | collective-permute-start | bytes 589832 | tf_op jit(solution)/shard_map/ppermute | solution.py:51
  7.0 16.5 %collective-permute-start.1 = (f32[192,256]{1,0:T(8,128)}, f32[192,256]{1,0:T(8,128)}, u32[]{:S(2)}, u32[]{:S(2)}) collective-permute-start(f32[192,256]{1,0:T(8,128)} %get-tuple-element.45), channel_id=1, source_target_pairs={{0,2},{1,3},{2,0},{3,1},{4,6},{5,7},{6,4},{7,5},{8,10},{9,11},{10,... | collective-permute-start | bytes 589832 | tf_op jit(solution)/shard_map/ppermute | solution.py:51
  8.0 18.3 %collective-permute-start.2 = (f32[192,256]{1,0:T(8,128)}, f32[192,256]{1,0:T(8,128)}, u32[]{:S(2)}, u32[]{:S(2)}) collective-permute-start(f32[192,256]{1,0:T(8,128)} %get-tuple-element.44), channel_id=1, source_target_pairs={{0,3},{1,0},{2,1},{3,2},{4,7},{5,4},{6,5},{7,6},{8,11},{9,8},{10,9... | collective-permute-start | bytes 589832 | tf_op jit(solution)/shard_map/ppermute | solution.py:51
  11.8 4.5 %copy-start.1 = (f32[256,256]{1,0:T(8,128)S(1)}, f32[256,256]{1,0:T(8,128)}, u32[]{:S(2)}) copy-start(f32[256,256]{1,0:T(8,128)} %param.13) | copy-start | bytes 786436
  19.6 26.4 %copy-start.2 = (f32[256,3,256]{2,0,1:T(8,128)S(1)}, f32[256,3,256]{2,0,1:T(8,128)}, u32[]{:S(2)}) copy-start(f32[256,3,256]{2,0,1:T(8,128)} %param.10) | copy-start | bytes 2359300
  27.6 6.0 %collective-permute-start.3 = (f32[192,256]{1,0:T(8,128)S(1)}, f32[192,256]{1,0:T(8,128)S(1)}, u32[]{:S(2)}, u32[]{:S(2)}) collective-permute-start(f32[192,256]{1,0:T(8,128)S(1)} %fusion.73), channel_id=1, source_target_pairs={{0,1},{1,2},{2,3},{3,0},{4,5},{5,6},{6,7},{7,4},{8,9},{9,10},{10,1... | collective-permute-start | bytes 589832 | tf_op jit(solution)/shard_map/ppermute | solution.py:62
  27.7 16.7 %collective-permute-start.4 = (f32[192,256]{1,0:T(8,128)S(1)}, f32[192,256]{1,0:T(8,128)S(1)}, u32[]{:S(2)}, u32[]{:S(2)}) collective-permute-start(f32[192,256]{1,0:T(8,128)S(1)} %fusion.73), channel_id=1, source_target_pairs={{0,2},{1,3},{2,0},{3,1},{4,6},{5,7},{6,4},{7,5},{8,10},{9,11},{10,... | collective-permute-start | bytes 589832 | tf_op jit(solution)/shard_map/ppermute | solution.py:62
  28.1 17.9 %collective-permute-start.5 = (f32[192,256]{1,0:T(8,128)S(1)}, f32[192,256]{1,0:T(8,128)S(1)}, u32[]{:S(2)}, u32[]{:S(2)}) collective-permute-start(f32[192,256]{1,0:T(8,128)S(1)} %fusion.73), channel_id=1, source_target_pairs={{0,3},{1,0},{2,1},{3,2},{4,7},{5,4},{6,5},{7,6},{8,11},{9,8},{10,9... | collective-permute-start | bytes 589832 | tf_op jit(solution)/shard_map/ppermute | solution.py:62
  48.1 3.1 %collective-permute-start.6 = (f32[10,8,256]{2,1,0:T(8,128)S(1)}, f32[10,8,256]{2,1,0:T(8,128)S(1)}, u32[]{:S(2)}, u32[]{:S(2)}) collective-permute-start(f32[10,8,256]{2,1,0:T(8,128)S(1)} %pad_maximum_fusion.3), channel_id=1, source_target_pairs={{0,4},{4,8},{8,12},{12,16},{16,20},{20,24},{24,28},{28,0},{1,5},{5... | collective-permute-start | bytes 245768 | tf_op jit(solution)/shard_map/ppermute | solution.py:16
  49.8 4.8 %collective-permute-start.7 = (f32[10,8,256]{2,1,0:T(8,128)S(1)}, f32[10,8,256]{2,1,0:T(8,128)S(1)}, u32[]{:S(2)}, u32[]{:S(2)}) collective-permute-start(f32[10,8,256]{2,1,0:T(8,128)S(1)} %pad_maximum_fusion.2), channel_id=1, source_target_pairs={{4,0},{8,4},{12,8},{16,12},{20,16},{24,20},{28,24},{0,28},{5,1},{9... | collective-permute-start | bytes 245768 | tf_op jit(solution)/shard_map/ppermute | solution.py:17
  63.3 1.7 %copy-start.7 = (f32[3,256,256]{1,2,0:T(8,128)S(1)}, f32[3,256,256]{1,2,0:T(8,128)}, u32[]{:S(2)}) copy-start(f32[3,256,256]{1,2,0:T(8,128)} %copy.10) | copy-start | bytes 2359300
  63.3 1.7 %copy-start.8 = (f32[256,256]{1,0:T(8,128)S(1)}, f32[256,256]{1,0:T(8,128)}, u32[]{:S(2)}) copy-start(f32[256,256]{1,0:T(8,128)} %param.14) | copy-start | bytes 786436
  65.0 2.0 %copy-start.9 = (f32[256,1,256]{2,0,1:T(8,128)S(1)}, f32[256,1,256]{2,0,1:T(8,128)}, u32[]{:S(2)}) copy-start(f32[256,1,256]{2,0,1:T(8,128)} %get-tuple-element.12) | copy-start | bytes 786436

commit v10 on v9

--- a/solution.py
+++ b/solution.py
@@ -1,6 +1,8 @@
 import jax
 import jax.numpy as jnp
 from jax import lax
+from jax.experimental import pallas as pl
+from jax.experimental.pallas import tpu as pltpu
 from jax.sharding import PartitionSpec as P
 
 STEPS = 2
@@ -18,11 +20,15 @@
     return before, after
 
 
-def slope(f, axis):
+def jnp_slope(f, axis):
     return 0.5 * (jnp.roll(f, -1, axis) - jnp.roll(f, 1, axis))
 
 
-def dynamics(h, u, v, dep, prec, meas, col=0, row=1):
+def kernel_slope(f, axis):
+    return 0.5 * (pltpu.roll(f, f.shape[axis] - 1, axis) - pltpu.roll(f, 1, axis))
+
+
+def dynamics(h, u, v, dep, prec, meas, col=0, row=1, slope=jnp_slope):
     for _ in range(STEPS):
         h = h - COURANT * dep * (slope(u, col) + slope(v, row))
         u = u - COURANT * slope(h, col)
@@ -36,6 +42,29 @@
         q = q + COURANT * slope(w, row)
         a = e
     return pred, (a, p, q)
+
+
+def block_kernel(state_ref, meas_ref, prec_ref, dep_ref, pred_ref, adj_ref):
+    count = state_ref.shape[0]
+    pred, adj = dynamics(*(state_ref[i] for i in range(count)), dep_ref[...],
+                         [prec_ref[i] for i in range(count)], [meas_ref[i] for i in range(count)],
+                         slope=kernel_slope)
+    for i in range(count):
+        pred_ref[i] = pred[i]
+        adj_ref[i] = adj[i]
+
+
+def block_dynamics(state, meas, prec, dep):
+    vmem = pl.BlockSpec(memory_space=pltpu.VMEM)
+    out = jax.ShapeDtypeStruct(state.shape, state.dtype)
+    return pl.pallas_call(
+        block_kernel,
+        out_shape=(out, out),
+        in_specs=[vmem] * 4,
+        out_specs=(vmem, vmem),
+        cost_estimate=pl.CostEstimate(
+            flops=120 * state.size, transcendentals=0, bytes_accessed=4 * (6 * state.size + dep.size)),
+    )(state, meas, prec, dep)
 
 
 def member_scatter(x):
@@ -120,7 +149,8 @@
     own_hi = jnp.concatenate([state_hi, fixed_hi], axis=0)
     before, after = shift_rows(None, (own_lo[:, :HALO], own_hi[:, HALO:]))
 
-    pred, adj = dynamics(*state, depth, prec, meas)
+    pred, adj = block_dynamics(jnp.stack(state), measured_values.transpose(1, 0, 2),
+                               precision_factor.transpose(1, 0, 2), depth)
 
     def strip(s):
         return dynamics(*s[:nfield], s[-1], s[2 * nfield:3 * nfield], s[nfield:2 * nfield],

time: 68 us -> 63.8 us (0.938); the launches traced: 67.8 us -> 62.6 us
  waiting for transfers between devices: 26.9 us -> 20.4 us
  Pallas kernels: 0 us -> 4.28 us
  other arithmetic: 7.49 us -> 5.25 us
    pallas_call x0 -> x1, Pallas kernels: none -> 4.28 us  [block_dynamics(): pl.pallas_call(block_kernel, out_shape=(out, out), in_specs=[vmem] * 4, o...]
    ppermute x3, waiting for transfers between devices: 6.71 us -> 3.94 us  [member_scatter(): acc = acc + lax.ppermute(sent, 'member', shift)]
    ppermute x1, waiting for transfers between devices: 2.33 us -> 0.01 us  [shift_rows(): after = lax.ppermute(lo, 'tile', down)]
    unnamed x28, local copies, waits for them, and re-layouts: 8.73 us -> 10.6 us
    ppermute x1, waiting for transfers between devices: 1.47 us -> 0.01 us  [shift_rows(): before = lax.ppermute(hi, 'tile', up)]
    select_n x4 -> x1, other arithmetic: 1.57 us -> 0.2 us  [assemble(): jnp.where(at_edge, edge[i], f)]
    slice x83 -> x65, local copies, waits for them, and re-layouts: 3.84 us -> 2.53 us  [jnp_slope(): return 0.5 * (jnp.roll(f, -1, axis) - jnp.roll(f, 1, axis))]
    concatenate x14 -> x0, local copies, waits for them, and re-layouts: 0.96 us -> none  [slope(): return 0.5 * (jnp.roll(f, -1, axis) - jnp.roll(f, 1, axis))]
  transfers between devices with their start and end apart: 8 -> 8, of which waited for: 7 -> 5; matrix products, arithmetic and copies ran while one was open for 16% -> 25% of each run, Pallas kernels for 0% -> 7%
where the time goes in v10:
time: 63.8 us; the launch traced here: 62.6 us
  waiting for transfers between devices  20.4 us (32%)
  local copies, waits for them, and re-layouts  14.9 us (23%)
  matrix products  9.36 us (15%)
  starting transfers between devices  7.22 us (11%)
  other arithmetic  5.25 us (8%)
  Pallas kernels  4.28 us (7%)
  between operations  1.25 us (2%)
    ppermute x3, waiting for transfers between devices, member_gather(): got = lax.ppermute(acc, 'member', shift)  16.4 us
    unnamed x28, local copies, waits for them, and re-layouts  10.6 us
    pallas_call x1, Pallas kernels, block_dynamics(): pl.pallas_call(block_kernel, out_shape=(out, out), in_specs=[vmem] * 4, o...  4.28 us
    ppermute x3, waiting for transfers between devices, member_scatter(): acc = acc + lax.ppermute(sent, 'member', shift)  3.94 us
    ppermute x3, starting transfers between devices, member_scatter(): acc = acc + lax.ppermute(sent, 'member', shift)  3.77 us
    dot_general x2, matrix products, ends(): lax.dot_general(select, jnp.stack(planes), (((1,), (2,)), ((), ())), prec...  3.06 us
    slice x65, local copies, waits for them, and re-layouts, jnp_slope(): return 0.5 * (jnp.roll(f, -1, axis) - jnp.roll(f, 1, axis))  2.53 us
    dot_general x1, matrix products, body(): localized = lax.dot_general(cols_b, alpha, batched(2, 1), precision=highest)  2.13 us
  transfers between devices with their start and end apart: 8, of which 5 were waited for; matrix products, arithmetic and copies ran while one was open for 25% of the time, Pallas kernels for 7%

profile of v10, /device:TPU:11, one launch (start us, length us, event | category | flops | bytes accessed | tf_op | source)
XLA Modules:
  0.0 62.6 jit_solution(12201564728262313200)
XLA Ops:
  0.7 2.1 %fusion.8 = f32[3,256,256]{2,1,0:T(8,128)S(1)} fusion(f32[3,256,256]{2,1,0:T(8,128)} %param.8, f32[256,256]{1,0:T(8,128)} %param.14), kind=kOutput, calls=%fused_computation.18 | convolution fusion | flops 603979776 | bytes 1835008 | tf_op jit(solution)/shard_map/dot_general | solution.py:126
  2.8 0.8 %fusion.5 = f32[3,256,256]{2,1,0:T(8,128)S(1)} fusion(f32[3,256,256]{2,1,0:T(8,128)S(1)} %fusion.8, f32[256,256]{1,0:T(8,128)S(1)} %copy-done), kind=kOutput, calls=%fused_computation.15 | convolution fusion | flops 603979776 | bytes 1835008 | tf_op jit(solution)/shard_map/dot_general | solution.py:127
  4.8 1.3 %collective-permute-start = (f32[192,256]{1,0:T(8,128)}, f32[192,256]{1,0:T(8,128)S(1)}, u32[]{:S(2)}, u32[]{:S(2)}) collective-permute-start(f32[192,256]{1,0:T(8,128)} %get-tuple-element.39), channel_id=1, source_target_pairs={{0,1},{1,2},{2,3},{3,0},{4,5},{5,6},{6,7},{7,4},{8,9},{9,10},{10,1... | collective-permute-start | bytes 589832 | tf_op jit(solution)/shard_map/ppermute | solution.py:80
  6.1 1.0 %collective-permute-start.1 = (f32[192,256]{1,0:T(8,128)}, f32[192,256]{1,0:T(8,128)}, u32[]{:S(2)}, u32[]{:S(2)}) collective-permute-start(f32[192,256]{1,0:T(8,128)} %get-tuple-element.41), channel_id=1, source_target_pairs={{0,2},{1,3},{2,0},{3,1},{4,6},{5,7},{6,4},{7,5},{8,10},{9,11},{10,... | collective-permute-start | bytes 589832 | tf_op jit(solution)/shard_map/ppermute | solution.py:80
  7.1 1.5 %collective-permute-start.2 = (f32[192,256]{1,0:T(8,128)}, f32[192,256]{1,0:T(8,128)}, u32[]{:S(2)}, u32[]{:S(2)}) collective-permute-start(f32[192,256]{1,0:T(8,128)} %get-tuple-element.40), channel_id=1, source_target_pairs={{0,3},{1,0},{2,1},{3,2},{4,7},{5,4},{6,5},{7,6},{8,11},{9,8},{10,9... | collective-permute-start | bytes 589832 | tf_op jit(solution)/shard_map/ppermute | solution.py:80
  8.6 1.1 %copy.10 = f32[3,256,256]{1,2,0:T(8,128)} copy(f32[3,256,256]{2,1,0:T(8,128)S(1)} %copy-done.2) | data formatting | bytes 1572864 | tf_op args[0]
  9.8 1.8 %bitcast_dynamic-update-slice_fusion.6 = f32[7,256,256]{2,1,0:T(8,128)} fusion(f32[256,3,256]{2,0,1:T(8,128)} %param.11), kind=kLoop, calls=%fused_computation.41 | loop fusion | bytes 524288
  11.5 1.7 %bitcast_dynamic-update-slice_fusion.5 = f32[7,256,256]{2,1,0:T(8,128)} fusion(f32[7,256,256]{2,1,0:T(8,128)} %bitcast_dynamic-update-slice_fusion.6, f32[256,3,256]{2,0,1:T(8,128)} %param.11), kind=kLoop, calls=%fused_computation.40 | loop fusion | bytes 524288
  13.2 1.7 %bitcast_dynamic-update-slice_fusion.4 = f32[7,256,256]{2,1,0:T(8,128)} fusion(f32[7,256,256]{2,1,0:T(8,128)} %bitcast_dynamic-update-slice_fusion.5, f32[256,3,256]{2,0,1:T(8,128)} %param.11), kind=kLoop, calls=%fused_computation.39 | loop fusion | bytes 524288
  14.9 1.7 %bitcast_dynamic-update-slice_fusion.3 = f32[7,256,256]{2,1,0:T(8,128)} fusion(f32[7,256,256]{2,1,0:T(8,128)} %bitcast_dynamic-update-slice_fusion.4, f32[256,3,256]{2,0,1:T(8,128)} %param.12), kind=kLoop, calls=%fused_computation.38 | loop fusion | bytes 524288
  18.9 2.5 %convolution_bitcast_fusion.1 = f32[7,32,256]{2,1,0:T(8,128)S(1)} fusion(f32[7,256,256]{2,1,0:T(8,128)} %bitcast_dynamic-update-slice_fusion, s32[32]{0:T(128)S(1)} %pad_add_fusion), kind=kOutput, calls=%fused_computation.6 | convolution fusion | flops 176168960 | bytes 2064512 | tf_op jit(solution)/shard_map/dot_general | solution.py:140
  21.5 1.1 %collective-permute-done.1 = f32[192,256]{1,0:T(8,128)} collective-permute-done((f32[192,256]{1,0:T(8,128)}, f32[192,256]{1,0:T(8,128)}, u32[]{:S(2)}, u32[]{:S(2)}) %collective-permute-start.1) | collective-permute-done | bytes 196640 | tf_op jit(solution)/shard_map/ppermute | solution.py:80
  22.6 2.8 %collective-permute-done.2 = f32[192,256]{1,0:T(8,128)} collective-permute-done((f32[192,256]{1,0:T(8,128)}, f32[192,256]{1,0:T(8,128)}, u32[]{:S(2)}, u32[]{:S(2)}) %collective-permute-start.2) | collective-permute-done | bytes 196640 | tf_op jit(solution)/shard_map/ppermute | solution.py:80
  25.5 1.1 %fusion.19 = f32[192,256]{1,0:T(8,128)S(1)} fusion(f32[192,256]{1,0:T(8,128)} %collective-permute-done.2, f32[192,256]{1,0:T(8,128)} %collective-permute-done.1, f32[192,256]{1,0:T(8,128)S(1)} %collective-permute-done, f32[4,192,256]{2,1,0:T(8,128)S(1)} %bitcast.244, s32[]{:T(128)S(6)} %select_n.103), kind=kLoop, calls=%fused_computation.52 | loop fusion | flops 147456 | bytes 983044 | tf_op jit(solution)/shard_map/add | solution.py:80
  27.0 1.4 %collective-permute-start.5 = (f32[192,256]{1,0:T(8,128)S(1)}, f32[192,256]{1,0:T(8,128)S(1)}, u32[]{:S(2)}, u32[]{:S(2)}) collective-permute-start(f32[192,256]{1,0:T(8,128)S(1)} %fusion.19), channel_id=1, source_target_pairs={{0,3},{1,0},{2,1},{3,2},{4,7},{5,4},{6,5},{7,6},{8,11},{9,8},{10,9... | collective-permute-start | bytes 589832 | tf_op jit(solution)/shard_map/ppermute | solution.py:91
  28.4 4.1 %collective-permute-done.3 = f32[192,256]{1,0:T(8,128)S(1)} collective-permute-done((f32[192,256]{1,0:T(8,128)S(1)}, f32[192,256]{1,0:T(8,128)S(1)}, u32[]{:S(2)}, u32[]{:S(2)}) %collective-permute-start.3) | collective-permute-done | bytes 196640 | tf_op jit(solution)/shard_map/ppermute | solution.py:91
  32.6 10.7 %collective-permute-done.4 = f32[192,256]{1,0:T(8,128)S(1)} collective-permute-done((f32[192,256]{1,0:T(8,128)S(1)}, f32[192,256]{1,0:T(8,128)S(1)}, u32[]{:S(2)}, u32[]{:S(2)}) %collective-permute-start.4) | collective-permute-done | bytes 196640 | tf_op jit(solution)/shard_map/ppermute | solution.py:91
  43.3 1.5 %collective-permute-done.5 = f32[192,256]{1,0:T(8,128)S(1)} collective-permute-done((f32[192,256]{1,0:T(8,128)S(1)}, f32[192,256]{1,0:T(8,128)S(1)}, u32[]{:S(2)}, u32[]{:S(2)}) %collective-permute-start.5) | collective-permute-done | bytes 196640 | tf_op jit(solution)/shard_map/ppermute | solution.py:91
  45.6 1.6 %collective-permute-start.6 = (f32[10,8,256]{2,1,0:T(8,128)S(1)}, f32[10,8,256]{2,1,0:T(8,128)S(1)}, u32[]{:S(2)}, u32[]{:S(2)}) collective-permute-start(f32[10,8,256]{2,1,0:T(8,128)S(1)} %pad_maximum_fusion.4), channel_id=1, source_target_pairs={{0,4},{4,8},{8,12},{12,16},{16,20},{20,24},{24,28},{28,0},{1,5},{5... | collective-permute-start | bytes 245768 | tf_op jit(solution)/shard_map/ppermute | solution.py:18
  47.3 0.9 %pad_maximum_fusion.state_ref = f32[3,256,256]{2,1,0:T(8,128)} fusion(f32[1,256,256]{2,1,0:T(8,128)S(1)} %get-tuple-element.37, f32[1,256,256]{2,1,0:T(8,128)S(1)} %get-tuple-element.38, f32[1,256,256]{2,1,0:T(8,128)S(1)} %get-tuple-element.36), kind=kLoop, calls=%fused_computation.8 | loop fusion | flops 393216 | bytes 1572864 | tf_op jit(solution)/shard_map/stack | solution.py:140
  48.2 4.3 %shard_map.95 = (f32[3,256,256]{2,1,0:T(8,128)}, f32[3,256,256]{2,1,0:T(8,128)}) custom-call(f32[3,256,256]{2,1,0:T(8,128)} %pad_maximum_fusion.state_ref, f32[3,256,256]{2,1,0:T(8,128)} %bitcast.245, f32[3,256,256]{2,1,0:T(8,128)} %bitcast.246, f32[256,256]{1,0:T(8,128)} %dep_ref.1), custom_call_target="tpu_custom_call" | custom-call | flops 23592960 | bytes 4980736 | tf_op jit(solution)/shard_map/pallas_call | solution.py:60
  58.4 1.4 %fusion.3 = f32[3,256,256]{1,2,0:T(8,128)S(1)} fusion(f32[3,256,256]{2,1,0:T(8,128)S(1)} %fusion.1, f32[256,256]{1,0:T(8,128)S(1)} %copy-done), kind=kOutput, calls=%fused_computation.13 | convolution fusion | flops 603979776 | bytes 1835008 | tf_op jit(solution)/shard_map/dot_general | solution.py:176
  59.9 0.9 %fusion.2 = f32[3,256,256]{1,2,0:T(8,128)S(1)} fusion(f32[3,256,256]{1,2,0:T(8,128)S(1)} %copy-done.3, f32[3,256,256]{1,2,0:T(8,128)S(1)} %fusion.3, f32[256,256]{1,0:T(8,128)S(1)} %copy-done.5), kind=kOutput, calls=%fused_computation.5 | convolution fusion | flops 604176384 | bytes 2621440 | tf_op jit(solution)/shard_map/dot_general | solution.py:177
  60.8 1.1 %copy.11 = f32[3,256,256]{2,1,0:T(8,128)} copy(f32[3,256,256]{1,2,0:T(8,128)S(1)} %fusion.2) | data formatting | bytes 1572864
  (155 shorter events, 11.0 us)
Async XLA Ops:
  0.6 2.2 %copy-start = (f32[256,256]{1,0:T(8,128)S(1)}, f32[256,256]{1,0:T(8,128)}, u32[]{:S(2)}) copy-start(f32[256,256]{1,0:T(8,128)} %param.15) | copy-start | bytes 786436
  0.7 3.0 %copy-start.1 = (bf16[3,256,3,256]{3,1,2,0:T(8,128)(2,1)S(1)}, bf16[3,256,3,256]{3,1,2,0:T(8,128)(2,1)}, u32[]{:S(2)}) copy-start(bf16[3,256,3,256]{3,1,2,0:T(8,128)(2,1)} %param.9) | copy-start | bytes 3538948
  3.7 4.9 %copy-start.2 = (f32[3,256,256]{2,1,0:T(8,128)S(1)}, f32[3,256,256]{2,1,0:T(8,128)}, u32[]{:S(2)}) copy-start(f32[3,256,256]{2,1,0:T(8,128)} %param.8) | copy-start | bytes 2359300
  4.8 16.7 %collective-permute-start = (f32[192,256]{1,0:T(8,128)}, f32[192,256]{1,0:T(8,128)S(1)}, u32[]{:S(2)}, u32[]{:S(2)}) collective-permute-start(f32[192,256]{1,0:T(8,128)} %get-tuple-element.39), channel_id=1, source_target_pairs={{0,1},{1,2},{2,3},{3,0},{4,5},{5,6},{6,7},{7,4},{8,9},{9,10},{10,1... | collective-permute-start | bytes 589832 | tf_op jit(solution)/shard_map/ppermute | solution.py:80
  6.1 16.5 %collective-permute-start.1 = (f32[192,256]{1,0:T(8,128)}, f32[192,256]{1,0:T(8,128)}, u32[]{:S(2)}, u32[]{:S(2)}) collective-permute-start(f32[192,256]{1,0:T(8,128)} %get-tuple-element.41), channel_id=1, source_target_pairs={{0,2},{1,3},{2,0},{3,1},{4,6},{5,7},{6,4},{7,5},{8,10},{9,11},{10,... | collective-permute-start | bytes 589832 | tf_op jit(solution)/shard_map/ppermute | solution.py:80
  7.1 18.3 %collective-permute-start.2 = (f32[192,256]{1,0:T(8,128)}, f32[192,256]{1,0:T(8,128)}, u32[]{:S(2)}, u32[]{:S(2)}) collective-permute-start(f32[192,256]{1,0:T(8,128)} %get-tuple-element.40), channel_id=1, source_target_pairs={{0,3},{1,0},{2,1},{3,2},{4,7},{5,4},{6,5},{7,6},{8,11},{9,8},{10,9... | collective-permute-start | bytes 589832 | tf_op jit(solution)/shard_map/ppermute | solution.py:80
  9.8 6.8 %copy-start.4 = (f32[256,3,256]{2,0,1:T(8,128)S(1)}, f32[256,3,256]{2,0,1:T(8,128)}, u32[]{:S(2)}) copy-start(f32[256,3,256]{2,0,1:T(8,128)} %param.12) | copy-start | bytes 2359300
  9.8 8.3 %copy-start.6 = (f32[256,256]{1,0:T(8,128)S(1)}, f32[256,256]{1,0:T(8,128)}, u32[]{:S(2)}) copy-start(f32[256,256]{1,0:T(8,128)} %dep_ref.1) | copy-start | bytes 786436
  21.5 23.4 %copy-start.9 = (f32[256,3,256]{2,0,1:T(8,128)S(1)}, f32[256,3,256]{2,0,1:T(8,128)}, u32[]{:S(2)}) copy-start(f32[256,3,256]{2,0,1:T(8,128)} %param.10) | copy-start | bytes 2359300
  26.5 6.0 %collective-permute-start.3 = (f32[192,256]{1,0:T(8,128)S(1)}, f32[192,256]{1,0:T(8,128)S(1)}, u32[]{:S(2)}, u32[]{:S(2)}) collective-permute-start(f32[192,256]{1,0:T(8,128)S(1)} %fusion.19), channel_id=1, source_target_pairs={{0,1},{1,2},{2,3},{3,0},{4,5},{5,6},{6,7},{7,4},{8,9},{9,10},{10,1... | collective-permute-start | bytes 589832 | tf_op jit(solution)/shard_map/ppermute | solution.py:91
  26.6 16.7 %collective-permute-start.4 = (f32[192,256]{1,0:T(8,128)S(1)}, f32[192,256]{1,0:T(8,128)S(1)}, u32[]{:S(2)}, u32[]{:S(2)}) collective-permute-start(f32[192,256]{1,0:T(8,128)S(1)} %fusion.19), channel_id=1, source_target_pairs={{0,2},{1,3},{2,0},{3,1},{4,6},{5,7},{6,4},{7,5},{8,10},{9,11},{10,... | collective-permute-start | bytes 589832 | tf_op jit(solution)/shard_map/ppermute | solution.py:91
  27.0 17.9 %collective-permute-start.5 = (f32[192,256]{1,0:T(8,128)S(1)}, f32[192,256]{1,0:T(8,128)S(1)}, u32[]{:S(2)}, u32[]{:S(2)}) collective-permute-start(f32[192,256]{1,0:T(8,128)S(1)} %fusion.19), channel_id=1, source_target_pairs={{0,3},{1,0},{2,1},{3,2},{4,7},{5,4},{6,5},{7,6},{8,11},{9,8},{10,9... | collective-permute-start | bytes 589832 | tf_op jit(solution)/shard_map/ppermute | solution.py:91
  45.6 6.9 %collective-permute-start.6 = (f32[10,8,256]{2,1,0:T(8,128)S(1)}, f32[10,8,256]{2,1,0:T(8,128)S(1)}, u32[]{:S(2)}, u32[]{:S(2)}) collective-permute-start(f32[10,8,256]{2,1,0:T(8,128)S(1)} %pad_maximum_fusion.4), channel_id=1, source_target_pairs={{0,4},{4,8},{8,12},{12,16},{16,20},{20,24},{24,28},{28,0},{1,5},{5... | collective-permute-start | bytes 245768 | tf_op jit(solution)/shard_map/ppermute | solution.py:18
  47.2 7.0 %collective-permute-start.7 = (f32[10,8,256]{2,1,0:T(8,128)S(1)}, f32[10,8,256]{2,1,0:T(8,128)S(1)}, u32[]{:S(2)}, u32[]{:S(2)}) collective-permute-start(f32[10,8,256]{2,1,0:T(8,128)S(1)} %pad_maximum_fusion.3), channel_id=1, source_target_pairs={{4,0},{8,4},{12,8},{16,12},{20,16},{24,20},{28,24},{0,28},{5,1},{9... | collective-permute-start | bytes 245768 | tf_op jit(solution)/shard_map/ppermute | solution.py:19
  55.8 2.1 %copy-start.7 = (f32[3,256,256]{2,1,0:T(8,128)S(1)}, f32[3,256,256]{2,1,0:T(8,128)}, u32[]{:S(2)}) copy-start(f32[3,256,256]{2,1,0:T(8,128)} %get-tuple-element.11) | copy-start | bytes 2359300
  55.8 2.1 %copy-start.8 = (f32[3,256,256]{2,1,0:T(8,128)S(1)}, f32[3,256,256]{2,1,0:T(8,128)}, u32[]{:S(2)}) copy-start(f32[3,256,256]{2,1,0:T(8,128)} %get-tuple-element.10) | copy-start | bytes 2359300
  58.2 1.7 %copy-start.3 = (f32[3,256,256]{1,2,0:T(8,128)S(1)}, f32[3,256,256]{1,2,0:T(8,128)}, u32[]{:S(2)}) copy-start(f32[3,256,256]{1,2,0:T(8,128)} %copy.10) | copy-start | bytes 2359300
  58.2 1.7 %copy-start.5 = (f32[256,256]{1,0:T(8,128)S(1)}, f32[256,256]{1,0:T(8,128)}, u32[]{:S(2)}) copy-start(f32[256,256]{1,0:T(8,128)} %param.14) | copy-start | bytes 786436

commit v11 on v10

--- a/solution.py
+++ b/solution.py
@@ -44,9 +44,9 @@
     return pred, (a, p, q)
 
 
-def block_kernel(state_ref, meas_ref, prec_ref, dep_ref, pred_ref, adj_ref):
-    count = state_ref.shape[0]
-    pred, adj = dynamics(*(state_ref[i] for i in range(count)), dep_ref[...],
+def block_kernel(back_ref, incr_ref, meas_ref, prec_ref, dep_ref, pred_ref, adj_ref):
+    count = back_ref.shape[0]
+    pred, adj = dynamics(*(back_ref[i] + incr_ref[i] for i in range(count)), dep_ref[...],
                          [prec_ref[i] for i in range(count)], [meas_ref[i] for i in range(count)],
                          slope=kernel_slope)
     for i in range(count):
@@ -54,17 +54,17 @@
         adj_ref[i] = adj[i]
 
 
-def block_dynamics(state, meas, prec, dep):
+def block_dynamics(back, incr, meas, prec, dep):
     vmem = pl.BlockSpec(memory_space=pltpu.VMEM)
-    out = jax.ShapeDtypeStruct(state.shape, state.dtype)
+    out = jax.ShapeDtypeStruct(back.shape, back.dtype)
     return pl.pallas_call(
         block_kernel,
         out_shape=(out, out),
-        in_specs=[vmem] * 4,
+        in_specs=[vmem] * 5,
         out_specs=(vmem, vmem),
         cost_estimate=pl.CostEstimate(
-            flops=120 * state.size, transcendentals=0, bytes_accessed=4 * (6 * state.size + dep.size)),
-    )(state, meas, prec, dep)
+            flops=120 * back.size, transcendentals=0, bytes_accessed=4 * (7 * back.size + dep.size)),
+    )(back, incr, meas, prec, dep)
 
 
 def member_scatter(x):
@@ -149,7 +149,7 @@
     own_hi = jnp.concatenate([state_hi, fixed_hi], axis=0)
     before, after = shift_rows(None, (own_lo[:, :HALO], own_hi[:, HALO:]))
 
-    pred, adj = block_dynamics(jnp.stack(state), measured_values.transpose(1, 0, 2),
+    pred, adj = block_dynamics(background.transpose(1, 0, 2), incr, measured_values.transpose(1, 0, 2),
                                precision_factor.transpose(1, 0, 2), depth)
 
     def strip(s):

time: 63.8 us -> 63.3 us (level)
  other arithmetic: 5.25 us -> 4.41 us
    another operation x1 -> x0, other arithmetic: 0.94 us -> none  [ends(): jnp.stack(planes)]
    unnamed x28 -> x30, local copies, waits for them, and re-layouts: 10.6 us -> 10.8 us
  transfers between devices with their start and end apart: 8 -> 8, of which waited for: 5 -> 5; matrix products, arithmetic and copies ran while one was open for 25% -> 24% of each run, Pallas kernels for 7% -> 7%
where the time goes in v11:
time: 63.3 us; the launch traced here: 62.1 us
  waiting for transfers between devices  20.4 us (32%)
  local copies, waits for them, and re-layouts  15 us (24%)
  matrix products  9.35 us (15%)
  starting transfers between devices  7.17 us (11%)
  Pallas kernels  4.53 us (7%)
  other arithmetic  4.41 us (7%)
  between operations  1.26 us (2%)
    ppermute x3, waiting for transfers between devices, member_gather(): got = lax.ppermute(acc, 'member', shift)  16.4 us
    unnamed x30, local copies, waits for them, and re-layouts  10.8 us
    pallas_call x1, Pallas kernels, block_dynamics(): pl.pallas_call(block_kernel, out_shape=(out, out), in_specs=[vmem] * 5, o...  4.53 us
    ppermute x3, waiting for transfers between devices, member_scatter(): acc = acc + lax.ppermute(sent, 'member', shift)  3.98 us
    ppermute x3, starting transfers between devices, member_scatter(): acc = acc + lax.ppermute(sent, 'member', shift)  3.77 us
    dot_general x2, matrix products, ends(): lax.dot_general(select, jnp.stack(planes), (((1,), (2,)), ((), ())), prec...  3.06 us
    slice x65, local copies, waits for them, and re-layouts, jnp_slope(): return 0.5 * (jnp.roll(f, -1, axis) - jnp.roll(f, 1, axis))  2.53 us
    dot_general x1, matrix products, body(): localized = lax.dot_general(cols_b, alpha, batched(2, 1), precision=highest)  2.13 us
  transfers between devices with their start and end apart: 8, of which 5 were waited for; matrix products, arithmetic and copies ran while one was open for 24% of the time, Pallas kernels for 7%

profile of v11, /device:TPU:11, one launch (start us, length us, event | category | flops | bytes accessed | tf_op | source)
XLA Modules:
  0.0 62.1 jit_solution(1055463585026888424)
XLA Ops:
  0.7 2.1 %fusion.13 = f32[3,256,256]{2,1,0:T(8,128)S(1)} fusion(f32[3,256,256]{2,1,0:T(8,128)} %param.8, f32[256,256]{1,0:T(8,128)} %param.14), kind=kOutput, calls=%fused_computation.22 | convolution fusion | flops 603979776 | bytes 1835008 | tf_op jit(solution)/shard_map/dot_general | solution.py:126
  2.8 0.8 %fusion.10 = f32[3,256,256]{2,1,0:T(8,128)S(1)} fusion(f32[3,256,256]{2,1,0:T(8,128)S(1)} %fusion.13, f32[256,256]{1,0:T(8,128)S(1)} %copy-done), kind=kOutput, calls=%fused_computation.19 | convolution fusion | flops 603979776 | bytes 1835008 | tf_op jit(solution)/shard_map/dot_general | solution.py:127
  4.0 0.8 %dynamic-slice_bitcast_fusion.2 = (f32[192,256]{1,0:T(8,128)}, f32[192,256]{1,0:T(8,128)}, f32[192,256]{1,0:T(8,128)}) fusion(f32[4,192,256]{2,1,0:T(8,128)S(1)} %bitcast.246, s32[]{:T(128)S(6)} %select_n.105, s32[]{:T(128)S(6)} %select_n.109, s32[]{:T(128)S(6)} %select_n.107), kind=kLoop, calls=%fused_computation.59 | loop fusion | bytes 1179660 | tf_op jit(solution)/shard_map/jit(dynamic_index_in_dim)/squeeze | solution.py:79
  4.8 1.3 %collective-permute-start = (f32[192,256]{1,0:T(8,128)}, f32[192,256]{1,0:T(8,128)}, u32[]{:S(2)}, u32[]{:S(2)}) collective-permute-start(f32[192,256]{1,0:T(8,128)} %get-tuple-element.39), channel_id=1, source_target_pairs={{0,1},{1,2},{2,3},{3,0},{4,5},{5,6},{6,7},{7,4},{8,9},{9,10},{10,1... | collective-permute-start | bytes 589832 | tf_op jit(solution)/shard_map/ppermute | solution.py:80
  6.1 1.0 %collective-permute-start.1 = (f32[192,256]{1,0:T(8,128)}, f32[192,256]{1,0:T(8,128)}, u32[]{:S(2)}, u32[]{:S(2)}) collective-permute-start(f32[192,256]{1,0:T(8,128)} %get-tuple-element.41), channel_id=1, source_target_pairs={{0,2},{1,3},{2,0},{3,1},{4,6},{5,7},{6,4},{7,5},{8,10},{9,11},{10,... | collective-permute-start | bytes 589832 | tf_op jit(solution)/shard_map/ppermute | solution.py:80
  7.1 1.5 %collective-permute-start.2 = (f32[192,256]{1,0:T(8,128)}, f32[192,256]{1,0:T(8,128)}, u32[]{:S(2)}, u32[]{:S(2)}) collective-permute-start(f32[192,256]{1,0:T(8,128)} %get-tuple-element.40), channel_id=1, source_target_pairs={{0,3},{1,0},{2,1},{3,2},{4,7},{5,4},{6,5},{7,6},{8,11},{9,8},{10,9... | collective-permute-start | bytes 589832 | tf_op jit(solution)/shard_map/ppermute | solution.py:80
  8.6 1.1 %copy.10 = f32[3,256,256]{1,2,0:T(8,128)} copy(f32[3,256,256]{2,1,0:T(8,128)S(1)} %copy-done.3) | data formatting | bytes 1572864 | tf_op args[0]
  9.8 1.8 %bitcast_dynamic-update-slice_fusion.6 = f32[7,256,256]{2,1,0:T(8,128)} fusion(f32[256,3,256]{2,0,1:T(8,128)} %param.11), kind=kLoop, calls=%fused_computation.45 | loop fusion | bytes 524288
  11.5 1.7 %bitcast_dynamic-update-slice_fusion.5 = f32[7,256,256]{2,1,0:T(8,128)} fusion(f32[7,256,256]{2,1,0:T(8,128)} %bitcast_dynamic-update-slice_fusion.6, f32[256,3,256]{2,0,1:T(8,128)} %param.11), kind=kLoop, calls=%fused_computation.44 | loop fusion | bytes 524288
  13.2 1.7 %bitcast_dynamic-update-slice_fusion.4 = f32[7,256,256]{2,1,0:T(8,128)} fusion(f32[7,256,256]{2,1,0:T(8,128)} %bitcast_dynamic-update-slice_fusion.5, f32[256,3,256]{2,0,1:T(8,128)} %param.11), kind=kLoop, calls=%fused_computation.43 | loop fusion | bytes 524288
  14.9 1.7 %bitcast_dynamic-update-slice_fusion.3 = f32[7,256,256]{2,1,0:T(8,128)} fusion(f32[7,256,256]{2,1,0:T(8,128)} %bitcast_dynamic-update-slice_fusion.4, f32[256,3,256]{2,0,1:T(8,128)} %param.12), kind=kLoop, calls=%fused_computation.42 | loop fusion | bytes 524288
  18.8 2.5 %convolution_bitcast_fusion.1 = f32[7,32,256]{2,1,0:T(8,128)S(1)} fusion(f32[7,256,256]{2,1,0:T(8,128)} %bitcast_dynamic-update-slice_fusion, s32[32]{0:T(128)S(1)} %pad_add_fusion), kind=kOutput, calls=%fused_computation.6 | convolution fusion | flops 176168960 | bytes 2064512 | tf_op jit(solution)/shard_map/dot_general | solution.py:140
  21.5 1.2 %collective-permute-done.1 = f32[192,256]{1,0:T(8,128)} collective-permute-done((f32[192,256]{1,0:T(8,128)}, f32[192,256]{1,0:T(8,128)}, u32[]{:S(2)}, u32[]{:S(2)}) %collective-permute-start.1) | collective-permute-done | bytes 196640 | tf_op jit(solution)/shard_map/ppermute | solution.py:80
  22.6 2.8 %collective-permute-done.2 = f32[192,256]{1,0:T(8,128)} collective-permute-done((f32[192,256]{1,0:T(8,128)}, f32[192,256]{1,0:T(8,128)}, u32[]{:S(2)}, u32[]{:S(2)}) %collective-permute-start.2) | collective-permute-done | bytes 196640 | tf_op jit(solution)/shard_map/ppermute | solution.py:80
  25.4 1.2 %fusion.24 = f32[192,256]{1,0:T(8,128)S(1)} fusion(f32[192,256]{1,0:T(8,128)} %collective-permute-done.2, f32[192,256]{1,0:T(8,128)} %collective-permute-done.1, f32[192,256]{1,0:T(8,128)} %collective-permute-done, f32[4,192,256]{2,1,0:T(8,128)S(1)} %bitcast.247, s32[]{:T(128)S(6)} %select_n.103), kind=kLoop, calls=%fused_computation.56 | loop fusion | flops 147456 | bytes 983044 | tf_op jit(solution)/shard_map/add | solution.py:80
  27.0 1.4 %collective-permute-start.5 = (f32[192,256]{1,0:T(8,128)S(1)}, f32[192,256]{1,0:T(8,128)S(1)}, u32[]{:S(2)}, u32[]{:S(2)}) collective-permute-start(f32[192,256]{1,0:T(8,128)S(1)} %fusion.24), channel_id=1, source_target_pairs={{0,3},{1,0},{2,1},{3,2},{4,7},{5,4},{6,5},{7,6},{8,11},{9,8},{10,9... | collective-permute-start | bytes 589832 | tf_op jit(solution)/shard_map/ppermute | solution.py:91
  28.5 4.1 %collective-permute-done.3 = f32[192,256]{1,0:T(8,128)S(1)} collective-permute-done((f32[192,256]{1,0:T(8,128)S(1)}, f32[192,256]{1,0:T(8,128)S(1)}, u32[]{:S(2)}, u32[]{:S(2)}) %collective-permute-start.3) | collective-permute-done | bytes 196640 | tf_op jit(solution)/shard_map/ppermute | solution.py:91
  32.7 10.7 %collective-permute-done.4 = f32[192,256]{1,0:T(8,128)S(1)} collective-permute-done((f32[192,256]{1,0:T(8,128)S(1)}, f32[192,256]{1,0:T(8,128)S(1)}, u32[]{:S(2)}, u32[]{:S(2)}) %collective-permute-start.4) | collective-permute-done | bytes 196640 | tf_op jit(solution)/shard_map/ppermute | solution.py:91
  43.4 1.5 %collective-permute-done.5 = f32[192,256]{1,0:T(8,128)S(1)} collective-permute-done((f32[192,256]{1,0:T(8,128)S(1)}, f32[192,256]{1,0:T(8,128)S(1)}, u32[]{:S(2)}, u32[]{:S(2)}) %collective-permute-start.5) | collective-permute-done | bytes 196640 | tf_op jit(solution)/shard_map/ppermute | solution.py:91
  45.9 1.6 %collective-permute-start.6 = (f32[10,8,256]{2,1,0:T(8,128)S(1)}, f32[10,8,256]{2,1,0:T(8,128)S(1)}, u32[]{:S(2)}, u32[]{:S(2)}) collective-permute-start(f32[10,8,256]{2,1,0:T(8,128)S(1)} %pad_maximum_fusion.3), channel_id=1, source_target_pairs={{0,4},{4,8},{8,12},{12,16},{16,20},{20,24},{24,28},{28,0},{1,5},{5... | collective-permute-start | bytes 245768 | tf_op jit(solution)/shard_map/ppermute | solution.py:18
  47.5 4.5 %shard_map.95 = (f32[3,256,256]{2,1,0:T(8,128)}, f32[3,256,256]{2,1,0:T(8,128)}) custom-call(f32[3,256,256]{2,1,0:T(8,128)} %bitcast.250, f32[3,256,256]{2,1,0:T(8,128)} %bitcast.245, f32[3,256,256]{2,1,0:T(8,128)} %bitcast.248, f32[3,256,256]{2,1,0:T(8,128)} %bitcast.249, f32[256,256]{1,0:T(8,128)} %dep_ref.1), custom_call_target="tpu_custom_call" | custom-call | flops 23592960 | bytes 5767168 | tf_op jit(solution)/shard_map/pallas_call | solution.py:60
  58.0 1.4 %fusion.8 = f32[3,256,256]{1,2,0:T(8,128)S(1)} fusion(f32[3,256,256]{2,1,0:T(8,128)S(1)} %fusion.1, f32[256,256]{1,0:T(8,128)S(1)} %copy-done), kind=kOutput, calls=%fused_computation.17 | convolution fusion | flops 603979776 | bytes 1835008 | tf_op jit(solution)/shard_map/dot_general | solution.py:176
  59.4 0.9 %fusion.2 = f32[3,256,256]{1,2,0:T(8,128)S(1)} fusion(f32[3,256,256]{1,2,0:T(8,128)S(1)} %copy-done.4, f32[3,256,256]{1,2,0:T(8,128)S(1)} %fusion.8, f32[256,256]{1,0:T(8,128)S(1)} %copy-done.7), kind=kOutput, calls=%fused_computation.5 | convolution fusion | flops 604176384 | bytes 2621440 | tf_op jit(solution)/shard_map/dot_general | solution.py:177
  60.3 1.1 %copy.11 = f32[3,256,256]{2,1,0:T(8,128)} copy(f32[3,256,256]{1,2,0:T(8,128)S(1)} %fusion.2) | data formatting | bytes 1572864
  (156 shorter events, 10.4 us)
Async XLA Ops:
  0.6 2.2 %copy-start = (f32[256,256]{1,0:T(8,128)S(1)}, f32[256,256]{1,0:T(8,128)}, u32[]{:S(2)}) copy-start(f32[256,256]{1,0:T(8,128)} %param.15) | copy-start | bytes 786436
  0.7 3.0 %copy-start.2 = (bf16[3,256,3,256]{3,1,2,0:T(8,128)(2,1)S(1)}, bf16[3,256,3,256]{3,1,2,0:T(8,128)(2,1)}, u32[]{:S(2)}) copy-start(bf16[3,256,3,256]{3,1,2,0:T(8,128)(2,1)} %param.9) | copy-start | bytes 3538948
  3.7 4.9 %copy-start.3 = (f32[3,256,256]{2,1,0:T(8,128)S(1)}, f32[3,256,256]{2,1,0:T(8,128)}, u32[]{:S(2)}) copy-start(f32[3,256,256]{2,1,0:T(8,128)} %param.8) | copy-start | bytes 2359300
  4.8 16.6 %collective-permute-start = (f32[192,256]{1,0:T(8,128)}, f32[192,256]{1,0:T(8,128)}, u32[]{:S(2)}, u32[]{:S(2)}) collective-permute-start(f32[192,256]{1,0:T(8,128)} %get-tuple-element.39), channel_id=1, source_target_pairs={{0,1},{1,2},{2,3},{3,0},{4,5},{5,6},{6,7},{7,4},{8,9},{9,10},{10,1... | collective-permute-start | bytes 589832 | tf_op jit(solution)/shard_map/ppermute | solution.py:80
  6.1 16.5 %collective-permute-start.1 = (f32[192,256]{1,0:T(8,128)}, f32[192,256]{1,0:T(8,128)}, u32[]{:S(2)}, u32[]{:S(2)}) collective-permute-start(f32[192,256]{1,0:T(8,128)} %get-tuple-element.41), channel_id=1, source_target_pairs={{0,2},{1,3},{2,0},{3,1},{4,6},{5,7},{6,4},{7,5},{8,10},{9,11},{10,... | collective-permute-start | bytes 589832 | tf_op jit(solution)/shard_map/ppermute | solution.py:80
  7.1 18.3 %collective-permute-start.2 = (f32[192,256]{1,0:T(8,128)}, f32[192,256]{1,0:T(8,128)}, u32[]{:S(2)}, u32[]{:S(2)}) collective-permute-start(f32[192,256]{1,0:T(8,128)} %get-tuple-element.40), channel_id=1, source_target_pairs={{0,3},{1,0},{2,1},{3,2},{4,7},{5,4},{6,5},{7,6},{8,11},{9,8},{10,9... | collective-permute-start | bytes 589832 | tf_op jit(solution)/shard_map/ppermute | solution.py:80
  9.8 6.8 %copy-start.5 = (f32[256,3,256]{2,0,1:T(8,128)S(1)}, f32[256,3,256]{2,0,1:T(8,128)}, u32[]{:S(2)}) copy-start(f32[256,3,256]{2,0,1:T(8,128)} %param.12) | copy-start | bytes 2359300
  9.8 8.3 %copy-start.8 = (f32[256,256]{1,0:T(8,128)S(1)}, f32[256,256]{1,0:T(8,128)}, u32[]{:S(2)}) copy-start(f32[256,256]{1,0:T(8,128)} %dep_ref.1) | copy-start | bytes 786436
  21.4 23.6 %copy-start.6 = (f32[256,3,256]{2,0,1:T(8,128)S(1)}, f32[256,3,256]{2,0,1:T(8,128)}, u32[]{:S(2)}) copy-start(f32[256,3,256]{2,0,1:T(8,128)} %param.10) | copy-start | bytes 2359300
  26.6 6.0 %collective-permute-start.3 = (f32[192,256]{1,0:T(8,128)S(1)}, f32[192,256]{1,0:T(8,128)S(1)}, u32[]{:S(2)}, u32[]{:S(2)}) collective-permute-start(f32[192,256]{1,0:T(8,128)S(1)} %fusion.24), channel_id=1, source_target_pairs={{0,1},{1,2},{2,3},{3,0},{4,5},{5,6},{6,7},{7,4},{8,9},{9,10},{10,1... | collective-permute-start | bytes 589832 | tf_op jit(solution)/shard_map/ppermute | solution.py:91
  26.7 16.7 %collective-permute-start.4 = (f32[192,256]{1,0:T(8,128)S(1)}, f32[192,256]{1,0:T(8,128)S(1)}, u32[]{:S(2)}, u32[]{:S(2)}) collective-permute-start(f32[192,256]{1,0:T(8,128)S(1)} %fusion.24), channel_id=1, source_target_pairs={{0,2},{1,3},{2,0},{3,1},{4,6},{5,7},{6,4},{7,5},{8,10},{9,11},{10,... | collective-permute-start | bytes 589832 | tf_op jit(solution)/shard_map/ppermute | solution.py:91
  27.0 17.9 %collective-permute-start.5 = (f32[192,256]{1,0:T(8,128)S(1)}, f32[192,256]{1,0:T(8,128)S(1)}, u32[]{:S(2)}, u32[]{:S(2)}) collective-permute-start(f32[192,256]{1,0:T(8,128)S(1)} %fusion.24), channel_id=1, source_target_pairs={{0,3},{1,0},{2,1},{3,2},{4,7},{5,4},{6,5},{7,6},{8,11},{9,8},{10,9... | collective-permute-start | bytes 589832 | tf_op jit(solution)/shard_map/ppermute | solution.py:91
  45.0 0.9 %copy-start.1 = (f32[4,192,256]{2,1,0:T(8,128)}, f32[4,192,256]{2,1,0:T(8,128)S(1)}, u32[]{:S(2)}) copy-start(f32[4,192,256]{2,1,0:T(8,128)S(1)} %bitcast_dynamic-update-slice_fusion.7) | copy-start | bytes 2359300
  45.9 6.1 %collective-permute-start.6 = (f32[10,8,256]{2,1,0:T(8,128)S(1)}, f32[10,8,256]{2,1,0:T(8,128)S(1)}, u32[]{:S(2)}, u32[]{:S(2)}) collective-permute-start(f32[10,8,256]{2,1,0:T(8,128)S(1)} %pad_maximum_fusion.3), channel_id=1, source_target_pairs={{0,4},{4,8},{8,12},{12,16},{16,20},{20,24},{24,28},{28,0},{1,5},{5... | collective-permute-start | bytes 245768 | tf_op jit(solution)/shard_map/ppermute | solution.py:18
  47.5 6.3 %collective-permute-start.7 = (f32[10,8,256]{2,1,0:T(8,128)S(1)}, f32[10,8,256]{2,1,0:T(8,128)S(1)}, u32[]{:S(2)}, u32[]{:S(2)}) collective-permute-start(f32[10,8,256]{2,1,0:T(8,128)S(1)} %pad_maximum_fusion.2), channel_id=1, source_target_pairs={{4,0},{8,4},{12,8},{16,12},{20,16},{24,20},{28,24},{0,28},{5,1},{9... | collective-permute-start | bytes 245768 | tf_op jit(solution)/shard_map/ppermute | solution.py:19
  55.3 2.1 %copy-start.9 = (f32[3,256,256]{2,1,0:T(8,128)S(1)}, f32[3,256,256]{2,1,0:T(8,128)}, u32[]{:S(2)}) copy-start(f32[3,256,256]{2,1,0:T(8,128)} %get-tuple-element.11) | copy-start | bytes 2359300
  55.3 2.1 %copy-start.10 = (f32[3,256,256]{2,1,0:T(8,128)S(1)}, f32[3,256,256]{2,1,0:T(8,128)}, u32[]{:S(2)}) copy-start(f32[3,256,256]{2,1,0:T(8,128)} %get-tuple-element.10) | copy-start | bytes 2359300
  57.7 1.7 %copy-start.4 = (f32[3,256,256]{1,2,0:T(8,128)S(1)}, f32[3,256,256]{1,2,0:T(8,128)}, u32[]{:S(2)}) copy-start(f32[3,256,256]{1,2,0:T(8,128)} %copy.10) | copy-start | bytes 2359300
  57.7 1.7 %copy-start.7 = (f32[256,256]{1,0:T(8,128)S(1)}, f32[256,256]{1,0:T(8,128)}, u32[]{:S(2)}) copy-start(f32[256,256]{1,0:T(8,128)} %param.14) | copy-start | bytes 786436

commit v12 on v11

--- a/solution.py
+++ b/solution.py
@@ -65,6 +65,32 @@
         cost_estimate=pl.CostEstimate(
             flops=120 * back.size, transcendentals=0, bytes_accessed=4 * (7 * back.size + dep.size)),
     )(back, incr, meas, prec, dep)
+
+
+def strip_kernel(planes_ref, pred_ref, adj_ref):
+    count = pred_ref.shape[1]
+    for k in range(planes_ref.shape[0]):
+        s = [planes_ref[k, i] for i in range(planes_ref.shape[1])]
+        pred, adj = dynamics(*s[:count], s[-1], s[2 * count:3 * count], s[count:2 * count],
+                             col=1, row=0, slope=kernel_slope)
+        for i in range(count):
+            pred_ref[k, i] = pred[i]
+            adj_ref[k, i] = adj[i]
+
+
+def strip_dynamics(planes):
+    strips, count, rows, cols = planes.shape[0], (planes.shape[1] - 1) // 3, planes.shape[2], planes.shape[3]
+    vmem = pl.BlockSpec(memory_space=pltpu.VMEM)
+    out = jax.ShapeDtypeStruct((strips, count, rows, cols), planes.dtype)
+    pred, adj = pl.pallas_call(
+        strip_kernel,
+        out_shape=(out, out),
+        in_specs=[vmem],
+        out_specs=(vmem, vmem),
+        cost_estimate=pl.CostEstimate(
+            flops=40 * planes.size, transcendentals=0, bytes_accessed=4 * (planes.size + 2 * out.size)),
+    )(planes)
+    return (pred[0], adj[0]), (pred[1], adj[1])
 
 
 def member_scatter(x):
@@ -137,14 +163,20 @@
     select = (picked[:, None] == jnp.arange(nrow)[None, :]).astype(jnp.float32)
 
     def ends(planes):
-        cut = lax.dot_general(select, jnp.stack(planes), (((1,), (2,)), ((), ())),
-                              precision=highest).transpose(1, 0, 2)
+        cut = lax.dot_general(select, planes, (((1,), (planes.ndim - 1,)), ((), ())),
+                              precision=highest)
+        cut = cut.transpose(1, 0, 2) if planes.ndim == 3 else cut[None]
         return cut[:, : 2 * HALO], cut[:, 2 * HALO:]
 
-    scattered, fixed_lo, fixed_hi = lax.optimization_barrier((scattered,) + ends(fixed))
+    def fixed_ends():
+        parts = [ends(x) for x in (measured_values.transpose(1, 0, 2),
+                                   precision_factor.transpose(1, 0, 2), depth)]
+        return tuple(jnp.concatenate([p[j] for p in parts], axis=0) for j in range(2))
+
+    scattered, fixed_lo, fixed_hi = lax.optimization_barrier((scattered,) + fixed_ends())
     incr = member_gather(*scattered).reshape(nfield, ncol, nrow)
     state = [background[:, i] + incr[i] for i in range(nfield)]
-    state_lo, state_hi = ends(state)
+    state_lo, state_hi = ends(jnp.stack(state))
     own_lo = jnp.concatenate([state_lo, fixed_lo], axis=0)
     own_hi = jnp.concatenate([state_hi, fixed_hi], axis=0)
     before, after = shift_rows(None, (own_lo[:, :HALO], own_hi[:, HALO:]))
@@ -152,12 +184,8 @@
     pred, adj = block_dynamics(background.transpose(1, 0, 2), incr, measured_values.transpose(1, 0, 2),
                                precision_factor.transpose(1, 0, 2), depth)
 
-    def strip(s):
-        return dynamics(*s[:nfield], s[-1], s[2 * nfield:3 * nfield], s[nfield:2 * nfield],
-                        col=1, row=0)
-
-    first = strip(jnp.concatenate([before, own_lo], axis=1))
-    last = strip(jnp.concatenate([own_hi, after], axis=1))
+    first, last = strip_dynamics(jnp.stack([jnp.concatenate([before, own_lo], axis=1),
+                                            jnp.concatenate([own_hi, after], axis=1)]))
     mid = slice(HALO, 2 * HALO)
 
     placed = jnp.concatenate([jnp.arange(HALO), jnp.arange(nrow - HALO, nrow)])

time: 63.3 us -> 64.9 us (1.025)
  waiting for transfers between devices: 20.4 us -> 29.5 us
  local copies, waits for them, and re-layouts: 15 us -> 6.14 us
  Pallas kernels: 4.53 us -> 7.02 us
  other arithmetic: 4.41 us -> 3.74 us
    ppermute x3, waiting for transfers between devices: 3.98 us -> 12.9 us  [member_scatter(): acc = acc + lax.ppermute(sent, 'member', shift)]
    unnamed x30 -> x24, local copies, waits for them, and re-layouts: 10.8 us -> 3.52 us
    slice x69 -> x0, local copies, waits for them, and re-layouts: 2.54 us -> none  [the longest x65 2.53 us: jnp_slope(): return 0.5 * (jnp.roll(f, -1, axis) - jnp.roll(f, 1, axis))]
    pallas_call x0 -> x1, Pallas kernels: none -> 2.45 us  [strip_dynamics(): pl.pallas_call(strip_kernel, out_shape=(out, out), in_specs=[vmem], out_s...]
    slice x4 -> x2, local copies, waits for them, and re-layouts: 0.01 us -> 1.64 us  [assemble(): f[mid]]
    another operation x0 -> x3, other arithmetic: none -> 0.87 us  [body(): jnp.stack([jnp.concatenate([before, own_lo], axis=1), jnp.concatenate([ow...]
    another operation x3 -> x0, local copies, waits for them, and re-layouts: 0.74 us -> none  [the longest x1 0.74 us: ends(): jnp.stack(planes)]
    dot_general x2 -> x4, matrix products: 3.06 us -> 3.03 us  [ends(): lax.dot_general(select, planes, (((1,), (planes.ndim - 1,)), ((), ())), p...]
  transfers between devices with their start and end apart: 8 -> 8, of which waited for: 5 -> 6; matrix products, arithmetic and copies ran while one was open for 24% -> 6% of each run, Pallas kernels for 7% -> 7%
where the time goes in v12:
time: 64.9 us; the launch traced here: 63.9 us
  waiting for transfers between devices  29.5 us (45%)
  matrix products  9.24 us (14%)
  starting transfers between devices  7.21 us (11%)
  Pallas kernels  7.02 us (11%)
  local copies, waits for them, and re-layouts  6.14 us (9%)
  other arithmetic  3.74 us (6%)
  between operations  1.05 us (2%)
    ppermute x3, waiting for transfers between devices, member_gather(): got = lax.ppermute(acc, 'member', shift)  16.4 us
    ppermute x3, waiting for transfers between devices, member_scatter(): acc = acc + lax.ppermute(sent, 'member', shift)  12.9 us
    pallas_call x1, Pallas kernels, block_dynamics(): pl.pallas_call(block_kernel, out_shape=(out, out), in_specs=[vmem] * 5, o...  4.57 us
    ppermute x3, starting transfers between devices, member_scatter(): acc = acc + lax.ppermute(sent, 'member', shift)  3.77 us
    unnamed x24, local copies, waits for them, and re-layouts  3.52 us
    dot_general x4, matrix products, ends(): lax.dot_general(select, planes, (((1,), (planes.ndim - 1,)), ((), ())), p...  3.03 us
    pallas_call x1, Pallas kernels, strip_dynamics(): pl.pallas_call(strip_kernel, out_shape=(out, out), in_specs=[vmem], out_s...  2.45 us
    dot_general x1, matrix products, body(): localized = lax.dot_general(cols_b, alpha, batched(2, 1), precision=highest)  2.06 us
  transfers between devices with their start and end apart: 8, of which 6 were waited for; matrix products, arithmetic and copies ran while one was open for 6% of the time, Pallas kernels for 7%

profile of v12, /device:TPU:11, one launch (start us, length us, event | category | flops | bytes accessed | tf_op | source)
XLA Modules:
  0.0 63.9 jit_solution(2276382637242949046)
XLA Ops:
  0.7 2.1 %fusion.13 = f32[3,256,256]{2,1,0:T(8,128)S(1)} fusion(f32[3,256,256]{2,1,0:T(8,128)} %param.8, f32[256,256]{1,0:T(8,128)} %param.14), kind=kOutput, calls=%fused_computation.25 | convolution fusion | flops 603979776 | bytes 1835008 | tf_op jit(solution)/shard_map/dot_general | solution.py:152
  2.8 0.8 %fusion.10 = f32[3,256,256]{2,1,0:T(8,128)S(1)} fusion(f32[3,256,256]{2,1,0:T(8,128)S(1)} %fusion.13, f32[256,256]{1,0:T(8,128)S(1)} %copy-done), kind=kOutput, calls=%fused_computation.22 | convolution fusion | flops 603979776 | bytes 1835008 | tf_op jit(solution)/shard_map/dot_general | solution.py:153
  4.3 0.8 %dynamic-slice_bitcast_fusion.2 = (f32[192,256]{1,0:T(8,128)}, f32[192,256]{1,0:T(8,128)S(1)}, f32[192,256]{1,0:T(8,128)}) fusion(f32[4,192,256]{2,1,0:T(8,128)S(1)} %bitcast.141, s32[]{:T(128)S(6)} %select_n.105, s32[]{:T(128)S(6)} %select_n.109, s32[]{:T(128)S(6)} %select_n.107), kind=kLoop, calls=%fused_computation.55 | loop fusion | bytes 1179660 | tf_op jit(solution)/shard_map/jit(dynamic_index_in_dim)/squeeze | solution.py:105
  5.1 1.3 %collective-permute-start = (f32[192,256]{1,0:T(8,128)}, f32[192,256]{1,0:T(8,128)S(1)}, u32[]{:S(2)}, u32[]{:S(2)}) collective-permute-start(f32[192,256]{1,0:T(8,128)} %get-tuple-element.27), channel_id=1, source_target_pairs={{0,1},{1,2},{2,3},{3,0},{4,5},{5,6},{6,7},{7,4},{8,9},{9,10},{10,1... | collective-permute-start | bytes 589832 | tf_op jit(solution)/shard_map/ppermute | solution.py:106
  6.4 1.0 %collective-permute-start.1 = (f32[192,256]{1,0:T(8,128)}, f32[192,256]{1,0:T(8,128)}, u32[]{:S(2)}, u32[]{:S(2)}) collective-permute-start(f32[192,256]{1,0:T(8,128)} %get-tuple-element.29), channel_id=1, source_target_pairs={{0,2},{1,3},{2,0},{3,1},{4,6},{5,7},{6,4},{7,5},{8,10},{9,11},{10,... | collective-permute-start | bytes 589832 | tf_op jit(solution)/shard_map/ppermute | solution.py:106
  7.4 1.5 %collective-permute-start.2 = (f32[192,256]{1,0:T(8,128)S(1)}, f32[192,256]{1,0:T(8,128)}, u32[]{:S(2)}, u32[]{:S(2)}) collective-permute-start(f32[192,256]{1,0:T(8,128)S(1)} %get-tuple-element.28), channel_id=1, source_target_pairs={{0,3},{1,0},{2,1},{3,2},{4,7},{5,4},{6,5},{7,6},{8,11},{9,8},{10,9... | collective-permute-start | bytes 589832 | tf_op jit(solution)/shard_map/ppermute | solution.py:106
  8.9 1.1 %copy.10 = f32[3,256,256]{1,2,0:T(8,128)} copy(f32[3,256,256]{2,1,0:T(8,128)S(1)} %copy-done.3) | data formatting | bytes 1572864 | tf_op args[0]
  10.2 1.7 %convolution_bitcast_fusion.3 = f32[3,32,256]{2,1,0:T(8,128)S(1)} fusion(s32[32]{0:T(128)S(1)} %pad_add_fusion, f32[256,3,256]{2,0,1:T(8,128)} %param.11), kind=kOutput, calls=%fused_computation.8 | convolution fusion | flops 75505664 | bytes 884864 | tf_op jit(solution)/shard_map/dot_general | solution.py:166
  12.9 10.1 %collective-permute-done.1 = f32[192,256]{1,0:T(8,128)} collective-permute-done((f32[192,256]{1,0:T(8,128)}, f32[192,256]{1,0:T(8,128)}, u32[]{:S(2)}, u32[]{:S(2)}) %collective-permute-start.1) | collective-permute-done | bytes 196640 | tf_op jit(solution)/shard_map/ppermute | solution.py:106
  22.9 2.8 %collective-permute-done.2 = f32[192,256]{1,0:T(8,128)} collective-permute-done((f32[192,256]{1,0:T(8,128)S(1)}, f32[192,256]{1,0:T(8,128)}, u32[]{:S(2)}, u32[]{:S(2)}) %collective-permute-start.2) | collective-permute-done | bytes 196640 | tf_op jit(solution)/shard_map/ppermute | solution.py:106
  25.8 1.1 %fusion.24 = f32[192,256]{1,0:T(8,128)S(1)} fusion(f32[192,256]{1,0:T(8,128)} %collective-permute-done.2, f32[192,256]{1,0:T(8,128)} %collective-permute-done.1, f32[192,256]{1,0:T(8,128)S(1)} %collective-permute-done, f32[4,192,256]{2,1,0:T(8,128)S(1)} %bitcast.142, s32[]{:T(128)S(6)} %select_n.103), kind=kLoop, calls=%fused_computation.52 | loop fusion | flops 147456 | bytes 983044 | tf_op jit(solution)/shard_map/add | solution.py:106
  27.3 1.4 %collective-permute-start.5 = (f32[192,256]{1,0:T(8,128)S(1)}, f32[192,256]{1,0:T(8,128)S(1)}, u32[]{:S(2)}, u32[]{:S(2)}) collective-permute-start(f32[192,256]{1,0:T(8,128)S(1)} %fusion.24), channel_id=1, source_target_pairs={{0,3},{1,0},{2,1},{3,2},{4,7},{5,4},{6,5},{7,6},{8,11},{9,8},{10,9... | collective-permute-start | bytes 589832 | tf_op jit(solution)/shard_map/ppermute | solution.py:117
  28.7 4.1 %collective-permute-done.3 = f32[192,256]{1,0:T(8,128)S(1)} collective-permute-done((f32[192,256]{1,0:T(8,128)S(1)}, f32[192,256]{1,0:T(8,128)S(1)}, u32[]{:S(2)}, u32[]{:S(2)}) %collective-permute-start.3) | collective-permute-done | bytes 196640 | tf_op jit(solution)/shard_map/ppermute | solution.py:117
  32.9 10.7 %collective-permute-done.4 = f32[192,256]{1,0:T(8,128)S(1)} collective-permute-done((f32[192,256]{1,0:T(8,128)S(1)}, f32[192,256]{1,0:T(8,128)S(1)}, u32[]{:S(2)}, u32[]{:S(2)}) %collective-permute-start.4) | collective-permute-done | bytes 196640 | tf_op jit(solution)/shard_map/ppermute | solution.py:117
  43.7 1.5 %collective-permute-done.5 = f32[192,256]{1,0:T(8,128)S(1)} collective-permute-done((f32[192,256]{1,0:T(8,128)S(1)}, f32[192,256]{1,0:T(8,128)S(1)}, u32[]{:S(2)}, u32[]{:S(2)}) %collective-permute-start.5) | collective-permute-done | bytes 196640 | tf_op jit(solution)/shard_map/ppermute | solution.py:117
  46.7 1.6 %collective-permute-start.6 = (f32[10,8,256]{2,1,0:T(8,128)S(1)}, f32[10,8,256]{2,1,0:T(8,128)S(1)}, u32[]{:S(2)}, u32[]{:S(2)}) collective-permute-start(f32[10,8,256]{2,1,0:T(8,128)S(1)} %pad_maximum_fusion.5), channel_id=1, source_target_pairs={{0,4},{4,8},{8,12},{12,16},{16,20},{20,24},{24,28},{28,0},{1,5},{5... | collective-permute-start | bytes 245768 | tf_op jit(solution)/shard_map/ppermute | solution.py:18
  48.3 4.6 %shard_map.96 = (f32[3,256,256]{2,1,0:T(8,128)}, f32[3,256,256]{2,1,0:T(8,128)}) custom-call(f32[3,256,256]{2,1,0:T(8,128)} %bitcast.145, f32[3,256,256]{2,1,0:T(8,128)} %bitcast.140, f32[3,256,256]{2,1,0:T(8,128)} %bitcast.144, f32[3,256,256]{2,1,0:T(8,128)} %bitcast.143, f32[256,256]{1,0:T(8,128)} %dep_ref.1), custom_call_target="tpu_custom_call" | custom-call | flops 23592960 | bytes 5767168 | tf_op jit(solution)/shard_map/pallas_call | solution.py:60
  53.1 0.8 %pad_maximum_fusion.1.planes_ref = f32[2,10,24,256]{3,2,1,0:T(8,128)} fusion(f32[1,10,24,256]{3,2,1,0:T(8,128)S(1)} %maximum_bitcast_fusion.1, f32[1,10,24,256]{3,2,1,0:T(8,128)S(1)} %maximum_bitcast_fusion), kind=kLoop, calls=%fused_computation.19 | loop fusion | flops 122880 | bytes 983040 | tf_op jit(solution)/shard_map/stack | solution.py:187
  53.9 2.5 %shard_map.95 = (f32[2,3,24,256]{3,2,1,0:T(8,128)}, f32[2,3,24,256]{3,2,1,0:T(8,128)}) custom-call(f32[2,10,24,256]{3,2,1,0:T(8,128)} %pad_maximum_fusion.1.planes_ref), custom_call_target="tpu_custom_call" | custom-call | flops 4915200 | bytes 786432 | tf_op jit(solution)/shard_map/pallas_call | solution.py:85
  56.4 0.9 %slice_bitcast_fusion.17 = (f32[8,256]{1,0:T(8,128)S(1)}, f32[8,256]{1,0:T(8,128)S(1)}, f32[8,256]{1,0:T(8,128)S(1)}, f32[8,256]{1,0:T(8,128)S(1)}, f32[8,256]{1,0:T(8,128)S(1)}, /*index=5*/f32[8,256]{1,0:T(8,128)S(1)}) fusion(f32[2,3,24,256]{3,2,1,0:T(8,128)} %get-tuple-element.12), kind=kLoop, calls=%fused_computation.99 | loop fusion | bytes 98304 | tf_op jit(solution)/shard_map/slice | solution.py:196
  57.2 0.8 %slice_bitcast_fusion.11 = (f32[8,256]{1,0:T(8,128)S(1)}, f32[8,256]{1,0:T(8,128)S(1)}, f32[8,256]{1,0:T(8,128)S(1)}, f32[8,256]{1,0:T(8,128)S(1)}, f32[8,256]{1,0:T(8,128)S(1)}, /*index=5*/f32[8,256]{1,0:T(8,128)S(1)}) fusion(f32[2,3,24,256]{3,2,1,0:T(8,128)} %get-tuple-element.14), kind=kLoop, calls=%fused_computation.91 | loop fusion | bytes 98304 | tf_op jit(solution)/shard_map/slice | solution.py:196
  59.7 1.4 %fusion.8 = f32[3,256,256]{1,2,0:T(8,128)S(1)} fusion(f32[3,256,256]{2,1,0:T(8,128)S(1)} %fusion.1, f32[256,256]{1,0:T(8,128)S(1)} %copy-done), kind=kOutput, calls=%fused_computation.20 | convolution fusion | flops 603979776 | bytes 1835008 | tf_op jit(solution)/shard_map/dot_general | solution.py:204
  61.2 0.8 %fusion.2 = f32[3,256,256]{1,2,0:T(8,128)S(1)} fusion(f32[3,256,256]{1,2,0:T(8,128)S(1)} %copy-done.4, f32[3,256,256]{1,2,0:T(8,128)S(1)} %fusion.8, f32[256,256]{1,0:T(8,128)S(1)} %copy-done.7), kind=kOutput, calls=%fused_computation.5 | convolution fusion | flops 604176384 | bytes 2621440 | tf_op jit(solution)/shard_map/dot_general | solution.py:205
  62.0 1.1 %copy.11 = f32[3,256,256]{2,1,0:T(8,128)} copy(f32[3,256,256]{1,2,0:T(8,128)S(1)} %fusion.2) | data formatting | bytes 1572864
  (66 shorter events, 6.2 us)
Async XLA Ops:
  0.6 2.1 %copy-start = (f32[256,256]{1,0:T(8,128)S(1)}, f32[256,256]{1,0:T(8,128)}, u32[]{:S(2)}) copy-start(f32[256,256]{1,0:T(8,128)} %param.15) | copy-start | bytes 786436
  2.8 1.3 %copy-start.2 = (bf16[3,256,3,256]{3,1,2,0:T(8,128)(2,1)S(1)}, bf16[3,256,3,256]{3,1,2,0:T(8,128)(2,1)}, u32[]{:S(2)}) copy-start(bf16[3,256,3,256]{3,1,2,0:T(8,128)(2,1)} %param.9) | copy-start | bytes 3538948
  4.3 4.6 %copy-start.3 = (f32[3,256,256]{2,1,0:T(8,128)S(1)}, f32[3,256,256]{2,1,0:T(8,128)}, u32[]{:S(2)}) copy-start(f32[3,256,256]{2,1,0:T(8,128)} %param.8) | copy-start | bytes 2359300
  5.1 7.7 %collective-permute-start = (f32[192,256]{1,0:T(8,128)}, f32[192,256]{1,0:T(8,128)S(1)}, u32[]{:S(2)}, u32[]{:S(2)}) collective-permute-start(f32[192,256]{1,0:T(8,128)} %get-tuple-element.27), channel_id=1, source_target_pairs={{0,1},{1,2},{2,3},{3,0},{4,5},{5,6},{6,7},{7,4},{8,9},{9,10},{10,1... | collective-permute-start | bytes 589832 | tf_op jit(solution)/shard_map/ppermute | solution.py:106
  6.4 16.5 %collective-permute-start.1 = (f32[192,256]{1,0:T(8,128)}, f32[192,256]{1,0:T(8,128)}, u32[]{:S(2)}, u32[]{:S(2)}) collective-permute-start(f32[192,256]{1,0:T(8,128)} %get-tuple-element.29), channel_id=1, source_target_pairs={{0,2},{1,3},{2,0},{3,1},{4,6},{5,7},{6,4},{7,5},{8,10},{9,11},{10,... | collective-permute-start | bytes 589832 | tf_op jit(solution)/shard_map/ppermute | solution.py:106
  7.4 18.3 %collective-permute-start.2 = (f32[192,256]{1,0:T(8,128)S(1)}, f32[192,256]{1,0:T(8,128)}, u32[]{:S(2)}, u32[]{:S(2)}) collective-permute-start(f32[192,256]{1,0:T(8,128)S(1)} %get-tuple-element.28), channel_id=1, source_target_pairs={{0,3},{1,0},{2,1},{3,2},{4,7},{5,4},{6,5},{7,6},{8,11},{9,8},{10,9... | collective-permute-start | bytes 589832 | tf_op jit(solution)/shard_map/ppermute | solution.py:106
  10.1 1.8 %copy-start.5 = (f32[256,3,256]{2,0,1:T(8,128)S(1)}, f32[256,3,256]{2,0,1:T(8,128)}, u32[]{:S(2)}) copy-start(f32[256,3,256]{2,0,1:T(8,128)} %param.12) | copy-start | bytes 2359300
  10.1 2.4 %copy-start.8 = (f32[256,256]{1,0:T(8,128)S(1)}, f32[256,256]{1,0:T(8,128)}, u32[]{:S(2)}) copy-start(f32[256,256]{1,0:T(8,128)} %dep_ref.1) | copy-start | bytes 786436
  26.9 18.4 %copy-start.6 = (f32[256,3,256]{2,0,1:T(8,128)S(1)}, f32[256,3,256]{2,0,1:T(8,128)}, u32[]{:S(2)}) copy-start(f32[256,3,256]{2,0,1:T(8,128)} %param.10) | copy-start | bytes 2359300
  26.9 6.0 %collective-permute-start.3 = (f32[192,256]{1,0:T(8,128)S(1)}, f32[192,256]{1,0:T(8,128)S(1)}, u32[]{:S(2)}, u32[]{:S(2)}) collective-permute-start(f32[192,256]{1,0:T(8,128)S(1)} %fusion.24), channel_id=1, source_target_pairs={{0,1},{1,2},{2,3},{3,0},{4,5},{5,6},{6,7},{7,4},{8,9},{9,10},{10,1... | collective-permute-start | bytes 589832 | tf_op jit(solution)/shard_map/ppermute | solution.py:117
  26.9 16.7 %collective-permute-start.4 = (f32[192,256]{1,0:T(8,128)S(1)}, f32[192,256]{1,0:T(8,128)S(1)}, u32[]{:S(2)}, u32[]{:S(2)}) collective-permute-start(f32[192,256]{1,0:T(8,128)S(1)} %fusion.24), channel_id=1, source_target_pairs={{0,2},{1,3},{2,0},{3,1},{4,6},{5,7},{6,4},{7,5},{8,10},{9,11},{10,... | collective-permute-start | bytes 589832 | tf_op jit(solution)/shard_map/ppermute | solution.py:117
  27.3 17.9 %collective-permute-start.5 = (f32[192,256]{1,0:T(8,128)S(1)}, f32[192,256]{1,0:T(8,128)S(1)}, u32[]{:S(2)}, u32[]{:S(2)}) collective-permute-start(f32[192,256]{1,0:T(8,128)S(1)} %fusion.24), channel_id=1, source_target_pairs={{0,3},{1,0},{2,1},{3,2},{4,7},{5,4},{6,5},{7,6},{8,11},{9,8},{10,9... | collective-permute-start | bytes 589832 | tf_op jit(solution)/shard_map/ppermute | solution.py:117
  45.2 0.9 %copy-start.1 = (f32[4,192,256]{2,1,0:T(8,128)}, f32[4,192,256]{2,1,0:T(8,128)S(1)}, u32[]{:S(2)}) copy-start(f32[4,192,256]{2,1,0:T(8,128)S(1)} %bitcast_dynamic-update-slice_fusion) | copy-start | bytes 2359300
  46.7 6.2 %collective-permute-start.6 = (f32[10,8,256]{2,1,0:T(8,128)S(1)}, f32[10,8,256]{2,1,0:T(8,128)S(1)}, u32[]{:S(2)}, u32[]{:S(2)}) collective-permute-start(f32[10,8,256]{2,1,0:T(8,128)S(1)} %pad_maximum_fusion.5), channel_id=1, source_target_pairs={{0,4},{4,8},{8,12},{12,16},{16,20},{20,24},{24,28},{28,0},{1,5},{5... | collective-permute-start | bytes 245768 | tf_op jit(solution)/shard_map/ppermute | solution.py:18
  48.3 4.8 %collective-permute-start.7 = (f32[10,8,256]{2,1,0:T(8,128)S(1)}, f32[10,8,256]{2,1,0:T(8,128)S(1)}, u32[]{:S(2)}, u32[]{:S(2)}) collective-permute-start(f32[10,8,256]{2,1,0:T(8,128)S(1)} %pad_maximum_fusion.4), channel_id=1, source_target_pairs={{4,0},{8,4},{12,8},{16,12},{20,16},{24,20},{28,24},{0,28},{5,1},{9... | collective-permute-start | bytes 245768 | tf_op jit(solution)/shard_map/ppermute | solution.py:19
  53.9 5.2 %copy-start.9 = (f32[3,256,256]{2,1,0:T(8,128)S(1)}, f32[3,256,256]{2,1,0:T(8,128)}, u32[]{:S(2)}) copy-start(f32[3,256,256]{2,1,0:T(8,128)} %get-tuple-element.15) | copy-start | bytes 2359300
  56.4 2.8 %copy-start.10 = (f32[3,256,256]{2,1,0:T(8,128)S(1)}, f32[3,256,256]{2,1,0:T(8,128)}, u32[]{:S(2)}) copy-start(f32[3,256,256]{2,1,0:T(8,128)} %get-tuple-element.13) | copy-start | bytes 2359300
  59.7 1.5 %copy-start.4 = (f32[3,256,256]{1,2,0:T(8,128)S(1)}, f32[3,256,256]{1,2,0:T(8,128)}, u32[]{:S(2)}) copy-start(f32[3,256,256]{1,2,0:T(8,128)} %copy.10) | copy-start | bytes 2359300
  59.7 1.5 %copy-start.7 = (f32[256,256]{1,0:T(8,128)S(1)}, f32[256,256]{1,0:T(8,128)}, u32[]{:S(2)}) copy-start(f32[256,256]{1,0:T(8,128)} %param.14) | copy-start | bytes 786436

commit v13 on v11

--- a/solution.py
+++ b/solution.py
@@ -65,6 +65,34 @@
         cost_estimate=pl.CostEstimate(
             flops=120 * back.size, transcendentals=0, bytes_accessed=4 * (7 * back.size + dep.size)),
     )(back, incr, meas, prec, dep)
+
+
+def strip_kernel(before_ref, own_lo_ref, own_hi_ref, after_ref, pred_ref, adj_ref):
+    count = pred_ref.shape[0]
+    halo = before_ref.shape[1]
+    planes = before_ref.shape[0]
+    for k, (top, bottom) in enumerate(((before_ref, own_lo_ref), (own_hi_ref, after_ref))):
+        s = [jnp.concatenate([top[i], bottom[i]], axis=0) for i in range(planes)]
+        pred, adj = dynamics(*s[:count], s[-1], s[2 * count:3 * count], s[count:2 * count],
+                             col=1, row=0, slope=kernel_slope)
+        for i in range(count):
+            pred_ref[i, k * halo:(k + 1) * halo] = pred[i][halo:2 * halo]
+            adj_ref[i, k * halo:(k + 1) * halo] = adj[i][halo:2 * halo]
+
+
+def strip_dynamics(before, own_lo, own_hi, after):
+    count = (before.shape[0] - 1) // 3
+    vmem = pl.BlockSpec(memory_space=pltpu.VMEM)
+    out = jax.ShapeDtypeStruct((count, 2 * before.shape[1], before.shape[2]), before.dtype)
+    size = 2 * (before.size + own_lo.size)
+    return pl.pallas_call(
+        strip_kernel,
+        out_shape=(out, out),
+        in_specs=[vmem] * 4,
+        out_specs=(vmem, vmem),
+        cost_estimate=pl.CostEstimate(
+            flops=40 * size, transcendentals=0, bytes_accessed=4 * (size + 2 * out.size)),
+    )(before, own_lo, own_hi, after)
 
 
 def member_scatter(x):
@@ -152,22 +180,14 @@
     pred, adj = block_dynamics(background.transpose(1, 0, 2), incr, measured_values.transpose(1, 0, 2),
                                precision_factor.transpose(1, 0, 2), depth)
 
-    def strip(s):
-        return dynamics(*s[:nfield], s[-1], s[2 * nfield:3 * nfield], s[nfield:2 * nfield],
-                        col=1, row=0)
-
-    first = strip(jnp.concatenate([before, own_lo], axis=1))
-    last = strip(jnp.concatenate([own_hi, after], axis=1))
-    mid = slice(HALO, 2 * HALO)
+    edge_rows = strip_dynamics(before, own_lo, own_hi, after)
 
     placed = jnp.concatenate([jnp.arange(HALO), jnp.arange(nrow - HALO, nrow)])
     place = (placed[:, None] == jnp.arange(nrow)[None, :]).astype(jnp.float32)
     at_edge = (jnp.arange(nrow) < HALO) | (jnp.arange(nrow) >= nrow - HALO)
 
     def assemble(k):
-        rows = jnp.stack([jnp.concatenate([f[mid], g[mid]], axis=0)
-                          for f, g in zip(first[k], last[k])])
-        edge = lax.dot_general(rows, place, (((1,), (0,)), ((), ())), precision=highest)
+        edge = lax.dot_general(edge_rows[k], place, (((1,), (0,)), ((), ())), precision=highest)
         return jnp.stack([jnp.where(at_edge, edge[i], f) for i, f in enumerate((pred, adj)[k])],
                          axis=1)
 

time: 63.3 us -> 64.7 us (1.022); the launches traced: 62.1 us -> 64.3 us
  Pallas kernels: 4.53 us -> 6.86 us
  local copies, waits for them, and re-layouts: 15 us -> 13.1 us
  matrix products: 9.35 us -> 11 us
  starting transfers between devices: 7.17 us -> 8.23 us
  other arithmetic: 4.41 us -> 3.67 us
    slice x73 -> x0, local copies, waits for them, and re-layouts: 2.55 us -> none  [the longest x65 2.53 us: jnp_slope(): return 0.5 * (jnp.roll(f, -1, axis) - jnp.roll(f, 1, axis))]
    pallas_call x0 -> x1, Pallas kernels: none -> 2.31 us  [strip_dynamics(): pl.pallas_call(strip_kernel, out_shape=(out, out), in_specs=[vmem] * 4, o...]
    dot_general x2, matrix products: 1.05 us -> 2.71 us  [assemble(): lax.dot_general(edge_rows[k], place, (((1,), (0,)), ((), ())), precision=...]
    concatenate x1 -> x2, other arithmetic: 0.01 us -> 0.74 us  [body(): own_hi = jnp.concatenate([state_hi, fixed_hi], axis=0)]
    unnamed x30 -> x34, local copies, waits for them, and re-layouts: 10.8 us -> 11.4 us
  transfers between devices with their start and end apart: 8 -> 8, of which waited for: 5 -> 5; matrix products, arithmetic and copies ran while one was open for 24% -> 21% of each run, Pallas kernels for 7% -> 7%
where the time goes in v13:
time: 64.7 us; the launch traced here: 64.3 us
  waiting for transfers between devices  20.5 us (32%)
  local copies, waits for them, and re-layouts  13.1 us (20%)
  matrix products  11 us (17%)
  starting transfers between devices  8.23 us (13%)
  Pallas kernels  6.86 us (11%)
  other arithmetic  3.67 us (6%)
  between operations  0.97 us (1%)
    ppermute x3, waiting for transfers between devices, member_gather(): got = lax.ppermute(acc, 'member', shift)  16.4 us
    unnamed x34, local copies, waits for them, and re-layouts  11.4 us
    pallas_call x1, Pallas kernels, block_dynamics(): pl.pallas_call(block_kernel, out_shape=(out, out), in_specs=[vmem] * 5, o...  4.56 us
    ppermute x3, waiting for transfers between devices, member_scatter(): acc = acc + lax.ppermute(sent, 'member', shift)  4.06 us
    ppermute x3, starting transfers between devices, member_scatter(): acc = acc + lax.ppermute(sent, 'member', shift)  3.77 us
    dot_general x2, matrix products, ends(): lax.dot_general(select, jnp.stack(planes), (((1,), (2,)), ((), ())), prec...  3.06 us
    dot_general x2, matrix products, assemble(): lax.dot_general(edge_rows[k], place, (((1,), (0,)), ((), ())), precision=...  2.71 us
    pallas_call x1, Pallas kernels, strip_dynamics(): pl.pallas_call(strip_kernel, out_shape=(out, out), in_specs=[vmem] * 4, o...  2.31 us
  transfers between devices with their start and end apart: 8, of which 5 were waited for; matrix products, arithmetic and copies ran while one was open for 21% of the time, Pallas kernels for 7%

profile of v13, /device:TPU:11, one launch (start us, length us, event | category | flops | bytes accessed | tf_op | source)
XLA Modules:
  0.0 64.3 jit_solution(8173489581098354617)
XLA Ops:
  0.7 2.1 %fusion.13 = f32[3,256,256]{2,1,0:T(8,128)S(1)} fusion(f32[3,256,256]{2,1,0:T(8,128)} %param.8, f32[256,256]{1,0:T(8,128)} %param.14), kind=kOutput, calls=%fused_computation.22 | convolution fusion | flops 603979776 | bytes 1835008 | tf_op jit(solution)/shard_map/dot_general | solution.py:154
  4.8 1.3 %collective-permute-start = (f32[192,256]{1,0:T(8,128)}, f32[192,256]{1,0:T(8,128)}, u32[]{:S(2)}, u32[]{:S(2)}) collective-permute-start(f32[192,256]{1,0:T(8,128)} %get-tuple-element.27), channel_id=1, source_target_pairs={{0,1},{1,2},{2,3},{3,0},{4,5},{5,6},{6,7},{7,4},{8,9},{9,10},{10,1... | collective-permute-start | bytes 589832 | tf_op jit(solution)/shard_map/ppermute | solution.py:108
  6.1 1.0 %collective-permute-start.1 = (f32[192,256]{1,0:T(8,128)}, f32[192,256]{1,0:T(8,128)}, u32[]{:S(2)}, u32[]{:S(2)}) collective-permute-start(f32[192,256]{1,0:T(8,128)} %get-tuple-element.29), channel_id=1, source_target_pairs={{0,2},{1,3},{2,0},{3,1},{4,6},{5,7},{6,4},{7,5},{8,10},{9,11},{10,... | collective-permute-start | bytes 589832 | tf_op jit(solution)/shard_map/ppermute | solution.py:108
  7.1 1.5 %collective-permute-start.2 = (f32[192,256]{1,0:T(8,128)}, f32[192,256]{1,0:T(8,128)}, u32[]{:S(2)}, u32[]{:S(2)}) collective-permute-start(f32[192,256]{1,0:T(8,128)} %get-tuple-element.28), channel_id=1, source_target_pairs={{0,3},{1,0},{2,1},{3,2},{4,7},{5,4},{6,5},{7,6},{8,11},{9,8},{10,9... | collective-permute-start | bytes 589832 | tf_op jit(solution)/shard_map/ppermute | solution.py:108
  8.6 1.1 %copy.10 = f32[3,256,256]{1,2,0:T(8,128)} copy(f32[3,256,256]{2,1,0:T(8,128)S(1)} %copy-done.3) | data formatting | bytes 1572864 | tf_op args[0]
  9.8 1.8 %bitcast_dynamic-update-slice_fusion.6 = f32[7,256,256]{2,1,0:T(8,128)} fusion(f32[256,3,256]{2,0,1:T(8,128)} %param.11), kind=kLoop, calls=%fused_computation.45 | loop fusion | bytes 524288
  11.5 1.7 %bitcast_dynamic-update-slice_fusion.5 = f32[7,256,256]{2,1,0:T(8,128)} fusion(f32[7,256,256]{2,1,0:T(8,128)} %bitcast_dynamic-update-slice_fusion.6, f32[256,3,256]{2,0,1:T(8,128)} %param.11), kind=kLoop, calls=%fused_computation.44 | loop fusion | bytes 524288
  13.2 1.7 %bitcast_dynamic-update-slice_fusion.4 = f32[7,256,256]{2,1,0:T(8,128)} fusion(f32[7,256,256]{2,1,0:T(8,128)} %bitcast_dynamic-update-slice_fusion.5, f32[256,3,256]{2,0,1:T(8,128)} %param.11), kind=kLoop, calls=%fused_computation.43 | loop fusion | bytes 524288
  14.9 1.7 %bitcast_dynamic-update-slice_fusion.3 = f32[7,256,256]{2,1,0:T(8,128)} fusion(f32[7,256,256]{2,1,0:T(8,128)} %bitcast_dynamic-update-slice_fusion.4, f32[256,3,256]{2,0,1:T(8,128)} %param.12), kind=kLoop, calls=%fused_computation.42 | loop fusion | bytes 524288
  18.7 2.5 %convolution_bitcast_fusion.1 = f32[7,32,256]{2,1,0:T(8,128)S(1)} fusion(f32[7,256,256]{2,1,0:T(8,128)} %bitcast_dynamic-update-slice_fusion, s32[32]{0:T(128)S(1)} %pad_add_fusion), kind=kOutput, calls=%fused_computation.6 | convolution fusion | flops 176168960 | bytes 2064512 | tf_op jit(solution)/shard_map/dot_general | solution.py:168
  21.4 1.3 %collective-permute-done.1 = f32[192,256]{1,0:T(8,128)} collective-permute-done((f32[192,256]{1,0:T(8,128)}, f32[192,256]{1,0:T(8,128)}, u32[]{:S(2)}, u32[]{:S(2)}) %collective-permute-start.1) | collective-permute-done | bytes 196640 | tf_op jit(solution)/shard_map/ppermute | solution.py:108
  22.7 2.8 %collective-permute-done.2 = f32[192,256]{1,0:T(8,128)} collective-permute-done((f32[192,256]{1,0:T(8,128)}, f32[192,256]{1,0:T(8,128)}, u32[]{:S(2)}, u32[]{:S(2)}) %collective-permute-start.2) | collective-permute-done | bytes 196640 | tf_op jit(solution)/shard_map/ppermute | solution.py:108
  25.5 1.2 %fusion.24 = f32[192,256]{1,0:T(8,128)S(1)} fusion(f32[192,256]{1,0:T(8,128)} %collective-permute-done.2, f32[192,256]{1,0:T(8,128)} %collective-permute-done.1, f32[192,256]{1,0:T(8,128)} %collective-permute-done, f32[4,192,256]{2,1,0:T(8,128)S(1)} %bitcast.109, s32[]{:T(128)S(6)} %select_n.103), kind=kLoop, calls=%fused_computation.58 | loop fusion | flops 147456 | bytes 983044 | tf_op jit(solution)/shard_map/add | solution.py:108
  27.1 1.4 %collective-permute-start.5 = (f32[192,256]{1,0:T(8,128)S(1)}, f32[192,256]{1,0:T(8,128)S(1)}, u32[]{:S(2)}, u32[]{:S(2)}) collective-permute-start(f32[192,256]{1,0:T(8,128)S(1)} %fusion.24), channel_id=1, source_target_pairs={{0,3},{1,0},{2,1},{3,2},{4,7},{5,4},{6,5},{7,6},{8,11},{9,8},{10,9... | collective-permute-start | bytes 589832 | tf_op jit(solution)/shard_map/ppermute | solution.py:119
  28.5 4.1 %collective-permute-done.3 = f32[192,256]{1,0:T(8,128)S(1)} collective-permute-done((f32[192,256]{1,0:T(8,128)S(1)}, f32[192,256]{1,0:T(8,128)S(1)}, u32[]{:S(2)}, u32[]{:S(2)}) %collective-permute-start.3) | collective-permute-done | bytes 196640 | tf_op jit(solution)/shard_map/ppermute | solution.py:119
  32.7 10.7 %collective-permute-done.4 = f32[192,256]{1,0:T(8,128)S(1)} collective-permute-done((f32[192,256]{1,0:T(8,128)S(1)}, f32[192,256]{1,0:T(8,128)S(1)}, u32[]{:S(2)}, u32[]{:S(2)}) %collective-permute-start.4) | collective-permute-done | bytes 196640 | tf_op jit(solution)/shard_map/ppermute | solution.py:119
  43.4 1.5 %collective-permute-done.5 = f32[192,256]{1,0:T(8,128)S(1)} collective-permute-done((f32[192,256]{1,0:T(8,128)S(1)}, f32[192,256]{1,0:T(8,128)S(1)}, u32[]{:S(2)}, u32[]{:S(2)}) %collective-permute-start.5) | collective-permute-done | bytes 196640 | tf_op jit(solution)/shard_map/ppermute | solution.py:119
  46.4 2.2 %collective-permute-start.6 = (f32[10,8,256]{2,1,0:T(8,128)S(1)}, f32[10,8,256]{2,1,0:T(8,128)S(1)}, u32[]{:S(2)}, u32[]{:S(2)}) collective-permute-start(f32[10,8,256]{2,1,0:T(8,128)S(1)} %fusion.26), channel_id=1, source_target_pairs={{0,4},{4,8},{8,12},{12,16},{16,20},{20,24},{24,28},{28,0},{1,5},{5... | collective-permute-start | bytes 245768 | tf_op jit(solution)/shard_map/ppermute | solution.py:18
  48.5 4.6 %shard_map.96 = (f32[3,256,256]{2,1,0:T(8,128)}, f32[3,256,256]{2,1,0:T(8,128)}) custom-call(f32[3,256,256]{2,1,0:T(8,128)} %bitcast.112, f32[3,256,256]{2,1,0:T(8,128)} %bitcast.107, f32[3,256,256]{2,1,0:T(8,128)} %bitcast.110, f32[3,256,256]{2,1,0:T(8,128)} %bitcast.111, f32[256,256]{1,0:T(8,128)} %dep_ref.1), custom_call_target="tpu_custom_call" | custom-call | flops 23592960 | bytes 5767168 | tf_op jit(solution)/shard_map/pallas_call | solution.py:60
  54.5 2.3 %shard_map.95 = (f32[3,16,256]{2,1,0:T(8,128)}, f32[3,16,256]{2,1,0:T(8,128)}) custom-call(f32[10,8,256]{2,1,0:T(8,128)} %copy-done.12, f32[10,16,256]{2,1,0:T(8,128)} %get-tuple-element.38.own_lo_ref, f32[10,16,256]{2,1,0:T(8,128)} %get-tuple-element.37.own_hi_ref, f32[10,8,256]{2,1,0:T(8,128)} %copy-done.11), custom_call_target="tpu_custom_call" | custom-call | flops 4915200 | bytes 589824 | tf_op jit(solution)/shard_map/pallas_call | solution.py:88
  56.8 1.4 %fusion.33 = f32[3,256,256]{2,1,0:T(8,128)S(1)} fusion(f32[3,16,256]{2,1,0:T(8,128)} %get-tuple-element.14, s32[16]{0:T(128)S(1)} %pad_add_fusion.1), kind=kOutput, calls=%fused_computation.72 | convolution fusion | flops 37752832 | bytes 835648 | tf_op jit(solution)/shard_map/dot_general | solution.py:190
  58.2 1.3 %fusion.35 = f32[3,256,256]{2,1,0:T(8,128)S(1)} fusion(f32[3,16,256]{2,1,0:T(8,128)} %get-tuple-element.12, s32[16]{0:T(128)S(1)} %pad_add_fusion.1), kind=kOutput, calls=%fused_computation.73 | convolution fusion | flops 37752832 | bytes 835648 | tf_op jit(solution)/shard_map/dot_general | solution.py:190
  60.1 1.4 %fusion.8 = f32[3,256,256]{1,2,0:T(8,128)S(1)} fusion(f32[3,256,256]{2,1,0:T(8,128)S(1)} %fusion.1, f32[256,256]{1,0:T(8,128)S(1)} %copy-done), kind=kOutput, calls=%fused_computation.17 | convolution fusion | flops 603979776 | bytes 1835008 | tf_op jit(solution)/shard_map/dot_general | solution.py:196
  62.4 1.1 %copy.11 = f32[3,256,256]{2,1,0:T(8,128)} copy(f32[3,256,256]{1,2,0:T(8,128)S(1)} %fusion.2) | data formatting | bytes 1572864
  (62 shorter events, 9.7 us)
Async XLA Ops:
  0.6 2.2 %copy-start = (f32[256,256]{1,0:T(8,128)S(1)}, f32[256,256]{1,0:T(8,128)}, u32[]{:S(2)}) copy-start(f32[256,256]{1,0:T(8,128)} %param.15) | copy-start | bytes 786436
  0.7 3.0 %copy-start.2 = (bf16[3,256,3,256]{3,1,2,0:T(8,128)(2,1)S(1)}, bf16[3,256,3,256]{3,1,2,0:T(8,128)(2,1)}, u32[]{:S(2)}) copy-start(bf16[3,256,3,256]{3,1,2,0:T(8,128)(2,1)} %param.9) | copy-start | bytes 3538948
  3.7 4.9 %copy-start.3 = (f32[3,256,256]{2,1,0:T(8,128)S(1)}, f32[3,256,256]{2,1,0:T(8,128)}, u32[]{:S(2)}) copy-start(f32[3,256,256]{2,1,0:T(8,128)} %param.8) | copy-start | bytes 2359300
  4.8 16.6 %collective-permute-start = (f32[192,256]{1,0:T(8,128)}, f32[192,256]{1,0:T(8,128)}, u32[]{:S(2)}, u32[]{:S(2)}) collective-permute-start(f32[192,256]{1,0:T(8,128)} %get-tuple-element.27), channel_id=1, source_target_pairs={{0,1},{1,2},{2,3},{3,0},{4,5},{5,6},{6,7},{7,4},{8,9},{9,10},{10,1... | collective-permute-start | bytes 589832 | tf_op jit(solution)/shard_map/ppermute | solution.py:108
  6.1 16.5 %collective-permute-start.1 = (f32[192,256]{1,0:T(8,128)}, f32[192,256]{1,0:T(8,128)}, u32[]{:S(2)}, u32[]{:S(2)}) collective-permute-start(f32[192,256]{1,0:T(8,128)} %get-tuple-element.29), channel_id=1, source_target_pairs={{0,2},{1,3},{2,0},{3,1},{4,6},{5,7},{6,4},{7,5},{8,10},{9,11},{10,... | collective-permute-start | bytes 589832 | tf_op jit(solution)/shard_map/ppermute | solution.py:108
  7.1 18.3 %collective-permute-start.2 = (f32[192,256]{1,0:T(8,128)}, f32[192,256]{1,0:T(8,128)}, u32[]{:S(2)}, u32[]{:S(2)}) collective-permute-start(f32[192,256]{1,0:T(8,128)} %get-tuple-element.28), channel_id=1, source_target_pairs={{0,3},{1,0},{2,1},{3,2},{4,7},{5,4},{6,5},{7,6},{8,11},{9,8},{10,9... | collective-permute-start | bytes 589832 | tf_op jit(solution)/shard_map/ppermute | solution.py:108
  9.8 6.7 %copy-start.5 = (f32[256,3,256]{2,0,1:T(8,128)S(1)}, f32[256,3,256]{2,0,1:T(8,128)}, u32[]{:S(2)}) copy-start(f32[256,3,256]{2,0,1:T(8,128)} %param.12) | copy-start | bytes 2359300
  9.8 8.2 %copy-start.8 = (f32[256,256]{1,0:T(8,128)S(1)}, f32[256,256]{1,0:T(8,128)}, u32[]{:S(2)}) copy-start(f32[256,256]{1,0:T(8,128)} %dep_ref.1) | copy-start | bytes 786436
  21.4 23.7 %copy-start.6 = (f32[256,3,256]{2,0,1:T(8,128)S(1)}, f32[256,3,256]{2,0,1:T(8,128)}, u32[]{:S(2)}) copy-start(f32[256,3,256]{2,0,1:T(8,128)} %param.10) | copy-start | bytes 2359300
  26.6 6.0 %collective-permute-start.3 = (f32[192,256]{1,0:T(8,128)S(1)}, f32[192,256]{1,0:T(8,128)S(1)}, u32[]{:S(2)}, u32[]{:S(2)}) collective-permute-start(f32[192,256]{1,0:T(8,128)S(1)} %fusion.24), channel_id=1, source_target_pairs={{0,1},{1,2},{2,3},{3,0},{4,5},{5,6},{6,7},{7,4},{8,9},{9,10},{10,1... | collective-permute-start | bytes 589832 | tf_op jit(solution)/shard_map/ppermute | solution.py:119
  26.7 16.7 %collective-permute-start.4 = (f32[192,256]{1,0:T(8,128)S(1)}, f32[192,256]{1,0:T(8,128)S(1)}, u32[]{:S(2)}, u32[]{:S(2)}) collective-permute-start(f32[192,256]{1,0:T(8,128)S(1)} %fusion.24), channel_id=1, source_target_pairs={{0,2},{1,3},{2,0},{3,1},{4,6},{5,7},{6,4},{7,5},{8,10},{9,11},{10,... | collective-permute-start | bytes 589832 | tf_op jit(solution)/shard_map/ppermute | solution.py:119
  27.1 17.9 %collective-permute-start.5 = (f32[192,256]{1,0:T(8,128)S(1)}, f32[192,256]{1,0:T(8,128)S(1)}, u32[]{:S(2)}, u32[]{:S(2)}) collective-permute-start(f32[192,256]{1,0:T(8,128)S(1)} %fusion.24), channel_id=1, source_target_pairs={{0,3},{1,0},{2,1},{3,2},{4,7},{5,4},{6,5},{7,6},{8,11},{9,8},{10,9... | collective-permute-start | bytes 589832 | tf_op jit(solution)/shard_map/ppermute | solution.py:119
  45.0 0.9 %copy-start.1 = (f32[4,192,256]{2,1,0:T(8,128)}, f32[4,192,256]{2,1,0:T(8,128)S(1)}, u32[]{:S(2)}) copy-start(f32[4,192,256]{2,1,0:T(8,128)S(1)} %bitcast_dynamic-update-slice_fusion.7) | copy-start | bytes 2359300
  45.9 7.9 %collective-permute-start.7 = (f32[10,8,256]{2,1,0:T(8,128)S(1)}, f32[10,8,256]{2,1,0:T(8,128)S(1)}, u32[]{:S(2)}, u32[]{:S(2)}) collective-permute-start(f32[10,8,256]{2,1,0:T(8,128)S(1)} %fusion.25), channel_id=1, source_target_pairs={{4,0},{8,4},{12,8},{16,12},{20,16},{24,20},{28,24},{0,28},{5,1},{9... | collective-permute-start | bytes 245768 | tf_op jit(solution)/shard_map/ppermute | solution.py:19
  46.4 7.5 %collective-permute-start.6 = (f32[10,8,256]{2,1,0:T(8,128)S(1)}, f32[10,8,256]{2,1,0:T(8,128)S(1)}, u32[]{:S(2)}, u32[]{:S(2)}) collective-permute-start(f32[10,8,256]{2,1,0:T(8,128)S(1)} %fusion.26), channel_id=1, source_target_pairs={{0,4},{4,8},{8,12},{12,16},{16,20},{20,24},{24,28},{28,0},{1,5},{5... | collective-permute-start | bytes 245768 | tf_op jit(solution)/shard_map/ppermute | solution.py:18
  53.1 6.4 %copy-start.9 = (f32[3,256,256]{2,1,0:T(8,128)S(1)}, f32[3,256,256]{2,1,0:T(8,128)}, u32[]{:S(2)}) copy-start(f32[3,256,256]{2,1,0:T(8,128)} %get-tuple-element.15) | copy-start | bytes 2359300
  53.8 0.6 copy-start.11
  53.8 0.7 %copy-start.12 = (f32[10,8,256]{2,1,0:T(8,128)}, f32[10,8,256]{2,1,0:T(8,128)S(1)}, u32[]{:S(2)}) copy-start(f32[10,8,256]{2,1,0:T(8,128)S(1)} %collective-permute-done.6.before_ref) | copy-start | bytes 245764
  56.8 2.7 %copy-start.10 = (f32[3,256,256]{2,1,0:T(8,128)S(1)}, f32[3,256,256]{2,1,0:T(8,128)}, u32[]{:S(2)}) copy-start(f32[3,256,256]{2,1,0:T(8,128)} %get-tuple-element.13) | copy-start | bytes 2359300
  59.8 1.7 %copy-start.4 = (f32[3,256,256]{1,2,0:T(8,128)S(1)}, f32[3,256,256]{1,2,0:T(8,128)}, u32[]{:S(2)}) copy-start(f32[3,256,256]{1,2,0:T(8,128)} %copy.10) | copy-start | bytes 2359300
  59.8 1.7 %copy-start.7 = (f32[256,256]{1,0:T(8,128)S(1)}, f32[256,256]{1,0:T(8,128)}, u32[]{:S(2)}) copy-start(f32[256,256]{1,0:T(8,128)} %param.14) | copy-start | bytes 786436

commit v14 on v11

--- a/solution.py
+++ b/solution.py
@@ -154,10 +154,12 @@
 
     def strip(s):
         return dynamics(*s[:nfield], s[-1], s[2 * nfield:3 * nfield], s[nfield:2 * nfield],
-                        col=1, row=0)
+                        col=2, row=1)
 
-    first = strip(jnp.concatenate([before, own_lo], axis=1))
-    last = strip(jnp.concatenate([own_hi, after], axis=1))
+    both = strip(jnp.stack([jnp.concatenate([before, own_lo], axis=1),
+                            jnp.concatenate([own_hi, after], axis=1)], axis=1))
+    first = tuple(tuple(f[0] for f in part) for part in both)
+    last = tuple(tuple(f[1] for f in part) for part in both)
     mid = slice(HALO, 2 * HALO)
 
     placed = jnp.concatenate([jnp.arange(HALO), jnp.arange(nrow - HALO, nrow)])

time: 63.3 us -> 61.8 us (0.976); the launches traced: 62.1 us -> 61.4 us
  local copies, waits for them, and re-layouts: 15 us -> 13.9 us
  starting transfers between devices: 7.17 us -> 8.23 us
    slice x65 -> x32, local copies, waits for them, and re-layouts: 2.53 us -> 1.34 us  [jnp_slope(): return 0.5 * (jnp.roll(f, -1, axis) - jnp.roll(f, 1, axis))]
  transfers between devices with their start and end apart: 8 -> 8, of which waited for: 5 -> 5; matrix products, arithmetic and copies ran while one was open for 24% -> 21% of each run, Pallas kernels for 7% -> 7%
where the time goes in v14:
time: 61.8 us; the launch traced here: 61.4 us
  waiting for transfers between devices  20.4 us (33%)
  local copies, waits for them, and re-layouts  13.9 us (22%)
  matrix products  9.35 us (15%)
  starting transfers between devices  8.23 us (13%)
  Pallas kernels  4.53 us (7%)
  other arithmetic  3.81 us (6%)
  between operations  1.25 us (2%)
    ppermute x3, waiting for transfers between devices, member_gather(): got = lax.ppermute(acc, 'member', shift)  16.4 us
    unnamed x30, local copies, waits for them, and re-layouts  10.9 us
    pallas_call x1, Pallas kernels, block_dynamics(): pl.pallas_call(block_kernel, out_shape=(out, out), in_specs=[vmem] * 5, o...  4.53 us
    ppermute x3, waiting for transfers between devices, member_scatter(): acc = acc + lax.ppermute(sent, 'member', shift)  3.95 us
    ppermute x3, starting transfers between devices, member_scatter(): acc = acc + lax.ppermute(sent, 'member', shift)  3.77 us
    dot_general x2, matrix products, ends(): lax.dot_general(select, jnp.stack(planes), (((1,), (2,)), ((), ())), prec...  3.06 us
    ppermute x1, starting transfers between devices, shift_rows(): before = lax.ppermute(hi, 'tile', up)  2.15 us
    dot_general x1, matrix products, body(): localized = lax.dot_general(cols_b, alpha, batched(2, 1), precision=highest)  2.13 us
  transfers between devices with their start and end apart: 8, of which 5 were waited for; matrix products, arithmetic and copies ran while one was open for 21% of the time, Pallas kernels for 7%

profile of v14, /device:TPU:11, one launch (start us, length us, event | category | flops | bytes accessed | tf_op | source)
XLA Modules:
  0.0 61.4 jit_solution(16053404777374042797)
XLA Ops:
  0.7 2.1 %fusion.13 = f32[3,256,256]{2,1,0:T(8,128)S(1)} fusion(f32[3,256,256]{2,1,0:T(8,128)} %param.8, f32[256,256]{1,0:T(8,128)} %param.14), kind=kOutput, calls=%fused_computation.40 | convolution fusion | flops 603979776 | bytes 1835008 | tf_op jit(solution)/shard_map/dot_general | solution.py:126
  2.8 0.8 %fusion.10 = f32[3,256,256]{2,1,0:T(8,128)S(1)} fusion(f32[3,256,256]{2,1,0:T(8,128)S(1)} %fusion.13, f32[256,256]{1,0:T(8,128)S(1)} %copy-done), kind=kOutput, calls=%fused_computation.37 | convolution fusion | flops 603979776 | bytes 1835008 | tf_op jit(solution)/shard_map/dot_general | solution.py:127
  4.0 0.8 %dynamic-slice_bitcast_fusion.2 = (f32[192,256]{1,0:T(8,128)}, f32[192,256]{1,0:T(8,128)}, f32[192,256]{1,0:T(8,128)}) fusion(f32[4,192,256]{2,1,0:T(8,128)S(1)} %bitcast.209, s32[]{:T(128)S(6)} %select_n.105, s32[]{:T(128)S(6)} %select_n.109, s32[]{:T(128)S(6)} %select_n.107), kind=kLoop, calls=%fused_computation.77 | loop fusion | bytes 1179660 | tf_op jit(solution)/shard_map/jit(dynamic_index_in_dim)/squeeze | solution.py:79
  4.8 1.3 %collective-permute-start = (f32[192,256]{1,0:T(8,128)}, f32[192,256]{1,0:T(8,128)}, u32[]{:S(2)}, u32[]{:S(2)}) collective-permute-start(f32[192,256]{1,0:T(8,128)} %get-tuple-element.33), channel_id=1, source_target_pairs={{0,1},{1,2},{2,3},{3,0},{4,5},{5,6},{6,7},{7,4},{8,9},{9,10},{10,1... | collective-permute-start | bytes 589832 | tf_op jit(solution)/shard_map/ppermute | solution.py:80
  6.1 1.0 %collective-permute-start.1 = (f32[192,256]{1,0:T(8,128)}, f32[192,256]{1,0:T(8,128)}, u32[]{:S(2)}, u32[]{:S(2)}) collective-permute-start(f32[192,256]{1,0:T(8,128)} %get-tuple-element.35), channel_id=1, source_target_pairs={{0,2},{1,3},{2,0},{3,1},{4,6},{5,7},{6,4},{7,5},{8,10},{9,11},{10,... | collective-permute-start | bytes 589832 | tf_op jit(solution)/shard_map/ppermute | solution.py:80
  7.1 1.5 %collective-permute-start.2 = (f32[192,256]{1,0:T(8,128)}, f32[192,256]{1,0:T(8,128)}, u32[]{:S(2)}, u32[]{:S(2)}) collective-permute-start(f32[192,256]{1,0:T(8,128)} %get-tuple-element.34), channel_id=1, source_target_pairs={{0,3},{1,0},{2,1},{3,2},{4,7},{5,4},{6,5},{7,6},{8,11},{9,8},{10,9... | collective-permute-start | bytes 589832 | tf_op jit(solution)/shard_map/ppermute | solution.py:80
  8.6 1.1 %copy.19 = f32[3,256,256]{1,2,0:T(8,128)} copy(f32[3,256,256]{2,1,0:T(8,128)S(1)} %copy-done.3) | data formatting | bytes 1572864 | tf_op args[0]
  9.8 1.8 %bitcast_dynamic-update-slice_fusion.6 = f32[7,256,256]{2,1,0:T(8,128)} fusion(f32[256,3,256]{2,0,1:T(8,128)} %param.11), kind=kLoop, calls=%fused_computation.63 | loop fusion | bytes 524288
  11.6 1.7 %bitcast_dynamic-update-slice_fusion.5 = f32[7,256,256]{2,1,0:T(8,128)} fusion(f32[7,256,256]{2,1,0:T(8,128)} %bitcast_dynamic-update-slice_fusion.6, f32[256,3,256]{2,0,1:T(8,128)} %param.11), kind=kLoop, calls=%fused_computation.62 | loop fusion | bytes 524288
  13.2 1.7 %bitcast_dynamic-update-slice_fusion.4 = f32[7,256,256]{2,1,0:T(8,128)} fusion(f32[7,256,256]{2,1,0:T(8,128)} %bitcast_dynamic-update-slice_fusion.5, f32[256,3,256]{2,0,1:T(8,128)} %param.11), kind=kLoop, calls=%fused_computation.61 | loop fusion | bytes 524288
  14.9 1.7 %bitcast_dynamic-update-slice_fusion.3 = f32[7,256,256]{2,1,0:T(8,128)} fusion(f32[7,256,256]{2,1,0:T(8,128)} %bitcast_dynamic-update-slice_fusion.4, f32[256,3,256]{2,0,1:T(8,128)} %param.12), kind=kLoop, calls=%fused_computation.60 | loop fusion | bytes 524288
  18.9 2.5 %convolution_bitcast_fusion.1 = f32[7,32,256]{2,1,0:T(8,128)S(1)} fusion(f32[7,256,256]{2,1,0:T(8,128)} %bitcast_dynamic-update-slice_fusion, s32[32]{0:T(128)S(1)} %pad_add_fusion), kind=kOutput, calls=%fused_computation.24 | convolution fusion | flops 176168960 | bytes 2064512 | tf_op jit(solution)/shard_map/dot_general | solution.py:140
  21.5 1.1 %collective-permute-done.1 = f32[192,256]{1,0:T(8,128)} collective-permute-done((f32[192,256]{1,0:T(8,128)}, f32[192,256]{1,0:T(8,128)}, u32[]{:S(2)}, u32[]{:S(2)}) %collective-permute-start.1) | collective-permute-done | bytes 196640 | tf_op jit(solution)/shard_map/ppermute | solution.py:80
  22.7 2.8 %collective-permute-done.2 = f32[192,256]{1,0:T(8,128)} collective-permute-done((f32[192,256]{1,0:T(8,128)}, f32[192,256]{1,0:T(8,128)}, u32[]{:S(2)}, u32[]{:S(2)}) %collective-permute-start.2) | collective-permute-done | bytes 196640 | tf_op jit(solution)/shard_map/ppermute | solution.py:80
  25.5 1.2 %fusion.24 = f32[192,256]{1,0:T(8,128)S(1)} fusion(f32[192,256]{1,0:T(8,128)} %collective-permute-done.2, f32[192,256]{1,0:T(8,128)} %collective-permute-done.1, f32[192,256]{1,0:T(8,128)} %collective-permute-done, f32[4,192,256]{2,1,0:T(8,128)S(1)} %bitcast.210, s32[]{:T(128)S(6)} %select_n.103), kind=kLoop, calls=%fused_computation.74 | loop fusion | flops 147456 | bytes 983044 | tf_op jit(solution)/shard_map/add | solution.py:80
  27.1 1.4 %collective-permute-start.5 = (f32[192,256]{1,0:T(8,128)S(1)}, f32[192,256]{1,0:T(8,128)S(1)}, u32[]{:S(2)}, u32[]{:S(2)}) collective-permute-start(f32[192,256]{1,0:T(8,128)S(1)} %fusion.24), channel_id=1, source_target_pairs={{0,3},{1,0},{2,1},{3,2},{4,7},{5,4},{6,5},{7,6},{8,11},{9,8},{10,9... | collective-permute-start | bytes 589832 | tf_op jit(solution)/shard_map/ppermute | solution.py:91
  28.5 4.1 %collective-permute-done.3 = f32[192,256]{1,0:T(8,128)S(1)} collective-permute-done((f32[192,256]{1,0:T(8,128)S(1)}, f32[192,256]{1,0:T(8,128)S(1)}, u32[]{:S(2)}, u32[]{:S(2)}) %collective-permute-start.3) | collective-permute-done | bytes 196640 | tf_op jit(solution)/shard_map/ppermute | solution.py:91
  32.7 10.7 %collective-permute-done.4 = f32[192,256]{1,0:T(8,128)S(1)} collective-permute-done((f32[192,256]{1,0:T(8,128)S(1)}, f32[192,256]{1,0:T(8,128)S(1)}, u32[]{:S(2)}, u32[]{:S(2)}) %collective-permute-start.4) | collective-permute-done | bytes 196640 | tf_op jit(solution)/shard_map/ppermute | solution.py:91
  43.4 1.5 %collective-permute-done.5 = f32[192,256]{1,0:T(8,128)S(1)} collective-permute-done((f32[192,256]{1,0:T(8,128)S(1)}, f32[192,256]{1,0:T(8,128)S(1)}, u32[]{:S(2)}, u32[]{:S(2)}) %collective-permute-start.5) | collective-permute-done | bytes 196640 | tf_op jit(solution)/shard_map/ppermute | solution.py:91
  46.4 2.2 %collective-permute-start.6 = (f32[10,8,256]{2,1,0:T(8,128)S(1)}, f32[10,8,256]{2,1,0:T(8,128)S(1)}, u32[]{:S(2)}, u32[]{:S(2)}) collective-permute-start(f32[10,8,256]{2,1,0:T(8,128)S(1)} %pad_maximum_fusion.2), channel_id=1, source_target_pairs={{0,4},{4,8},{8,12},{12,16},{16,20},{20,24},{24,28},{28,0},{1,5},{5... | collective-permute-start | bytes 245768 | tf_op jit(solution)/shard_map/ppermute | solution.py:18
  48.6 4.5 %shard_map.95 = (f32[3,256,256]{2,1,0:T(8,128)}, f32[3,256,256]{2,1,0:T(8,128)}) custom-call(f32[3,256,256]{2,1,0:T(8,128)} %bitcast.213, f32[3,256,256]{2,1,0:T(8,128)} %bitcast.208, f32[3,256,256]{2,1,0:T(8,128)} %bitcast.211, f32[3,256,256]{2,1,0:T(8,128)} %bitcast.212, f32[256,256]{1,0:T(8,128)} %dep_ref.1), custom_call_target="tpu_custom_call" | custom-call | flops 23592960 | bytes 5767168 | tf_op jit(solution)/shard_map/pallas_call | solution.py:60
  57.3 1.4 %fusion.8 = f32[3,256,256]{1,2,0:T(8,128)S(1)} fusion(f32[3,256,256]{2,1,0:T(8,128)S(1)} %fusion.1, f32[256,256]{1,0:T(8,128)S(1)} %copy-done), kind=kOutput, calls=%fused_computation.35 | convolution fusion | flops 603979776 | bytes 1835008 | tf_op jit(solution)/shard_map/dot_general | solution.py:178
  58.7 0.9 %fusion.2 = f32[3,256,256]{1,2,0:T(8,128)S(1)} fusion(f32[3,256,256]{1,2,0:T(8,128)S(1)} %copy-done.4, f32[3,256,256]{1,2,0:T(8,128)S(1)} %fusion.8, f32[256,256]{1,0:T(8,128)S(1)} %copy-done.7), kind=kOutput, calls=%fused_computation.5 | convolution fusion | flops 604176384 | bytes 2621440 | tf_op jit(solution)/shard_map/dot_general | solution.py:179
  59.6 1.1 %copy.20 = f32[3,256,256]{2,1,0:T(8,128)} copy(f32[3,256,256]{1,2,0:T(8,128)S(1)} %fusion.2) | data formatting | bytes 1572864
  (113 shorter events, 9.1 us)
Async XLA Ops:
  0.6 2.2 %copy-start = (f32[256,256]{1,0:T(8,128)S(1)}, f32[256,256]{1,0:T(8,128)}, u32[]{:S(2)}) copy-start(f32[256,256]{1,0:T(8,128)} %param.15) | copy-start | bytes 786436
  0.7 3.0 %copy-start.2 = (bf16[3,256,3,256]{3,1,2,0:T(8,128)(2,1)S(1)}, bf16[3,256,3,256]{3,1,2,0:T(8,128)(2,1)}, u32[]{:S(2)}) copy-start(bf16[3,256,3,256]{3,1,2,0:T(8,128)(2,1)} %param.9) | copy-start | bytes 3538948
  3.7 4.9 %copy-start.3 = (f32[3,256,256]{2,1,0:T(8,128)S(1)}, f32[3,256,256]{2,1,0:T(8,128)}, u32[]{:S(2)}) copy-start(f32[3,256,256]{2,1,0:T(8,128)} %param.8) | copy-start | bytes 2359300
  4.8 16.7 %collective-permute-start = (f32[192,256]{1,0:T(8,128)}, f32[192,256]{1,0:T(8,128)}, u32[]{:S(2)}, u32[]{:S(2)}) collective-permute-start(f32[192,256]{1,0:T(8,128)} %get-tuple-element.33), channel_id=1, source_target_pairs={{0,1},{1,2},{2,3},{3,0},{4,5},{5,6},{6,7},{7,4},{8,9},{9,10},{10,1... | collective-permute-start | bytes 589832 | tf_op jit(solution)/shard_map/ppermute | solution.py:80
  6.1 16.5 %collective-permute-start.1 = (f32[192,256]{1,0:T(8,128)}, f32[192,256]{1,0:T(8,128)}, u32[]{:S(2)}, u32[]{:S(2)}) collective-permute-start(f32[192,256]{1,0:T(8,128)} %get-tuple-element.35), channel_id=1, source_target_pairs={{0,2},{1,3},{2,0},{3,1},{4,6},{5,7},{6,4},{7,5},{8,10},{9,11},{10,... | collective-permute-start | bytes 589832 | tf_op jit(solution)/shard_map/ppermute | solution.py:80
  7.1 18.3 %collective-permute-start.2 = (f32[192,256]{1,0:T(8,128)}, f32[192,256]{1,0:T(8,128)}, u32[]{:S(2)}, u32[]{:S(2)}) collective-permute-start(f32[192,256]{1,0:T(8,128)} %get-tuple-element.34), channel_id=1, source_target_pairs={{0,3},{1,0},{2,1},{3,2},{4,7},{5,4},{6,5},{7,6},{8,11},{9,8},{10,9... | collective-permute-start | bytes 589832 | tf_op jit(solution)/shard_map/ppermute | solution.py:80
  9.8 6.8 %copy-start.5 = (f32[256,3,256]{2,0,1:T(8,128)S(1)}, f32[256,3,256]{2,0,1:T(8,128)}, u32[]{:S(2)}) copy-start(f32[256,3,256]{2,0,1:T(8,128)} %param.12) | copy-start | bytes 2359300
  9.8 8.4 %copy-start.8 = (f32[256,256]{1,0:T(8,128)S(1)}, f32[256,256]{1,0:T(8,128)}, u32[]{:S(2)}) copy-start(f32[256,256]{1,0:T(8,128)} %dep_ref.1) | copy-start | bytes 786436
  21.5 23.5 %copy-start.6 = (f32[256,3,256]{2,0,1:T(8,128)S(1)}, f32[256,3,256]{2,0,1:T(8,128)}, u32[]{:S(2)}) copy-start(f32[256,3,256]{2,0,1:T(8,128)} %param.10) | copy-start | bytes 2359300
  26.6 6.0 %collective-permute-start.3 = (f32[192,256]{1,0:T(8,128)S(1)}, f32[192,256]{1,0:T(8,128)S(1)}, u32[]{:S(2)}, u32[]{:S(2)}) collective-permute-start(f32[192,256]{1,0:T(8,128)S(1)} %fusion.24), channel_id=1, source_target_pairs={{0,1},{1,2},{2,3},{3,0},{4,5},{5,6},{6,7},{7,4},{8,9},{9,10},{10,1... | collective-permute-start | bytes 589832 | tf_op jit(solution)/shard_map/ppermute | solution.py:91
  26.7 16.7 %collective-permute-start.4 = (f32[192,256]{1,0:T(8,128)S(1)}, f32[192,256]{1,0:T(8,128)S(1)}, u32[]{:S(2)}, u32[]{:S(2)}) collective-permute-start(f32[192,256]{1,0:T(8,128)S(1)} %fusion.24), channel_id=1, source_target_pairs={{0,2},{1,3},{2,0},{3,1},{4,6},{5,7},{6,4},{7,5},{8,10},{9,11},{10,... | collective-permute-start | bytes 589832 | tf_op jit(solution)/shard_map/ppermute | solution.py:91
  27.1 17.9 %collective-permute-start.5 = (f32[192,256]{1,0:T(8,128)S(1)}, f32[192,256]{1,0:T(8,128)S(1)}, u32[]{:S(2)}, u32[]{:S(2)}) collective-permute-start(f32[192,256]{1,0:T(8,128)S(1)} %fusion.24), channel_id=1, source_target_pairs={{0,3},{1,0},{2,1},{3,2},{4,7},{5,4},{6,5},{7,6},{8,11},{9,8},{10,9... | collective-permute-start | bytes 589832 | tf_op jit(solution)/shard_map/ppermute | solution.py:91
  45.0 0.9 %copy-start.1 = (f32[4,192,256]{2,1,0:T(8,128)}, f32[4,192,256]{2,1,0:T(8,128)S(1)}, u32[]{:S(2)}) copy-start(f32[4,192,256]{2,1,0:T(8,128)S(1)} %bitcast_dynamic-update-slice_fusion.7) | copy-start | bytes 2359300
  45.9 7.2 %collective-permute-start.7 = (f32[10,8,256]{2,1,0:T(8,128)S(1)}, f32[10,8,256]{2,1,0:T(8,128)S(1)}, u32[]{:S(2)}, u32[]{:S(2)}) collective-permute-start(f32[10,8,256]{2,1,0:T(8,128)S(1)} %pad_maximum_fusion.1), channel_id=1, source_target_pairs={{4,0},{8,4},{12,8},{16,12},{20,16},{24,20},{28,24},{0,28},{5,1},{9... | collective-permute-start | bytes 245768 | tf_op jit(solution)/shard_map/ppermute | solution.py:19
  46.4 6.7 %collective-permute-start.6 = (f32[10,8,256]{2,1,0:T(8,128)S(1)}, f32[10,8,256]{2,1,0:T(8,128)S(1)}, u32[]{:S(2)}, u32[]{:S(2)}) collective-permute-start(f32[10,8,256]{2,1,0:T(8,128)S(1)} %pad_maximum_fusion.2), channel_id=1, source_target_pairs={{0,4},{4,8},{8,12},{12,16},{16,20},{20,24},{24,28},{28,0},{1,5},{5... | collective-permute-start | bytes 245768 | tf_op jit(solution)/shard_map/ppermute | solution.py:18
  55.1 1.7 %copy-start.9 = (f32[3,256,256]{2,1,0:T(8,128)S(1)}, f32[3,256,256]{2,1,0:T(8,128)}, u32[]{:S(2)}) copy-start(f32[3,256,256]{2,1,0:T(8,128)} %get-tuple-element.11) | copy-start | bytes 2359300
  55.1 1.7 %copy-start.10 = (f32[3,256,256]{2,1,0:T(8,128)S(1)}, f32[3,256,256]{2,1,0:T(8,128)}, u32[]{:S(2)}) copy-start(f32[3,256,256]{2,1,0:T(8,128)} %get-tuple-element.10) | copy-start | bytes 2359300
  57.0 1.7 %copy-start.4 = (f32[3,256,256]{1,2,0:T(8,128)S(1)}, f32[3,256,256]{1,2,0:T(8,128)}, u32[]{:S(2)}) copy-start(f32[3,256,256]{1,2,0:T(8,128)} %copy.19) | copy-start | bytes 2359300
  57.0 1.7 %copy-start.7 = (f32[256,256]{1,0:T(8,128)S(1)}, f32[256,256]{1,0:T(8,128)}, u32[]{:S(2)}) copy-start(f32[256,256]{1,0:T(8,128)} %param.14) | copy-start | bytes 786436

commit v15 on v14

--- a/solution.py
+++ b/solution.py
@@ -141,13 +141,18 @@
                               precision=highest).transpose(1, 0, 2)
         return cut[:, : 2 * HALO], cut[:, 2 * HALO:]
 
-    scattered, fixed_lo, fixed_hi = lax.optimization_barrier((scattered,) + ends(fixed))
+    fixed_lo, fixed_hi = ends(fixed)
+    fixed_before, fixed_after = shift_rows(None, (fixed_lo[:, :HALO], fixed_hi[:, HALO:]))
+    scattered, fixed_lo, fixed_hi, fixed_before, fixed_after = lax.optimization_barrier(
+        (scattered, fixed_lo, fixed_hi, fixed_before, fixed_after))
     incr = member_gather(*scattered).reshape(nfield, ncol, nrow)
     state = [background[:, i] + incr[i] for i in range(nfield)]
     state_lo, state_hi = ends(state)
     own_lo = jnp.concatenate([state_lo, fixed_lo], axis=0)
     own_hi = jnp.concatenate([state_hi, fixed_hi], axis=0)
-    before, after = shift_rows(None, (own_lo[:, :HALO], own_hi[:, HALO:]))
+    state_before, state_after = shift_rows(None, (state_lo[:, :HALO], state_hi[:, HALO:]))
+    before = jnp.concatenate([state_before, fixed_before], axis=0)
+    after = jnp.concatenate([state_after, fixed_after], axis=0)
 
     pred, adj = block_dynamics(background.transpose(1, 0, 2), incr, measured_values.transpose(1, 0, 2),
                                precision_factor.transpose(1, 0, 2), depth)

time: 61.8 us -> 63.4 us (1.026)
  local copies, waits for them, and re-layouts: 13.9 us -> 5.52 us
  waiting for transfers between devices: 20.4 us -> 27.4 us
  starting transfers between devices: 8.23 us -> 11.1 us
  other arithmetic: 3.81 us -> 5.44 us
  matrix products: 9.35 us -> 7.86 us
    unnamed x30 -> x32, local copies, waits for them, and re-layouts: 10.9 us -> 2.48 us
    ppermute x3, waiting for transfers between devices: 3.95 us -> 10.9 us  [member_scatter(): acc = acc + lax.ppermute(sent, 'member', shift)]
    ppermute x1 -> x2, starting transfers between devices: 2.15 us -> 5 us  [shift_rows(): before = lax.ppermute(hi, 'tile', up)]
    another operation x2, other arithmetic: 0.04 us -> 1.68 us  [body(): jnp.stack([jnp.concatenate([before, own_lo], axis=1), jnp.concatenate([ow...]
    dot_general x2, matrix products: 3.06 us -> 1.58 us  [ends(): lax.dot_general(select, jnp.stack(planes), (((1,), (2,)), ((), ())), prec...]
    another operation x1, local copies, waits for them, and re-layouts: 0.72 us -> 0.02 us  [ends(): jnp.stack(planes)]
    slice x0 -> x2, local copies, waits for them, and re-layouts: none -> 0.66 us  [the longest x1 0.65 us: body(): fixed_lo[:, :HALO]]
  transfers between devices with their start and end apart: 8 -> 10, of which waited for: 5 -> 5; matrix products, arithmetic and copies ran while one was open for 21% -> 8% of each run, Pallas kernels for 7% -> 7%
where the time goes in v15:
time: 63.4 us; the launch traced here: 63.1 us
  waiting for transfers between devices  27.4 us (43%)
  starting transfers between devices  11.1 us (18%)
  matrix products  7.86 us (12%)
  local copies, waits for them, and re-layouts  5.52 us (9%)
  other arithmetic  5.44 us (9%)
  Pallas kernels  4.51 us (7%)
  between operations  1.32 us (2%)
    ppermute x3, waiting for transfers between devices, member_gather(): got = lax.ppermute(acc, 'member', shift)  16.4 us
    ppermute x3, waiting for transfers between devices, member_scatter(): acc = acc + lax.ppermute(sent, 'member', shift)  10.9 us
    ppermute x2, starting transfers between devices, shift_rows(): before = lax.ppermute(hi, 'tile', up)  5 us
    pallas_call x1, Pallas kernels, block_dynamics(): pl.pallas_call(block_kernel, out_shape=(out, out), in_specs=[vmem] * 5, o...  4.51 us
    ppermute x3, starting transfers between devices, member_scatter(): acc = acc + lax.ppermute(sent, 'member', shift)  3.77 us
    unnamed x32, local copies, waits for them, and re-layouts  2.48 us
    dot_general x1, matrix products, body(): localized = lax.dot_general(cols_b, alpha, batched(2, 1), precision=highest)  2.13 us
    ppermute x3, starting transfers between devices, member_gather(): got = lax.ppermute(acc, 'member', shift)  1.81 us
  transfers between devices with their start and end apart: 10, of which 5 were waited for; matrix products, arithmetic and copies ran while one was open for 8% of the time, Pallas kernels for 7%

profile of v15, /device:TPU:11, one launch (start us, length us, event | category | flops | bytes accessed | tf_op | source)
XLA Modules:
  0.0 63.1 jit_solution(714262786989246679)
XLA Ops:
  0.7 2.1 %fusion.13 = f32[3,256,256]{2,1,0:T(8,128)S(1)} fusion(f32[3,256,256]{2,1,0:T(8,128)} %param.8, f32[256,256]{1,0:T(8,128)} %param.14), kind=kOutput, calls=%fused_computation.40 | convolution fusion | flops 603979776 | bytes 1835008 | tf_op jit(solution)/shard_map/dot_general | solution.py:126
  2.8 0.8 %fusion.10 = f32[3,256,256]{2,1,0:T(8,128)S(1)} fusion(f32[3,256,256]{2,1,0:T(8,128)S(1)} %fusion.13, f32[256,256]{1,0:T(8,128)S(1)} %copy-done), kind=kOutput, calls=%fused_computation.37 | convolution fusion | flops 603979776 | bytes 1835008 | tf_op jit(solution)/shard_map/dot_general | solution.py:127
  4.0 0.8 %dynamic-slice_bitcast_fusion.2 = (f32[192,256]{1,0:T(8,128)}, f32[192,256]{1,0:T(8,128)}, f32[192,256]{1,0:T(8,128)}) fusion(f32[4,192,256]{2,1,0:T(8,128)S(1)} %bitcast.209, s32[]{:T(128)S(6)} %select_n.105, s32[]{:T(128)S(6)} %select_n.109, s32[]{:T(128)S(6)} %select_n.107), kind=kLoop, calls=%fused_computation.77 | loop fusion | bytes 1179660 | tf_op jit(solution)/shard_map/jit(dynamic_index_in_dim)/squeeze | solution.py:79
  4.9 1.3 %collective-permute-start = (f32[192,256]{1,0:T(8,128)}, f32[192,256]{1,0:T(8,128)}, u32[]{:S(2)}, u32[]{:S(2)}) collective-permute-start(f32[192,256]{1,0:T(8,128)} %get-tuple-element.37), channel_id=1, source_target_pairs={{0,1},{1,2},{2,3},{3,0},{4,5},{5,6},{6,7},{7,4},{8,9},{9,10},{10,1... | collective-permute-start | bytes 589832 | tf_op jit(solution)/shard_map/ppermute | solution.py:80
  6.2 1.0 %collective-permute-start.1 = (f32[192,256]{1,0:T(8,128)}, f32[192,256]{1,0:T(8,128)}, u32[]{:S(2)}, u32[]{:S(2)}) collective-permute-start(f32[192,256]{1,0:T(8,128)} %get-tuple-element.39), channel_id=1, source_target_pairs={{0,2},{1,3},{2,0},{3,1},{4,6},{5,7},{6,4},{7,5},{8,10},{9,11},{10,... | collective-permute-start | bytes 589832 | tf_op jit(solution)/shard_map/ppermute | solution.py:80
  7.2 1.5 %collective-permute-start.2 = (f32[192,256]{1,0:T(8,128)}, f32[192,256]{1,0:T(8,128)}, u32[]{:S(2)}, u32[]{:S(2)}) collective-permute-start(f32[192,256]{1,0:T(8,128)} %get-tuple-element.38), channel_id=1, source_target_pairs={{0,3},{1,0},{2,1},{3,2},{4,7},{5,4},{6,5},{7,6},{8,11},{9,8},{10,9... | collective-permute-start | bytes 589832 | tf_op jit(solution)/shard_map/ppermute | solution.py:80
  8.9 1.1 %convolution_bitcast_fusion.1 = f32[7,32,256]{2,1,0:T(8,128)S(1)} fusion(f32[7,256,256]{2,1,0:T(8,128)S(1)} %bitcast_dynamic-update-slice_fusion, s32[32]{0:T(128)S(1)} %pad_add_fusion), kind=kOutput, calls=%fused_computation.24 | convolution fusion | flops 176168960 | bytes 2064512 | tf_op jit(solution)/shard_map/dot_general | solution.py:140
  10.6 2.6 %collective-permute-start.3 = (f32[7,8,256]{2,1,0:T(8,128)}, f32[7,8,256]{2,1,0:T(8,128)}, u32[]{:S(2)}, u32[]{:S(2)}) collective-permute-start(f32[7,8,256]{2,1,0:T(8,128)} %get-tuple-element.45), channel_id=1, source_target_pairs={{0,4},{4,8},{8,12},{12,16},{16,20},{20,24},{24,28},{28,0},{1,5},{5... | collective-permute-start | bytes 172040 | tf_op jit(solution)/shard_map/ppermute | solution.py:18
  13.3 1.1 %copy.19 = f32[3,256,256]{1,2,0:T(8,128)} copy(f32[3,256,256]{2,1,0:T(8,128)S(1)} %copy-done.3) | data formatting | bytes 1572864 | tf_op args[0]
  14.5 8.1 %collective-permute-done.1 = f32[192,256]{1,0:T(8,128)} collective-permute-done((f32[192,256]{1,0:T(8,128)}, f32[192,256]{1,0:T(8,128)}, u32[]{:S(2)}, u32[]{:S(2)}) %collective-permute-start.1) | collective-permute-done | bytes 196640 | tf_op jit(solution)/shard_map/ppermute | solution.py:80
  22.7 2.8 %collective-permute-done.2 = f32[192,256]{1,0:T(8,128)} collective-permute-done((f32[192,256]{1,0:T(8,128)}, f32[192,256]{1,0:T(8,128)}, u32[]{:S(2)}, u32[]{:S(2)}) %collective-permute-start.2) | collective-permute-done | bytes 196640 | tf_op jit(solution)/shard_map/ppermute | solution.py:80
  25.5 1.2 %fusion.24 = f32[192,256]{1,0:T(8,128)S(1)} fusion(f32[192,256]{1,0:T(8,128)} %collective-permute-done.2, f32[192,256]{1,0:T(8,128)} %collective-permute-done.1, f32[192,256]{1,0:T(8,128)} %collective-permute-done, f32[4,192,256]{2,1,0:T(8,128)S(1)} %bitcast.210, s32[]{:T(128)S(6)} %select_n.103), kind=kLoop, calls=%fused_computation.74 | loop fusion | flops 147456 | bytes 983044 | tf_op jit(solution)/shard_map/add | solution.py:80
  27.1 1.4 %collective-permute-start.7 = (f32[192,256]{1,0:T(8,128)S(1)}, f32[192,256]{1,0:T(8,128)S(1)}, u32[]{:S(2)}, u32[]{:S(2)}) collective-permute-start(f32[192,256]{1,0:T(8,128)S(1)} %fusion.24), channel_id=1, source_target_pairs={{0,3},{1,0},{2,1},{3,2},{4,7},{5,4},{6,5},{7,6},{8,11},{9,8},{10,9... | collective-permute-start | bytes 589832 | tf_op jit(solution)/shard_map/ppermute | solution.py:91
  28.6 4.1 %collective-permute-done.5 = f32[192,256]{1,0:T(8,128)S(1)} collective-permute-done((f32[192,256]{1,0:T(8,128)S(1)}, f32[192,256]{1,0:T(8,128)S(1)}, u32[]{:S(2)}, u32[]{:S(2)}) %collective-permute-start.5) | collective-permute-done | bytes 196640 | tf_op jit(solution)/shard_map/ppermute | solution.py:91
  32.7 10.7 %collective-permute-done.6 = f32[192,256]{1,0:T(8,128)S(1)} collective-permute-done((f32[192,256]{1,0:T(8,128)S(1)}, f32[192,256]{1,0:T(8,128)S(1)}, u32[]{:S(2)}, u32[]{:S(2)}) %collective-permute-start.6) | collective-permute-done | bytes 196640 | tf_op jit(solution)/shard_map/ppermute | solution.py:91
  43.5 1.5 %collective-permute-done.7 = f32[192,256]{1,0:T(8,128)S(1)} collective-permute-done((f32[192,256]{1,0:T(8,128)S(1)}, f32[192,256]{1,0:T(8,128)S(1)}, u32[]{:S(2)}, u32[]{:S(2)}) %collective-permute-start.7) | collective-permute-done | bytes 196640 | tf_op jit(solution)/shard_map/ppermute | solution.py:91
  46.3 2.4 %collective-permute-start.8 = (f32[3,8,256]{2,1,0:T(8,128)S(1)}, f32[3,8,256]{2,1,0:T(8,128)S(1)}, u32[]{:S(2)}, u32[]{:S(2)}) collective-permute-start(f32[3,8,256]{2,1,0:T(8,128)S(1)} %get-tuple-element.51), channel_id=1, source_target_pairs={{0,4},{4,8},{8,12},{12,16},{16,20},{20,24},{24,28},{28,0},{1,5},{5... | collective-permute-start | bytes 73736 | tf_op jit(solution)/shard_map/ppermute | solution.py:18
  48.6 4.5 %shard_map.95 = (f32[3,256,256]{2,1,0:T(8,128)}, f32[3,256,256]{2,1,0:T(8,128)}) custom-call(f32[3,256,256]{2,1,0:T(8,128)} %bitcast.213, f32[3,256,256]{2,1,0:T(8,128)} %bitcast.208, f32[3,256,256]{2,1,0:T(8,128)} %bitcast.211, f32[3,256,256]{2,1,0:T(8,128)} %bitcast.212, f32[256,256]{1,0:T(8,128)} %dep_ref.1), custom_call_target="tpu_custom_call" | custom-call | flops 23592960 | bytes 5767168 | tf_op jit(solution)/shard_map/pallas_call | solution.py:60
  53.2 0.8 %maximum_bitcast_fusion.1 = f32[10,1,24,256]{3,2,0,1:T(8,128)S(1)} fusion(f32[7,8,256]{2,1,0:T(8,128)} %collective-permute-done.4, f32[3,8,256]{2,1,0:T(8,128)S(1)} %collective-permute-done.9, f32[7,16,256]{2,1,0:T(8,128)S(1)} %get-tuple-element.12, f32[3,16,256]{2,1,0:T(8,128)S(1)} %get-tuple-element.48), kind=kLoop, calls=%fused_computation.65 | loop fusion | flops 184320 | bytes 491520 | tf_op jit(solution)/shard_map/stack | solution.py:164
  54.0 0.8 %maximum_bitcast_fusion = f32[10,1,24,256]{3,2,0,1:T(8,128)S(1)} fusion(f32[7,16,256]{2,1,0:T(8,128)S(1)} %get-tuple-element.11, f32[3,16,256]{2,1,0:T(8,128)S(1)} %get-tuple-element.49, f32[7,8,256]{2,1,0:T(8,128)} %collective-permute-done.3, f32[3,8,256]{2,1,0:T(8,128)S(1)} %collective-permute-done.8), kind=kLoop, calls=%fused_computation.64 | loop fusion | flops 184320 | bytes 491520 | tf_op jit(solution)/shard_map/stack | solution.py:164
  59.0 1.4 %fusion.8 = f32[3,256,256]{1,2,0:T(8,128)S(1)} fusion(f32[3,256,256]{2,1,0:T(8,128)S(1)} %fusion.1, f32[256,256]{1,0:T(8,128)S(1)} %copy-done), kind=kOutput, calls=%fused_computation.35 | convolution fusion | flops 603979776 | bytes 1835008 | tf_op jit(solution)/shard_map/dot_general | solution.py:183
  60.4 0.9 %fusion.2 = f32[3,256,256]{1,2,0:T(8,128)S(1)} fusion(f32[3,256,256]{1,2,0:T(8,128)S(1)} %copy-done.4, f32[3,256,256]{1,2,0:T(8,128)S(1)} %fusion.8, f32[256,256]{1,0:T(8,128)S(1)} %copy-done.8), kind=kOutput, calls=%fused_computation.5 | convolution fusion | flops 604176384 | bytes 2621440 | tf_op jit(solution)/shard_map/dot_general | solution.py:184
  61.3 1.1 %copy.20 = f32[3,256,256]{2,1,0:T(8,128)} copy(f32[3,256,256]{1,2,0:T(8,128)S(1)} %fusion.2) | data formatting | bytes 1572864
  62.4 0.7 %fusion.22 = f32[64,3,256]{2,0,1:T(8,128)} fusion(s32[]{:T(128)S(6)} %select_n.116, f32[256,1,256]{2,0,1:T(8,128)S(1)} %get-tuple-element.30, f32[256,1,256]{2,0,1:T(8,128)S(1)} %get-tuple-element.29, f32[256,1,256]{2,0,1:T(8,128)S(1)} %get-tuple-element.28), kind=kLoop, calls=%fused_computation.67 | loop fusion | flops 98304 | bytes 983044 | tf_op jit(solution)/shard_map/stack | solution.py:178
  (119 shorter events, 6.8 us)
Async XLA Ops:
  0.6 2.2 %copy-start = (f32[256,256]{1,0:T(8,128)S(1)}, f32[256,256]{1,0:T(8,128)}, u32[]{:S(2)}) copy-start(f32[256,256]{1,0:T(8,128)} %param.15) | copy-start | bytes 786436
  0.7 3.0 %copy-start.2 = (bf16[3,256,3,256]{3,1,2,0:T(8,128)(2,1)S(1)}, bf16[3,256,3,256]{3,1,2,0:T(8,128)(2,1)}, u32[]{:S(2)}) copy-start(bf16[3,256,3,256]{3,1,2,0:T(8,128)(2,1)} %param.9) | copy-start | bytes 3538948
  3.7 4.9 %copy-start.5 = (f32[256,3,256]{2,0,1:T(8,128)S(1)}, f32[256,3,256]{2,0,1:T(8,128)}, u32[]{:S(2)}) copy-start(f32[256,3,256]{2,0,1:T(8,128)} %param.11) | copy-start | bytes 2359300
  4.0 4.7 %copy-start.6 = (f32[256,3,256]{2,0,1:T(8,128)S(1)}, f32[256,3,256]{2,0,1:T(8,128)}, u32[]{:S(2)}) copy-start(f32[256,3,256]{2,0,1:T(8,128)} %param.12) | copy-start | bytes 2359300
  4.9 4.1 %copy-start.9 = (f32[256,256]{1,0:T(8,128)S(1)}, f32[256,256]{1,0:T(8,128)}, u32[]{:S(2)}) copy-start(f32[256,256]{1,0:T(8,128)} %dep_ref.1) | copy-start | bytes 786436
  4.9 9.7 %collective-permute-start = (f32[192,256]{1,0:T(8,128)}, f32[192,256]{1,0:T(8,128)}, u32[]{:S(2)}, u32[]{:S(2)}) collective-permute-start(f32[192,256]{1,0:T(8,128)} %get-tuple-element.37), channel_id=1, source_target_pairs={{0,1},{1,2},{2,3},{3,0},{4,5},{5,6},{6,7},{7,4},{8,9},{9,10},{10,1... | collective-permute-start | bytes 589832 | tf_op jit(solution)/shard_map/ppermute | solution.py:80
  6.2 16.5 %collective-permute-start.1 = (f32[192,256]{1,0:T(8,128)}, f32[192,256]{1,0:T(8,128)}, u32[]{:S(2)}, u32[]{:S(2)}) collective-permute-start(f32[192,256]{1,0:T(8,128)} %get-tuple-element.39), channel_id=1, source_target_pairs={{0,2},{1,3},{2,0},{3,1},{4,6},{5,7},{6,4},{7,5},{8,10},{9,11},{10,... | collective-permute-start | bytes 589832 | tf_op jit(solution)/shard_map/ppermute | solution.py:80
  7.2 18.3 %collective-permute-start.2 = (f32[192,256]{1,0:T(8,128)}, f32[192,256]{1,0:T(8,128)}, u32[]{:S(2)}, u32[]{:S(2)}) collective-permute-start(f32[192,256]{1,0:T(8,128)} %get-tuple-element.38), channel_id=1, source_target_pairs={{0,3},{1,0},{2,1},{3,2},{4,7},{5,4},{6,5},{7,6},{8,11},{9,8},{10,9... | collective-permute-start | bytes 589832 | tf_op jit(solution)/shard_map/ppermute | solution.py:80
  8.8 4.5 %copy-start.3 = (f32[3,256,256]{2,1,0:T(8,128)S(1)}, f32[3,256,256]{2,1,0:T(8,128)}, u32[]{:S(2)}) copy-start(f32[3,256,256]{2,1,0:T(8,128)} %param.8) | copy-start | bytes 2359300
  10.6 16.0 %collective-permute-start.3 = (f32[7,8,256]{2,1,0:T(8,128)}, f32[7,8,256]{2,1,0:T(8,128)}, u32[]{:S(2)}, u32[]{:S(2)}) collective-permute-start(f32[7,8,256]{2,1,0:T(8,128)} %get-tuple-element.45), channel_id=1, source_target_pairs={{0,4},{4,8},{8,12},{12,16},{16,20},{20,24},{24,28},{28,0},{1,5},{5... | collective-permute-start | bytes 172040 | tf_op jit(solution)/shard_map/ppermute | solution.py:18
  13.3 13.4 %collective-permute-start.4 = (f32[7,8,256]{2,1,0:T(8,128)S(1)}, f32[7,8,256]{2,1,0:T(8,128)}, u32[]{:S(2)}, u32[]{:S(2)}) collective-permute-start(f32[7,8,256]{2,1,0:T(8,128)S(1)} %get-tuple-element.44), channel_id=1, source_target_pairs={{4,0},{8,4},{12,8},{16,12},{20,16},{24,20},{28,24},{0,28},{5,1},{9... | collective-permute-start | bytes 172040 | tf_op jit(solution)/shard_map/ppermute | solution.py:19
  14.5 30.5 %copy-start.7 = (f32[256,3,256]{2,0,1:T(8,128)S(1)}, f32[256,3,256]{2,0,1:T(8,128)}, u32[]{:S(2)}) copy-start(f32[256,3,256]{2,0,1:T(8,128)} %param.10) | copy-start | bytes 2359300
  26.7 6.0 %collective-permute-start.5 = (f32[192,256]{1,0:T(8,128)S(1)}, f32[192,256]{1,0:T(8,128)S(1)}, u32[]{:S(2)}, u32[]{:S(2)}) collective-permute-start(f32[192,256]{1,0:T(8,128)S(1)} %fusion.24), channel_id=1, source_target_pairs={{0,1},{1,2},{2,3},{3,0},{4,5},{5,6},{6,7},{7,4},{8,9},{9,10},{10,1... | collective-permute-start | bytes 589832 | tf_op jit(solution)/shard_map/ppermute | solution.py:91
  26.7 16.7 %collective-permute-start.6 = (f32[192,256]{1,0:T(8,128)S(1)}, f32[192,256]{1,0:T(8,128)S(1)}, u32[]{:S(2)}, u32[]{:S(2)}) collective-permute-start(f32[192,256]{1,0:T(8,128)S(1)} %fusion.24), channel_id=1, source_target_pairs={{0,2},{1,3},{2,0},{3,1},{4,6},{5,7},{6,4},{7,5},{8,10},{9,11},{10,... | collective-permute-start | bytes 589832 | tf_op jit(solution)/shard_map/ppermute | solution.py:91
  27.1 17.9 %collective-permute-start.7 = (f32[192,256]{1,0:T(8,128)S(1)}, f32[192,256]{1,0:T(8,128)S(1)}, u32[]{:S(2)}, u32[]{:S(2)}) collective-permute-start(f32[192,256]{1,0:T(8,128)S(1)} %fusion.24), channel_id=1, source_target_pairs={{0,3},{1,0},{2,1},{3,2},{4,7},{5,4},{6,5},{7,6},{8,11},{9,8},{10,9... | collective-permute-start | bytes 589832 | tf_op jit(solution)/shard_map/ppermute | solution.py:91
  45.0 3.6 %copy-start.1 = (f32[4,192,256]{2,1,0:T(8,128)}, f32[4,192,256]{2,1,0:T(8,128)S(1)}, u32[]{:S(2)}) copy-start(f32[4,192,256]{2,1,0:T(8,128)S(1)} %bitcast_dynamic-update-slice_fusion.7) | copy-start | bytes 2359300
  45.7 7.4 %collective-permute-start.9 = (f32[3,8,256]{2,1,0:T(8,128)S(1)}, f32[3,8,256]{2,1,0:T(8,128)S(1)}, u32[]{:S(2)}, u32[]{:S(2)}) collective-permute-start(f32[3,8,256]{2,1,0:T(8,128)S(1)} %get-tuple-element.50), channel_id=1, source_target_pairs={{4,0},{8,4},{12,8},{16,12},{20,16},{24,20},{28,24},{0,28},{5,1},{9... | collective-permute-start | bytes 73736 | tf_op jit(solution)/shard_map/ppermute | solution.py:19
  46.3 7.7 %collective-permute-start.8 = (f32[3,8,256]{2,1,0:T(8,128)S(1)}, f32[3,8,256]{2,1,0:T(8,128)S(1)}, u32[]{:S(2)}, u32[]{:S(2)}) collective-permute-start(f32[3,8,256]{2,1,0:T(8,128)S(1)} %get-tuple-element.51), channel_id=1, source_target_pairs={{0,4},{4,8},{8,12},{12,16},{16,20},{20,24},{24,28},{28,0},{1,5},{5... | collective-permute-start | bytes 73736 | tf_op jit(solution)/shard_map/ppermute | solution.py:18
  56.7 1.7 %copy-start.10 = (f32[3,256,256]{2,1,0:T(8,128)S(1)}, f32[3,256,256]{2,1,0:T(8,128)}, u32[]{:S(2)}) copy-start(f32[3,256,256]{2,1,0:T(8,128)} %get-tuple-element.15) | copy-start | bytes 2359300
  56.8 1.7 %copy-start.11 = (f32[3,256,256]{2,1,0:T(8,128)S(1)}, f32[3,256,256]{2,1,0:T(8,128)}, u32[]{:S(2)}) copy-start(f32[3,256,256]{2,1,0:T(8,128)} %get-tuple-element.14) | copy-start | bytes 2359300
  58.7 1.7 %copy-start.4 = (f32[3,256,256]{1,2,0:T(8,128)S(1)}, f32[3,256,256]{1,2,0:T(8,128)}, u32[]{:S(2)}) copy-start(f32[3,256,256]{1,2,0:T(8,128)} %copy.19) | copy-start | bytes 2359300
  58.7 1.7 %copy-start.8 = (f32[256,256]{1,0:T(8,128)S(1)}, f32[256,256]{1,0:T(8,128)}, u32[]{:S(2)}) copy-start(f32[256,256]{1,0:T(8,128)} %param.14) | copy-start | bytes 786436

commit v16 on v14

--- a/solution.py
+++ b/solution.py
@@ -112,6 +112,7 @@
 
 def body(alpha, ensemble, background, measured_values, precision_factor, depth, loc_cols, loc_rows):
     highest = lax.Precision.HIGHEST
+    high = lax.Precision.HIGH
     ncol, nfield, nrow = background.shape
     block_cols = ncol // lax.axis_size("member")
     col_start = lax.axis_index("member") * block_cols
@@ -123,8 +124,8 @@
     def batched(lhs_dim, rhs_dim):
         return (((lhs_dim,), (rhs_dim,)), ((0,), (0,)))
 
-    localized = lax.dot_general(cols_b, alpha, batched(2, 1), precision=highest)
-    localized = lax.dot_general(localized, rows_b, batched(2, 2), precision=highest)
+    localized = lax.dot_general(cols_b, alpha, batched(2, 1), precision=high)
+    localized = lax.dot_general(localized, rows_b, batched(2, 2), precision=high)
     ens = ensemble.astype(jnp.float32)
     partial = jnp.sum(ens * localized[:, :, None, :], axis=0)
     scattered = member_scatter(partial.transpose(1, 0, 2).reshape(nfield * ncol, nrow))
@@ -175,8 +176,8 @@
 
     predicted_final = lax.dynamic_slice_in_dim(assemble(0), col_start, block_cols, 0)
     projected = jnp.sum(ens * assemble(1)[None], axis=2)
-    rows_done = lax.dot_general(projected, rows_b, batched(2, 1), precision=highest)
-    cost_derivative = alpha + lax.dot_general(cols_b, rows_done, batched(1, 1), precision=highest)
+    rows_done = lax.dot_general(projected, rows_b, batched(2, 1), precision=high)
+    cost_derivative = alpha + lax.dot_general(cols_b, rows_done, batched(1, 1), precision=high)
     return (cost_derivative, predicted_final)
 
 

time: 61.8 us -> 60.3 us (0.976)
  matrix products: 9.35 us -> 7.78 us
    dot_general x4, matrix products: 5.25 us -> 3.67 us  [the longest x1 1.84 us: body(): localized = lax.dot_general(cols_b, alpha, batched(2, 1), precision=high)]
  transfers between devices with their start and end apart: 8 -> 8, of which waited for: 5 -> 5; matrix products, arithmetic and copies ran while one was open for 21% -> 22% of each run, Pallas kernels for 7% -> 8%
where the time goes in v16:
time: 60.3 us; the launch traced here: 59.9 us
  waiting for transfers between devices  20.4 us (34%)
  local copies, waits for them, and re-layouts  14 us (23%)
  starting transfers between devices  8.23 us (14%)
  matrix products  7.78 us (13%)
  Pallas kernels  4.53 us (8%)
  other arithmetic  3.81 us (6%)
  between operations  1.23 us (2%)
    ppermute x3, waiting for transfers between devices, member_gather(): got = lax.ppermute(acc, 'member', shift)  16.4 us
    unnamed x30, local copies, waits for them, and re-layouts  10.9 us
    pallas_call x1, Pallas kernels, block_dynamics(): pl.pallas_call(block_kernel, out_shape=(out, out), in_specs=[vmem] * 5, o...  4.53 us
    ppermute x3, waiting for transfers between devices, member_scatter(): acc = acc + lax.ppermute(sent, 'member', shift)  3.95 us
    ppermute x3, starting transfers between devices, member_scatter(): acc = acc + lax.ppermute(sent, 'member', shift)  3.77 us
    dot_general x2, matrix products, ends(): lax.dot_general(select, jnp.stack(planes), (((1,), (2,)), ((), ())), prec...  3.06 us
    ppermute x1, starting transfers between devices, shift_rows(): before = lax.ppermute(hi, 'tile', up)  2.15 us
    dot_general x1, matrix products, body(): localized = lax.dot_general(cols_b, alpha, batched(2, 1), precision=high)  1.84 us
  transfers between devices with their start and end apart: 8, of which 5 were waited for; matrix products, arithmetic and copies ran while one was open for 22% of the time, Pallas kernels for 8%

profile of v16, /device:TPU:11, one launch (start us, length us, event | category | flops | bytes accessed | tf_op | source)
XLA Modules:
  0.0 59.9 jit_solution(11405786832667244888)
XLA Ops:
  0.7 1.8 %fusion.13 = f32[3,256,256]{2,1,0:T(8,128)S(1)} fusion(f32[3,256,256]{2,1,0:T(8,128)} %param.8, f32[256,256]{1,0:T(8,128)} %param.14), kind=kOutput, calls=%fused_computation.40 | convolution fusion | flops 301989888 | bytes 1835008 | tf_op jit(solution)/shard_map/dot_general | solution.py:127
  3.4 0.8 %dynamic-slice_bitcast_fusion.2 = (f32[192,256]{1,0:T(8,128)}, f32[192,256]{1,0:T(8,128)}, f32[192,256]{1,0:T(8,128)}) fusion(f32[4,192,256]{2,1,0:T(8,128)S(1)} %bitcast.209, s32[]{:T(128)S(6)} %select_n.105, s32[]{:T(128)S(6)} %select_n.109, s32[]{:T(128)S(6)} %select_n.107), kind=kLoop, calls=%fused_computation.77 | loop fusion | bytes 1179660 | tf_op jit(solution)/shard_map/jit(dynamic_index_in_dim)/squeeze | solution.py:79
  4.2 1.3 %collective-permute-start = (f32[192,256]{1,0:T(8,128)}, f32[192,256]{1,0:T(8,128)}, u32[]{:S(2)}, u32[]{:S(2)}) collective-permute-start(f32[192,256]{1,0:T(8,128)} %get-tuple-element.33), channel_id=1, source_target_pairs={{0,1},{1,2},{2,3},{3,0},{4,5},{5,6},{6,7},{7,4},{8,9},{9,10},{10,1... | collective-permute-start | bytes 589832 | tf_op jit(solution)/shard_map/ppermute | solution.py:80
  5.5 1.0 %collective-permute-start.1 = (f32[192,256]{1,0:T(8,128)}, f32[192,256]{1,0:T(8,128)}, u32[]{:S(2)}, u32[]{:S(2)}) collective-permute-start(f32[192,256]{1,0:T(8,128)} %get-tuple-element.35), channel_id=1, source_target_pairs={{0,2},{1,3},{2,0},{3,1},{4,6},{5,7},{6,4},{7,5},{8,10},{9,11},{10,... | collective-permute-start | bytes 589832 | tf_op jit(solution)/shard_map/ppermute | solution.py:80
  6.5 1.5 %collective-permute-start.2 = (f32[192,256]{1,0:T(8,128)}, f32[192,256]{1,0:T(8,128)}, u32[]{:S(2)}, u32[]{:S(2)}) collective-permute-start(f32[192,256]{1,0:T(8,128)} %get-tuple-element.34), channel_id=1, source_target_pairs={{0,3},{1,0},{2,1},{3,2},{4,7},{5,4},{6,5},{7,6},{8,11},{9,8},{10,9... | collective-permute-start | bytes 589832 | tf_op jit(solution)/shard_map/ppermute | solution.py:80
  8.0 1.1 %copy.19 = f32[3,256,256]{1,2,0:T(8,128)} copy(f32[3,256,256]{2,1,0:T(8,128)S(1)} %copy-done.3) | data formatting | bytes 1572864 | tf_op args[0]
  9.2 1.8 %bitcast_dynamic-update-slice_fusion.6 = f32[7,256,256]{2,1,0:T(8,128)} fusion(f32[256,3,256]{2,0,1:T(8,128)} %param.11), kind=kLoop, calls=%fused_computation.63 | loop fusion | bytes 524288
  10.9 1.7 %bitcast_dynamic-update-slice_fusion.5 = f32[7,256,256]{2,1,0:T(8,128)} fusion(f32[7,256,256]{2,1,0:T(8,128)} %bitcast_dynamic-update-slice_fusion.6, f32[256,3,256]{2,0,1:T(8,128)} %param.11), kind=kLoop, calls=%fused_computation.62 | loop fusion | bytes 524288
  12.6 1.7 %bitcast_dynamic-update-slice_fusion.4 = f32[7,256,256]{2,1,0:T(8,128)} fusion(f32[7,256,256]{2,1,0:T(8,128)} %bitcast_dynamic-update-slice_fusion.5, f32[256,3,256]{2,0,1:T(8,128)} %param.11), kind=kLoop, calls=%fused_computation.61 | loop fusion | bytes 524288
  14.3 1.7 %bitcast_dynamic-update-slice_fusion.3 = f32[7,256,256]{2,1,0:T(8,128)} fusion(f32[7,256,256]{2,1,0:T(8,128)} %bitcast_dynamic-update-slice_fusion.4, f32[256,3,256]{2,0,1:T(8,128)} %param.12), kind=kLoop, calls=%fused_computation.60 | loop fusion | bytes 524288
  16.0 0.7 %bitcast_dynamic-update-slice_fusion.2 = f32[7,256,256]{2,1,0:T(8,128)} fusion(f32[7,256,256]{2,1,0:T(8,128)} %bitcast_dynamic-update-slice_fusion.3, f32[256,3,256]{2,0,1:T(8,128)S(1)} %copy-done.5), kind=kLoop, calls=%fused_computation.59 | loop fusion | bytes 524288
  17.5 0.7 %bitcast_dynamic-update-slice_fusion = f32[7,256,256]{2,1,0:T(8,128)} fusion(f32[7,256,256]{2,1,0:T(8,128)} %bitcast_dynamic-update-slice_fusion.1, f32[256,256]{1,0:T(8,128)S(1)} %copy-done.8), kind=kLoop, calls=%fused_computation.57 | loop fusion | bytes 524288 | tf_op jit(solution)/shard_map/stack | solution.py:141
  18.2 2.5 %convolution_bitcast_fusion.1 = f32[7,32,256]{2,1,0:T(8,128)S(1)} fusion(f32[7,256,256]{2,1,0:T(8,128)} %bitcast_dynamic-update-slice_fusion, s32[32]{0:T(128)S(1)} %pad_add_fusion), kind=kOutput, calls=%fused_computation.24 | convolution fusion | flops 176168960 | bytes 2064512 | tf_op jit(solution)/shard_map/dot_general | solution.py:141
  20.9 1.1 %collective-permute-done.1 = f32[192,256]{1,0:T(8,128)} collective-permute-done((f32[192,256]{1,0:T(8,128)}, f32[192,256]{1,0:T(8,128)}, u32[]{:S(2)}, u32[]{:S(2)}) %collective-permute-start.1) | collective-permute-done | bytes 196640 | tf_op jit(solution)/shard_map/ppermute | solution.py:80
  22.0 2.8 %collective-permute-done.2 = f32[192,256]{1,0:T(8,128)} collective-permute-done((f32[192,256]{1,0:T(8,128)}, f32[192,256]{1,0:T(8,128)}, u32[]{:S(2)}, u32[]{:S(2)}) %collective-permute-start.2) | collective-permute-done | bytes 196640 | tf_op jit(solution)/shard_map/ppermute | solution.py:80
  24.8 1.2 %fusion.24 = f32[192,256]{1,0:T(8,128)S(1)} fusion(f32[192,256]{1,0:T(8,128)} %collective-permute-done.2, f32[192,256]{1,0:T(8,128)} %collective-permute-done.1, f32[192,256]{1,0:T(8,128)} %collective-permute-done, f32[4,192,256]{2,1,0:T(8,128)S(1)} %bitcast.210, s32[]{:T(128)S(6)} %select_n.103), kind=kLoop, calls=%fused_computation.74 | loop fusion | flops 147456 | bytes 983044 | tf_op jit(solution)/shard_map/add | solution.py:80
  26.4 1.4 %collective-permute-start.5 = (f32[192,256]{1,0:T(8,128)S(1)}, f32[192,256]{1,0:T(8,128)S(1)}, u32[]{:S(2)}, u32[]{:S(2)}) collective-permute-start(f32[192,256]{1,0:T(8,128)S(1)} %fusion.24), channel_id=1, source_target_pairs={{0,3},{1,0},{2,1},{3,2},{4,7},{5,4},{6,5},{7,6},{8,11},{9,8},{10,9... | collective-permute-start | bytes 589832 | tf_op jit(solution)/shard_map/ppermute | solution.py:91
  27.9 4.1 %collective-permute-done.3 = f32[192,256]{1,0:T(8,128)S(1)} collective-permute-done((f32[192,256]{1,0:T(8,128)S(1)}, f32[192,256]{1,0:T(8,128)S(1)}, u32[]{:S(2)}, u32[]{:S(2)}) %collective-permute-start.3) | collective-permute-done | bytes 196640 | tf_op jit(solution)/shard_map/ppermute | solution.py:91
  32.1 10.7 %collective-permute-done.4 = f32[192,256]{1,0:T(8,128)S(1)} collective-permute-done((f32[192,256]{1,0:T(8,128)S(1)}, f32[192,256]{1,0:T(8,128)S(1)}, u32[]{:S(2)}, u32[]{:S(2)}) %collective-permute-start.4) | collective-permute-done | bytes 196640 | tf_op jit(solution)/shard_map/ppermute | solution.py:91
  42.8 1.5 %collective-permute-done.5 = f32[192,256]{1,0:T(8,128)S(1)} collective-permute-done((f32[192,256]{1,0:T(8,128)S(1)}, f32[192,256]{1,0:T(8,128)S(1)}, u32[]{:S(2)}, u32[]{:S(2)}) %collective-permute-start.5) | collective-permute-done | bytes 196640 | tf_op jit(solution)/shard_map/ppermute | solution.py:91
  45.8 2.2 %collective-permute-start.6 = (f32[10,8,256]{2,1,0:T(8,128)S(1)}, f32[10,8,256]{2,1,0:T(8,128)S(1)}, u32[]{:S(2)}, u32[]{:S(2)}) collective-permute-start(f32[10,8,256]{2,1,0:T(8,128)S(1)} %pad_maximum_fusion.2), channel_id=1, source_target_pairs={{0,4},{4,8},{8,12},{12,16},{16,20},{20,24},{24,28},{28,0},{1,5},{5... | collective-permute-start | bytes 245768 | tf_op jit(solution)/shard_map/ppermute | solution.py:18
  48.0 4.5 %shard_map.95 = (f32[3,256,256]{2,1,0:T(8,128)}, f32[3,256,256]{2,1,0:T(8,128)}) custom-call(f32[3,256,256]{2,1,0:T(8,128)} %bitcast.213, f32[3,256,256]{2,1,0:T(8,128)} %bitcast.208, f32[3,256,256]{2,1,0:T(8,128)} %bitcast.211, f32[3,256,256]{2,1,0:T(8,128)} %bitcast.212, f32[256,256]{1,0:T(8,128)} %dep_ref.1), custom_call_target="tpu_custom_call" | custom-call | flops 23592960 | bytes 5767168 | tf_op jit(solution)/shard_map/pallas_call | solution.py:60
  56.7 0.8 %fusion.8 = f32[3,256,256]{1,2,0:T(8,128)S(1)} fusion(f32[3,256,256]{2,1,0:T(8,128)S(1)} %fusion.1, f32[256,256]{1,0:T(8,128)S(1)} %copy-done), kind=kOutput, calls=%fused_computation.35 | convolution fusion | flops 301989888 | bytes 1835008 | tf_op jit(solution)/shard_map/dot_general | solution.py:179
  58.1 1.1 %copy.20 = f32[3,256,256]{2,1,0:T(8,128)} copy(f32[3,256,256]{1,2,0:T(8,128)S(1)} %fusion.2) | data formatting | bytes 1572864
  (113 shorter events, 8.8 us)
Async XLA Ops:
  0.6 1.9 %copy-start = (f32[256,256]{1,0:T(8,128)S(1)}, f32[256,256]{1,0:T(8,128)}, u32[]{:S(2)}) copy-start(f32[256,256]{1,0:T(8,128)} %param.15) | copy-start | bytes 786436
  0.7 2.4 %copy-start.2 = (bf16[3,256,3,256]{3,1,2,0:T(8,128)(2,1)S(1)}, bf16[3,256,3,256]{3,1,2,0:T(8,128)(2,1)}, u32[]{:S(2)}) copy-start(bf16[3,256,3,256]{3,1,2,0:T(8,128)(2,1)} %param.9) | copy-start | bytes 3538948
  3.1 4.9 %copy-start.3 = (f32[3,256,256]{2,1,0:T(8,128)S(1)}, f32[3,256,256]{2,1,0:T(8,128)}, u32[]{:S(2)}) copy-start(f32[3,256,256]{2,1,0:T(8,128)} %param.8) | copy-start | bytes 2359300
  4.2 16.7 %collective-permute-start = (f32[192,256]{1,0:T(8,128)}, f32[192,256]{1,0:T(8,128)}, u32[]{:S(2)}, u32[]{:S(2)}) collective-permute-start(f32[192,256]{1,0:T(8,128)} %get-tuple-element.33), channel_id=1, source_target_pairs={{0,1},{1,2},{2,3},{3,0},{4,5},{5,6},{6,7},{7,4},{8,9},{9,10},{10,1... | collective-permute-start | bytes 589832 | tf_op jit(solution)/shard_map/ppermute | solution.py:80
  5.5 16.5 %collective-permute-start.1 = (f32[192,256]{1,0:T(8,128)}, f32[192,256]{1,0:T(8,128)}, u32[]{:S(2)}, u32[]{:S(2)}) collective-permute-start(f32[192,256]{1,0:T(8,128)} %get-tuple-element.35), channel_id=1, source_target_pairs={{0,2},{1,3},{2,0},{3,1},{4,6},{5,7},{6,4},{7,5},{8,10},{9,11},{10,... | collective-permute-start | bytes 589832 | tf_op jit(solution)/shard_map/ppermute | solution.py:80
  6.5 18.3 %collective-permute-start.2 = (f32[192,256]{1,0:T(8,128)}, f32[192,256]{1,0:T(8,128)}, u32[]{:S(2)}, u32[]{:S(2)}) collective-permute-start(f32[192,256]{1,0:T(8,128)} %get-tuple-element.34), channel_id=1, source_target_pairs={{0,3},{1,0},{2,1},{3,2},{4,7},{5,4},{6,5},{7,6},{8,11},{9,8},{10,9... | collective-permute-start | bytes 589832 | tf_op jit(solution)/shard_map/ppermute | solution.py:80
  9.2 6.8 %copy-start.5 = (f32[256,3,256]{2,0,1:T(8,128)S(1)}, f32[256,3,256]{2,0,1:T(8,128)}, u32[]{:S(2)}) copy-start(f32[256,3,256]{2,0,1:T(8,128)} %param.12) | copy-start | bytes 2359300
  9.2 8.4 %copy-start.8 = (f32[256,256]{1,0:T(8,128)S(1)}, f32[256,256]{1,0:T(8,128)}, u32[]{:S(2)}) copy-start(f32[256,256]{1,0:T(8,128)} %dep_ref.1) | copy-start | bytes 786436
  20.9 23.5 %copy-start.6 = (f32[256,3,256]{2,0,1:T(8,128)S(1)}, f32[256,3,256]{2,0,1:T(8,128)}, u32[]{:S(2)}) copy-start(f32[256,3,256]{2,0,1:T(8,128)} %param.10) | copy-start | bytes 2359300
  26.0 6.0 %collective-permute-start.3 = (f32[192,256]{1,0:T(8,128)S(1)}, f32[192,256]{1,0:T(8,128)S(1)}, u32[]{:S(2)}, u32[]{:S(2)}) collective-permute-start(f32[192,256]{1,0:T(8,128)S(1)} %fusion.24), channel_id=1, source_target_pairs={{0,1},{1,2},{2,3},{3,0},{4,5},{5,6},{6,7},{7,4},{8,9},{9,10},{10,1... | collective-permute-start | bytes 589832 | tf_op jit(solution)/shard_map/ppermute | solution.py:91
  26.1 16.7 %collective-permute-start.4 = (f32[192,256]{1,0:T(8,128)S(1)}, f32[192,256]{1,0:T(8,128)S(1)}, u32[]{:S(2)}, u32[]{:S(2)}) collective-permute-start(f32[192,256]{1,0:T(8,128)S(1)} %fusion.24), channel_id=1, source_target_pairs={{0,2},{1,3},{2,0},{3,1},{4,6},{5,7},{6,4},{7,5},{8,10},{9,11},{10,... | collective-permute-start | bytes 589832 | tf_op jit(solution)/shard_map/ppermute | solution.py:91
  26.4 17.9 %collective-permute-start.5 = (f32[192,256]{1,0:T(8,128)S(1)}, f32[192,256]{1,0:T(8,128)S(1)}, u32[]{:S(2)}, u32[]{:S(2)}) collective-permute-start(f32[192,256]{1,0:T(8,128)S(1)} %fusion.24), channel_id=1, source_target_pairs={{0,3},{1,0},{2,1},{3,2},{4,7},{5,4},{6,5},{7,6},{8,11},{9,8},{10,9... | collective-permute-start | bytes 589832 | tf_op jit(solution)/shard_map/ppermute | solution.py:91
  44.4 0.9 %copy-start.1 = (f32[4,192,256]{2,1,0:T(8,128)}, f32[4,192,256]{2,1,0:T(8,128)S(1)}, u32[]{:S(2)}) copy-start(f32[4,192,256]{2,1,0:T(8,128)S(1)} %bitcast_dynamic-update-slice_fusion.7) | copy-start | bytes 2359300
  45.3 7.2 %collective-permute-start.7 = (f32[10,8,256]{2,1,0:T(8,128)S(1)}, f32[10,8,256]{2,1,0:T(8,128)S(1)}, u32[]{:S(2)}, u32[]{:S(2)}) collective-permute-start(f32[10,8,256]{2,1,0:T(8,128)S(1)} %pad_maximum_fusion.1), channel_id=1, source_target_pairs={{4,0},{8,4},{12,8},{16,12},{20,16},{24,20},{28,24},{0,28},{5,1},{9... | collective-permute-start | bytes 245768 | tf_op jit(solution)/shard_map/ppermute | solution.py:19
  45.8 6.7 %collective-permute-start.6 = (f32[10,8,256]{2,1,0:T(8,128)S(1)}, f32[10,8,256]{2,1,0:T(8,128)S(1)}, u32[]{:S(2)}, u32[]{:S(2)}) collective-permute-start(f32[10,8,256]{2,1,0:T(8,128)S(1)} %pad_maximum_fusion.2), channel_id=1, source_target_pairs={{0,4},{4,8},{8,12},{12,16},{16,20},{20,24},{24,28},{28,0},{1,5},{5... | collective-permute-start | bytes 245768 | tf_op jit(solution)/shard_map/ppermute | solution.py:18
  54.4 1.7 %copy-start.9 = (f32[3,256,256]{2,1,0:T(8,128)S(1)}, f32[3,256,256]{2,1,0:T(8,128)}, u32[]{:S(2)}) copy-start(f32[3,256,256]{2,1,0:T(8,128)} %get-tuple-element.11) | copy-start | bytes 2359300
  54.4 1.7 %copy-start.10 = (f32[3,256,256]{2,1,0:T(8,128)S(1)}, f32[3,256,256]{2,1,0:T(8,128)}, u32[]{:S(2)}) copy-start(f32[3,256,256]{2,1,0:T(8,128)} %get-tuple-element.10) | copy-start | bytes 2359300
  56.4 1.1 %copy-start.4 = (f32[3,256,256]{1,2,0:T(8,128)S(1)}, f32[3,256,256]{1,2,0:T(8,128)}, u32[]{:S(2)}) copy-start(f32[3,256,256]{1,2,0:T(8,128)} %copy.19) | copy-start | bytes 2359300
  56.4 1.2 %copy-start.7 = (f32[256,256]{1,0:T(8,128)S(1)}, f32[256,256]{1,0:T(8,128)}, u32[]{:S(2)}) copy-start(f32[256,256]{1,0:T(8,128)} %param.14) | copy-start | bytes 786436

commit v17 on v16

--- a/solution.py
+++ b/solution.py
@@ -111,7 +111,6 @@
 
 
 def body(alpha, ensemble, background, measured_values, precision_factor, depth, loc_cols, loc_rows):
-    highest = lax.Precision.HIGHEST
     high = lax.Precision.HIGH
     ncol, nfield, nrow = background.shape
     block_cols = ncol // lax.axis_size("member")
@@ -139,7 +138,7 @@
 
     def ends(planes):
         cut = lax.dot_general(select, jnp.stack(planes), (((1,), (2,)), ((), ())),
-                              precision=highest).transpose(1, 0, 2)
+                              precision=high).transpose(1, 0, 2)
         return cut[:, : 2 * HALO], cut[:, 2 * HALO:]
 
     scattered, fixed_lo, fixed_hi = lax.optimization_barrier((scattered,) + ends(fixed))
@@ -170,7 +169,7 @@
     def assemble(k):
         rows = jnp.stack([jnp.concatenate([f[mid], g[mid]], axis=0)
                           for f, g in zip(first[k], last[k])])
-        edge = lax.dot_general(rows, place, (((1,), (0,)), ((), ())), precision=highest)
+        edge = lax.dot_general(rows, place, (((1,), (0,)), ((), ())), precision=high)
         return jnp.stack([jnp.where(at_edge, edge[i], f) for i, f in enumerate((pred, adj)[k])],
                          axis=1)
 

time: 60.3 us -> 60.1 us (level)
  matrix products: 7.78 us -> 7 us
  transfers between devices with their start and end apart: 8 -> 8, of which waited for: 5 -> 5; matrix products, arithmetic and copies ran while one was open for 22% -> 21% of each run, Pallas kernels for 8% -> 8%
where the time goes in v17:
time: 60.1 us; the launch traced here: 59.7 us
  waiting for transfers between devices  20.7 us (34%)
  local copies, waits for them, and re-layouts  14.2 us (24%)
  starting transfers between devices  8.23 us (14%)
  matrix products  7 us (12%)
  Pallas kernels  4.53 us (8%)
  other arithmetic  3.8 us (6%)
  between operations  1.25 us (2%)
    ppermute x3, waiting for transfers between devices, member_gather(): got = lax.ppermute(acc, 'member', shift)  16.4 us
    unnamed x30, local copies, waits for them, and re-layouts  11.1 us
    pallas_call x1, Pallas kernels, block_dynamics(): pl.pallas_call(block_kernel, out_shape=(out, out), in_specs=[vmem] * 5, o...  4.53 us
    ppermute x3, waiting for transfers between devices, member_scatter(): acc = acc + lax.ppermute(sent, 'member', shift)  4.33 us
    ppermute x3, starting transfers between devices, member_scatter(): acc = acc + lax.ppermute(sent, 'member', shift)  3.77 us
    dot_general x2, matrix products, ends(): lax.dot_general(select, jnp.stack(planes), (((1,), (2,)), ((), ())), prec...  2.48 us
    ppermute x1, starting transfers between devices, shift_rows(): before = lax.ppermute(hi, 'tile', up)  2.15 us
    dot_general x1, matrix products, body(): localized = lax.dot_general(cols_b, alpha, batched(2, 1), precision=high)  1.84 us
  transfers between devices with their start and end apart: 8, of which 5 were waited for; matrix products, arithmetic and copies ran while one was open for 21% of the time, Pallas kernels for 8%

profile of v17, /device:TPU:11, one launch (start us, length us, event | category | flops | bytes accessed | tf_op | source)
XLA Modules:
  0.0 59.7 jit_solution(660535644609908239)
XLA Ops:
  0.7 1.8 %fusion.13 = f32[3,256,256]{2,1,0:T(8,128)S(1)} fusion(f32[3,256,256]{2,1,0:T(8,128)} %param.8, f32[256,256]{1,0:T(8,128)} %param.14), kind=kOutput, calls=%fused_computation.40 | convolution fusion | flops 301989888 | bytes 1835008 | tf_op jit(solution)/shard_map/dot_general | solution.py:126
  3.4 0.8 %dynamic-slice_bitcast_fusion.2 = (f32[192,256]{1,0:T(8,128)}, f32[192,256]{1,0:T(8,128)}, f32[192,256]{1,0:T(8,128)}) fusion(f32[4,192,256]{2,1,0:T(8,128)S(1)} %bitcast.209, s32[]{:T(128)S(6)} %select_n.105, s32[]{:T(128)S(6)} %select_n.109, s32[]{:T(128)S(6)} %select_n.107), kind=kLoop, calls=%fused_computation.77 | loop fusion | bytes 1179660 | tf_op jit(solution)/shard_map/jit(dynamic_index_in_dim)/squeeze | solution.py:79
  4.2 1.3 %collective-permute-start = (f32[192,256]{1,0:T(8,128)}, f32[192,256]{1,0:T(8,128)}, u32[]{:S(2)}, u32[]{:S(2)}) collective-permute-start(f32[192,256]{1,0:T(8,128)} %get-tuple-element.33), channel_id=1, source_target_pairs={{0,1},{1,2},{2,3},{3,0},{4,5},{5,6},{6,7},{7,4},{8,9},{9,10},{10,1... | collective-permute-start | bytes 589832 | tf_op jit(solution)/shard_map/ppermute | solution.py:80
  5.5 1.0 %collective-permute-start.1 = (f32[192,256]{1,0:T(8,128)}, f32[192,256]{1,0:T(8,128)}, u32[]{:S(2)}, u32[]{:S(2)}) collective-permute-start(f32[192,256]{1,0:T(8,128)} %get-tuple-element.35), channel_id=1, source_target_pairs={{0,2},{1,3},{2,0},{3,1},{4,6},{5,7},{6,4},{7,5},{8,10},{9,11},{10,... | collective-permute-start | bytes 589832 | tf_op jit(solution)/shard_map/ppermute | solution.py:80
  6.5 1.5 %collective-permute-start.2 = (f32[192,256]{1,0:T(8,128)}, f32[192,256]{1,0:T(8,128)}, u32[]{:S(2)}, u32[]{:S(2)}) collective-permute-start(f32[192,256]{1,0:T(8,128)} %get-tuple-element.34), channel_id=1, source_target_pairs={{0,3},{1,0},{2,1},{3,2},{4,7},{5,4},{6,5},{7,6},{8,11},{9,8},{10,9... | collective-permute-start | bytes 589832 | tf_op jit(solution)/shard_map/ppermute | solution.py:80
  8.0 1.1 %copy.19 = f32[3,256,256]{1,2,0:T(8,128)} copy(f32[3,256,256]{2,1,0:T(8,128)S(1)} %copy-done.3) | data formatting | bytes 1572864 | tf_op args[0]
  9.2 1.8 %bitcast_dynamic-update-slice_fusion.6 = f32[7,256,256]{2,1,0:T(8,128)} fusion(f32[256,3,256]{2,0,1:T(8,128)} %param.11), kind=kLoop, calls=%fused_computation.63 | loop fusion | bytes 524288
  10.9 1.7 %bitcast_dynamic-update-slice_fusion.5 = f32[7,256,256]{2,1,0:T(8,128)} fusion(f32[7,256,256]{2,1,0:T(8,128)} %bitcast_dynamic-update-slice_fusion.6, f32[256,3,256]{2,0,1:T(8,128)} %param.11), kind=kLoop, calls=%fused_computation.62 | loop fusion | bytes 524288
  12.6 1.7 %bitcast_dynamic-update-slice_fusion.4 = f32[7,256,256]{2,1,0:T(8,128)} fusion(f32[7,256,256]{2,1,0:T(8,128)} %bitcast_dynamic-update-slice_fusion.5, f32[256,3,256]{2,0,1:T(8,128)} %param.11), kind=kLoop, calls=%fused_computation.61 | loop fusion | bytes 524288
  14.3 1.7 %bitcast_dynamic-update-slice_fusion.3 = f32[7,256,256]{2,1,0:T(8,128)} fusion(f32[7,256,256]{2,1,0:T(8,128)} %bitcast_dynamic-update-slice_fusion.4, f32[256,3,256]{2,0,1:T(8,128)} %param.12), kind=kLoop, calls=%fused_computation.60 | loop fusion | bytes 524288
  16.0 0.7 %bitcast_dynamic-update-slice_fusion.2 = f32[7,256,256]{2,1,0:T(8,128)} fusion(f32[7,256,256]{2,1,0:T(8,128)} %bitcast_dynamic-update-slice_fusion.3, f32[256,3,256]{2,0,1:T(8,128)S(1)} %copy-done.5), kind=kLoop, calls=%fused_computation.59 | loop fusion | bytes 524288
  17.5 0.7 %bitcast_dynamic-update-slice_fusion = f32[7,256,256]{2,1,0:T(8,128)} fusion(f32[7,256,256]{2,1,0:T(8,128)} %bitcast_dynamic-update-slice_fusion.1, f32[256,256]{1,0:T(8,128)S(1)} %copy-done.8), kind=kLoop, calls=%fused_computation.57 | loop fusion | bytes 524288 | tf_op jit(solution)/shard_map/stack | solution.py:140
  18.2 2.1 %convolution_bitcast_fusion.1 = f32[7,32,256]{2,1,0:T(8,128)S(1)} fusion(f32[7,256,256]{2,1,0:T(8,128)} %bitcast_dynamic-update-slice_fusion, s32[32]{0:T(128)S(1)} %pad_add_fusion), kind=kOutput, calls=%fused_computation.24 | convolution fusion | flops 88088576 | bytes 2064512 | tf_op jit(solution)/shard_map/dot_general | solution.py:140
  20.5 1.5 %collective-permute-done.1 = f32[192,256]{1,0:T(8,128)} collective-permute-done((f32[192,256]{1,0:T(8,128)}, f32[192,256]{1,0:T(8,128)}, u32[]{:S(2)}, u32[]{:S(2)}) %collective-permute-start.1) | collective-permute-done | bytes 196640 | tf_op jit(solution)/shard_map/ppermute | solution.py:80
  22.0 2.8 %collective-permute-done.2 = f32[192,256]{1,0:T(8,128)} collective-permute-done((f32[192,256]{1,0:T(8,128)}, f32[192,256]{1,0:T(8,128)}, u32[]{:S(2)}, u32[]{:S(2)}) %collective-permute-start.2) | collective-permute-done | bytes 196640 | tf_op jit(solution)/shard_map/ppermute | solution.py:80
  24.8 1.2 %fusion.24 = f32[192,256]{1,0:T(8,128)S(1)} fusion(f32[192,256]{1,0:T(8,128)} %collective-permute-done.2, f32[192,256]{1,0:T(8,128)} %collective-permute-done.1, f32[192,256]{1,0:T(8,128)} %collective-permute-done, f32[4,192,256]{2,1,0:T(8,128)S(1)} %bitcast.210, s32[]{:T(128)S(6)} %select_n.103), kind=kLoop, calls=%fused_computation.74 | loop fusion | flops 147456 | bytes 983044 | tf_op jit(solution)/shard_map/add | solution.py:80
  26.4 1.4 %collective-permute-start.5 = (f32[192,256]{1,0:T(8,128)S(1)}, f32[192,256]{1,0:T(8,128)S(1)}, u32[]{:S(2)}, u32[]{:S(2)}) collective-permute-start(f32[192,256]{1,0:T(8,128)S(1)} %fusion.24), channel_id=1, source_target_pairs={{0,3},{1,0},{2,1},{3,2},{4,7},{5,4},{6,5},{7,6},{8,11},{9,8},{10,9... | collective-permute-start | bytes 589832 | tf_op jit(solution)/shard_map/ppermute | solution.py:91
  27.9 4.1 %collective-permute-done.3 = f32[192,256]{1,0:T(8,128)S(1)} collective-permute-done((f32[192,256]{1,0:T(8,128)S(1)}, f32[192,256]{1,0:T(8,128)S(1)}, u32[]{:S(2)}, u32[]{:S(2)}) %collective-permute-start.3) | collective-permute-done | bytes 196640 | tf_op jit(solution)/shard_map/ppermute | solution.py:91
  32.1 10.7 %collective-permute-done.4 = f32[192,256]{1,0:T(8,128)S(1)} collective-permute-done((f32[192,256]{1,0:T(8,128)S(1)}, f32[192,256]{1,0:T(8,128)S(1)}, u32[]{:S(2)}, u32[]{:S(2)}) %collective-permute-start.4) | collective-permute-done | bytes 196640 | tf_op jit(solution)/shard_map/ppermute | solution.py:91
  42.8 1.5 %collective-permute-done.5 = f32[192,256]{1,0:T(8,128)S(1)} collective-permute-done((f32[192,256]{1,0:T(8,128)S(1)}, f32[192,256]{1,0:T(8,128)S(1)}, u32[]{:S(2)}, u32[]{:S(2)}) %collective-permute-start.5) | collective-permute-done | bytes 196640 | tf_op jit(solution)/shard_map/ppermute | solution.py:91
  45.8 2.2 %collective-permute-start.6 = (f32[10,8,256]{2,1,0:T(8,128)S(1)}, f32[10,8,256]{2,1,0:T(8,128)S(1)}, u32[]{:S(2)}, u32[]{:S(2)}) collective-permute-start(f32[10,8,256]{2,1,0:T(8,128)S(1)} %pad_maximum_fusion.2), channel_id=1, source_target_pairs={{0,4},{4,8},{8,12},{12,16},{16,20},{20,24},{24,28},{28,0},{1,5},{5... | collective-permute-start | bytes 245768 | tf_op jit(solution)/shard_map/ppermute | solution.py:18
  48.0 4.5 %shard_map.95 = (f32[3,256,256]{2,1,0:T(8,128)}, f32[3,256,256]{2,1,0:T(8,128)}) custom-call(f32[3,256,256]{2,1,0:T(8,128)} %bitcast.213, f32[3,256,256]{2,1,0:T(8,128)} %bitcast.208, f32[3,256,256]{2,1,0:T(8,128)} %bitcast.211, f32[3,256,256]{2,1,0:T(8,128)} %bitcast.212, f32[256,256]{1,0:T(8,128)} %dep_ref.1), custom_call_target="tpu_custom_call" | custom-call | flops 23592960 | bytes 5767168 | tf_op jit(solution)/shard_map/pallas_call | solution.py:60
  56.5 0.8 %fusion.8 = f32[3,256,256]{1,2,0:T(8,128)S(1)} fusion(f32[3,256,256]{2,1,0:T(8,128)S(1)} %fusion.1, f32[256,256]{1,0:T(8,128)S(1)} %copy-done), kind=kOutput, calls=%fused_computation.35 | convolution fusion | flops 301989888 | bytes 1835008 | tf_op jit(solution)/shard_map/dot_general | solution.py:178
  57.9 1.1 %copy.20 = f32[3,256,256]{2,1,0:T(8,128)} copy(f32[3,256,256]{1,2,0:T(8,128)S(1)} %fusion.2) | data formatting | bytes 1572864
  (113 shorter events, 8.6 us)
Async XLA Ops:
  0.6 1.9 %copy-start = (f32[256,256]{1,0:T(8,128)S(1)}, f32[256,256]{1,0:T(8,128)}, u32[]{:S(2)}) copy-start(f32[256,256]{1,0:T(8,128)} %param.15) | copy-start | bytes 786436
  0.7 2.4 %copy-start.2 = (bf16[3,256,3,256]{3,1,2,0:T(8,128)(2,1)S(1)}, bf16[3,256,3,256]{3,1,2,0:T(8,128)(2,1)}, u32[]{:S(2)}) copy-start(bf16[3,256,3,256]{3,1,2,0:T(8,128)(2,1)} %param.9) | copy-start | bytes 3538948
  3.1 4.9 %copy-start.3 = (f32[3,256,256]{2,1,0:T(8,128)S(1)}, f32[3,256,256]{2,1,0:T(8,128)}, u32[]{:S(2)}) copy-start(f32[3,256,256]{2,1,0:T(8,128)} %param.8) | copy-start | bytes 2359300
  4.2 16.3 %collective-permute-start = (f32[192,256]{1,0:T(8,128)}, f32[192,256]{1,0:T(8,128)}, u32[]{:S(2)}, u32[]{:S(2)}) collective-permute-start(f32[192,256]{1,0:T(8,128)} %get-tuple-element.33), channel_id=1, source_target_pairs={{0,1},{1,2},{2,3},{3,0},{4,5},{5,6},{6,7},{7,4},{8,9},{9,10},{10,1... | collective-permute-start | bytes 589832 | tf_op jit(solution)/shard_map/ppermute | solution.py:80
  5.5 16.5 %collective-permute-start.1 = (f32[192,256]{1,0:T(8,128)}, f32[192,256]{1,0:T(8,128)}, u32[]{:S(2)}, u32[]{:S(2)}) collective-permute-start(f32[192,256]{1,0:T(8,128)} %get-tuple-element.35), channel_id=1, source_target_pairs={{0,2},{1,3},{2,0},{3,1},{4,6},{5,7},{6,4},{7,5},{8,10},{9,11},{10,... | collective-permute-start | bytes 589832 | tf_op jit(solution)/shard_map/ppermute | solution.py:80
  6.5 18.3 %collective-permute-start.2 = (f32[192,256]{1,0:T(8,128)}, f32[192,256]{1,0:T(8,128)}, u32[]{:S(2)}, u32[]{:S(2)}) collective-permute-start(f32[192,256]{1,0:T(8,128)} %get-tuple-element.34), channel_id=1, source_target_pairs={{0,3},{1,0},{2,1},{3,2},{4,7},{5,4},{6,5},{7,6},{8,11},{9,8},{10,9... | collective-permute-start | bytes 589832 | tf_op jit(solution)/shard_map/ppermute | solution.py:80
  9.2 6.8 %copy-start.5 = (f32[256,3,256]{2,0,1:T(8,128)S(1)}, f32[256,3,256]{2,0,1:T(8,128)}, u32[]{:S(2)}) copy-start(f32[256,3,256]{2,0,1:T(8,128)} %param.12) | copy-start | bytes 2359300
  9.2 8.4 %copy-start.8 = (f32[256,256]{1,0:T(8,128)S(1)}, f32[256,256]{1,0:T(8,128)}, u32[]{:S(2)}) copy-start(f32[256,256]{1,0:T(8,128)} %dep_ref.1) | copy-start | bytes 786436
  20.5 23.9 %copy-start.6 = (f32[256,3,256]{2,0,1:T(8,128)S(1)}, f32[256,3,256]{2,0,1:T(8,128)}, u32[]{:S(2)}) copy-start(f32[256,3,256]{2,0,1:T(8,128)} %param.10) | copy-start | bytes 2359300
  26.0 6.0 %collective-permute-start.3 = (f32[192,256]{1,0:T(8,128)S(1)}, f32[192,256]{1,0:T(8,128)S(1)}, u32[]{:S(2)}, u32[]{:S(2)}) collective-permute-start(f32[192,256]{1,0:T(8,128)S(1)} %fusion.24), channel_id=1, source_target_pairs={{0,1},{1,2},{2,3},{3,0},{4,5},{5,6},{6,7},{7,4},{8,9},{9,10},{10,1... | collective-permute-start | bytes 589832 | tf_op jit(solution)/shard_map/ppermute | solution.py:91
  26.1 16.7 %collective-permute-start.4 = (f32[192,256]{1,0:T(8,128)S(1)}, f32[192,256]{1,0:T(8,128)S(1)}, u32[]{:S(2)}, u32[]{:S(2)}) collective-permute-start(f32[192,256]{1,0:T(8,128)S(1)} %fusion.24), channel_id=1, source_target_pairs={{0,2},{1,3},{2,0},{3,1},{4,6},{5,7},{6,4},{7,5},{8,10},{9,11},{10,... | collective-permute-start | bytes 589832 | tf_op jit(solution)/shard_map/ppermute | solution.py:91
  26.4 17.9 %collective-permute-start.5 = (f32[192,256]{1,0:T(8,128)S(1)}, f32[192,256]{1,0:T(8,128)S(1)}, u32[]{:S(2)}, u32[]{:S(2)}) collective-permute-start(f32[192,256]{1,0:T(8,128)S(1)} %fusion.24), channel_id=1, source_target_pairs={{0,3},{1,0},{2,1},{3,2},{4,7},{5,4},{6,5},{7,6},{8,11},{9,8},{10,9... | collective-permute-start | bytes 589832 | tf_op jit(solution)/shard_map/ppermute | solution.py:91
  44.4 0.9 %copy-start.1 = (f32[4,192,256]{2,1,0:T(8,128)}, f32[4,192,256]{2,1,0:T(8,128)S(1)}, u32[]{:S(2)}) copy-start(f32[4,192,256]{2,1,0:T(8,128)S(1)} %bitcast_dynamic-update-slice_fusion.7) | copy-start | bytes 2359300
  45.3 7.2 %collective-permute-start.7 = (f32[10,8,256]{2,1,0:T(8,128)S(1)}, f32[10,8,256]{2,1,0:T(8,128)S(1)}, u32[]{:S(2)}, u32[]{:S(2)}) collective-permute-start(f32[10,8,256]{2,1,0:T(8,128)S(1)} %pad_maximum_fusion.1), channel_id=1, source_target_pairs={{4,0},{8,4},{12,8},{16,12},{20,16},{24,20},{28,24},{0,28},{5,1},{9... | collective-permute-start | bytes 245768 | tf_op jit(solution)/shard_map/ppermute | solution.py:19
  45.8 6.7 %collective-permute-start.6 = (f32[10,8,256]{2,1,0:T(8,128)S(1)}, f32[10,8,256]{2,1,0:T(8,128)S(1)}, u32[]{:S(2)}, u32[]{:S(2)}) collective-permute-start(f32[10,8,256]{2,1,0:T(8,128)S(1)} %pad_maximum_fusion.2), channel_id=1, source_target_pairs={{0,4},{4,8},{8,12},{12,16},{16,20},{20,24},{24,28},{28,0},{1,5},{5... | collective-permute-start | bytes 245768 | tf_op jit(solution)/shard_map/ppermute | solution.py:18
  54.4 1.5 %copy-start.9 = (f32[3,256,256]{2,1,0:T(8,128)S(1)}, f32[3,256,256]{2,1,0:T(8,128)}, u32[]{:S(2)}) copy-start(f32[3,256,256]{2,1,0:T(8,128)} %get-tuple-element.11) | copy-start | bytes 2359300
  54.4 1.5 %copy-start.10 = (f32[3,256,256]{2,1,0:T(8,128)S(1)}, f32[3,256,256]{2,1,0:T(8,128)}, u32[]{:S(2)}) copy-start(f32[3,256,256]{2,1,0:T(8,128)} %get-tuple-element.10) | copy-start | bytes 2359300
  56.2 1.1 %copy-start.4 = (f32[3,256,256]{1,2,0:T(8,128)S(1)}, f32[3,256,256]{1,2,0:T(8,128)}, u32[]{:S(2)}) copy-start(f32[3,256,256]{1,2,0:T(8,128)} %copy.19) | copy-start | bytes 2359300
  56.2 1.2 %copy-start.7 = (f32[256,256]{1,0:T(8,128)S(1)}, f32[256,256]{1,0:T(8,128)}, u32[]{:S(2)}) copy-start(f32[256,256]{1,0:T(8,128)} %param.14) | copy-start | bytes 786436

commit v18 on v16

--- a/solution.py
+++ b/solution.py
@@ -167,12 +167,13 @@
     place = (placed[:, None] == jnp.arange(nrow)[None, :]).astype(jnp.float32)
     at_edge = (jnp.arange(nrow) < HALO) | (jnp.arange(nrow) >= nrow - HALO)
 
+    rows = jnp.stack([jnp.concatenate([f[mid], g[mid]], axis=0)
+                      for k in range(2) for f, g in zip(first[k], last[k])])
+    edges = lax.dot_general(rows, place, (((1,), (0,)), ((), ())), precision=highest)
+
     def assemble(k):
-        rows = jnp.stack([jnp.concatenate([f[mid], g[mid]], axis=0)
-                          for f, g in zip(first[k], last[k])])
-        edge = lax.dot_general(rows, place, (((1,), (0,)), ((), ())), precision=highest)
-        return jnp.stack([jnp.where(at_edge, edge[i], f) for i, f in enumerate((pred, adj)[k])],
-                         axis=1)
+        return jnp.stack([jnp.where(at_edge, edges[k * nfield + i], f)
+                          for i, f in enumerate((pred, adj)[k])], axis=1)
 
     predicted_final = lax.dynamic_slice_in_dim(assemble(0), col_start, block_cols, 0)
     projected = jnp.sum(ens * assemble(1)[None], axis=2)

time: 60.3 us -> 60.1 us (level)
  no operation moved by 1% of the time
where the time goes in v18:
time: 60.1 us; the launch traced here: 59.7 us
  waiting for transfers between devices  20.4 us (34%)
  local copies, waits for them, and re-layouts  14 us (23%)
  starting transfers between devices  8.23 us (14%)
  matrix products  7.56 us (13%)
  Pallas kernels  4.53 us (8%)
  other arithmetic  3.82 us (6%)
  between operations  1.22 us (2%)
    ppermute x3, waiting for transfers between devices, member_gather(): got = lax.ppermute(acc, 'member', shift)  16.4 us
    unnamed x30, local copies, waits for them, and re-layouts  10.9 us
    pallas_call x1, Pallas kernels, block_dynamics(): pl.pallas_call(block_kernel, out_shape=(out, out), in_specs=[vmem] * 5, o...  4.53 us
    ppermute x3, waiting for transfers between devices, member_scatter(): acc = acc + lax.ppermute(sent, 'member', shift)  3.95 us
    ppermute x3, starting transfers between devices, member_scatter(): acc = acc + lax.ppermute(sent, 'member', shift)  3.77 us
    dot_general x2, matrix products, ends(): lax.dot_general(select, jnp.stack(planes), (((1,), (2,)), ((), ())), prec...  3.06 us
    ppermute x1, starting transfers between devices, shift_rows(): before = lax.ppermute(hi, 'tile', up)  2.15 us
    dot_general x1, matrix products, body(): localized = lax.dot_general(cols_b, alpha, batched(2, 1), precision=high)  1.84 us
  transfers between devices with their start and end apart: 8, of which 5 were waited for; matrix products, arithmetic and copies ran while one was open for 22% of the time, Pallas kernels for 8%

profile of v18, /device:TPU:11, one launch (start us, length us, event | category | flops | bytes accessed | tf_op | source)
XLA Modules:
  0.0 59.7 jit_solution(12677477777552110134)
XLA Ops:
  0.7 1.8 %fusion.13 = f32[3,256,256]{2,1,0:T(8,128)S(1)} fusion(f32[3,256,256]{2,1,0:T(8,128)} %param.8, f32[256,256]{1,0:T(8,128)} %param.14), kind=kOutput, calls=%fused_computation.40 | convolution fusion | flops 301989888 | bytes 1835008 | tf_op jit(solution)/shard_map/dot_general | solution.py:127
  3.4 0.8 %dynamic-slice_bitcast_fusion.2 = (f32[192,256]{1,0:T(8,128)}, f32[192,256]{1,0:T(8,128)}, f32[192,256]{1,0:T(8,128)}) fusion(f32[4,192,256]{2,1,0:T(8,128)S(1)} %bitcast.221, s32[]{:T(128)S(6)} %select_n.105, s32[]{:T(128)S(6)} %select_n.109, s32[]{:T(128)S(6)} %select_n.107), kind=kLoop, calls=%fused_computation.77 | loop fusion | bytes 1179660 | tf_op jit(solution)/shard_map/jit(dynamic_index_in_dim)/squeeze | solution.py:79
  4.2 1.3 %collective-permute-start = (f32[192,256]{1,0:T(8,128)}, f32[192,256]{1,0:T(8,128)}, u32[]{:S(2)}, u32[]{:S(2)}) collective-permute-start(f32[192,256]{1,0:T(8,128)} %get-tuple-element.36), channel_id=1, source_target_pairs={{0,1},{1,2},{2,3},{3,0},{4,5},{5,6},{6,7},{7,4},{8,9},{9,10},{10,1... | collective-permute-start | bytes 589832 | tf_op jit(solution)/shard_map/ppermute | solution.py:80
  5.5 1.0 %collective-permute-start.1 = (f32[192,256]{1,0:T(8,128)}, f32[192,256]{1,0:T(8,128)}, u32[]{:S(2)}, u32[]{:S(2)}) collective-permute-start(f32[192,256]{1,0:T(8,128)} %get-tuple-element.38), channel_id=1, source_target_pairs={{0,2},{1,3},{2,0},{3,1},{4,6},{5,7},{6,4},{7,5},{8,10},{9,11},{10,... | collective-permute-start | bytes 589832 | tf_op jit(solution)/shard_map/ppermute | solution.py:80
  6.5 1.5 %collective-permute-start.2 = (f32[192,256]{1,0:T(8,128)}, f32[192,256]{1,0:T(8,128)}, u32[]{:S(2)}, u32[]{:S(2)}) collective-permute-start(f32[192,256]{1,0:T(8,128)} %get-tuple-element.37), channel_id=1, source_target_pairs={{0,3},{1,0},{2,1},{3,2},{4,7},{5,4},{6,5},{7,6},{8,11},{9,8},{10,9... | collective-permute-start | bytes 589832 | tf_op jit(solution)/shard_map/ppermute | solution.py:80
  8.0 1.1 %copy.19 = f32[3,256,256]{1,2,0:T(8,128)} copy(f32[3,256,256]{2,1,0:T(8,128)S(1)} %copy-done.3) | data formatting | bytes 1572864 | tf_op args[0]
  9.2 1.8 %bitcast_dynamic-update-slice_fusion.6 = f32[7,256,256]{2,1,0:T(8,128)} fusion(f32[256,3,256]{2,0,1:T(8,128)} %param.11), kind=kLoop, calls=%fused_computation.63 | loop fusion | bytes 524288
  10.9 1.7 %bitcast_dynamic-update-slice_fusion.5 = f32[7,256,256]{2,1,0:T(8,128)} fusion(f32[7,256,256]{2,1,0:T(8,128)} %bitcast_dynamic-update-slice_fusion.6, f32[256,3,256]{2,0,1:T(8,128)} %param.11), kind=kLoop, calls=%fused_computation.62 | loop fusion | bytes 524288
  12.6 1.7 %bitcast_dynamic-update-slice_fusion.4 = f32[7,256,256]{2,1,0:T(8,128)} fusion(f32[7,256,256]{2,1,0:T(8,128)} %bitcast_dynamic-update-slice_fusion.5, f32[256,3,256]{2,0,1:T(8,128)} %param.11), kind=kLoop, calls=%fused_computation.61 | loop fusion | bytes 524288
  14.3 1.7 %bitcast_dynamic-update-slice_fusion.3 = f32[7,256,256]{2,1,0:T(8,128)} fusion(f32[7,256,256]{2,1,0:T(8,128)} %bitcast_dynamic-update-slice_fusion.4, f32[256,3,256]{2,0,1:T(8,128)} %param.12), kind=kLoop, calls=%fused_computation.60 | loop fusion | bytes 524288
  16.0 0.7 %bitcast_dynamic-update-slice_fusion.2 = f32[7,256,256]{2,1,0:T(8,128)} fusion(f32[7,256,256]{2,1,0:T(8,128)} %bitcast_dynamic-update-slice_fusion.3, f32[256,3,256]{2,0,1:T(8,128)S(1)} %copy-done.5), kind=kLoop, calls=%fused_computation.59 | loop fusion | bytes 524288
  18.2 2.5 %convolution_bitcast_fusion.1 = f32[7,32,256]{2,1,0:T(8,128)S(1)} fusion(f32[7,256,256]{2,1,0:T(8,128)} %bitcast_dynamic-update-slice_fusion, s32[32]{0:T(128)S(1)} %pad_add_fusion), kind=kOutput, calls=%fused_computation.24 | convolution fusion | flops 176168960 | bytes 2064512 | tf_op jit(solution)/shard_map/dot_general | solution.py:141
  20.9 1.1 %collective-permute-done.1 = f32[192,256]{1,0:T(8,128)} collective-permute-done((f32[192,256]{1,0:T(8,128)}, f32[192,256]{1,0:T(8,128)}, u32[]{:S(2)}, u32[]{:S(2)}) %collective-permute-start.1) | collective-permute-done | bytes 196640 | tf_op jit(solution)/shard_map/ppermute | solution.py:80
  22.0 2.8 %collective-permute-done.2 = f32[192,256]{1,0:T(8,128)} collective-permute-done((f32[192,256]{1,0:T(8,128)}, f32[192,256]{1,0:T(8,128)}, u32[]{:S(2)}, u32[]{:S(2)}) %collective-permute-start.2) | collective-permute-done | bytes 196640 | tf_op jit(solution)/shard_map/ppermute | solution.py:80
  24.8 1.2 %fusion.24 = f32[192,256]{1,0:T(8,128)S(1)} fusion(f32[192,256]{1,0:T(8,128)} %collective-permute-done.2, f32[192,256]{1,0:T(8,128)} %collective-permute-done.1, f32[192,256]{1,0:T(8,128)} %collective-permute-done, f32[4,192,256]{2,1,0:T(8,128)S(1)} %bitcast.222, s32[]{:T(128)S(6)} %select_n.103), kind=kLoop, calls=%fused_computation.74 | loop fusion | flops 147456 | bytes 983044 | tf_op jit(solution)/shard_map/add | solution.py:80
  26.4 1.4 %collective-permute-start.5 = (f32[192,256]{1,0:T(8,128)S(1)}, f32[192,256]{1,0:T(8,128)S(1)}, u32[]{:S(2)}, u32[]{:S(2)}) collective-permute-start(f32[192,256]{1,0:T(8,128)S(1)} %fusion.24), channel_id=1, source_target_pairs={{0,3},{1,0},{2,1},{3,2},{4,7},{5,4},{6,5},{7,6},{8,11},{9,8},{10,9... | collective-permute-start | bytes 589832 | tf_op jit(solution)/shard_map/ppermute | solution.py:91
  27.9 4.1 %collective-permute-done.3 = f32[192,256]{1,0:T(8,128)S(1)} collective-permute-done((f32[192,256]{1,0:T(8,128)S(1)}, f32[192,256]{1,0:T(8,128)S(1)}, u32[]{:S(2)}, u32[]{:S(2)}) %collective-permute-start.3) | collective-permute-done | bytes 196640 | tf_op jit(solution)/shard_map/ppermute | solution.py:91
  32.1 10.7 %collective-permute-done.4 = f32[192,256]{1,0:T(8,128)S(1)} collective-permute-done((f32[192,256]{1,0:T(8,128)S(1)}, f32[192,256]{1,0:T(8,128)S(1)}, u32[]{:S(2)}, u32[]{:S(2)}) %collective-permute-start.4) | collective-permute-done | bytes 196640 | tf_op jit(solution)/shard_map/ppermute | solution.py:91
  42.8 1.5 %collective-permute-done.5 = f32[192,256]{1,0:T(8,128)S(1)} collective-permute-done((f32[192,256]{1,0:T(8,128)S(1)}, f32[192,256]{1,0:T(8,128)S(1)}, u32[]{:S(2)}, u32[]{:S(2)}) %collective-permute-start.5) | collective-permute-done | bytes 196640 | tf_op jit(solution)/shard_map/ppermute | solution.py:91
  45.8 2.2 %collective-permute-start.6 = (f32[10,8,256]{2,1,0:T(8,128)S(1)}, f32[10,8,256]{2,1,0:T(8,128)S(1)}, u32[]{:S(2)}, u32[]{:S(2)}) collective-permute-start(f32[10,8,256]{2,1,0:T(8,128)S(1)} %pad_maximum_fusion.2), channel_id=1, source_target_pairs={{0,4},{4,8},{8,12},{12,16},{16,20},{20,24},{24,28},{28,0},{1,5},{5... | collective-permute-start | bytes 245768 | tf_op jit(solution)/shard_map/ppermute | solution.py:18
  48.0 4.5 %shard_map.95 = (f32[3,256,256]{2,1,0:T(8,128)}, f32[3,256,256]{2,1,0:T(8,128)}) custom-call(f32[3,256,256]{2,1,0:T(8,128)} %bitcast.225, f32[3,256,256]{2,1,0:T(8,128)} %bitcast.220, f32[3,256,256]{2,1,0:T(8,128)} %bitcast.223, f32[3,256,256]{2,1,0:T(8,128)} %bitcast.224, f32[256,256]{1,0:T(8,128)} %dep_ref.1), custom_call_target="tpu_custom_call" | custom-call | flops 23592960 | bytes 5767168 | tf_op jit(solution)/shard_map/pallas_call | solution.py:60
  55.0 0.8 %fusion.86 = f32[6,256,256]{2,1,0:T(8,128)S(1)} fusion(f32[6,16,256]{2,1,0:T(8,128)S(1)} %constant_dynamic-update-slice_fusion, s32[16]{0:T(128)S(1)} %pad_add_fusion.1), kind=kOutput, calls=%fused_computation.170 | convolution fusion | flops 75501568 | bytes 1671232 | tf_op jit(solution)/shard_map/dot_general | solution.py:172
  56.4 0.8 %fusion.8 = f32[3,256,256]{1,2,0:T(8,128)S(1)} fusion(f32[3,256,256]{2,1,0:T(8,128)S(1)} %fusion.1, f32[256,256]{1,0:T(8,128)S(1)} %copy-done), kind=kOutput, calls=%fused_computation.35 | convolution fusion | flops 301989888 | bytes 1835008 | tf_op jit(solution)/shard_map/dot_general | solution.py:180
  57.9 1.1 %copy.20 = f32[3,256,256]{2,1,0:T(8,128)} copy(f32[3,256,256]{1,2,0:T(8,128)S(1)} %fusion.2) | data formatting | bytes 1572864
  (112 shorter events, 8.4 us)
Async XLA Ops:
  0.6 1.9 %copy-start = (f32[256,256]{1,0:T(8,128)S(1)}, f32[256,256]{1,0:T(8,128)}, u32[]{:S(2)}) copy-start(f32[256,256]{1,0:T(8,128)} %param.15) | copy-start | bytes 786436
  0.7 2.4 %copy-start.2 = (bf16[3,256,3,256]{3,1,2,0:T(8,128)(2,1)S(1)}, bf16[3,256,3,256]{3,1,2,0:T(8,128)(2,1)}, u32[]{:S(2)}) copy-start(bf16[3,256,3,256]{3,1,2,0:T(8,128)(2,1)} %param.9) | copy-start | bytes 3538948
  3.1 4.9 %copy-start.3 = (f32[3,256,256]{2,1,0:T(8,128)S(1)}, f32[3,256,256]{2,1,0:T(8,128)}, u32[]{:S(2)}) copy-start(f32[3,256,256]{2,1,0:T(8,128)} %param.8) | copy-start | bytes 2359300
  4.2 16.7 %collective-permute-start = (f32[192,256]{1,0:T(8,128)}, f32[192,256]{1,0:T(8,128)}, u32[]{:S(2)}, u32[]{:S(2)}) collective-permute-start(f32[192,256]{1,0:T(8,128)} %get-tuple-element.36), channel_id=1, source_target_pairs={{0,1},{1,2},{2,3},{3,0},{4,5},{5,6},{6,7},{7,4},{8,9},{9,10},{10,1... | collective-permute-start | bytes 589832 | tf_op jit(solution)/shard_map/ppermute | solution.py:80
  5.5 16.5 %collective-permute-start.1 = (f32[192,256]{1,0:T(8,128)}, f32[192,256]{1,0:T(8,128)}, u32[]{:S(2)}, u32[]{:S(2)}) collective-permute-start(f32[192,256]{1,0:T(8,128)} %get-tuple-element.38), channel_id=1, source_target_pairs={{0,2},{1,3},{2,0},{3,1},{4,6},{5,7},{6,4},{7,5},{8,10},{9,11},{10,... | collective-permute-start | bytes 589832 | tf_op jit(solution)/shard_map/ppermute | solution.py:80
  6.5 18.3 %collective-permute-start.2 = (f32[192,256]{1,0:T(8,128)}, f32[192,256]{1,0:T(8,128)}, u32[]{:S(2)}, u32[]{:S(2)}) collective-permute-start(f32[192,256]{1,0:T(8,128)} %get-tuple-element.37), channel_id=1, source_target_pairs={{0,3},{1,0},{2,1},{3,2},{4,7},{5,4},{6,5},{7,6},{8,11},{9,8},{10,9... | collective-permute-start | bytes 589832 | tf_op jit(solution)/shard_map/ppermute | solution.py:80
  9.2 6.8 %copy-start.5 = (f32[256,3,256]{2,0,1:T(8,128)S(1)}, f32[256,3,256]{2,0,1:T(8,128)}, u32[]{:S(2)}) copy-start(f32[256,3,256]{2,0,1:T(8,128)} %param.12) | copy-start | bytes 2359300
  9.2 8.4 %copy-start.8 = (f32[256,256]{1,0:T(8,128)S(1)}, f32[256,256]{1,0:T(8,128)}, u32[]{:S(2)}) copy-start(f32[256,256]{1,0:T(8,128)} %dep_ref.1) | copy-start | bytes 786436
  20.9 23.5 %copy-start.6 = (f32[256,3,256]{2,0,1:T(8,128)S(1)}, f32[256,3,256]{2,0,1:T(8,128)}, u32[]{:S(2)}) copy-start(f32[256,3,256]{2,0,1:T(8,128)} %param.10) | copy-start | bytes 2359300
  26.0 6.0 %collective-permute-start.3 = (f32[192,256]{1,0:T(8,128)S(1)}, f32[192,256]{1,0:T(8,128)S(1)}, u32[]{:S(2)}, u32[]{:S(2)}) collective-permute-start(f32[192,256]{1,0:T(8,128)S(1)} %fusion.24), channel_id=1, source_target_pairs={{0,1},{1,2},{2,3},{3,0},{4,5},{5,6},{6,7},{7,4},{8,9},{9,10},{10,1... | collective-permute-start | bytes 589832 | tf_op jit(solution)/shard_map/ppermute | solution.py:91
  26.1 16.7 %collective-permute-start.4 = (f32[192,256]{1,0:T(8,128)S(1)}, f32[192,256]{1,0:T(8,128)S(1)}, u32[]{:S(2)}, u32[]{:S(2)}) collective-permute-start(f32[192,256]{1,0:T(8,128)S(1)} %fusion.24), channel_id=1, source_target_pairs={{0,2},{1,3},{2,0},{3,1},{4,6},{5,7},{6,4},{7,5},{8,10},{9,11},{10,... | collective-permute-start | bytes 589832 | tf_op jit(solution)/shard_map/ppermute | solution.py:91
  26.4 17.9 %collective-permute-start.5 = (f32[192,256]{1,0:T(8,128)S(1)}, f32[192,256]{1,0:T(8,128)S(1)}, u32[]{:S(2)}, u32[]{:S(2)}) collective-permute-start(f32[192,256]{1,0:T(8,128)S(1)} %fusion.24), channel_id=1, source_target_pairs={{0,3},{1,0},{2,1},{3,2},{4,7},{5,4},{6,5},{7,6},{8,11},{9,8},{10,9... | collective-permute-start | bytes 589832 | tf_op jit(solution)/shard_map/ppermute | solution.py:91
  44.4 0.9 %copy-start.1 = (f32[4,192,256]{2,1,0:T(8,128)}, f32[4,192,256]{2,1,0:T(8,128)S(1)}, u32[]{:S(2)}) copy-start(f32[4,192,256]{2,1,0:T(8,128)S(1)} %bitcast_dynamic-update-slice_fusion.7) | copy-start | bytes 2359300
  45.3 7.2 %collective-permute-start.7 = (f32[10,8,256]{2,1,0:T(8,128)S(1)}, f32[10,8,256]{2,1,0:T(8,128)S(1)}, u32[]{:S(2)}, u32[]{:S(2)}) collective-permute-start(f32[10,8,256]{2,1,0:T(8,128)S(1)} %pad_maximum_fusion.1), channel_id=1, source_target_pairs={{4,0},{8,4},{12,8},{16,12},{20,16},{24,20},{28,24},{0,28},{5,1},{9... | collective-permute-start | bytes 245768 | tf_op jit(solution)/shard_map/ppermute | solution.py:19
  45.8 6.7 %collective-permute-start.6 = (f32[10,8,256]{2,1,0:T(8,128)S(1)}, f32[10,8,256]{2,1,0:T(8,128)S(1)}, u32[]{:S(2)}, u32[]{:S(2)}) collective-permute-start(f32[10,8,256]{2,1,0:T(8,128)S(1)} %pad_maximum_fusion.2), channel_id=1, source_target_pairs={{0,4},{4,8},{8,12},{12,16},{16,20},{20,24},{24,28},{28,0},{1,5},{5... | collective-permute-start | bytes 245768 | tf_op jit(solution)/shard_map/ppermute | solution.py:18
  54.4 1.4 %copy-start.9 = (f32[3,256,256]{2,1,0:T(8,128)S(1)}, f32[3,256,256]{2,1,0:T(8,128)}, u32[]{:S(2)}) copy-start(f32[3,256,256]{2,1,0:T(8,128)} %get-tuple-element.11) | copy-start | bytes 2359300
  54.5 1.4 %copy-start.10 = (f32[3,256,256]{2,1,0:T(8,128)S(1)}, f32[3,256,256]{2,1,0:T(8,128)}, u32[]{:S(2)}) copy-start(f32[3,256,256]{2,1,0:T(8,128)} %get-tuple-element.10) | copy-start | bytes 2359300
  56.2 1.1 %copy-start.4 = (f32[3,256,256]{1,2,0:T(8,128)S(1)}, f32[3,256,256]{1,2,0:T(8,128)}, u32[]{:S(2)}) copy-start(f32[3,256,256]{1,2,0:T(8,128)} %copy.19) | copy-start | bytes 2359300
  56.2 1.2 %copy-start.7 = (f32[256,256]{1,0:T(8,128)S(1)}, f32[256,256]{1,0:T(8,128)}, u32[]{:S(2)}) copy-start(f32[256,256]{1,0:T(8,128)} %param.14) | copy-start | bytes 786436
